TPU v7x, 128 devices: a whole 4x4x4 slice. The times are simulated.
128 devices in a mesh: pb: 8 (over z, y_lo), kv: 16 (over x, y_hi, core).
Axes of the slice: x: 4, y: 4 (y_hi: 2, y_lo: 2; y = y_hi * 2 + y_lo), z: 4, core: 2. Of those that a mesh axis runs over, the one named last changes fastest.
Arguments:
- slab_start: int32 [1], replicated, may hold values from 0 to 12288
- queries: bfloat16 [4096, 4096], P('pb', 'kv'), may hold values from -6 to 6
- keys: bfloat16 [16384, 2048], P('kv'), may hold values from -6 to 6
- values: bfloat16 [16384, 2048], P('kv'), may hold values from -6 to 6
- out_weight: bfloat16 [4096, 4608], P('kv'), may hold values from -0.09375 to 0.09375
Outputs:
- projected: float32 [4096, 4608], P(('pb', 'kv'))
Inputs may be any that keep to these rules, and one draw needn't show every extreme that they name: The slab lies inside the context: slab_start + 4096 <= 16384.
All inputs are finite; a program needn't handle non-finite values.
Results may differ from a plain program's by a relative error of at most 0.01.
Values may be sent and summed in bfloat16 or wider, within the bound.
No kernel may reach another device: no remote copies, remote signals or barrier semaphores. Data moves between devices by JAX's collectives and lax.ppermute only.
A program may use at most 128 MiB of HBM per device.

v0:
```python
import jax
import jax.numpy as jnp
from jax import lax
from jax.experimental import pallas as pl
from jax.experimental.pallas import tpu as pltpu
from jax.sharding import Mesh, PartitionSpec as P

HQ = 32
KVH = 16
HD = 128
CAP = 50
SCALAR = 144
KV = ("kx", "kc")
TQ = 256


def block_kernel(sc_ref, q_ref, k_ref, v_ref, l_ref, acc_ref, l_out, acc_out):
    tq = q_ref.shape[0]
    tk = k_ref.shape[0]
    row_first = sc_ref[0] + (pl.program_id(0) * tq) % sc_ref[2]
    row_last = row_first + tq - 1
    key_first = sc_ref[1]
    key_last = key_first + tk - 1

    def update(masked):
        raw = lax.dot_general(
            q_ref[...], k_ref[...], (((1,), (1,)), ((), ())), preferred_element_type=jnp.float32
        )
        prob = jnp.exp(CAP * jnp.tanh(raw * (SCALAR ** (-0.5) / CAP)))
        if masked:
            q_pos = row_first + lax.broadcasted_iota(jnp.int32, (tq, tk), 0)
            k_pos = key_first + lax.broadcasted_iota(jnp.int32, (tq, tk), 1)
            prob = jnp.where(k_pos <= q_pos, prob, 0.0)
        l_out[...] = l_ref[...] + jnp.sum(prob, axis=1, keepdims=True)
        acc_out[...] = acc_ref[...] + jnp.dot(
            prob.astype(jnp.bfloat16), v_ref[...], preferred_element_type=jnp.float32
        )

    @pl.when(key_first > row_last)
    def _skip():
        l_out[...] = l_ref[...]
        acc_out[...] = acc_ref[...]

    @pl.when(key_last <= row_first)
    def _full():
        update(False)

    @pl.when(jnp.logical_and(key_first <= row_last, key_last > row_first))
    def _diagonal():
        update(True)


def attend_kernel(scalars, q, block, total, summed):
    n_q, hd = q.shape
    n_k = block.shape[1]
    tq = min(TQ, n_q)
    row = lambda i, sc: (i, 0)
    grid_spec = pltpu.PrefetchScalarGridSpec(
        num_scalar_prefetch=1,
        grid=(n_q // tq,),
        in_specs=[
            pl.BlockSpec((tq, hd), row),
            pl.BlockSpec((None, n_k, hd), lambda i, sc: (0, 0, 0)),
            pl.BlockSpec((None, n_k, hd), lambda i, sc: (1, 0, 0)),
            pl.BlockSpec((tq, 1), row),
            pl.BlockSpec((tq, hd), row),
        ],
        out_specs=[
            pl.BlockSpec((tq, 1), row),
            pl.BlockSpec((tq, hd), row),
        ],
    )
    return pl.pallas_call(
        block_kernel,
        grid_spec=grid_spec,
        out_shape=(
            jax.ShapeDtypeStruct(total.shape, jnp.float32),
            jax.ShapeDtypeStruct(summed.shape, jnp.float32),
        ),
        input_output_aliases={4: 0, 5: 1},
        cost_estimate=pl.CostEstimate(
            flops=4 * n_q * n_k * hd,
            transcendentals=2 * n_q * n_k,
            bytes_accessed=2 * (n_q + 2 * n_k) * hd + 8 * n_q * (hd + 1),
        ),
    )(scalars, q, block, block, total, summed)


def by_heads(queries, keys, values, row_first):
    n_kv = lax.axis_size(KV)
    me = lax.axis_index(KV)
    group = HQ // KVH
    rows_dev = queries.shape[0]
    key_dev = keys.shape[0]
    kv_local = keys.shape[1] // (n_kv * HD)
    kv_feat = kv_local * HD
    n_q = kv_local * group * rows_dev
    q_block = queries.reshape(rows_dev, kv_local * group, HD).transpose(1, 0, 2).reshape(n_q, HD)
    total = jnp.zeros((n_q, 1), jnp.float32)
    summed = jnp.zeros((n_q, HD), jnp.float32)
    for shift in range(n_kv):
        dest = (me + shift) % n_kv
        src = (me - shift) % n_kv
        block = jnp.stack(
            (
                lax.dynamic_slice_in_dim(keys, dest * kv_feat, kv_feat, 1),
                lax.dynamic_slice_in_dim(values, dest * kv_feat, kv_feat, 1),
            ),
            axis=0,
        )
        if shift:
            block = lax.ppermute(block, KV, [(j, (j + shift) % n_kv) for j in range(n_kv)])
        scalars = jnp.stack([row_first, src * key_dev, jnp.int32(rows_dev)]).astype(jnp.int32)
        total, summed = attend_kernel(scalars, q_block, block, total, summed)
    mixed = (summed / total).astype(jnp.bfloat16)
    return mixed.reshape(kv_local * group, rows_dev, HD).transpose(1, 0, 2).reshape(rows_dev, n_q // rows_dev * HD)


def per_device(slab_start, queries, keys, values, out_weight):
    rows_dev = queries.shape[0]
    row_first = slab_start[0] + lax.axis_index("pb") * rows_dev
    attended = by_heads(queries, keys, values, row_first)
    partial = jnp.dot(attended, out_weight, preferred_element_type=jnp.float32)
    n_chip = lax.axis_size("kx")
    n_core = lax.axis_size("kc")
    partial = partial.reshape(n_chip, n_core, rows_dev // (n_chip * n_core), partial.shape[1])
    core = lax.axis_index("kc")
    mine = lax.dynamic_index_in_dim(partial, core, 1, keepdims=False)
    theirs = lax.dynamic_index_in_dim(partial, 1 - core, 1, keepdims=False)
    on_chip = mine + lax.ppermute(theirs, "kc", [(0, 1), (1, 0)])
    parts = lax.all_to_all(
        on_chip.astype(jnp.bfloat16), "kx", split_axis=0, concat_axis=0, tiled=True
    )
    return jnp.sum(parts.astype(jnp.float32), axis=0)


def solution(mesh):
    n_pb, n_kv = mesh.devices.shape
    split = Mesh(mesh.devices.reshape(n_pb, n_kv // 2, 2), ("pb", "kx", "kc"))
    in_specs = (P(), P("pb", KV), P(KV, None), P(KV, None), P(KV, None))
    out_specs = P(("pb",) + KV, None)
    return jax.shard_map(
        per_device, mesh=split, in_specs=in_specs, out_specs=out_specs, check_vma=False
    )
```

profile of v0, /device:TPU:120, one launch (start us, length us, event | category | flops | bytes accessed | tf_op | source)
XLA Modules:
  0.0 245.3 jit_solution(12719287546928492303)
XLA Ops:
  0.0 6.7 %dynamic-slice_bitcast_fusion.1 = (bf16[1,1024,128]{2,1,0:T(8,128)(2,1)}, bf16[1,1024,128]{2,1,0:T(8,128)(2,1)}, bf16[1,1024,128]{2,1,0:T(8,128)(2,1)}, bf16[1,1...) fusion(bf16[1024,2048]{1,0:T(8,128)(2,1)} %param.8, ...), kind=kLoop, calls=%fused_computation.24 | loop fusion | bytes 16777280 | tf_op jit(solution)/shard_map/stack | solution.py:104
  8.4 3.4 %collective-permute-start.5 = (bf16[2,1024,128]{2,1,0:T(8,128)(2,1)}, bf16[2,1024,128]{2,1,0:T(8,128)(2,1)}, u32[]{:S(2)}, u32[]{:S(2)}) collective-permute-start(bf16[2,1024,128]{2,1,0:T(8,128)(2,1)} %pad_maximum_fusion.5), channel_id=1, source_target_pairs={{0,10},{1,11},{2,12},{3,13},{4,14},{5,15},{6,0},{7,1},{8,2},{9,3},... | collective-permute-start | bytes 1572872 | tf_op jit(solution)/shard_map/ppermute | solution.py:112
  12.7 2.5 %collective-permute-start.6 = (bf16[2,1024,128]{2,1,0:T(8,128)(2,1)}, bf16[2,1024,128]{2,1,0:T(8,128)(2,1)}, u32[]{:S(2)}, u32[]{:S(2)}) collective-permute-start(bf16[2,1024,128]{2,1,0:T(8,128)(2,1)} %pad_maximum_fusion.6), channel_id=1, source_target_pairs={{0,9},{1,10},{2,11},{3,12},{4,13},{5,14},{6,15},{7,0},{8,1},{9,2},... | collective-permute-start | bytes 1572872 | tf_op jit(solution)/shard_map/ppermute | solution.py:112
  16.1 2.7 %collective-permute-start.7 = (bf16[2,1024,128]{2,1,0:T(8,128)(2,1)}, bf16[2,1024,128]{2,1,0:T(8,128)(2,1)}, u32[]{:S(2)}, u32[]{:S(2)}) collective-permute-start(bf16[2,1024,128]{2,1,0:T(8,128)(2,1)} %pad_maximum_fusion.7), channel_id=1, source_target_pairs={{0,8},{1,9},{2,10},{3,11},{4,12},{5,13},{6,14},{7,15},{8,0},{9,1},... | collective-permute-start | bytes 1572872 | tf_op jit(solution)/shard_map/ppermute | solution.py:112
  43.4 3.4 %collective-permute-start.9 = (bf16[2,1024,128]{2,1,0:T(8,128)(2,1)}, bf16[2,1024,128]{2,1,0:T(8,128)(2,1)S(1)}, u32[]{:S(2)}, u32[]{:S(2)}) collective-permute-start(bf16[2,1024,128]{2,1,0:T(8,128)(2,1)} %pad_maximum_fusion.9), channel_id=1, source_target_pairs={{0,6},{1,7},{2,8},{3,9},{4,10},{5,11},{6,12},{7,13},{8,14},{9,15},... | collective-permute-start | bytes 1572872 | tf_op jit(solution)/shard_map/ppermute | solution.py:112
  49.9 3.3 %collective-permute-start.13 = (bf16[2,1024,128]{2,1,0:T(8,128)(2,1)}, bf16[2,1024,128]{2,1,0:T(8,128)(2,1)}, u32[]{:S(2)}, u32[]{:S(2)}) collective-permute-start(bf16[2,1024,128]{2,1,0:T(8,128)(2,1)} %pad_maximum_fusion.13), channel_id=1, source_target_pairs={{0,2},{1,3},{2,4},{3,5},{4,6},{5,7},{6,8},{7,9},{8,10},{9,11},{10,... | collective-permute-start | bytes 1572872 | tf_op jit(solution)/shard_map/ppermute | solution.py:112
  53.9 11.8 %collective-permute-start.11 = (bf16[2,1024,128]{2,1,0:T(8,128)(2,1)}, bf16[2,1024,128]{2,1,0:T(8,128)(2,1)}, u32[]{:S(2)}, u32[]{:S(2)}) collective-permute-start(bf16[2,1024,128]{2,1,0:T(8,128)(2,1)} %pad_maximum_fusion.11), channel_id=1, source_target_pairs={{0,4},{1,5},{2,6},{3,7},{4,8},{5,9},{6,10},{7,11},{8,12},{9,13},{1... | collective-permute-start | bytes 1572872 | tf_op jit(solution)/shard_map/ppermute | solution.py:112
  68.0 9.5 %collective-permute-done.9.k_ref.v_ref = bf16[2,1024,128]{2,1,0:T(8,128)(2,1)S(1)} collective-permute-done((bf16[2,1024,128]{2,1,0:T(8,128)(2,1)}, bf16[2,1024,128]{2,1,0:T(8,128)(2,1)S(1)}, u32[]{:S(2)}, u32[]{:S(2)}) %collective-permute-start.9) | collective-permute-done | bytes 524320 | tf_op jit(solution)/shard_map/ppermute | solution.py:112
  77.5 4.0 %collective-permute-start.4 = (bf16[2,1024,128]{2,1,0:T(8,128)(2,1)}, bf16[2,1024,128]{2,1,0:T(8,128)(2,1)}, u32[]{:S(2)}, u32[]{:S(2)}) collective-permute-start(bf16[2,1024,128]{2,1,0:T(8,128)(2,1)} %pad_maximum_fusion.4), channel_id=1, source_target_pairs={{0,11},{1,12},{2,13},{3,14},{4,15},{5,0},{6,1},{7,2},{8,3},{9,4},{... | collective-permute-start | bytes 1572872 | tf_op jit(solution)/shard_map/ppermute | solution.py:112
  83.1 5.6 %shard_map.55 = (f32[1024,1]{1,0:T(8,128)}, f32[1024,128]{1,0:T(8,128)}) custom-call(s32[3]{0:T(128)} %pad_add_fusion.sc_ref, bf16[1024,128]{1,0:T(8,128)(2,1)} %bitcast.107, bf16[2,1024,128]{2,1,0:T(8,128)(2,1)} %pad_maximum_fusion.15.k_ref.v_ref, ...), custom_call_target="tpu_custom_call", output_to_operand_aliasing={{0}: (4, {}), {1}: (5, {})} | custom-call | flops 536870912 | bytes 1843200 | tf_op jit(solution)/shard_map/pallas_call | solution.py:73
  88.9 5.6 %shard_map.56 = (f32[1024,1]{1,0:T(8,128)}, f32[1024,128]{1,0:T(8,128)}) custom-call(s32[3]{0:T(128)} %pad_add_fusion.1.sc_ref, bf16[1024,128]{1,0:T(8,128)(2,1)} %bitcast.108, bf16[2,1024,128]{2,1,0:T(8,128)(2,1)} %collective-permute-done.14.k_ref.v_ref, ...), custom_call_target="tpu_custom_call", output_to_operand_aliasing={{0}: (4, {}), {1}: (5, {})} | custom-call | flops 536870912 | bytes 1843200 | tf_op jit(solution)/shard_map/pallas_call | solution.py:73
  94.5 7.2 %collective-permute-done.13.k_ref.v_ref = bf16[2,1024,128]{2,1,0:T(8,128)(2,1)} collective-permute-done((bf16[2,1024,128]{2,1,0:T(8,128)(2,1)}, bf16[2,1024,128]{2,1,0:T(8,128)(2,1)}, u32[]{:S(2)}, u32[]{:S(2)}) %collective-permute-start.13) | collective-permute-done | bytes 524320 | tf_op jit(solution)/shard_map/ppermute | solution.py:112
  101.7 5.6 %shard_map.57 = (f32[1024,1]{1,0:T(8,128)}, f32[1024,128]{1,0:T(8,128)}) custom-call(s32[3]{0:T(128)} %pad_add_fusion.2.sc_ref, bf16[1024,128]{1,0:T(8,128)(2,1)} %bitcast.109, bf16[2,1024,128]{2,1,0:T(8,128)(2,1)} %collective-permute-done.13.k_ref.v_ref, ...), custom_call_target="tpu_custom_call", output_to_operand_aliasing={{0}: (4, {}), {1}: (5, {})} | custom-call | flops 536870912 | bytes 1843200 | tf_op jit(solution)/shard_map/pallas_call | solution.py:73
  107.3 4.9 %collective-permute-start.1 = (bf16[2,1024,128]{2,1,0:T(8,128)(2,1)}, bf16[2,1024,128]{2,1,0:T(8,128)(2,1)}, u32[]{:S(2)}, u32[]{:S(2)}) collective-permute-start(bf16[2,1024,128]{2,1,0:T(8,128)(2,1)} %pad_maximum_fusion.1), channel_id=1, source_target_pairs={{0,14},{1,15},{2,0},{3,1},{4,2},{5,3},{6,4},{7,5},{8,6},{9,7},{10,... | collective-permute-start | bytes 1572872 | tf_op jit(solution)/shard_map/ppermute | solution.py:112
  112.2 4.4 %shard_map.58 = (f32[1024,1]{1,0:T(8,128)}, f32[1024,128]{1,0:T(8,128)}) custom-call(s32[3]{0:T(128)} %pad_add_fusion.3.sc_ref, bf16[1024,128]{1,0:T(8,128)(2,1)} %bitcast.110, bf16[2,1024,128]{2,1,0:T(8,128)(2,1)} %collective-permute-done.12.k_ref.v_ref, ...), custom_call_target="tpu_custom_call", output_to_operand_aliasing={{0}: (4, {}), {1}: (5, {})} | custom-call | flops 536870912 | bytes 1843200 | tf_op jit(solution)/shard_map/pallas_call | solution.py:73
  116.7 3.1 %collective-permute-start = (bf16[2,1024,128]{2,1,0:T(8,128)(2,1)}, bf16[2,1024,128]{2,1,0:T(8,128)(2,1)}, u32[]{:S(2)}, u32[]{:S(2)}) collective-permute-start(bf16[2,1024,128]{2,1,0:T(8,128)(2,1)} %pad_maximum_fusion), channel_id=1, source_target_pairs={{0,15},{1,0},{2,1},{3,2},{4,3},{5,4},{6,5},{7,6},{8,7},{9,8},{10,9... | collective-permute-start | bytes 1572872 | tf_op jit(solution)/shard_map/ppermute | solution.py:112
  119.7 4.6 %shard_map.59 = (f32[1024,1]{1,0:T(8,128)}, f32[1024,128]{1,0:T(8,128)}) custom-call(s32[3]{0:T(128)} %pad_add_fusion.4.sc_ref, bf16[1024,128]{1,0:T(8,128)(2,1)} %bitcast.111, bf16[2,1024,128]{2,1,0:T(8,128)(2,1)} %collective-permute-done.11.k_ref.v_ref, ...), custom_call_target="tpu_custom_call", output_to_operand_aliasing={{0}: (4, {}), {1}: (5, {})} | custom-call | flops 536870912 | bytes 1843200 | tf_op jit(solution)/shard_map/pallas_call | solution.py:73
  124.4 4.4 %shard_map.60 = (f32[1024,1]{1,0:T(8,128)}, f32[1024,128]{1,0:T(8,128)}) custom-call(s32[3]{0:T(128)} %pad_add_fusion.5.sc_ref, bf16[1024,128]{1,0:T(8,128)(2,1)} %bitcast.112, bf16[2,1024,128]{2,1,0:T(8,128)(2,1)} %collective-permute-done.10.k_ref.v_ref, ...), custom_call_target="tpu_custom_call", output_to_operand_aliasing={{0}: (4, {}), {1}: (5, {})} | custom-call | flops 536870912 | bytes 1843200 | tf_op jit(solution)/shard_map/pallas_call | solution.py:73
  128.8 5.1 %shard_map.61 = (f32[1024,1]{1,0:T(8,128)}, f32[1024,128]{1,0:T(8,128)}) custom-call(s32[3]{0:T(128)} %pad_add_fusion.6.sc_ref, bf16[1024,128]{1,0:T(8,128)(2,1)} %bitcast.113, bf16[2,1024,128]{2,1,0:T(8,128)(2,1)} %copy-done.14, bf16[2,1024,128]{2,1,0:T(8,128)(2,1)} %copy-done.14, ...), custom_call_target="tpu_custom_call", output_to_operand_aliasing={{0}: (4, {}), {1}: (5, {})} | custom-call | flops 536870912 | bytes 1843200 | tf_op jit(solution)/shard_map/pallas_call | solution.py:73
  133.9 5.7 %shard_map.62 = (f32[1024,1]{1,0:T(8,128)}, f32[1024,128]{1,0:T(8,128)}) custom-call(s32[3]{0:T(128)} %pad_add_fusion.7.sc_ref, bf16[1024,128]{1,0:T(8,128)(2,1)} %bitcast.114, bf16[2,1024,128]{2,1,0:T(8,128)(2,1)} %collective-permute-done.8.k_ref.v_ref, ...), custom_call_target="tpu_custom_call", output_to_operand_aliasing={{0}: (4, {}), {1}: (5, {})} | custom-call | flops 536870912 | bytes 1843200 | tf_op jit(solution)/shard_map/pallas_call | solution.py:73
  139.6 5.6 %shard_map.63 = (f32[1024,1]{1,0:T(8,128)}, f32[1024,128]{1,0:T(8,128)}) custom-call(s32[3]{0:T(128)} %pad_add_fusion.8.sc_ref, bf16[1024,128]{1,0:T(8,128)(2,1)} %bitcast.115, bf16[2,1024,128]{2,1,0:T(8,128)(2,1)} %collective-permute-done.7.k_ref.v_ref, ...), custom_call_target="tpu_custom_call", output_to_operand_aliasing={{0}: (4, {}), {1}: (5, {})} | custom-call | flops 536870912 | bytes 1843200 | tf_op jit(solution)/shard_map/pallas_call | solution.py:73
  145.2 5.6 %shard_map.64 = (f32[1024,1]{1,0:T(8,128)}, f32[1024,128]{1,0:T(8,128)}) custom-call(s32[3]{0:T(128)} %pad_add_fusion.9.sc_ref, bf16[1024,128]{1,0:T(8,128)(2,1)} %bitcast.116, bf16[2,1024,128]{2,1,0:T(8,128)(2,1)} %collective-permute-done.6.k_ref.v_ref, ...), custom_call_target="tpu_custom_call", output_to_operand_aliasing={{0}: (4, {}), {1}: (5, {})} | custom-call | flops 536870912 | bytes 1843200 | tf_op jit(solution)/shard_map/pallas_call | solution.py:73
  150.8 5.6 %shard_map.65 = (f32[1024,1]{1,0:T(8,128)}, f32[1024,128]{1,0:T(8,128)}) custom-call(s32[3]{0:T(128)} %pad_add_fusion.10.sc_ref, bf16[1024,128]{1,0:T(8,128)(2,1)} %bitcast.117, bf16[2,1024,128]{2,1,0:T(8,128)(2,1)} %collective-permute-done.5.k_ref.v_ref, ...), custom_call_target="tpu_custom_call", output_to_operand_aliasing={{0}: (4, {}), {1}: (5, {})} | custom-call | flops 536870912 | bytes 1843200 | tf_op jit(solution)/shard_map/pallas_call | solution.py:73
  156.5 5.6 %shard_map.66 = (f32[1024,1]{1,0:T(8,128)}, f32[1024,128]{1,0:T(8,128)}) custom-call(s32[3]{0:T(128)} %pad_add_fusion.11.sc_ref, bf16[1024,128]{1,0:T(8,128)(2,1)} %bitcast.118, bf16[2,1024,128]{2,1,0:T(8,128)(2,1)} %collective-permute-done.4.k_ref.v_ref, ...), custom_call_target="tpu_custom_call", output_to_operand_aliasing={{0}: (4, {}), {1}: (5, {})} | custom-call | flops 536870912 | bytes 1843200 | tf_op jit(solution)/shard_map/pallas_call | solution.py:73
  162.1 5.6 %shard_map.67 = (f32[1024,1]{1,0:T(8,128)}, f32[1024,128]{1,0:T(8,128)}) custom-call(s32[3]{0:T(128)} %pad_add_fusion.12.sc_ref, bf16[1024,128]{1,0:T(8,128)(2,1)} %bitcast.119, bf16[2,1024,128]{2,1,0:T(8,128)(2,1)} %collective-permute-done.3.k_ref.v_ref, ...), custom_call_target="tpu_custom_call", output_to_operand_aliasing={{0}: (4, {}), {1}: (5, {})} | custom-call | flops 536870912 | bytes 1843200 | tf_op jit(solution)/shard_map/pallas_call | solution.py:73
  167.7 5.6 %shard_map.68 = (f32[1024,1]{1,0:T(8,128)}, f32[1024,128]{1,0:T(8,128)}) custom-call(s32[3]{0:T(128)} %pad_add_fusion.13.sc_ref, bf16[1024,128]{1,0:T(8,128)(2,1)} %bitcast.120, bf16[2,1024,128]{2,1,0:T(8,128)(2,1)} %collective-permute-done.2.k_ref.v_ref, ...), custom_call_target="tpu_custom_call", output_to_operand_aliasing={{0}: (4, {}), {1}: (5, {})} | custom-call | flops 536870912 | bytes 1843200 | tf_op jit(solution)/shard_map/pallas_call | solution.py:73
  173.3 5.6 %shard_map.69 = (f32[1024,1]{1,0:T(8,128)}, f32[1024,128]{1,0:T(8,128)}) custom-call(s32[3]{0:T(128)} %pad_add_fusion.14.sc_ref, bf16[1024,128]{1,0:T(8,128)(2,1)} %bitcast.121, bf16[2,1024,128]{2,1,0:T(8,128)(2,1)} %collective-permute-done.1.k_ref.v_ref, ...), custom_call_target="tpu_custom_call", output_to_operand_aliasing={{0}: (4, {}), {1}: (5, {})} | custom-call | flops 536870912 | bytes 1843200 | tf_op jit(solution)/shard_map/pallas_call | solution.py:73
  179.0 5.6 %shard_map.70 = (f32[1024,1]{1,0:T(8,128)}, f32[1024,128]{1,0:T(8,128)}) custom-call(s32[3]{0:T(128)} %pad_add_fusion.15.sc_ref, bf16[1024,128]{1,0:T(8,128)(2,1)} %bitcast.122, bf16[2,1024,128]{2,1,0:T(8,128)(2,1)} %collective-permute-done.k_ref.v_ref, ...), custom_call_target="tpu_custom_call", output_to_operand_aliasing={{0}: (4, {}), {1}: (5, {})} | custom-call | flops 536870912 | bytes 1843200 | tf_op jit(solution)/shard_map/pallas_call | solution.py:73
  189.0 2.8 %dynamic-slice_bitcast_fusion = f32[8,32,4608]{2,1,0:T(8,128)} fusion(f32[8,2,32,4608]{3,2,1,0:T(8,128)S(1)} %fusion.1, s32[]{:T(128)S(6)} %select_n.248), kind=kLoop, calls=%fused_computation.3 | loop fusion | bytes 9437188 | tf_op jit(solution)/shard_map/jit(dynamic_index_in_dim)/squeeze | solution.py:129
  194.0 8.2 %collective-permute-done.15 = f32[8,32,4608]{2,1,0:T(8,128)} collective-permute-done((f32[8,32,4608]{2,1,0:T(8,128)}, f32[8,32,4608]{2,1,0:T(8,128)}, u32[]{:S(2)}, u32[]{:S(2)}) %collective-permute-start.15) | collective-permute-done | bytes 4718624 | tf_op jit(solution)/shard_map/ppermute | solution.py:130
  202.3 4.3 %fusion = bf16[8,32,4608]{2,1,0:T(8,128)(2,1)S(1)} fusion(f32[8,32,4608]{2,1,0:T(8,128)} %collective-permute-done.15, f32[8,2,32,4608]{3,2,1,0:T(8,128)} %copy-done.1, s32[]{:T(128)S(6)} %select_n.247), kind=kLoop, calls=%fused_computation.1 | loop fusion | flops 2359296 | bytes 11796484 | tf_op jit(solution)/shard_map/convert_element_type | solution.py:132
  206.6 37.6 %all_to_all.5 = bf16[8,32,4608]{2,1,0:T(8,128)(2,1)S(1)} all-to-all(bf16[8,32,4608]{2,1,0:T(8,128)(2,1)S(1)} %fusion), channel_id=1, replica_groups=mesh['pb'=8,'kx'=8,'kc'=2] {'kx'}, dimensions={0} | all-to-all | bytes 4718592 | tf_op jit(solution)/shard_map/all_to_all | solution.py:131
  (91 shorter events, 42.8 us)
Async XLA Ops:
  0.0 187.6 %copy-start = (bf16[256,4608]{1,0:T(8,128)(2,1)S(1)}, bf16[256,4608]{1,0:T(8,128)(2,1)}, u32[]{:S(2)}) copy-start(bf16[256,4608]{1,0:T(8,128)(2,1)} %param.9) | copy-start | bytes 7077892
  7.5 35.9 %collective-permute-start.14 = (bf16[2,1024,128]{2,1,0:T(8,128)(2,1)}, bf16[2,1024,128]{2,1,0:T(8,128)(2,1)}, u32[]{:S(2)}, u32[]{:S(2)}) collective-permute-start(bf16[2,1024,128]{2,1,0:T(8,128)(2,1)} %pad_maximum_fusion.14), channel_id=1, source_target_pairs={{0,1},{1,2},{2,3},{3,4},{4,5},{5,6},{6,7},{7,8},{8,9},{9,10},{10,1... | collective-permute-start | bytes 1572872 | tf_op jit(solution)/shard_map/ppermute | solution.py:112
  8.4 38.5 %collective-permute-start.5 = (bf16[2,1024,128]{2,1,0:T(8,128)(2,1)}, bf16[2,1024,128]{2,1,0:T(8,128)(2,1)}, u32[]{:S(2)}, u32[]{:S(2)}) collective-permute-start(bf16[2,1024,128]{2,1,0:T(8,128)(2,1)} %pad_maximum_fusion.5), channel_id=1, source_target_pairs={{0,10},{1,11},{2,12},{3,13},{4,14},{5,15},{6,0},{7,1},{8,2},{9,3},... | collective-permute-start | bytes 1572872 | tf_op jit(solution)/shard_map/ppermute | solution.py:112
  12.7 34.8 %collective-permute-start.6 = (bf16[2,1024,128]{2,1,0:T(8,128)(2,1)}, bf16[2,1024,128]{2,1,0:T(8,128)(2,1)}, u32[]{:S(2)}, u32[]{:S(2)}) collective-permute-start(bf16[2,1024,128]{2,1,0:T(8,128)(2,1)} %pad_maximum_fusion.6), channel_id=1, source_target_pairs={{0,9},{1,10},{2,11},{3,12},{4,13},{5,14},{6,15},{7,0},{8,1},{9,2},... | collective-permute-start | bytes 1572872 | tf_op jit(solution)/shard_map/ppermute | solution.py:112
  16.1 33.9 %collective-permute-start.7 = (bf16[2,1024,128]{2,1,0:T(8,128)(2,1)}, bf16[2,1024,128]{2,1,0:T(8,128)(2,1)}, u32[]{:S(2)}, u32[]{:S(2)}) collective-permute-start(bf16[2,1024,128]{2,1,0:T(8,128)(2,1)} %pad_maximum_fusion.7), channel_id=1, source_target_pairs={{0,8},{1,9},{2,10},{3,11},{4,12},{5,13},{6,14},{7,15},{8,0},{9,1},... | collective-permute-start | bytes 1572872 | tf_op jit(solution)/shard_map/ppermute | solution.py:112
  19.6 34.2 %collective-permute-start.8 = (bf16[2,1024,128]{2,1,0:T(8,128)(2,1)}, bf16[2,1024,128]{2,1,0:T(8,128)(2,1)}, u32[]{:S(2)}, u32[]{:S(2)}) collective-permute-start(bf16[2,1024,128]{2,1,0:T(8,128)(2,1)} %pad_maximum_fusion.8), channel_id=1, source_target_pairs={{0,7},{1,8},{2,9},{3,10},{4,11},{5,12},{6,13},{7,14},{8,15},{9,0},... | collective-permute-start | bytes 1572872 | tf_op jit(solution)/shard_map/ppermute | solution.py:112
  21.6 13.9 %copy-start.10 = (bf16[1,1024,128]{2,1,0:T(8,128)(2,1)S(1)}, bf16[1,1024,128]{2,1,0:T(8,128)(2,1)}, u32[]{:S(2)}) copy-start(bf16[1,1024,128]{2,1,0:T(8,128)(2,1)} %get-tuple-element.89) | copy-start | bytes 786436
  21.6 13.9 %copy-start.11 = (bf16[1,1024,128]{2,1,0:T(8,128)(2,1)S(1)}, bf16[1,1024,128]{2,1,0:T(8,128)(2,1)}, u32[]{:S(2)}) copy-start(bf16[1,1024,128]{2,1,0:T(8,128)(2,1)} %get-tuple-element.112) | copy-start | bytes 786436
  21.6 14.8 %copy-start.8 = (bf16[1,1024,128]{2,1,0:T(8,128)(2,1)S(1)}, bf16[1,1024,128]{2,1,0:T(8,128)(2,1)}, u32[]{:S(2)}) copy-start(bf16[1,1024,128]{2,1,0:T(8,128)(2,1)} %get-tuple-element.90) | copy-start | bytes 786436
  21.6 14.8 %copy-start.9 = (bf16[1,1024,128]{2,1,0:T(8,128)(2,1)S(1)}, bf16[1,1024,128]{2,1,0:T(8,128)(2,1)}, u32[]{:S(2)}) copy-start(bf16[1,1024,128]{2,1,0:T(8,128)(2,1)} %get-tuple-element.111) | copy-start | bytes 786436
  21.6 15.6 %copy-start.6 = (bf16[1,1024,128]{2,1,0:T(8,128)(2,1)S(1)}, bf16[1,1024,128]{2,1,0:T(8,128)(2,1)}, u32[]{:S(2)}) copy-start(bf16[1,1024,128]{2,1,0:T(8,128)(2,1)} %get-tuple-element.95) | copy-start | bytes 786436
  21.6 15.6 %copy-start.7 = (bf16[1,1024,128]{2,1,0:T(8,128)(2,1)S(1)}, bf16[1,1024,128]{2,1,0:T(8,128)(2,1)}, u32[]{:S(2)}) copy-start(bf16[1,1024,128]{2,1,0:T(8,128)(2,1)} %get-tuple-element.106) | copy-start | bytes 786436
  21.6 16.5 %copy-start.4 = (bf16[1,1024,128]{2,1,0:T(8,128)(2,1)S(1)}, bf16[1,1024,128]{2,1,0:T(8,128)(2,1)}, u32[]{:S(2)}) copy-start(bf16[1,1024,128]{2,1,0:T(8,128)(2,1)} %get-tuple-element.96) | copy-start | bytes 786436
  21.7 16.5 %copy-start.5 = (bf16[1,1024,128]{2,1,0:T(8,128)(2,1)S(1)}, bf16[1,1024,128]{2,1,0:T(8,128)(2,1)}, u32[]{:S(2)}) copy-start(bf16[1,1024,128]{2,1,0:T(8,128)(2,1)} %get-tuple-element.105) | copy-start | bytes 786436
  27.9 11.1 %copy-start.2 = (bf16[1,1024,128]{2,1,0:T(8,128)(2,1)S(1)}, bf16[1,1024,128]{2,1,0:T(8,128)(2,1)}, u32[]{:S(2)}) copy-start(bf16[1,1024,128]{2,1,0:T(8,128)(2,1)} %get-tuple-element.97) | copy-start | bytes 786436
  27.9 11.1 %copy-start.3 = (bf16[1,1024,128]{2,1,0:T(8,128)(2,1)S(1)}, bf16[1,1024,128]{2,1,0:T(8,128)(2,1)}, u32[]{:S(2)}) copy-start(bf16[1,1024,128]{2,1,0:T(8,128)(2,1)} %get-tuple-element.104) | copy-start | bytes 786436
  42.6 46.2 %copy-start.13 = (bf16[2,1024,128]{2,1,0:T(8,128)(2,1)S(1)}, bf16[2,1024,128]{2,1,0:T(8,128)(2,1)}, u32[]{:S(2)}) copy-start(bf16[2,1024,128]{2,1,0:T(8,128)(2,1)} %pad_maximum_fusion.3) | copy-start | bytes 1572868
  43.4 34.1 %collective-permute-start.9 = (bf16[2,1024,128]{2,1,0:T(8,128)(2,1)}, bf16[2,1024,128]{2,1,0:T(8,128)(2,1)S(1)}, u32[]{:S(2)}, u32[]{:S(2)}) collective-permute-start(bf16[2,1024,128]{2,1,0:T(8,128)(2,1)} %pad_maximum_fusion.9), channel_id=1, source_target_pairs={{0,6},{1,7},{2,8},{3,9},{4,10},{5,11},{6,12},{7,13},{8,14},{9,15},... | collective-permute-start | bytes 1572872 | tf_op jit(solution)/shard_map/ppermute | solution.py:112
  46.9 41.9 %collective-permute-start.10 = (bf16[2,1024,128]{2,1,0:T(8,128)(2,1)}, bf16[2,1024,128]{2,1,0:T(8,128)(2,1)}, u32[]{:S(2)}, u32[]{:S(2)}) collective-permute-start(bf16[2,1024,128]{2,1,0:T(8,128)(2,1)} %pad_maximum_fusion.10), channel_id=1, source_target_pairs={{0,5},{1,6},{2,7},{3,8},{4,9},{5,10},{6,11},{7,12},{8,13},{9,14},{... | collective-permute-start | bytes 1572872 | tf_op jit(solution)/shard_map/ppermute | solution.py:112
  47.5 59.9 %collective-permute-start.12 = (bf16[2,1024,128]{2,1,0:T(8,128)(2,1)}, bf16[2,1024,128]{2,1,0:T(8,128)(2,1)}, u32[]{:S(2)}, u32[]{:S(2)}) collective-permute-start(bf16[2,1024,128]{2,1,0:T(8,128)(2,1)} %pad_maximum_fusion.12), channel_id=1, source_target_pairs={{0,3},{1,4},{2,5},{3,6},{4,7},{5,8},{6,9},{7,10},{8,11},{9,12},{10... | collective-permute-start | bytes 1572872 | tf_op jit(solution)/shard_map/ppermute | solution.py:112
  49.9 51.8 %collective-permute-start.13 = (bf16[2,1024,128]{2,1,0:T(8,128)(2,1)}, bf16[2,1024,128]{2,1,0:T(8,128)(2,1)}, u32[]{:S(2)}, u32[]{:S(2)}) collective-permute-start(bf16[2,1024,128]{2,1,0:T(8,128)(2,1)} %pad_maximum_fusion.13), channel_id=1, source_target_pairs={{0,2},{1,3},{2,4},{3,5},{4,6},{5,7},{6,8},{7,9},{8,10},{9,11},{10,... | collective-permute-start | bytes 1572872 | tf_op jit(solution)/shard_map/ppermute | solution.py:112
  53.9 62.8 %collective-permute-start.11 = (bf16[2,1024,128]{2,1,0:T(8,128)(2,1)}, bf16[2,1024,128]{2,1,0:T(8,128)(2,1)}, u32[]{:S(2)}, u32[]{:S(2)}) collective-permute-start(bf16[2,1024,128]{2,1,0:T(8,128)(2,1)} %pad_maximum_fusion.11), channel_id=1, source_target_pairs={{0,4},{1,5},{2,6},{3,7},{4,8},{5,9},{6,10},{7,11},{8,12},{9,13},{1... | collective-permute-start | bytes 1572872 | tf_op jit(solution)/shard_map/ppermute | solution.py:112
  77.5 4.0 %copy-start.14 = (bf16[2,1024,128]{2,1,0:T(8,128)(2,1)}, bf16[2,1024,128]{2,1,0:T(8,128)(2,1)S(1)}, u32[]{:S(2)}) copy-start(bf16[2,1024,128]{2,1,0:T(8,128)(2,1)S(1)} %collective-permute-done.9.k_ref.v_ref) | copy-start | bytes 1572868
  77.5 79.0 %collective-permute-start.4 = (bf16[2,1024,128]{2,1,0:T(8,128)(2,1)}, bf16[2,1024,128]{2,1,0:T(8,128)(2,1)}, u32[]{:S(2)}, u32[]{:S(2)}) collective-permute-start(bf16[2,1024,128]{2,1,0:T(8,128)(2,1)} %pad_maximum_fusion.4), channel_id=1, source_target_pairs={{0,11},{1,12},{2,13},{3,14},{4,15},{5,0},{6,1},{7,2},{8,3},{9,4},{... | collective-permute-start | bytes 1572872 | tf_op jit(solution)/shard_map/ppermute | solution.py:112
  82.3 19.4 %copy-start.12 = (bf16[2,1024,128]{2,1,0:T(8,128)(2,1)S(1)}, bf16[2,1024,128]{2,1,0:T(8,128)(2,1)}, u32[]{:S(2)}) copy-start(bf16[2,1024,128]{2,1,0:T(8,128)(2,1)} %pad_maximum_fusion.2) | copy-start | bytes 1572868
  88.8 73.3 %collective-permute-start.3 = (bf16[2,1024,128]{2,1,0:T(8,128)(2,1)S(1)}, bf16[2,1024,128]{2,1,0:T(8,128)(2,1)}, u32[]{:S(2)}, u32[]{:S(2)}) collective-permute-start(bf16[2,1024,128]{2,1,0:T(8,128)(2,1)S(1)} %copy-done.13), channel_id=1, source_target_pairs={{0,12},{1,13},{2,14},{3,15},{4,0},{5,1},{6,2},{7,3},{8,4},{9,5},{1... | collective-permute-start | bytes 1572872 | tf_op jit(solution)/shard_map/ppermute | solution.py:112
  101.7 66.0 %collective-permute-start.2 = (bf16[2,1024,128]{2,1,0:T(8,128)(2,1)S(1)}, bf16[2,1024,128]{2,1,0:T(8,128)(2,1)}, u32[]{:S(2)}, u32[]{:S(2)}) collective-permute-start(bf16[2,1024,128]{2,1,0:T(8,128)(2,1)S(1)} %copy-done.12), channel_id=1, source_target_pairs={{0,13},{1,14},{2,15},{3,0},{4,1},{5,2},{6,3},{7,4},{8,5},{9,6},{10... | collective-permute-start | bytes 1572872 | tf_op jit(solution)/shard_map/ppermute | solution.py:112
  107.3 66.0 %collective-permute-start.1 = (bf16[2,1024,128]{2,1,0:T(8,128)(2,1)}, bf16[2,1024,128]{2,1,0:T(8,128)(2,1)}, u32[]{:S(2)}, u32[]{:S(2)}) collective-permute-start(bf16[2,1024,128]{2,1,0:T(8,128)(2,1)} %pad_maximum_fusion.1), channel_id=1, source_target_pairs={{0,14},{1,15},{2,0},{3,1},{4,2},{5,3},{6,4},{7,5},{8,6},{9,7},{10,... | collective-permute-start | bytes 1572872 | tf_op jit(solution)/shard_map/ppermute | solution.py:112
  116.7 62.3 %collective-permute-start = (bf16[2,1024,128]{2,1,0:T(8,128)(2,1)}, bf16[2,1024,128]{2,1,0:T(8,128)(2,1)}, u32[]{:S(2)}, u32[]{:S(2)}) collective-permute-start(bf16[2,1024,128]{2,1,0:T(8,128)(2,1)} %pad_maximum_fusion), channel_id=1, source_target_pairs={{0,15},{1,0},{2,1},{3,2},{4,3},{5,4},{6,5},{7,6},{8,7},{9,8},{10,9... | collective-permute-start | bytes 1572872 | tf_op jit(solution)/shard_map/ppermute | solution.py:112
  189.0 5.0 %copy-start.1 = (f32[8,2,32,4608]{3,2,1,0:T(8,128)}, f32[8,2,32,4608]{3,2,1,0:T(8,128)S(1)}, u32[]{:S(2)}) copy-start(f32[8,2,32,4608]{3,2,1,0:T(8,128)S(1)} %fusion.1) | copy-start | bytes 28311556
  194.0 8.3 %collective-permute-start.15 = (f32[8,32,4608]{2,1,0:T(8,128)}, f32[8,32,4608]{2,1,0:T(8,128)}, u32[]{:S(2)}, u32[]{:S(2)}) collective-permute-start(f32[8,32,4608]{2,1,0:T(8,128)} %dynamic-slice_bitcast_fusion), channel_id=1, source_target_pairs={{0,1},{1,0},{2,3},{3,2},{4,5},{5,4},{6,7},{7,6},{8,9},{9,8},{10,11... | collective-permute-start | bytes 14155784 | tf_op jit(solution)/shard_map/ppermute | solution.py:130
where the time goes:
time: 247 us; the launch traced here: 245 us
  Pallas kernels  86.2 us (35%)
  starting transfers between devices  42.9 us (17%)
  blocking collectives  37.6 us (15%)
  other arithmetic  35.8 us (14%)
  waiting for transfers between devices  25 us (10%)
  local copies, waits for them, and re-layouts  15.5 us (6%)
    pallas_call x16, Pallas kernels, attend_kernel(): pl.pallas_call(block_kernel, grid_spec=grid_spec, out_shape=(jax.ShapeDty...  86.2 us
    ppermute x15, starting transfers between devices, by_heads(): lax.ppermute(block, KV, [(j, (j + shift) % n_kv) for j in range(n_kv)])  42.9 us
    all_to_all x1, blocking collectives, per_device(): lax.all_to_all(on_chip.astype(jnp.bfloat16), 'kx', split_axis=0, concat_a...  37.6 us
    another operation x16, other arithmetic, by_heads(): jnp.stack((lax.dynamic_slice_in_dim(keys, dest * kv_feat, kv_feat, 1), la...  17.9 us
    ppermute x15, waiting for transfers between devices, by_heads(): lax.ppermute(block, KV, [(j, (j + shift) % n_kv) for j in range(n_kv)])  16.8 us
    another operation x16, other arithmetic, by_heads(): jnp.stack([row_first, src * key_dev, jnp.int32(rows_dev)]).astype(jnp.int32)  9.96 us
    ppermute x1, waiting for transfers between devices, per_device(): on_chip = mine + lax.ppermute(theirs, 'kc', [(0, 1), (1, 0)])  8.25 us
    another operation x1, local copies, waits for them, and re-layouts, by_heads(): jnp.stack((lax.dynamic_slice_in_dim(keys, dest * kv_feat, kv_feat, 1), la...  6.65 us
  transfers between devices with their start and end apart: 16, of which 3 were waited for; matrix products, arithmetic and copies ran while one was open for 12% of the time, Pallas kernels for 33%

commit v1 on v0

--- a/solution.py
+++ b/solution.py
@@ -126,12 +126,17 @@
     partial = partial.reshape(n_chip, n_core, rows_dev // (n_chip * n_core), partial.shape[1])
     core = lax.axis_index("kc")
     mine = lax.dynamic_index_in_dim(partial, core, 1, keepdims=False)
-    theirs = lax.dynamic_index_in_dim(partial, 1 - core, 1, keepdims=False)
-    on_chip = mine + lax.ppermute(theirs, "kc", [(0, 1), (1, 0)])
-    parts = lax.all_to_all(
-        on_chip.astype(jnp.bfloat16), "kx", split_axis=0, concat_axis=0, tiled=True
-    )
-    return jnp.sum(parts.astype(jnp.float32), axis=0)
+    theirs = lax.dynamic_index_in_dim(partial, 1 - core, 1, keepdims=False).astype(jnp.bfloat16)
+    on_chip = mine + lax.ppermute(theirs, "kc", [(0, 1), (1, 0)]).astype(jnp.float32)
+    chip = lax.axis_index("kx")
+    result = lax.dynamic_index_in_dim(on_chip, chip, 0, keepdims=False)
+    for shift in range(1, n_chip):
+        part = lax.dynamic_index_in_dim(on_chip, (chip + shift) % n_chip, 0, keepdims=False)
+        moved = lax.ppermute(
+            part.astype(jnp.bfloat16), "kx", [(k, (k + shift) % n_chip) for k in range(n_chip)]
+        )
+        result = result + moved.astype(jnp.float32)
+    return result
 
 
 def solution(mesh):

time: 247 us -> 252 us (1.020); the launches traced: 245 us -> 256 us
  blocking collectives: 37.6 us -> 0 us
  waiting for transfers between devices: 25 us -> 59 us
  starting transfers between devices: 42.9 us -> 48.3 us
  local copies, waits for them, and re-layouts: 15.5 us -> 20.6 us
  Pallas kernels: 86.2 us -> 88.9 us
    all_to_all x1 -> x0, blocking collectives: 37.6 us -> none  [per_device(): lax.all_to_all(on_chip.astype(jnp.bfloat16), 'kx', split_axis=0, concat_a...]
    ppermute x1 -> x8, waiting for transfers between devices: 8.25 us -> 34.4 us  [the longest x7 29.9 us: per_device(): lax.ppermute(part.astype(jnp.bfloat16), 'kx', [(k, (k + shift) % n_chip)...]
    ppermute x1 -> x8, starting transfers between devices: 0.01 us -> 16.8 us  [the longest x7 15.6 us: per_device(): lax.ppermute(part.astype(jnp.bfloat16), 'kx', [(k, (k + shift) % n_chip)...]
    ppermute x15, starting transfers between devices: 42.9 us -> 31.5 us  [by_heads(): lax.ppermute(block, KV, [(j, (j + shift) % n_kv) for j in range(n_kv)])]
    ppermute x15, waiting for transfers between devices: 16.8 us -> 24.7 us  [by_heads(): lax.ppermute(block, KV, [(j, (j + shift) % n_kv) for j in range(n_kv)])]
    add x0 -> x2, other arithmetic: none -> 6.37 us  [the longest x1 3.6 us: per_device(): mine + lax.ppermute(theirs, 'kc', [(0, 1), (1, 0)]).astype(jnp.float32)]
    unnamed x30 -> x36, local copies, waits for them, and re-layouts: 2.24 us -> 7.45 us
    convert_element_type x1 -> x0, other arithmetic: 4.3 us -> none  [per_device(): on_chip.astype(jnp.bfloat16)]
  transfers between devices with their start and end apart: 16 -> 23, of which waited for: 3 -> 7; matrix products, arithmetic and copies ran while one was open for 12% -> 12% of each run, Pallas kernels for 33% -> 33%
where the time goes in v1:
time: 252 us; the launch traced here: 256 us
  Pallas kernels  88.9 us (35%)
  waiting for transfers between devices  59 us (23%)
  starting transfers between devices  48.3 us (19%)
  other arithmetic  36.8 us (15%)
  local copies, waits for them, and re-layouts  20.6 us (8%)
    pallas_call x16, Pallas kernels, attend_kernel(): pl.pallas_call(block_kernel, grid_spec=grid_spec, out_shape=(jax.ShapeDty...  88.9 us
    ppermute x15, starting transfers between devices, by_heads(): lax.ppermute(block, KV, [(j, (j + shift) % n_kv) for j in range(n_kv)])  31.5 us
    ppermute x7, waiting for transfers between devices, per_device(): lax.ppermute(part.astype(jnp.bfloat16), 'kx', [(k, (k + shift) % n_chip)...  29.9 us
    ppermute x15, waiting for transfers between devices, by_heads(): lax.ppermute(block, KV, [(j, (j + shift) % n_kv) for j in range(n_kv)])  24.7 us
    another operation x16, other arithmetic, by_heads(): jnp.stack((lax.dynamic_slice_in_dim(keys, dest * kv_feat, kv_feat, 1), la...  18 us
    ppermute x7, starting transfers between devices, per_device(): lax.ppermute(part.astype(jnp.bfloat16), 'kx', [(k, (k + shift) % n_chip)...  15.6 us
    another operation x16, other arithmetic, by_heads(): jnp.stack([row_first, src * key_dev, jnp.int32(rows_dev)]).astype(jnp.int32)  9.97 us
    unnamed x36, local copies, waits for them, and re-layouts  7.45 us
  transfers between devices with their start and end apart: 23, of which 7 were waited for; matrix products, arithmetic and copies ran while one was open for 12% of the time, Pallas kernels for 33%

profile of v1, /device:TPU:120, one launch (start us, length us, event | category | flops | bytes accessed | tf_op | source)
XLA Modules:
  0.0 255.9 jit_solution(10391310918117147117)
XLA Ops:
  0.0 6.8 %dynamic-slice_bitcast_fusion = (bf16[1,1024,128]{2,1,0:T(8,128)(2,1)}, bf16[1,1024,128]{2,1,0:T(8,128)(2,1)S(1)}, bf16[1,1024,128]{2,1,0:T(8,128)(2,1)S(1)}, bf...) fusion(bf16[1024,2048]{1,0:T(8,128)(2,1)} %param.8, ...), kind=kLoop, calls=%fused_computation.44 | loop fusion | bytes 16777280 | tf_op jit(solution)/shard_map/stack | solution.py:104
  11.5 3.9 %collective-permute-start.12 = (bf16[2,1024,128]{2,1,0:T(8,128)(2,1)}, bf16[2,1024,128]{2,1,0:T(8,128)(2,1)}, u32[]{:S(2)}, u32[]{:S(2)}) collective-permute-start(bf16[2,1024,128]{2,1,0:T(8,128)(2,1)} %pad_maximum_fusion.12), channel_id=1, source_target_pairs={{0,3},{1,4},{2,5},{3,6},{4,7},{5,8},{6,9},{7,10},{8,11},{9,12},{10... | collective-permute-start | bytes 1572872 | tf_op jit(solution)/shard_map/ppermute | solution.py:112
  40.8 2.8 %collective-permute-start.9 = (bf16[2,1024,128]{2,1,0:T(8,128)(2,1)}, bf16[2,1024,128]{2,1,0:T(8,128)(2,1)S(1)}, u32[]{:S(2)}, u32[]{:S(2)}) collective-permute-start(bf16[2,1024,128]{2,1,0:T(8,128)(2,1)} %pad_maximum_fusion.9), channel_id=1, source_target_pairs={{0,6},{1,7},{2,8},{3,9},{4,10},{5,11},{6,12},{7,13},{8,14},{9,15},... | collective-permute-start | bytes 1572872 | tf_op jit(solution)/shard_map/ppermute | solution.py:112
  43.6 5.5 %collective-permute-start.8 = (bf16[2,1024,128]{2,1,0:T(8,128)(2,1)}, bf16[2,1024,128]{2,1,0:T(8,128)(2,1)}, u32[]{:S(2)}, u32[]{:S(2)}) collective-permute-start(bf16[2,1024,128]{2,1,0:T(8,128)(2,1)} %pad_maximum_fusion.8), channel_id=1, source_target_pairs={{0,7},{1,8},{2,9},{3,10},{4,11},{5,12},{6,13},{7,14},{8,15},{9,0},... | collective-permute-start | bytes 1572872 | tf_op jit(solution)/shard_map/ppermute | solution.py:112
  51.3 10.8 %collective-permute-start.6 = (bf16[2,1024,128]{2,1,0:T(8,128)(2,1)}, bf16[2,1024,128]{2,1,0:T(8,128)(2,1)}, u32[]{:S(2)}, u32[]{:S(2)}) collective-permute-start(bf16[2,1024,128]{2,1,0:T(8,128)(2,1)} %pad_maximum_fusion.6), channel_id=1, source_target_pairs={{0,9},{1,10},{2,11},{3,12},{4,13},{5,14},{6,15},{7,0},{8,1},{9,2},... | collective-permute-start | bytes 1572872 | tf_op jit(solution)/shard_map/ppermute | solution.py:112
  65.2 8.6 %collective-permute-done.9.k_ref.v_ref = bf16[2,1024,128]{2,1,0:T(8,128)(2,1)S(1)} collective-permute-done((bf16[2,1024,128]{2,1,0:T(8,128)(2,1)}, bf16[2,1024,128]{2,1,0:T(8,128)(2,1)S(1)}, u32[]{:S(2)}, u32[]{:S(2)}) %collective-permute-start.9) | collective-permute-done | bytes 524320 | tf_op jit(solution)/shard_map/ppermute | solution.py:112
  76.3 5.6 %shard_map.55 = (f32[1024,1]{1,0:T(8,128)}, f32[1024,128]{1,0:T(8,128)}) custom-call(s32[3]{0:T(128)} %pad_add_fusion.sc_ref, bf16[1024,128]{1,0:T(8,128)(2,1)} %bitcast.133, bf16[2,1024,128]{2,1,0:T(8,128)(2,1)} %pad_maximum_fusion.15.k_ref.v_ref, ...), custom_call_target="tpu_custom_call", output_to_operand_aliasing={{0}: (4, {}), {1}: (5, {})} | custom-call | flops 536870912 | bytes 1843200 | tf_op jit(solution)/shard_map/pallas_call | solution.py:73
  81.9 15.2 %collective-permute-done.8.k_ref.v_ref = bf16[2,1024,128]{2,1,0:T(8,128)(2,1)} collective-permute-done((bf16[2,1024,128]{2,1,0:T(8,128)(2,1)}, bf16[2,1024,128]{2,1,0:T(8,128)(2,1)}, u32[]{:S(2)}, u32[]{:S(2)}) %collective-permute-start.8) | collective-permute-done | bytes 524320 | tf_op jit(solution)/shard_map/ppermute | solution.py:112
  97.1 5.6 %shard_map.56 = (f32[1024,1]{1,0:T(8,128)}, f32[1024,128]{1,0:T(8,128)}) custom-call(s32[3]{0:T(128)} %pad_add_fusion.1.sc_ref, bf16[1024,128]{1,0:T(8,128)(2,1)} %bitcast.134, bf16[2,1024,128]{2,1,0:T(8,128)(2,1)} %collective-permute-done.14.k_ref.v_ref, ...), custom_call_target="tpu_custom_call", output_to_operand_aliasing={{0}: (4, {}), {1}: (5, {})} | custom-call | flops 536870912 | bytes 1843200 | tf_op jit(solution)/shard_map/pallas_call | solution.py:73
  102.8 5.6 %shard_map.57 = (f32[1024,1]{1,0:T(8,128)}, f32[1024,128]{1,0:T(8,128)}) custom-call(s32[3]{0:T(128)} %pad_add_fusion.2.sc_ref, bf16[1024,128]{1,0:T(8,128)(2,1)} %bitcast.135, bf16[2,1024,128]{2,1,0:T(8,128)(2,1)} %collective-permute-done.13.k_ref.v_ref, ...), custom_call_target="tpu_custom_call", output_to_operand_aliasing={{0}: (4, {}), {1}: (5, {})} | custom-call | flops 536870912 | bytes 1843200 | tf_op jit(solution)/shard_map/pallas_call | solution.py:73
  109.5 4.5 %shard_map.58 = (f32[1024,1]{1,0:T(8,128)}, f32[1024,128]{1,0:T(8,128)}) custom-call(s32[3]{0:T(128)} %pad_add_fusion.3.sc_ref, bf16[1024,128]{1,0:T(8,128)(2,1)} %bitcast.136, bf16[2,1024,128]{2,1,0:T(8,128)(2,1)} %collective-permute-done.12.k_ref.v_ref, ...), custom_call_target="tpu_custom_call", output_to_operand_aliasing={{0}: (4, {}), {1}: (5, {})} | custom-call | flops 536870912 | bytes 1843200 | tf_op jit(solution)/shard_map/pallas_call | solution.py:73
  114.0 3.2 %collective-permute-start = (bf16[2,1024,128]{2,1,0:T(8,128)(2,1)}, bf16[2,1024,128]{2,1,0:T(8,128)(2,1)}, u32[]{:S(2)}, u32[]{:S(2)}) collective-permute-start(bf16[2,1024,128]{2,1,0:T(8,128)(2,1)} %pad_maximum_fusion), channel_id=1, source_target_pairs={{0,15},{1,0},{2,1},{3,2},{4,3},{5,4},{6,5},{7,6},{8,7},{9,8},{10,9... | collective-permute-start | bytes 1572872 | tf_op jit(solution)/shard_map/ppermute | solution.py:112
  117.2 5.9 %shard_map.59 = (f32[1024,1]{1,0:T(8,128)}, f32[1024,128]{1,0:T(8,128)}) custom-call(s32[3]{0:T(128)} %pad_add_fusion.4.sc_ref, bf16[1024,128]{1,0:T(8,128)(2,1)} %bitcast.137, bf16[2,1024,128]{2,1,0:T(8,128)(2,1)} %collective-permute-done.11.k_ref.v_ref, ...), custom_call_target="tpu_custom_call", output_to_operand_aliasing={{0}: (4, {}), {1}: (5, {})} | custom-call | flops 536870912 | bytes 1843200 | tf_op jit(solution)/shard_map/pallas_call | solution.py:73
  123.0 5.6 %shard_map.60 = (f32[1024,1]{1,0:T(8,128)}, f32[1024,128]{1,0:T(8,128)}) custom-call(s32[3]{0:T(128)} %pad_add_fusion.5.sc_ref, bf16[1024,128]{1,0:T(8,128)(2,1)} %bitcast.138, bf16[2,1024,128]{2,1,0:T(8,128)(2,1)} %collective-permute-done.10.k_ref.v_ref, ...), custom_call_target="tpu_custom_call", output_to_operand_aliasing={{0}: (4, {}), {1}: (5, {})} | custom-call | flops 536870912 | bytes 1843200 | tf_op jit(solution)/shard_map/pallas_call | solution.py:73
  128.6 5.6 %shard_map.61 = (f32[1024,1]{1,0:T(8,128)}, f32[1024,128]{1,0:T(8,128)}) custom-call(s32[3]{0:T(128)} %pad_add_fusion.6.sc_ref, bf16[1024,128]{1,0:T(8,128)(2,1)} %bitcast.139, bf16[2,1024,128]{2,1,0:T(8,128)(2,1)} %copy-done.17, bf16[2,1024,128]{2,1,0:T(8,128)(2,1)} %copy-done.17, ...), custom_call_target="tpu_custom_call", output_to_operand_aliasing={{0}: (4, {}), {1}: (5, {})} | custom-call | flops 536870912 | bytes 1843200 | tf_op jit(solution)/shard_map/pallas_call | solution.py:73
  134.2 5.6 %shard_map.62 = (f32[1024,1]{1,0:T(8,128)}, f32[1024,128]{1,0:T(8,128)}) custom-call(s32[3]{0:T(128)} %pad_add_fusion.7.sc_ref, bf16[1024,128]{1,0:T(8,128)(2,1)} %bitcast.140, bf16[2,1024,128]{2,1,0:T(8,128)(2,1)} %collective-permute-done.8.k_ref.v_ref, ...), custom_call_target="tpu_custom_call", output_to_operand_aliasing={{0}: (4, {}), {1}: (5, {})} | custom-call | flops 536870912 | bytes 1843200 | tf_op jit(solution)/shard_map/pallas_call | solution.py:73
  139.9 5.6 %shard_map.63 = (f32[1024,1]{1,0:T(8,128)}, f32[1024,128]{1,0:T(8,128)}) custom-call(s32[3]{0:T(128)} %pad_add_fusion.8.sc_ref, bf16[1024,128]{1,0:T(8,128)(2,1)} %bitcast.141, bf16[2,1024,128]{2,1,0:T(8,128)(2,1)} %collective-permute-done.7.k_ref.v_ref, ...), custom_call_target="tpu_custom_call", output_to_operand_aliasing={{0}: (4, {}), {1}: (5, {})} | custom-call | flops 536870912 | bytes 1843200 | tf_op jit(solution)/shard_map/pallas_call | solution.py:73
  145.5 5.6 %shard_map.64 = (f32[1024,1]{1,0:T(8,128)}, f32[1024,128]{1,0:T(8,128)}) custom-call(s32[3]{0:T(128)} %pad_add_fusion.9.sc_ref, bf16[1024,128]{1,0:T(8,128)(2,1)} %bitcast.142, bf16[2,1024,128]{2,1,0:T(8,128)(2,1)} %collective-permute-done.6.k_ref.v_ref, ...), custom_call_target="tpu_custom_call", output_to_operand_aliasing={{0}: (4, {}), {1}: (5, {})} | custom-call | flops 536870912 | bytes 1843200 | tf_op jit(solution)/shard_map/pallas_call | solution.py:73
  151.1 5.6 %shard_map.65 = (f32[1024,1]{1,0:T(8,128)}, f32[1024,128]{1,0:T(8,128)}) custom-call(s32[3]{0:T(128)} %pad_add_fusion.10.sc_ref, bf16[1024,128]{1,0:T(8,128)(2,1)} %bitcast.143, bf16[2,1024,128]{2,1,0:T(8,128)(2,1)} %collective-permute-done.5.k_ref.v_ref, ...), custom_call_target="tpu_custom_call", output_to_operand_aliasing={{0}: (4, {}), {1}: (5, {})} | custom-call | flops 536870912 | bytes 1843200 | tf_op jit(solution)/shard_map/pallas_call | solution.py:73
  156.7 5.6 %shard_map.66 = (f32[1024,1]{1,0:T(8,128)}, f32[1024,128]{1,0:T(8,128)}) custom-call(s32[3]{0:T(128)} %pad_add_fusion.11.sc_ref, bf16[1024,128]{1,0:T(8,128)(2,1)} %bitcast.144, bf16[2,1024,128]{2,1,0:T(8,128)(2,1)} %collective-permute-done.4.k_ref.v_ref, ...), custom_call_target="tpu_custom_call", output_to_operand_aliasing={{0}: (4, {}), {1}: (5, {})} | custom-call | flops 536870912 | bytes 1843200 | tf_op jit(solution)/shard_map/pallas_call | solution.py:73
  162.3 5.6 %shard_map.67 = (f32[1024,1]{1,0:T(8,128)}, f32[1024,128]{1,0:T(8,128)}) custom-call(s32[3]{0:T(128)} %pad_add_fusion.12.sc_ref, bf16[1024,128]{1,0:T(8,128)(2,1)} %bitcast.145, bf16[2,1024,128]{2,1,0:T(8,128)(2,1)} %collective-permute-done.3.k_ref.v_ref, ...), custom_call_target="tpu_custom_call", output_to_operand_aliasing={{0}: (4, {}), {1}: (5, {})} | custom-call | flops 536870912 | bytes 1843200 | tf_op jit(solution)/shard_map/pallas_call | solution.py:73
  167.9 5.6 %shard_map.68 = (f32[1024,1]{1,0:T(8,128)}, f32[1024,128]{1,0:T(8,128)}) custom-call(s32[3]{0:T(128)} %pad_add_fusion.13.sc_ref, bf16[1024,128]{1,0:T(8,128)(2,1)} %bitcast.146, bf16[2,1024,128]{2,1,0:T(8,128)(2,1)} %collective-permute-done.2.k_ref.v_ref, ...), custom_call_target="tpu_custom_call", output_to_operand_aliasing={{0}: (4, {}), {1}: (5, {})} | custom-call | flops 536870912 | bytes 1843200 | tf_op jit(solution)/shard_map/pallas_call | solution.py:73
  173.5 5.6 %shard_map.69 = (f32[1024,1]{1,0:T(8,128)}, f32[1024,128]{1,0:T(8,128)}) custom-call(s32[3]{0:T(128)} %pad_add_fusion.14.sc_ref, bf16[1024,128]{1,0:T(8,128)(2,1)} %bitcast.147, bf16[2,1024,128]{2,1,0:T(8,128)(2,1)} %collective-permute-done.1.k_ref.v_ref, ...), custom_call_target="tpu_custom_call", output_to_operand_aliasing={{0}: (4, {}), {1}: (5, {})} | custom-call | flops 536870912 | bytes 1843200 | tf_op jit(solution)/shard_map/pallas_call | solution.py:73
  179.2 5.6 %shard_map.70 = (f32[1024,1]{1,0:T(8,128)}, f32[1024,128]{1,0:T(8,128)}) custom-call(s32[3]{0:T(128)} %pad_add_fusion.15.sc_ref, bf16[1024,128]{1,0:T(8,128)(2,1)} %bitcast.148, bf16[2,1024,128]{2,1,0:T(8,128)(2,1)} %collective-permute-done.k_ref.v_ref, ...), custom_call_target="tpu_custom_call", output_to_operand_aliasing={{0}: (4, {}), {1}: (5, {})} | custom-call | flops 536870912 | bytes 1843200 | tf_op jit(solution)/shard_map/pallas_call | solution.py:73
  189.2 3.6 %copy-done.1 = f32[8,2,32,4608]{3,2,1,0:T(8,128)} copy-done((f32[8,2,32,4608]{3,2,1,0:T(8,128)}, f32[8,2,32,4608]{3,2,1,0:T(8,128)S(1)}, u32[]{:S(2)}) %copy-start.1) | copy-done | bytes 9437208
  195.7 4.5 %collective-permute-done.15 = bf16[8,32,4608]{2,1,0:T(8,128)(2,1)} collective-permute-done((bf16[8,32,4608]{2,1,0:T(8,128)(2,1)}, bf16[8,32,4608]{2,1,0:T(8,128)(2,1)}, u32[]{:S(2)}, u32[]{:S(2)}) %collective-permute-start.15) | collective-permute-done | bytes 2359328 | tf_op jit(solution)/shard_map/ppermute | solution.py:130
  200.2 3.6 %bitcast_add_fusion = f32[8,32,4608]{2,1,0:T(8,128)S(1)} fusion(bf16[8,32,4608]{2,1,0:T(8,128)(2,1)} %collective-permute-done.15, f32[8,2,32,4608]{3,2,1,0:T(8,128)} %copy-done.1, s32[]{:T(128)S(6)} %select_n.300), kind=kLoop, calls=%fused_computation | loop fusion | flops 2359296 | bytes 11796484 | tf_op jit(solution)/shard_map/add | solution.py:130
  207.0 4.4 %collective-permute-start.16 = (bf16[32,4608]{1,0:T(8,128)(2,1)S(1)}, bf16[32,4608]{1,0:T(8,128)(2,1)S(1)}, u32[]{:S(2)}, u32[]{:S(2)}) collective-permute-start(bf16[32,4608]{1,0:T(8,128)(2,1)S(1)} %get-tuple-element.69), channel_id=1, source_target_pairs={{0,2},{2,4},{4,6},{6,8},{8,10},{10,12},{12,14},{14,0},{1,3},{3,5},... | collective-permute-start | bytes 884744 | tf_op jit(solution)/shard_map/ppermute | solution.py:135
  218.1 3.5 %collective-permute-start.20 = (bf16[32,4608]{1,0:T(8,128)(2,1)S(1)}, bf16[32,4608]{1,0:T(8,128)(2,1)}, u32[]{:S(2)}, u32[]{:S(2)}) collective-permute-start(bf16[32,4608]{1,0:T(8,128)(2,1)S(1)} %get-tuple-element.72), channel_id=1, source_target_pairs={{0,10},{2,12},{4,14},{6,0},{8,2},{10,4},{12,6},{14,8},{1,11},{3,13... | collective-permute-start | bytes 884744 | tf_op jit(solution)/shard_map/ppermute | solution.py:135
  222.5 18.8 %collective-permute-done.17 = bf16[32,4608]{1,0:T(8,128)(2,1)S(1)} collective-permute-done((bf16[32,4608]{1,0:T(8,128)(2,1)S(1)}, bf16[32,4608]{1,0:T(8,128)(2,1)S(1)}, u32[]{:S(2)}, u32[]{:S(2)}) %collective-permute-start.17) | collective-permute-done | bytes 294944 | tf_op jit(solution)/shard_map/ppermute | solution.py:135
  242.1 3.2 %collective-permute-done.21 = bf16[32,4608]{1,0:T(8,128)(2,1)} collective-permute-done((bf16[32,4608]{1,0:T(8,128)(2,1)S(1)}, bf16[32,4608]{1,0:T(8,128)(2,1)}, u32[]{:S(2)}, u32[]{:S(2)}) %collective-permute-start.21) | collective-permute-done | bytes 294944 | tf_op jit(solution)/shard_map/ppermute | solution.py:135
  245.3 7.9 %collective-permute-done.22 = bf16[32,4608]{1,0:T(8,128)(2,1)} collective-permute-done((bf16[32,4608]{1,0:T(8,128)(2,1)S(1)}, bf16[32,4608]{1,0:T(8,128)(2,1)}, u32[]{:S(2)}, u32[]{:S(2)}) %collective-permute-start.22) | collective-permute-done | bytes 294944 | tf_op jit(solution)/shard_map/ppermute | solution.py:135
  (111 shorter events, 59.9 us)
Async XLA Ops:
  0.0 187.7 %copy-start = (bf16[256,4608]{1,0:T(8,128)(2,1)S(1)}, bf16[256,4608]{1,0:T(8,128)(2,1)}, u32[]{:S(2)}) copy-start(bf16[256,4608]{1,0:T(8,128)(2,1)} %param.9) | copy-start | bytes 7077892
  7.6 33.1 %collective-permute-start.14 = (bf16[2,1024,128]{2,1,0:T(8,128)(2,1)}, bf16[2,1024,128]{2,1,0:T(8,128)(2,1)}, u32[]{:S(2)}, u32[]{:S(2)}) collective-permute-start(bf16[2,1024,128]{2,1,0:T(8,128)(2,1)} %pad_maximum_fusion.14), channel_id=1, source_target_pairs={{0,1},{1,2},{2,3},{3,4},{4,5},{5,6},{6,7},{7,8},{8,9},{9,10},{10,1... | collective-permute-start | bytes 1572872 | tf_op jit(solution)/shard_map/ppermute | solution.py:112
  8.5 35.1 %collective-permute-start.13 = (bf16[2,1024,128]{2,1,0:T(8,128)(2,1)}, bf16[2,1024,128]{2,1,0:T(8,128)(2,1)}, u32[]{:S(2)}, u32[]{:S(2)}) collective-permute-start(bf16[2,1024,128]{2,1,0:T(8,128)(2,1)} %pad_maximum_fusion.13), channel_id=1, source_target_pairs={{0,2},{1,3},{2,4},{3,5},{4,6},{5,7},{6,8},{7,9},{8,10},{9,11},{10,... | collective-permute-start | bytes 1572872 | tf_op jit(solution)/shard_map/ppermute | solution.py:112
  11.5 38.2 %collective-permute-start.12 = (bf16[2,1024,128]{2,1,0:T(8,128)(2,1)}, bf16[2,1024,128]{2,1,0:T(8,128)(2,1)}, u32[]{:S(2)}, u32[]{:S(2)}) collective-permute-start(bf16[2,1024,128]{2,1,0:T(8,128)(2,1)} %pad_maximum_fusion.12), channel_id=1, source_target_pairs={{0,3},{1,4},{2,5},{3,6},{4,7},{5,8},{6,9},{7,10},{8,11},{9,12},{10... | collective-permute-start | bytes 1572872 | tf_op jit(solution)/shard_map/ppermute | solution.py:112
  16.3 35.1 %collective-permute-start.11 = (bf16[2,1024,128]{2,1,0:T(8,128)(2,1)}, bf16[2,1024,128]{2,1,0:T(8,128)(2,1)}, u32[]{:S(2)}, u32[]{:S(2)}) collective-permute-start(bf16[2,1024,128]{2,1,0:T(8,128)(2,1)} %pad_maximum_fusion.11), channel_id=1, source_target_pairs={{0,4},{1,5},{2,6},{3,7},{4,8},{5,9},{6,10},{7,11},{8,12},{9,13},{1... | collective-permute-start | bytes 1572872 | tf_op jit(solution)/shard_map/ppermute | solution.py:112
  18.3 44.5 %collective-permute-start.10 = (bf16[2,1024,128]{2,1,0:T(8,128)(2,1)}, bf16[2,1024,128]{2,1,0:T(8,128)(2,1)}, u32[]{:S(2)}, u32[]{:S(2)}) collective-permute-start(bf16[2,1024,128]{2,1,0:T(8,128)(2,1)} %pad_maximum_fusion.10), channel_id=1, source_target_pairs={{0,5},{1,6},{2,7},{3,8},{4,9},{5,10},{6,11},{7,12},{8,13},{9,14},{... | collective-permute-start | bytes 1572872 | tf_op jit(solution)/shard_map/ppermute | solution.py:112
  25.1 9.5 %copy-start.7 = (bf16[1,1024,128]{2,1,0:T(8,128)(2,1)S(1)}, bf16[1,1024,128]{2,1,0:T(8,128)(2,1)}, u32[]{:S(2)}) copy-start(bf16[1,1024,128]{2,1,0:T(8,128)(2,1)} %get-tuple-element.102) | copy-start | bytes 786436
  25.1 10.4 %copy-start.5 = (bf16[1,1024,128]{2,1,0:T(8,128)(2,1)S(1)}, bf16[1,1024,128]{2,1,0:T(8,128)(2,1)}, u32[]{:S(2)}) copy-start(bf16[1,1024,128]{2,1,0:T(8,128)(2,1)} %get-tuple-element.103) | copy-start | bytes 786436
  25.1 10.4 %copy-start.6 = (bf16[1,1024,128]{2,1,0:T(8,128)(2,1)S(1)}, bf16[1,1024,128]{2,1,0:T(8,128)(2,1)}, u32[]{:S(2)}) copy-start(bf16[1,1024,128]{2,1,0:T(8,128)(2,1)} %get-tuple-element.112) | copy-start | bytes 786436
  25.2 11.2 %copy-start.3 = (bf16[1,1024,128]{2,1,0:T(8,128)(2,1)S(1)}, bf16[1,1024,128]{2,1,0:T(8,128)(2,1)}, u32[]{:S(2)}) copy-start(bf16[1,1024,128]{2,1,0:T(8,128)(2,1)} %get-tuple-element.104) | copy-start | bytes 786436
  25.2 11.2 %copy-start.4 = (bf16[1,1024,128]{2,1,0:T(8,128)(2,1)S(1)}, bf16[1,1024,128]{2,1,0:T(8,128)(2,1)}, u32[]{:S(2)}) copy-start(bf16[1,1024,128]{2,1,0:T(8,128)(2,1)} %get-tuple-element.111) | copy-start | bytes 786436
  39.9 57.2 %copy-start.14 = (bf16[2,1024,128]{2,1,0:T(8,128)(2,1)S(1)}, bf16[2,1024,128]{2,1,0:T(8,128)(2,1)}, u32[]{:S(2)}) copy-start(bf16[2,1024,128]{2,1,0:T(8,128)(2,1)} %pad_maximum_fusion.3) | copy-start | bytes 1572868
  40.8 33.0 %collective-permute-start.9 = (bf16[2,1024,128]{2,1,0:T(8,128)(2,1)}, bf16[2,1024,128]{2,1,0:T(8,128)(2,1)S(1)}, u32[]{:S(2)}, u32[]{:S(2)}) collective-permute-start(bf16[2,1024,128]{2,1,0:T(8,128)(2,1)} %pad_maximum_fusion.9), channel_id=1, source_target_pairs={{0,6},{1,7},{2,8},{3,9},{4,10},{5,11},{6,12},{7,13},{8,14},{9,15},... | collective-permute-start | bytes 1572872 | tf_op jit(solution)/shard_map/ppermute | solution.py:112
  43.6 53.5 %collective-permute-start.8 = (bf16[2,1024,128]{2,1,0:T(8,128)(2,1)}, bf16[2,1024,128]{2,1,0:T(8,128)(2,1)}, u32[]{:S(2)}, u32[]{:S(2)}) collective-permute-start(bf16[2,1024,128]{2,1,0:T(8,128)(2,1)} %pad_maximum_fusion.8), channel_id=1, source_target_pairs={{0,7},{1,8},{2,9},{3,10},{4,11},{5,12},{6,13},{7,14},{8,15},{9,0},... | collective-permute-start | bytes 1572872 | tf_op jit(solution)/shard_map/ppermute | solution.py:112
  49.7 53.1 %collective-permute-start.7 = (bf16[2,1024,128]{2,1,0:T(8,128)(2,1)}, bf16[2,1024,128]{2,1,0:T(8,128)(2,1)}, u32[]{:S(2)}, u32[]{:S(2)}) collective-permute-start(bf16[2,1024,128]{2,1,0:T(8,128)(2,1)} %pad_maximum_fusion.7), channel_id=1, source_target_pairs={{0,8},{1,9},{2,10},{3,11},{4,12},{5,13},{6,14},{7,15},{8,0},{9,1},... | collective-permute-start | bytes 1572872 | tf_op jit(solution)/shard_map/ppermute | solution.py:112
  51.3 57.1 %collective-permute-start.6 = (bf16[2,1024,128]{2,1,0:T(8,128)(2,1)}, bf16[2,1024,128]{2,1,0:T(8,128)(2,1)}, u32[]{:S(2)}, u32[]{:S(2)}) collective-permute-start(bf16[2,1024,128]{2,1,0:T(8,128)(2,1)} %pad_maximum_fusion.6), channel_id=1, source_target_pairs={{0,9},{1,10},{2,11},{3,12},{4,13},{5,14},{6,15},{7,0},{8,1},{9,2},... | collective-permute-start | bytes 1572872 | tf_op jit(solution)/shard_map/ppermute | solution.py:112
  62.8 51.2 %collective-permute-start.5 = (bf16[2,1024,128]{2,1,0:T(8,128)(2,1)}, bf16[2,1024,128]{2,1,0:T(8,128)(2,1)}, u32[]{:S(2)}, u32[]{:S(2)}) collective-permute-start(bf16[2,1024,128]{2,1,0:T(8,128)(2,1)} %pad_maximum_fusion.5), channel_id=1, source_target_pairs={{0,10},{1,11},{2,12},{3,13},{4,14},{5,15},{6,0},{7,1},{8,2},{9,3},... | collective-permute-start | bytes 1572872 | tf_op jit(solution)/shard_map/ppermute | solution.py:112
  73.8 82.9 %collective-permute-start.4 = (bf16[2,1024,128]{2,1,0:T(8,128)(2,1)}, bf16[2,1024,128]{2,1,0:T(8,128)(2,1)}, u32[]{:S(2)}, u32[]{:S(2)}) collective-permute-start(bf16[2,1024,128]{2,1,0:T(8,128)(2,1)} %pad_maximum_fusion.4), channel_id=1, source_target_pairs={{0,11},{1,12},{2,13},{3,14},{4,15},{5,0},{6,1},{7,2},{8,3},{9,4},{... | collective-permute-start | bytes 1572872 | tf_op jit(solution)/shard_map/ppermute | solution.py:112
  75.4 27.3 %copy-start.13 = (bf16[2,1024,128]{2,1,0:T(8,128)(2,1)S(1)}, bf16[2,1024,128]{2,1,0:T(8,128)(2,1)}, u32[]{:S(2)}) copy-start(bf16[2,1024,128]{2,1,0:T(8,128)(2,1)} %pad_maximum_fusion.2) | copy-start | bytes 1572868
  97.1 65.2 %collective-permute-start.3 = (bf16[2,1024,128]{2,1,0:T(8,128)(2,1)S(1)}, bf16[2,1024,128]{2,1,0:T(8,128)(2,1)}, u32[]{:S(2)}, u32[]{:S(2)}) collective-permute-start(bf16[2,1024,128]{2,1,0:T(8,128)(2,1)S(1)} %copy-done.14), channel_id=1, source_target_pairs={{0,12},{1,13},{2,14},{3,15},{4,0},{5,1},{6,2},{7,3},{8,4},{9,5},{1... | collective-permute-start | bytes 1572872 | tf_op jit(solution)/shard_map/ppermute | solution.py:112
  102.8 65.2 %collective-permute-start.2 = (bf16[2,1024,128]{2,1,0:T(8,128)(2,1)S(1)}, bf16[2,1024,128]{2,1,0:T(8,128)(2,1)}, u32[]{:S(2)}, u32[]{:S(2)}) collective-permute-start(bf16[2,1024,128]{2,1,0:T(8,128)(2,1)S(1)} %copy-done.13), channel_id=1, source_target_pairs={{0,13},{1,14},{2,15},{3,0},{4,1},{5,2},{6,3},{7,4},{8,5},{9,6},{10... | collective-permute-start | bytes 1572872 | tf_op jit(solution)/shard_map/ppermute | solution.py:112
  108.5 65.1 %collective-permute-start.1 = (bf16[2,1024,128]{2,1,0:T(8,128)(2,1)}, bf16[2,1024,128]{2,1,0:T(8,128)(2,1)}, u32[]{:S(2)}, u32[]{:S(2)}) collective-permute-start(bf16[2,1024,128]{2,1,0:T(8,128)(2,1)} %pad_maximum_fusion.1), channel_id=1, source_target_pairs={{0,14},{1,15},{2,0},{3,1},{4,2},{5,3},{6,4},{7,5},{8,6},{9,7},{10,... | collective-permute-start | bytes 1572872 | tf_op jit(solution)/shard_map/ppermute | solution.py:112
  114.0 65.2 %collective-permute-start = (bf16[2,1024,128]{2,1,0:T(8,128)(2,1)}, bf16[2,1024,128]{2,1,0:T(8,128)(2,1)}, u32[]{:S(2)}, u32[]{:S(2)}) collective-permute-start(bf16[2,1024,128]{2,1,0:T(8,128)(2,1)} %pad_maximum_fusion), channel_id=1, source_target_pairs={{0,15},{1,0},{2,1},{3,2},{4,3},{5,4},{6,5},{7,6},{8,7},{9,8},{10,9... | collective-permute-start | bytes 1572872 | tf_op jit(solution)/shard_map/ppermute | solution.py:112
  194.5 5.8 %collective-permute-start.15 = (bf16[8,32,4608]{2,1,0:T(8,128)(2,1)}, bf16[8,32,4608]{2,1,0:T(8,128)(2,1)}, u32[]{:S(2)}, u32[]{:S(2)}) collective-permute-start(bf16[8,32,4608]{2,1,0:T(8,128)(2,1)} %fusion), channel_id=1, source_target_pairs={{0,1},{1,0},{2,3},{3,2},{4,5},{5,4},{6,7},{7,6},{8,9},{9,8},{10,11... | collective-permute-start | bytes 7077896 | tf_op jit(solution)/shard_map/ppermute | solution.py:130
  207.0 14.7 %collective-permute-start.16 = (bf16[32,4608]{1,0:T(8,128)(2,1)S(1)}, bf16[32,4608]{1,0:T(8,128)(2,1)S(1)}, u32[]{:S(2)}, u32[]{:S(2)}) collective-permute-start(bf16[32,4608]{1,0:T(8,128)(2,1)S(1)} %get-tuple-element.69), channel_id=1, source_target_pairs={{0,2},{2,4},{4,6},{6,8},{8,10},{10,12},{12,14},{14,0},{1,3},{3,5},... | collective-permute-start | bytes 884744 | tf_op jit(solution)/shard_map/ppermute | solution.py:135
  211.3 30.0 %collective-permute-start.17 = (bf16[32,4608]{1,0:T(8,128)(2,1)S(1)}, bf16[32,4608]{1,0:T(8,128)(2,1)S(1)}, u32[]{:S(2)}, u32[]{:S(2)}) collective-permute-start(bf16[32,4608]{1,0:T(8,128)(2,1)S(1)} %get-tuple-element.75), channel_id=1, source_target_pairs={{0,4},{2,6},{4,8},{6,10},{8,12},{10,14},{12,0},{14,2},{1,5},{3,7},... | collective-permute-start | bytes 884744 | tf_op jit(solution)/shard_map/ppermute | solution.py:135
  213.5 28.6 %collective-permute-start.18 = (bf16[32,4608]{1,0:T(8,128)(2,1)}, bf16[32,4608]{1,0:T(8,128)(2,1)}, u32[]{:S(2)}, u32[]{:S(2)}) collective-permute-start(bf16[32,4608]{1,0:T(8,128)(2,1)} %get-tuple-element.74), channel_id=1, source_target_pairs={{0,6},{2,8},{4,10},{6,12},{8,14},{10,0},{12,2},{14,4},{1,7},{3,9},... | collective-permute-start | bytes 884744 | tf_op jit(solution)/shard_map/ppermute | solution.py:135
  215.3 26.8 %collective-permute-start.19 = (bf16[32,4608]{1,0:T(8,128)(2,1)S(1)}, bf16[32,4608]{1,0:T(8,128)(2,1)}, u32[]{:S(2)}, u32[]{:S(2)}) collective-permute-start(bf16[32,4608]{1,0:T(8,128)(2,1)S(1)} %get-tuple-element.73), channel_id=1, source_target_pairs={{0,8},{2,10},{4,12},{6,14},{8,0},{10,2},{12,4},{14,6},{1,9},{3,11}... | collective-permute-start | bytes 884744 | tf_op jit(solution)/shard_map/ppermute | solution.py:135
  218.1 24.0 %collective-permute-start.20 = (bf16[32,4608]{1,0:T(8,128)(2,1)S(1)}, bf16[32,4608]{1,0:T(8,128)(2,1)}, u32[]{:S(2)}, u32[]{:S(2)}) collective-permute-start(bf16[32,4608]{1,0:T(8,128)(2,1)S(1)} %get-tuple-element.72), channel_id=1, source_target_pairs={{0,10},{2,12},{4,14},{6,0},{8,2},{10,4},{12,6},{14,8},{1,11},{3,13... | collective-permute-start | bytes 884744 | tf_op jit(solution)/shard_map/ppermute | solution.py:135
  221.6 19.7 %copy-start.15 = (bf16[32,4608]{1,0:T(8,128)(2,1)}, bf16[32,4608]{1,0:T(8,128)(2,1)S(1)}, u32[]{:S(2)}) copy-start(bf16[32,4608]{1,0:T(8,128)(2,1)S(1)} %collective-permute-done.16) | copy-start | bytes 884740
  221.6 23.7 %collective-permute-start.21 = (bf16[32,4608]{1,0:T(8,128)(2,1)S(1)}, bf16[32,4608]{1,0:T(8,128)(2,1)}, u32[]{:S(2)}, u32[]{:S(2)}) collective-permute-start(bf16[32,4608]{1,0:T(8,128)(2,1)S(1)} %get-tuple-element.71), channel_id=1, source_target_pairs={{0,12},{2,14},{4,0},{6,2},{8,4},{10,6},{12,8},{14,10},{1,13},{3,15... | collective-permute-start | bytes 884744 | tf_op jit(solution)/shard_map/ppermute | solution.py:135
  242.1 11.0 %collective-permute-start.22 = (bf16[32,4608]{1,0:T(8,128)(2,1)S(1)}, bf16[32,4608]{1,0:T(8,128)(2,1)}, u32[]{:S(2)}, u32[]{:S(2)}) collective-permute-start(bf16[32,4608]{1,0:T(8,128)(2,1)S(1)} %get-tuple-element.70), channel_id=1, source_target_pairs={{0,14},{2,0},{4,2},{6,4},{8,6},{10,8},{12,10},{14,12},{1,15},{3,1}... | collective-permute-start | bytes 884744 | tf_op jit(solution)/shard_map/ppermute | solution.py:135
  (9 other events, 50.0 us)

commit v2 on v0

v2 whole, which is shorter than its diff:
```python
import functools

import jax
import jax.numpy as jnp
from jax import lax
from jax.experimental import pallas as pl
from jax.experimental.pallas import tpu as pltpu
from jax.sharding import Mesh, PartitionSpec as P

HQ = 32
KVH = 16
HD = 128
CAP = 50
SCALAR = 144
KV = ("kx", "kc")
HALVES = 2


def block_kernel(sc_ref, q_ref, k_ref, v_ref, l_ref, acc_ref, l_out, acc_out, *, run, stride):
    tq = q_ref.shape[0]
    tk = k_ref.shape[0]
    row_first = sc_ref[0]
    row_last = row_first + (tq // run - 1) * stride + run - 1
    key_first = sc_ref[1]
    key_last = key_first + tk - 1

    def update(masked):
        raw = lax.dot_general(
            q_ref[...], k_ref[...], (((1,), (1,)), ((), ())), preferred_element_type=jnp.float32
        )
        prob = jnp.exp(CAP * jnp.tanh(raw * (SCALAR ** (-0.5) / CAP)))
        if masked:
            rows = lax.broadcasted_iota(jnp.int32, (tq, tk), 0)
            shift = run.bit_length() - 1
            q_pos = row_first + lax.shift_right_logical(rows, shift) * stride + (rows & (run - 1))
            k_pos = key_first + lax.broadcasted_iota(jnp.int32, (tq, tk), 1)
            prob = jnp.where(k_pos <= q_pos, prob, 0.0)
        l_out[...] = l_ref[...] + jnp.sum(prob, axis=1, keepdims=True)
        acc_out[...] = acc_ref[...] + jnp.dot(
            prob.astype(jnp.bfloat16), v_ref[...], preferred_element_type=jnp.float32
        )

    @pl.when(key_first > row_last)
    def _skip():
        l_out[...] = l_ref[...]
        acc_out[...] = acc_ref[...]

    @pl.when(key_last <= row_first)
    def _full():
        update(False)

    @pl.when(jnp.logical_and(key_first <= row_last, key_last > row_first))
    def _diagonal():
        update(True)


def attend_kernel(scalars, q, block, total, summed, run, stride, tq):
    n_q, hd = q.shape
    n_k = block.shape[1]
    row = lambda i, sc: (i, 0)
    grid_spec = pltpu.PrefetchScalarGridSpec(
        num_scalar_prefetch=1,
        grid=(n_q // tq,),
        in_specs=[
            pl.BlockSpec((tq, hd), row),
            pl.BlockSpec((None, n_k, hd), lambda i, sc: (0, 0, 0)),
            pl.BlockSpec((None, n_k, hd), lambda i, sc: (1, 0, 0)),
            pl.BlockSpec((tq, 1), row),
            pl.BlockSpec((tq, hd), row),
        ],
        out_specs=[
            pl.BlockSpec((tq, 1), row),
            pl.BlockSpec((tq, hd), row),
        ],
    )
    return pl.pallas_call(
        functools.partial(block_kernel, run=run, stride=stride),
        grid_spec=grid_spec,
        out_shape=(
            jax.ShapeDtypeStruct(total.shape, jnp.float32),
            jax.ShapeDtypeStruct(summed.shape, jnp.float32),
        ),
        input_output_aliases={4: 0, 5: 1},
        cost_estimate=pl.CostEstimate(
            flops=4 * n_q * n_k * hd,
            transcendentals=2 * n_q * n_k,
            bytes_accessed=2 * (n_q + 2 * n_k) * hd + 8 * n_q * (hd + 1),
        ),
    )(scalars, q, block, block, total, summed)


def reduce_pieces(partial):
    n_chip = lax.axis_size("kx")
    n_core = lax.axis_size("kc")
    partial = partial.reshape(n_chip, n_core, -1, partial.shape[1])
    core = lax.axis_index("kc")
    mine = lax.dynamic_index_in_dim(partial, core, 1, keepdims=False)
    theirs = lax.dynamic_index_in_dim(partial, 1 - core, 1, keepdims=False).astype(jnp.bfloat16)
    on_chip = mine + lax.ppermute(theirs, "kc", [(0, 1), (1, 0)]).astype(jnp.float32)
    chip = lax.axis_index("kx")
    pieces = [lax.dynamic_index_in_dim(on_chip, chip, 0, keepdims=False)]
    for shift in range(1, n_chip):
        part = lax.dynamic_index_in_dim(on_chip, (chip + shift) % n_chip, 0, keepdims=False)
        pieces.append(
            lax.ppermute(
                part.astype(jnp.bfloat16), "kx", [(k, (k + shift) % n_chip) for k in range(n_chip)]
            )
        )
    return pieces


def add_pieces(pieces):
    result = pieces[0]
    for piece in pieces[1:]:
        result = result + piece.astype(jnp.float32)
    return result


def per_device(slab_start, queries, keys, values, out_weight):
    n_kv = lax.axis_size(KV)
    me = lax.axis_index(KV)
    group = HQ // KVH
    rows_dev = queries.shape[0]
    row_first = slab_start[0] + lax.axis_index("pb") * rows_dev
    key_dev = keys.shape[0]
    kv_local = keys.shape[1] // (n_kv * HD)
    kv_feat = kv_local * HD
    heads = kv_local * group
    chunk = rows_dev // n_kv
    run = chunk // HALVES
    q_halves = (
        queries.reshape(n_kv, HALVES, run, heads, HD)
        .transpose(1, 3, 0, 2, 4)
        .reshape(HALVES, heads * n_kv * run, HD)
    )
    n_q = heads * n_kv * run
    tq = n_kv * run
    state = [
        (jnp.zeros((n_q, 1), jnp.float32), jnp.zeros((n_q, HD), jnp.float32))
        for _ in range(HALVES)
    ]
    blocks = []
    for shift in range(n_kv):
        dest = (me + shift) % n_kv
        src = (me - shift) % n_kv
        block = jnp.stack(
            (
                lax.dynamic_slice_in_dim(keys, dest * kv_feat, kv_feat, 1),
                lax.dynamic_slice_in_dim(values, dest * kv_feat, kv_feat, 1),
            ),
            axis=0,
        )
        if shift:
            block = lax.ppermute(block, KV, [(j, (j + shift) % n_kv) for j in range(n_kv)])
        blocks.append((block, src))
    results = []
    pending = []
    late = n_kv // 2 - 2
    for half in range(HALVES):
        for index, (block, src) in enumerate(blocks):
            at = index - late
            if 0 <= at < len(pending):
                pending[at], state[half] = lax.optimization_barrier((pending[at], state[half]))
            scalars = jnp.stack([row_first + half * run, src * key_dev]).astype(jnp.int32)
            state[half] = attend_kernel(
                scalars, q_halves[half], block, *state[half], run, chunk, tq
            )
        if pending:
            results.append(add_pieces(pending))
        total, summed = state[half]
        mixed = (summed / total).astype(jnp.bfloat16)
        attended = (
            mixed.reshape(heads, n_kv * run, HD).transpose(1, 0, 2).reshape(n_kv * run, heads * HD)
        )
        partial = jnp.dot(attended, out_weight, preferred_element_type=jnp.float32)
        pending = reduce_pieces(partial)
    results.append(add_pieces(pending))
    return jnp.concatenate(results, axis=0)


def solution(mesh):
    n_pb, n_kv = mesh.devices.shape
    split = Mesh(mesh.devices.reshape(n_pb, n_kv // 2, 2), ("pb", "kx", "kc"))
    in_specs = (P(), P("pb", KV), P(KV, None), P(KV, None), P(KV, None))
    out_specs = P(("pb",) + KV, None)
    return jax.shard_map(
        per_device, mesh=split, in_specs=in_specs, out_specs=out_specs, check_vma=False
    )
```

time: 247 us -> 311 us (1.26); the launches traced: 245 us -> 306 us
  Pallas kernels: 86.2 us -> 124 us
  blocking collectives: 37.6 us -> 0 us
  waiting for transfers between devices: 25 us -> 61.5 us
  starting transfers between devices: 42.9 us -> 55.6 us
  other arithmetic: 35.8 us -> 43.1 us
    pallas_call x16 -> x32, Pallas kernels: 86.2 us -> 124 us  [attend_kernel(): pl.pallas_call(functools.partial(block_kernel, run=run, stride=stride), g...]
    all_to_all x1 -> x0, blocking collectives: 37.6 us -> none  [per_device(): lax.all_to_all(on_chip.astype(jnp.bfloat16), 'kx', split_axis=0, concat_a...]
    ppermute x16 -> x31, waiting for transfers between devices: 25 us -> 61.5 us  [the longest x15 42.9 us: per_device(): lax.ppermute(block, KV, [(j, (j + shift) % n_kv) for j in range(n_kv)])]
    ppermute x16 -> x31, starting transfers between devices: 42.9 us -> 55.6 us  [the longest x15 28.5 us: per_device(): lax.ppermute(block, KV, [(j, (j + shift) % n_kv) for j in range(n_kv)])]
    another operation x32 -> x40, other arithmetic: 27.9 us -> 34.1 us  [the longest x16 18.9 us: per_device(): jnp.stack((lax.dynamic_slice_in_dim(keys, dest * kv_feat, kv_feat, 1), la...]
    add x0 -> x4, other arithmetic: none -> 3.76 us  [the longest x2 2.49 us: reduce_pieces(): mine + lax.ppermute(theirs, 'kc', [(0, 1), (1, 0)]).astype(jnp.float32)]
    convert_element_type x2, other arithmetic: 5.55 us -> 2.19 us  [per_device(): mixed = (summed / total).astype(jnp.bfloat16)]
    another operation x1 -> x5, local copies, waits for them, and re-layouts: 6.65 us -> 9.66 us  [the longest x1 6.8 us: per_device(): jnp.stack((lax.dynamic_slice_in_dim(keys, dest * kv_feat, kv_feat, 1), la...]
  transfers between devices with their start and end apart: 16 -> 31, of which waited for: 3 -> 11; matrix products, arithmetic and copies ran while one was open for 12% -> 13% of each run, Pallas kernels for 33% -> 36%
where the time goes in v2:
time: 311 us; the launch traced here: 306 us
  Pallas kernels  124 us (40%)
  waiting for transfers between devices  61.5 us (20%)
  starting transfers between devices  55.6 us (18%)
  other arithmetic  43.1 us (14%)
  local copies, waits for them, and re-layouts  17.7 us (6%)
    pallas_call x32, Pallas kernels, attend_kernel(): pl.pallas_call(functools.partial(block_kernel, run=run, stride=stride), g...  124 us
    ppermute x15, waiting for transfers between devices, per_device(): lax.ppermute(block, KV, [(j, (j + shift) % n_kv) for j in range(n_kv)])  42.9 us
    ppermute x15, starting transfers between devices, per_device(): lax.ppermute(block, KV, [(j, (j + shift) % n_kv) for j in range(n_kv)])  28.5 us
    ppermute x14, starting transfers between devices, reduce_pieces(): lax.ppermute(part.astype(jnp.bfloat16), 'kx', [(k, (k + shift) % n_chip)...  24.8 us
    another operation x16, other arithmetic, per_device(): jnp.stack((lax.dynamic_slice_in_dim(keys, dest * kv_feat, kv_feat, 1), la...  18.9 us
    ppermute x14, waiting for transfers between devices, reduce_pieces(): lax.ppermute(part.astype(jnp.bfloat16), 'kx', [(k, (k + shift) % n_chip)...  15.8 us
    another operation x24, other arithmetic, per_device(): jnp.stack([row_first + half * run, src * key_dev]).astype(jnp.int32)  15.2 us
    another operation x1, local copies, waits for them, and re-layouts, per_device(): jnp.stack((lax.dynamic_slice_in_dim(keys, dest * kv_feat, kv_feat, 1), la...  6.8 us
  transfers between devices with their start and end apart: 31, of which 11 were waited for; matrix products, arithmetic and copies ran while one was open for 13% of the time, Pallas kernels for 36%

profile of v2, /device:TPU:120, one launch (start us, length us, event | category | flops | bytes accessed | tf_op | source)
XLA Modules:
  0.0 306.2 jit_solution(10817319554863400994)
XLA Ops:
  0.0 6.8 %dynamic-slice_bitcast_fusion.1 = (bf16[1,1024,128]{2,1,0:T(8,128)(2,1)}, bf16[1,1024,128]{2,1,0:T(8,128)(2,1)S(1)}, bf16[1,1024,128]{2,1,0:T(8,128)(2,1)S(1)}, ...) fusion(bf16[1024,2048]{1,0:T(8,128)(2,1)} %param.8, ...), kind=kLoop, calls=%fused_computation.53 | loop fusion | bytes 16777280 | tf_op jit(solution)/shard_map/stack | solution.py:146
  11.5 3.9 %collective-permute-start.12 = (bf16[2,1024,128]{2,1,0:T(8,128)(2,1)}, bf16[2,1024,128]{2,1,0:T(8,128)(2,1)}, u32[]{:S(2)}, u32[]{:S(2)}) collective-permute-start(bf16[2,1024,128]{2,1,0:T(8,128)(2,1)} %pad_maximum_fusion.13), channel_id=1, source_target_pairs={{0,3},{1,4},{2,5},{3,6},{4,7},{5,8},{6,9},{7,10},{8,11},{9,12},{10... | collective-permute-start | bytes 1572872 | tf_op jit(solution)/shard_map/ppermute | solution.py:154
  43.4 5.5 %collective-permute-start.8 = (bf16[2,1024,128]{2,1,0:T(8,128)(2,1)}, bf16[2,1024,128]{2,1,0:T(8,128)(2,1)}, u32[]{:S(2)}, u32[]{:S(2)}) collective-permute-start(bf16[2,1024,128]{2,1,0:T(8,128)(2,1)} %pad_maximum_fusion.9), channel_id=1, source_target_pairs={{0,7},{1,8},{2,9},{3,10},{4,11},{5,12},{6,13},{7,14},{8,15},{9,0},... | collective-permute-start | bytes 1572872 | tf_op jit(solution)/shard_map/ppermute | solution.py:154
  51.3 10.8 %collective-permute-start.6 = (bf16[2,1024,128]{2,1,0:T(8,128)(2,1)}, bf16[2,1024,128]{2,1,0:T(8,128)(2,1)}, u32[]{:S(2)}, u32[]{:S(2)}) collective-permute-start(bf16[2,1024,128]{2,1,0:T(8,128)(2,1)} %pad_maximum_fusion.7), channel_id=1, source_target_pairs={{0,9},{1,10},{2,11},{3,12},{4,13},{5,14},{6,15},{7,0},{8,1},{9,2},... | collective-permute-start | bytes 1572872 | tf_op jit(solution)/shard_map/ppermute | solution.py:154
  65.8 8.0 %collective-permute-done.9.k_ref.v_ref = bf16[2,1024,128]{2,1,0:T(8,128)(2,1)} collective-permute-done((bf16[2,1024,128]{2,1,0:T(8,128)(2,1)}, bf16[2,1024,128]{2,1,0:T(8,128)(2,1)}, u32[]{:S(2)}, u32[]{:S(2)}) %collective-permute-start.9) | collective-permute-done | bytes 524320 | tf_op jit(solution)/shard_map/ppermute | solution.py:154
  74.4 23.2 %collective-permute-done.8.k_ref.v_ref = bf16[2,1024,128]{2,1,0:T(8,128)(2,1)} collective-permute-done((bf16[2,1024,128]{2,1,0:T(8,128)(2,1)}, bf16[2,1024,128]{2,1,0:T(8,128)(2,1)}, u32[]{:S(2)}, u32[]{:S(2)}) %collective-permute-start.8) | collective-permute-done | bytes 524320 | tf_op jit(solution)/shard_map/ppermute | solution.py:154
  100.4 6.7 %collective-permute-done.6.k_ref.v_ref = bf16[2,1024,128]{2,1,0:T(8,128)(2,1)} collective-permute-done((bf16[2,1024,128]{2,1,0:T(8,128)(2,1)}, bf16[2,1024,128]{2,1,0:T(8,128)(2,1)}, u32[]{:S(2)}, u32[]{:S(2)}) %collective-permute-start.6) | collective-permute-done | bytes 524320 | tf_op jit(solution)/shard_map/ppermute | solution.py:154
  122.7 3.9 %shard_map.58 = (f32[512,1]{1,0:T(8,128)}, f32[512,128]{1,0:T(8,128)}) custom-call(s32[2]{0:T(128)} %get-tuple-element.238.sc_ref, bf16[512,128]{1,0:T(8,128)(2,1)} %bitcast.182, bf16[2,1024,128]{2,1,0:T(8,128)(2,1)} %collective-permute-done.12.k_ref.v_ref, ...), custom_call_target="tpu_custom_call", output_to_operand_aliasing={{0}: (4, {}), {1}: (5, {})} | custom-call | flops 268435456 | bytes 1183744 | tf_op jit(solution)/shard_map/pallas_call | solution.py:76
  126.6 3.9 %shard_map.59 = (f32[512,1]{1,0:T(8,128)}, f32[512,128]{1,0:T(8,128)}) custom-call(s32[2]{0:T(128)} %get-tuple-element.236.sc_ref, bf16[512,128]{1,0:T(8,128)(2,1)} %bitcast.183, bf16[2,1024,128]{2,1,0:T(8,128)(2,1)} %collective-permute-done.11.k_ref.v_ref, ...), custom_call_target="tpu_custom_call", output_to_operand_aliasing={{0}: (4, {}), {1}: (5, {})} | custom-call | flops 268435456 | bytes 1183744 | tf_op jit(solution)/shard_map/pallas_call | solution.py:76
  149.8 4.0 %shard_map.65 = (f32[512,1]{1,0:T(8,128)}, f32[512,128]{1,0:T(8,128)}) custom-call(s32[2]{0:T(128)} %pad_add_fusion.11.sc_ref, bf16[512,128]{1,0:T(8,128)(2,1)} %bitcast.189, bf16[2,1024,128]{2,1,0:T(8,128)(2,1)} %collective-permute-done.5.k_ref.v_ref, ...), custom_call_target="tpu_custom_call", output_to_operand_aliasing={{0}: (4, {}), {1}: (5, {})} | custom-call | flops 268435456 | bytes 1183744 | tf_op jit(solution)/shard_map/pallas_call | solution.py:76
  158.5 3.9 %shard_map.67 = (f32[512,1]{1,0:T(8,128)}, f32[512,128]{1,0:T(8,128)}) custom-call(s32[2]{0:T(128)} %pad_add_fusion.7.sc_ref, bf16[512,128]{1,0:T(8,128)(2,1)} %bitcast.191, bf16[2,1024,128]{2,1,0:T(8,128)(2,1)} %collective-permute-done.3.k_ref.v_ref, ...), custom_call_target="tpu_custom_call", output_to_operand_aliasing={{0}: (4, {}), {1}: (5, {})} | custom-call | flops 268435456 | bytes 1183744 | tf_op jit(solution)/shard_map/pallas_call | solution.py:76
  162.3 3.9 %shard_map.68 = (f32[512,1]{1,0:T(8,128)}, f32[512,128]{1,0:T(8,128)}) custom-call(s32[2]{0:T(128)} %pad_add_fusion.5.sc_ref, bf16[512,128]{1,0:T(8,128)(2,1)} %bitcast.192, bf16[2,1024,128]{2,1,0:T(8,128)(2,1)} %collective-permute-done.2.k_ref.v_ref, ...), custom_call_target="tpu_custom_call", output_to_operand_aliasing={{0}: (4, {}), {1}: (5, {})} | custom-call | flops 268435456 | bytes 1183744 | tf_op jit(solution)/shard_map/pallas_call | solution.py:76
  166.2 3.9 %shard_map.69 = (f32[512,1]{1,0:T(8,128)}, f32[512,128]{1,0:T(8,128)}) custom-call(s32[2]{0:T(128)} %get-tuple-element.232.sc_ref, bf16[512,128]{1,0:T(8,128)(2,1)} %bitcast.193, bf16[2,1024,128]{2,1,0:T(8,128)(2,1)} %collective-permute-done.1.k_ref.v_ref, ...), custom_call_target="tpu_custom_call", output_to_operand_aliasing={{0}: (4, {}), {1}: (5, {})} | custom-call | flops 268435456 | bytes 1183744 | tf_op jit(solution)/shard_map/pallas_call | solution.py:76
  183.9 4.1 %shard_map.71 = (f32[512,1]{1,0:T(8,128)}, f32[512,128]{1,0:T(8,128)}) custom-call(s32[2]{0:T(128)} %get-tuple-element.243.sc_ref, bf16[512,128]{1,0:T(8,128)(2,1)} %bitcast.163, bf16[2,1024,128]{2,1,0:T(8,128)(2,1)} %pad_maximum_fusion.16.k_ref.v_ref, ...), custom_call_target="tpu_custom_call", output_to_operand_aliasing={{0}: (4, {}), {1}: (5, {})} | custom-call | flops 268435456 | bytes 1183744 | tf_op jit(solution)/shard_map/pallas_call | solution.py:76
  193.0 3.9 %shard_map.72 = (f32[512,1]{1,0:T(8,128)}, f32[512,128]{1,0:T(8,128)}) custom-call(s32[2]{0:T(128)} %get-tuple-element.241.sc_ref, bf16[512,128]{1,0:T(8,128)(2,1)} %bitcast.164, bf16[2,1024,128]{2,1,0:T(8,128)(2,1)} %collective-permute-done.14.k_ref.v_ref, ...), custom_call_target="tpu_custom_call", output_to_operand_aliasing={{0}: (4, {}), {1}: (5, {})} | custom-call | flops 268435456 | bytes 1183744 | tf_op jit(solution)/shard_map/pallas_call | solution.py:76
  196.9 3.9 %shard_map.73 = (f32[512,1]{1,0:T(8,128)}, f32[512,128]{1,0:T(8,128)}) custom-call(s32[2]{0:T(128)} %get-tuple-element.239.sc_ref, bf16[512,128]{1,0:T(8,128)(2,1)} %bitcast.165, bf16[2,1024,128]{2,1,0:T(8,128)(2,1)} %collective-permute-done.13.k_ref.v_ref, ...), custom_call_target="tpu_custom_call", output_to_operand_aliasing={{0}: (4, {}), {1}: (5, {})} | custom-call | flops 268435456 | bytes 1183744 | tf_op jit(solution)/shard_map/pallas_call | solution.py:76
  200.8 3.9 %shard_map.74 = (f32[512,1]{1,0:T(8,128)}, f32[512,128]{1,0:T(8,128)}) custom-call(s32[2]{0:T(128)} %get-tuple-element.237.sc_ref, bf16[512,128]{1,0:T(8,128)(2,1)} %bitcast.166, bf16[2,1024,128]{2,1,0:T(8,128)(2,1)} %collective-permute-done.12.k_ref.v_ref, ...), custom_call_target="tpu_custom_call", output_to_operand_aliasing={{0}: (4, {}), {1}: (5, {})} | custom-call | flops 268435456 | bytes 1183744 | tf_op jit(solution)/shard_map/pallas_call | solution.py:76
  204.7 3.9 %shard_map.75 = (f32[512,1]{1,0:T(8,128)}, f32[512,128]{1,0:T(8,128)}) custom-call(s32[2]{0:T(128)} %get-tuple-element.235.sc_ref, bf16[512,128]{1,0:T(8,128)(2,1)} %bitcast.167, bf16[2,1024,128]{2,1,0:T(8,128)(2,1)} %collective-permute-done.11.k_ref.v_ref, ...), custom_call_target="tpu_custom_call", output_to_operand_aliasing={{0}: (4, {}), {1}: (5, {})} | custom-call | flops 268435456 | bytes 1183744 | tf_op jit(solution)/shard_map/pallas_call | solution.py:76
  208.6 3.9 %shard_map.76 = (f32[512,1]{1,0:T(8,128)}, f32[512,128]{1,0:T(8,128)}) custom-call(s32[2]{0:T(128)} %get-tuple-element.233.sc_ref, bf16[512,128]{1,0:T(8,128)(2,1)} %bitcast.168, bf16[2,1024,128]{2,1,0:T(8,128)(2,1)} %collective-permute-done.10.k_ref.v_ref, ...), custom_call_target="tpu_custom_call", output_to_operand_aliasing={{0}: (4, {}), {1}: (5, {})} | custom-call | flops 268435456 | bytes 1183744 | tf_op jit(solution)/shard_map/pallas_call | solution.py:76
  215.7 4.1 %collective-permute-start.16 = (bf16[16,4608]{1,0:T(8,128)(2,1)S(1)}, bf16[16,4608]{1,0:T(8,128)(2,1)S(1)}, u32[]{:S(2)}, u32[]{:S(2)}) collective-permute-start(bf16[16,4608]{1,0:T(8,128)(2,1)S(1)} %get-tuple-element.220), channel_id=1, source_target_pairs={{0,2},{2,4},{4,6},{6,8},{8,10},{10,12},{12,14},{14,0},{1,3},{3,5},... | collective-permute-start | bytes 442376 | tf_op jit(solution)/shard_map/ppermute | solution.py:105
  228.2 3.9 %shard_map.77 = (f32[512,1]{1,0:T(8,128)}, f32[512,128]{1,0:T(8,128)}) custom-call(s32[2]{0:T(128)} %pad_add_fusion.18.sc_ref, bf16[512,128]{1,0:T(8,128)(2,1)} %bitcast.169, bf16[2,1024,128]{2,1,0:T(8,128)(2,1)} %collective-permute-done.9.k_ref.v_ref, ...), custom_call_target="tpu_custom_call", output_to_operand_aliasing={{0}: (4, {}), {1}: (5, {})} | custom-call | flops 268435456 | bytes 1183744 | tf_op jit(solution)/shard_map/pallas_call | solution.py:76
  236.2 4.1 %shard_map.78 = (f32[512,1]{1,0:T(8,128)}, f32[512,128]{1,0:T(8,128)}) custom-call(s32[2]{0:T(128)} %pad_add_fusion.16.sc_ref, bf16[512,128]{1,0:T(8,128)(2,1)} %bitcast.170, bf16[2,1024,128]{2,1,0:T(8,128)(2,1)} %collective-permute-done.8.k_ref.v_ref, ...), custom_call_target="tpu_custom_call", output_to_operand_aliasing={{0}: (4, {}), {1}: (5, {})} | custom-call | flops 268435456 | bytes 1183744 | tf_op jit(solution)/shard_map/pallas_call | solution.py:76
  240.3 3.9 %shard_map.79 = (f32[512,1]{1,0:T(8,128)}, f32[512,128]{1,0:T(8,128)}) custom-call(s32[2]{0:T(128)} %pad_add_fusion.14.sc_ref, bf16[512,128]{1,0:T(8,128)(2,1)} %bitcast.171, bf16[2,1024,128]{2,1,0:T(8,128)(2,1)} %collective-permute-done.7.k_ref.v_ref, ...), custom_call_target="tpu_custom_call", output_to_operand_aliasing={{0}: (4, {}), {1}: (5, {})} | custom-call | flops 268435456 | bytes 1183744 | tf_op jit(solution)/shard_map/pallas_call | solution.py:76
  244.2 3.9 %shard_map.80 = (f32[512,1]{1,0:T(8,128)}, f32[512,128]{1,0:T(8,128)}) custom-call(s32[2]{0:T(128)} %pad_add_fusion.12.sc_ref, bf16[512,128]{1,0:T(8,128)(2,1)} %bitcast.172, bf16[2,1024,128]{2,1,0:T(8,128)(2,1)} %collective-permute-done.6.k_ref.v_ref, ...), custom_call_target="tpu_custom_call", output_to_operand_aliasing={{0}: (4, {}), {1}: (5, {})} | custom-call | flops 268435456 | bytes 1183744 | tf_op jit(solution)/shard_map/pallas_call | solution.py:76
  248.1 3.9 %shard_map.81 = (f32[512,1]{1,0:T(8,128)}, f32[512,128]{1,0:T(8,128)}) custom-call(s32[2]{0:T(128)} %pad_add_fusion.10.sc_ref, bf16[512,128]{1,0:T(8,128)(2,1)} %bitcast.173, bf16[2,1024,128]{2,1,0:T(8,128)(2,1)} %collective-permute-done.5.k_ref.v_ref, ...), custom_call_target="tpu_custom_call", output_to_operand_aliasing={{0}: (4, {}), {1}: (5, {})} | custom-call | flops 268435456 | bytes 1183744 | tf_op jit(solution)/shard_map/pallas_call | solution.py:76
  251.9 3.9 %shard_map.82 = (f32[512,1]{1,0:T(8,128)}, f32[512,128]{1,0:T(8,128)}) custom-call(s32[2]{0:T(128)} %pad_add_fusion.8.sc_ref, bf16[512,128]{1,0:T(8,128)(2,1)} %bitcast.174, bf16[2,1024,128]{2,1,0:T(8,128)(2,1)} %copy-done.10, bf16[2,1024,128]{2,1,0:T(8,128)(2,1)} %copy-done.10, ...), custom_call_target="tpu_custom_call", output_to_operand_aliasing={{0}: (4, {}), {1}: (5, {})} | custom-call | flops 268435456 | bytes 1183744 | tf_op jit(solution)/shard_map/pallas_call | solution.py:76
  255.8 3.9 %shard_map.83 = (f32[512,1]{1,0:T(8,128)}, f32[512,128]{1,0:T(8,128)}) custom-call(s32[2]{0:T(128)} %pad_add_fusion.6.sc_ref, bf16[512,128]{1,0:T(8,128)(2,1)} %bitcast.175, bf16[2,1024,128]{2,1,0:T(8,128)(2,1)} %collective-permute-done.3.k_ref.v_ref, ...), custom_call_target="tpu_custom_call", output_to_operand_aliasing={{0}: (4, {}), {1}: (5, {})} | custom-call | flops 268435456 | bytes 1183744 | tf_op jit(solution)/shard_map/pallas_call | solution.py:76
  259.7 3.9 %shard_map.84 = (f32[512,1]{1,0:T(8,128)}, f32[512,128]{1,0:T(8,128)}) custom-call(s32[2]{0:T(128)} %pad_add_fusion.4.sc_ref, bf16[512,128]{1,0:T(8,128)(2,1)} %bitcast.176, bf16[2,1024,128]{2,1,0:T(8,128)(2,1)} %collective-permute-done.2.k_ref.v_ref, ...), custom_call_target="tpu_custom_call", output_to_operand_aliasing={{0}: (4, {}), {1}: (5, {})} | custom-call | flops 268435456 | bytes 1183744 | tf_op jit(solution)/shard_map/pallas_call | solution.py:76
  263.5 3.9 %shard_map.85 = (f32[512,1]{1,0:T(8,128)}, f32[512,128]{1,0:T(8,128)}) custom-call(s32[2]{0:T(128)} %get-tuple-element.231.sc_ref, bf16[512,128]{1,0:T(8,128)(2,1)} %bitcast.177, bf16[2,1024,128]{2,1,0:T(8,128)(2,1)} %collective-permute-done.1.k_ref.v_ref, ...), custom_call_target="tpu_custom_call", output_to_operand_aliasing={{0}: (4, {}), {1}: (5, {})} | custom-call | flops 268435456 | bytes 1183744 | tf_op jit(solution)/shard_map/pallas_call | solution.py:76
  267.4 3.9 %shard_map.86 = (f32[512,1]{1,0:T(8,128)}, f32[512,128]{1,0:T(8,128)}) custom-call(s32[2]{0:T(128)} %get-tuple-element.229.sc_ref, bf16[512,128]{1,0:T(8,128)(2,1)} %bitcast.178, bf16[2,1024,128]{2,1,0:T(8,128)(2,1)} %copy-done.11, bf16[2,1024,128]{2,1,0:T(8,128)(2,1)} %copy-done.11, ...), custom_call_target="tpu_custom_call", output_to_operand_aliasing={{0}: (4, {}), {1}: (5, {})} | custom-call | flops 268435456 | bytes 1183744 | tf_op jit(solution)/shard_map/pallas_call | solution.py:76
  290.6 6.6 %collective-permute-done.25 = bf16[16,4608]{1,0:T(8,128)(2,1)S(1)} collective-permute-done((bf16[16,4608]{1,0:T(8,128)(2,1)S(1)}, bf16[16,4608]{1,0:T(8,128)(2,1)S(1)}, u32[]{:S(2)}, u32[]{:S(2)}) %collective-permute-start.25) | collective-permute-done | bytes 147488 | tf_op jit(solution)/shard_map/ppermute | solution.py:105
  300.5 4.2 %collective-permute-done.30 = bf16[16,4608]{1,0:T(8,128)(2,1)S(1)} collective-permute-done((bf16[16,4608]{1,0:T(8,128)(2,1)S(1)}, bf16[16,4608]{1,0:T(8,128)(2,1)S(1)}, u32[]{:S(2)}, u32[]{:S(2)}) %collective-permute-start.30) | collective-permute-done | bytes 147488 | tf_op jit(solution)/shard_map/ppermute | solution.py:105
  (154 shorter events, 139.3 us)
Async XLA Ops:
  0.0 177.1 %copy-start = (bf16[256,4608]{1,0:T(8,128)(2,1)S(1)}, bf16[256,4608]{1,0:T(8,128)(2,1)}, u32[]{:S(2)}) copy-start(bf16[256,4608]{1,0:T(8,128)(2,1)} %param.9) | copy-start | bytes 7077892
  7.6 32.2 %collective-permute-start.14 = (bf16[2,1024,128]{2,1,0:T(8,128)(2,1)}, bf16[2,1024,128]{2,1,0:T(8,128)(2,1)}, u32[]{:S(2)}, u32[]{:S(2)}) collective-permute-start(bf16[2,1024,128]{2,1,0:T(8,128)(2,1)} %pad_maximum_fusion.15), channel_id=1, source_target_pairs={{0,1},{1,2},{2,3},{3,4},{4,5},{5,6},{6,7},{7,8},{8,9},{9,10},{10,1... | collective-permute-start | bytes 1572872 | tf_op jit(solution)/shard_map/ppermute | solution.py:154
  8.5 34.8 %collective-permute-start.13 = (bf16[2,1024,128]{2,1,0:T(8,128)(2,1)}, bf16[2,1024,128]{2,1,0:T(8,128)(2,1)}, u32[]{:S(2)}, u32[]{:S(2)}) collective-permute-start(bf16[2,1024,128]{2,1,0:T(8,128)(2,1)} %pad_maximum_fusion.14), channel_id=1, source_target_pairs={{0,2},{1,3},{2,4},{3,5},{4,6},{5,7},{6,8},{7,9},{8,10},{9,11},{10,... | collective-permute-start | bytes 1572872 | tf_op jit(solution)/shard_map/ppermute | solution.py:154
  11.5 37.3 %collective-permute-start.12 = (bf16[2,1024,128]{2,1,0:T(8,128)(2,1)}, bf16[2,1024,128]{2,1,0:T(8,128)(2,1)}, u32[]{:S(2)}, u32[]{:S(2)}) collective-permute-start(bf16[2,1024,128]{2,1,0:T(8,128)(2,1)} %pad_maximum_fusion.13), channel_id=1, source_target_pairs={{0,3},{1,4},{2,5},{3,6},{4,7},{5,8},{6,9},{7,10},{8,11},{9,12},{10... | collective-permute-start | bytes 1572872 | tf_op jit(solution)/shard_map/ppermute | solution.py:154
  16.3 35.1 %collective-permute-start.11 = (bf16[2,1024,128]{2,1,0:T(8,128)(2,1)}, bf16[2,1024,128]{2,1,0:T(8,128)(2,1)}, u32[]{:S(2)}, u32[]{:S(2)}) collective-permute-start(bf16[2,1024,128]{2,1,0:T(8,128)(2,1)} %pad_maximum_fusion.12), channel_id=1, source_target_pairs={{0,4},{1,5},{2,6},{3,7},{4,8},{5,9},{6,10},{7,11},{8,12},{9,13},{1... | collective-permute-start | bytes 1572872 | tf_op jit(solution)/shard_map/ppermute | solution.py:154
  18.3 44.3 %collective-permute-start.10 = (bf16[2,1024,128]{2,1,0:T(8,128)(2,1)}, bf16[2,1024,128]{2,1,0:T(8,128)(2,1)}, u32[]{:S(2)}, u32[]{:S(2)}) collective-permute-start(bf16[2,1024,128]{2,1,0:T(8,128)(2,1)} %pad_maximum_fusion.11), channel_id=1, source_target_pairs={{0,5},{1,6},{2,7},{3,8},{4,9},{5,10},{6,11},{7,12},{8,13},{9,14},{... | collective-permute-start | bytes 1572872 | tf_op jit(solution)/shard_map/ppermute | solution.py:154
  39.9 33.9 %collective-permute-start.9 = (bf16[2,1024,128]{2,1,0:T(8,128)(2,1)}, bf16[2,1024,128]{2,1,0:T(8,128)(2,1)}, u32[]{:S(2)}, u32[]{:S(2)}) collective-permute-start(bf16[2,1024,128]{2,1,0:T(8,128)(2,1)} %pad_maximum_fusion.10), channel_id=1, source_target_pairs={{0,6},{1,7},{2,8},{3,9},{4,10},{5,11},{6,12},{7,13},{8,14},{9,15},... | collective-permute-start | bytes 1572872 | tf_op jit(solution)/shard_map/ppermute | solution.py:154
  43.4 54.2 %collective-permute-start.8 = (bf16[2,1024,128]{2,1,0:T(8,128)(2,1)}, bf16[2,1024,128]{2,1,0:T(8,128)(2,1)}, u32[]{:S(2)}, u32[]{:S(2)}) collective-permute-start(bf16[2,1024,128]{2,1,0:T(8,128)(2,1)} %pad_maximum_fusion.9), channel_id=1, source_target_pairs={{0,7},{1,8},{2,9},{3,10},{4,11},{5,12},{6,13},{7,14},{8,15},{9,0},... | collective-permute-start | bytes 1572872 | tf_op jit(solution)/shard_map/ppermute | solution.py:154
  48.8 51.6 %collective-permute-start.7 = (bf16[2,1024,128]{2,1,0:T(8,128)(2,1)}, bf16[2,1024,128]{2,1,0:T(8,128)(2,1)}, u32[]{:S(2)}, u32[]{:S(2)}) collective-permute-start(bf16[2,1024,128]{2,1,0:T(8,128)(2,1)} %pad_maximum_fusion.8), channel_id=1, source_target_pairs={{0,8},{1,9},{2,10},{3,11},{4,12},{5,13},{6,14},{7,15},{8,0},{9,1},... | collective-permute-start | bytes 1572872 | tf_op jit(solution)/shard_map/ppermute | solution.py:154
  51.3 55.8 %collective-permute-start.6 = (bf16[2,1024,128]{2,1,0:T(8,128)(2,1)}, bf16[2,1024,128]{2,1,0:T(8,128)(2,1)}, u32[]{:S(2)}, u32[]{:S(2)}) collective-permute-start(bf16[2,1024,128]{2,1,0:T(8,128)(2,1)} %pad_maximum_fusion.7), channel_id=1, source_target_pairs={{0,9},{1,10},{2,11},{3,12},{4,13},{5,14},{6,15},{7,0},{8,1},{9,2},... | collective-permute-start | bytes 1572872 | tf_op jit(solution)/shard_map/ppermute | solution.py:154
  62.6 44.6 %collective-permute-start.5 = (bf16[2,1024,128]{2,1,0:T(8,128)(2,1)}, bf16[2,1024,128]{2,1,0:T(8,128)(2,1)}, u32[]{:S(2)}, u32[]{:S(2)}) collective-permute-start(bf16[2,1024,128]{2,1,0:T(8,128)(2,1)} %pad_maximum_fusion.6), channel_id=1, source_target_pairs={{0,10},{1,11},{2,12},{3,13},{4,14},{5,15},{6,0},{7,1},{8,2},{9,3},... | collective-permute-start | bytes 1572872 | tf_op jit(solution)/shard_map/ppermute | solution.py:154
  73.8 80.0 %collective-permute-start.4 = (bf16[2,1024,128]{2,1,0:T(8,128)(2,1)}, bf16[2,1024,128]{2,1,0:T(8,128)(2,1)S(1)}, u32[]{:S(2)}, u32[]{:S(2)}) collective-permute-start(bf16[2,1024,128]{2,1,0:T(8,128)(2,1)} %pad_maximum_fusion.5), channel_id=1, source_target_pairs={{0,11},{1,12},{2,13},{3,14},{4,15},{5,0},{6,1},{7,2},{8,3},{9,4},{... | collective-permute-start | bytes 1572872 | tf_op jit(solution)/shard_map/ppermute | solution.py:154
  97.6 60.9 %collective-permute-start.3 = (bf16[2,1024,128]{2,1,0:T(8,128)(2,1)}, bf16[2,1024,128]{2,1,0:T(8,128)(2,1)}, u32[]{:S(2)}, u32[]{:S(2)}) collective-permute-start(bf16[2,1024,128]{2,1,0:T(8,128)(2,1)} %pad_maximum_fusion.4), channel_id=1, source_target_pairs={{0,12},{1,13},{2,14},{3,15},{4,0},{5,1},{6,2},{7,3},{8,4},{9,5},{1... | collective-permute-start | bytes 1572872 | tf_op jit(solution)/shard_map/ppermute | solution.py:154
  100.4 61.9 %collective-permute-start.2 = (bf16[2,1024,128]{2,1,0:T(8,128)(2,1)}, bf16[2,1024,128]{2,1,0:T(8,128)(2,1)}, u32[]{:S(2)}, u32[]{:S(2)}) collective-permute-start(bf16[2,1024,128]{2,1,0:T(8,128)(2,1)} %pad_maximum_fusion.3), channel_id=1, source_target_pairs={{0,13},{1,14},{2,15},{3,0},{4,1},{5,2},{6,3},{7,4},{8,5},{9,6},{10... | collective-permute-start | bytes 1572872 | tf_op jit(solution)/shard_map/ppermute | solution.py:154
  107.1 59.1 %collective-permute-start.1 = (bf16[2,1024,128]{2,1,0:T(8,128)(2,1)}, bf16[2,1024,128]{2,1,0:T(8,128)(2,1)}, u32[]{:S(2)}, u32[]{:S(2)}) collective-permute-start(bf16[2,1024,128]{2,1,0:T(8,128)(2,1)} %pad_maximum_fusion.2), channel_id=1, source_target_pairs={{0,14},{1,15},{2,0},{3,1},{4,2},{5,3},{6,4},{7,5},{8,6},{9,7},{10,... | collective-permute-start | bytes 1572872 | tf_op jit(solution)/shard_map/ppermute | solution.py:154
  107.1 62.9 %collective-permute-start = (bf16[2,1024,128]{2,1,0:T(8,128)(2,1)}, bf16[2,1024,128]{2,1,0:T(8,128)(2,1)S(1)}, u32[]{:S(2)}, u32[]{:S(2)}) collective-permute-start(bf16[2,1024,128]{2,1,0:T(8,128)(2,1)} %pad_maximum_fusion.1), channel_id=1, source_target_pairs={{0,15},{1,0},{2,1},{3,2},{4,3},{5,4},{6,5},{7,6},{8,7},{9,8},{10,9... | collective-permute-start | bytes 1572872 | tf_op jit(solution)/shard_map/ppermute | solution.py:154
  180.2 32.2 %collective-permute-start.15 = (bf16[8,16,4608]{2,1,0:T(8,128)(2,1)S(1)}, bf16[8,16,4608]{2,1,0:T(8,128)(2,1)}, u32[]{:S(2)}, u32[]{:S(2)}) collective-permute-start(bf16[8,16,4608]{2,1,0:T(8,128)(2,1)S(1)} %fusion.4), channel_id=1, source_target_pairs={{0,1},{1,0},{2,3},{3,2},{4,5},{5,4},{6,7},{7,6},{8,9},{9,8},{10,11... | collective-permute-start | bytes 3538952 | tf_op jit(solution)/shard_map/ppermute | solution.py:99
  215.7 12.3 %collective-permute-start.16 = (bf16[16,4608]{1,0:T(8,128)(2,1)S(1)}, bf16[16,4608]{1,0:T(8,128)(2,1)S(1)}, u32[]{:S(2)}, u32[]{:S(2)}) collective-permute-start(bf16[16,4608]{1,0:T(8,128)(2,1)S(1)} %get-tuple-element.220), channel_id=1, source_target_pairs={{0,2},{2,4},{4,6},{6,8},{8,10},{10,12},{12,14},{14,0},{1,3},{3,5},... | collective-permute-start | bytes 442376 | tf_op jit(solution)/shard_map/ppermute | solution.py:105
  219.8 15.0 %collective-permute-start.17 = (bf16[16,4608]{1,0:T(8,128)(2,1)}, bf16[16,4608]{1,0:T(8,128)(2,1)S(1)}, u32[]{:S(2)}, u32[]{:S(2)}) collective-permute-start(bf16[16,4608]{1,0:T(8,128)(2,1)} %get-tuple-element.226), channel_id=1, source_target_pairs={{0,4},{2,6},{4,8},{6,10},{8,12},{10,14},{12,0},{14,2},{1,5},{3,7},... | collective-permute-start | bytes 442376 | tf_op jit(solution)/shard_map/ppermute | solution.py:105
  220.7 23.4 %collective-permute-start.18 = (bf16[16,4608]{1,0:T(8,128)(2,1)}, bf16[16,4608]{1,0:T(8,128)(2,1)S(1)}, u32[]{:S(2)}, u32[]{:S(2)}) collective-permute-start(bf16[16,4608]{1,0:T(8,128)(2,1)} %get-tuple-element.225), channel_id=1, source_target_pairs={{0,6},{2,8},{4,10},{6,12},{8,14},{10,0},{12,2},{14,4},{1,7},{3,9},... | collective-permute-start | bytes 442376 | tf_op jit(solution)/shard_map/ppermute | solution.py:105
  224.0 24.1 %collective-permute-start.19 = (bf16[16,4608]{1,0:T(8,128)(2,1)}, bf16[16,4608]{1,0:T(8,128)(2,1)S(1)}, u32[]{:S(2)}, u32[]{:S(2)}) collective-permute-start(bf16[16,4608]{1,0:T(8,128)(2,1)} %get-tuple-element.224), channel_id=1, source_target_pairs={{0,8},{2,10},{4,12},{6,14},{8,0},{10,2},{12,4},{14,6},{1,9},{3,11}... | collective-permute-start | bytes 442376 | tf_op jit(solution)/shard_map/ppermute | solution.py:105
  226.5 25.4 %collective-permute-start.20 = (bf16[16,4608]{1,0:T(8,128)(2,1)}, bf16[16,4608]{1,0:T(8,128)(2,1)S(1)}, u32[]{:S(2)}, u32[]{:S(2)}) collective-permute-start(bf16[16,4608]{1,0:T(8,128)(2,1)} %get-tuple-element.223), channel_id=1, source_target_pairs={{0,10},{2,12},{4,14},{6,0},{8,2},{10,4},{12,6},{14,8},{1,11},{3,13... | collective-permute-start | bytes 442376 | tf_op jit(solution)/shard_map/ppermute | solution.py:105
  228.1 27.7 %collective-permute-start.21 = (bf16[16,4608]{1,0:T(8,128)(2,1)}, bf16[16,4608]{1,0:T(8,128)(2,1)}, u32[]{:S(2)}, u32[]{:S(2)}) collective-permute-start(bf16[16,4608]{1,0:T(8,128)(2,1)} %get-tuple-element.222), channel_id=1, source_target_pairs={{0,12},{2,14},{4,0},{6,2},{8,4},{10,6},{12,8},{14,10},{1,13},{3,15... | collective-permute-start | bytes 442376 | tf_op jit(solution)/shard_map/ppermute | solution.py:105
  234.9 24.8 %collective-permute-start.22 = (bf16[16,4608]{1,0:T(8,128)(2,1)}, bf16[16,4608]{1,0:T(8,128)(2,1)}, u32[]{:S(2)}, u32[]{:S(2)}) collective-permute-start(bf16[16,4608]{1,0:T(8,128)(2,1)} %get-tuple-element.221), channel_id=1, source_target_pairs={{0,14},{2,0},{4,2},{6,4},{8,6},{10,8},{12,10},{14,12},{1,15},{3,1}... | collective-permute-start | bytes 442376 | tf_op jit(solution)/shard_map/ppermute | solution.py:105
  276.2 2.9 collective-permute-start.23
  279.4 10.8 %collective-permute-start.24 = (bf16[16,4608]{1,0:T(8,128)(2,1)S(1)}, bf16[16,4608]{1,0:T(8,128)(2,1)S(1)}, u32[]{:S(2)}, u32[]{:S(2)}) collective-permute-start(bf16[16,4608]{1,0:T(8,128)(2,1)S(1)} %get-tuple-element.213), channel_id=1, source_target_pairs={{0,2},{2,4},{4,6},{6,8},{8,10},{10,12},{12,14},{14,0},{1,3},{3,5},... | collective-permute-start | bytes 442376 | tf_op jit(solution)/shard_map/ppermute | solution.py:105
  282.9 14.2 %collective-permute-start.25 = (bf16[16,4608]{1,0:T(8,128)(2,1)S(1)}, bf16[16,4608]{1,0:T(8,128)(2,1)S(1)}, u32[]{:S(2)}, u32[]{:S(2)}) collective-permute-start(bf16[16,4608]{1,0:T(8,128)(2,1)S(1)} %get-tuple-element.219), channel_id=1, source_target_pairs={{0,4},{2,6},{4,8},{6,10},{8,12},{10,14},{12,0},{14,2},{1,5},{3,7},... | collective-permute-start | bytes 442376 | tf_op jit(solution)/shard_map/ppermute | solution.py:105
  282.9 15.4 %collective-permute-start.26 = (bf16[16,4608]{1,0:T(8,128)(2,1)S(1)}, bf16[16,4608]{1,0:T(8,128)(2,1)S(1)}, u32[]{:S(2)}, u32[]{:S(2)}) collective-permute-start(bf16[16,4608]{1,0:T(8,128)(2,1)S(1)} %get-tuple-element.218), channel_id=1, source_target_pairs={{0,6},{2,8},{4,10},{6,12},{8,14},{10,0},{12,2},{14,4},{1,7},{3,9},... | collective-permute-start | bytes 442376 | tf_op jit(solution)/shard_map/ppermute | solution.py:105
  285.7 12.6 %collective-permute-start.27 = (bf16[16,4608]{1,0:T(8,128)(2,1)S(1)}, bf16[16,4608]{1,0:T(8,128)(2,1)S(1)}, u32[]{:S(2)}, u32[]{:S(2)}) collective-permute-start(bf16[16,4608]{1,0:T(8,128)(2,1)S(1)} %get-tuple-element.217), channel_id=1, source_target_pairs={{0,8},{2,10},{4,12},{6,14},{8,0},{10,2},{12,4},{14,6},{1,9},{3,11}... | collective-permute-start | bytes 442376 | tf_op jit(solution)/shard_map/ppermute | solution.py:105
  286.8 13.7 %collective-permute-start.28 = (bf16[16,4608]{1,0:T(8,128)(2,1)S(1)}, bf16[16,4608]{1,0:T(8,128)(2,1)S(1)}, u32[]{:S(2)}, u32[]{:S(2)}) collective-permute-start(bf16[16,4608]{1,0:T(8,128)(2,1)S(1)} %get-tuple-element.216), channel_id=1, source_target_pairs={{0,10},{2,12},{4,14},{6,0},{8,2},{10,4},{12,6},{14,8},{1,11},{3,13... | collective-permute-start | bytes 442376 | tf_op jit(solution)/shard_map/ppermute | solution.py:105
  290.3 10.2 %collective-permute-start.29 = (bf16[16,4608]{1,0:T(8,128)(2,1)S(1)}, bf16[16,4608]{1,0:T(8,128)(2,1)S(1)}, u32[]{:S(2)}, u32[]{:S(2)}) collective-permute-start(bf16[16,4608]{1,0:T(8,128)(2,1)S(1)} %get-tuple-element.215), channel_id=1, source_target_pairs={{0,12},{2,14},{4,0},{6,2},{8,4},{10,6},{12,8},{14,10},{1,13},{3,15... | collective-permute-start | bytes 442376 | tf_op jit(solution)/shard_map/ppermute | solution.py:105
  297.1 7.5 %collective-permute-start.30 = (bf16[16,4608]{1,0:T(8,128)(2,1)S(1)}, bf16[16,4608]{1,0:T(8,128)(2,1)S(1)}, u32[]{:S(2)}, u32[]{:S(2)}) collective-permute-start(bf16[16,4608]{1,0:T(8,128)(2,1)S(1)} %get-tuple-element.214), channel_id=1, source_target_pairs={{0,14},{2,0},{4,2},{6,4},{8,6},{10,8},{12,10},{14,12},{1,15},{3,1}... | collective-permute-start | bytes 442376 | tf_op jit(solution)/shard_map/ppermute | solution.py:105
  (11 other events, 51.3 us)

commit v3 on v0

--- a/solution.py
+++ b/solution.py
@@ -50,9 +50,9 @@
         update(True)
 
 
-def attend_kernel(scalars, q, block, total, summed):
+def attend_kernel(scalars, q, block, index, total, summed):
     n_q, hd = q.shape
-    n_k = block.shape[1]
+    n_k = block.shape[2]
     tq = min(TQ, n_q)
     row = lambda i, sc: (i, 0)
     grid_spec = pltpu.PrefetchScalarGridSpec(
@@ -60,8 +60,8 @@
         grid=(n_q // tq,),
         in_specs=[
             pl.BlockSpec((tq, hd), row),
-            pl.BlockSpec((None, n_k, hd), lambda i, sc: (0, 0, 0)),
-            pl.BlockSpec((None, n_k, hd), lambda i, sc: (1, 0, 0)),
+            pl.BlockSpec((None, None, n_k, hd), lambda i, sc: (0, index, 0, 0)),
+            pl.BlockSpec((None, None, n_k, hd), lambda i, sc: (1, index, 0, 0)),
             pl.BlockSpec((tq, 1), row),
             pl.BlockSpec((tq, hd), row),
         ],
@@ -87,33 +87,48 @@
 
 
 def by_heads(queries, keys, values, row_first):
-    n_kv = lax.axis_size(KV)
-    me = lax.axis_index(KV)
+    n_chip = lax.axis_size("kx")
+    n_core = lax.axis_size("kc")
+    chip = lax.axis_index("kx")
+    core = lax.axis_index("kc")
     group = HQ // KVH
     rows_dev = queries.shape[0]
     key_dev = keys.shape[0]
-    kv_local = keys.shape[1] // (n_kv * HD)
-    kv_feat = kv_local * HD
-    n_q = kv_local * group * rows_dev
-    q_block = queries.reshape(rows_dev, kv_local * group, HD).transpose(1, 0, 2).reshape(n_q, HD)
+    n_q = group * rows_dev
+    q_block = queries.reshape(rows_dev, group, HD).transpose(1, 0, 2).reshape(n_q, HD)
     total = jnp.zeros((n_q, 1), jnp.float32)
     summed = jnp.zeros((n_q, HD), jnp.float32)
-    for shift in range(n_kv):
-        dest = (me + shift) % n_kv
-        src = (me - shift) % n_kv
-        block = jnp.stack(
-            (
-                lax.dynamic_slice_in_dim(keys, dest * kv_feat, kv_feat, 1),
-                lax.dynamic_slice_in_dim(values, dest * kv_feat, kv_feat, 1),
-            ),
-            axis=0,
+    per_core = (keys.reshape(key_dev, n_chip, n_core, HD), values.reshape(key_dev, n_chip, n_core, HD))
+
+    def heads_of(which):
+        return jnp.stack(
+            [lax.dynamic_index_in_dim(part, which, 2, keepdims=False) for part in per_core]
+        ).transpose(0, 2, 1, 3)
+
+    own = heads_of(core)
+    other = lax.ppermute(heads_of(1 - core), "kc", [(0, 1), (1, 0)])
+    own_first = (chip * n_core + core) * key_dev
+    other_first = (chip * n_core + 1 - core) * key_dev
+    arrived = [
+        (lax.dynamic_slice_in_dim(own, chip, 1, 1), own_first),
+        (lax.dynamic_slice_in_dim(other, chip, 1, 1), other_first),
+    ]
+    for shift in range(1, n_chip):
+        dest = (chip + shift) % n_chip
+        src = (chip - shift) % n_chip
+        payload = jnp.concatenate(
+            [lax.dynamic_slice_in_dim(own, dest, 1, 1), lax.dynamic_slice_in_dim(other, dest, 1, 1)],
+            axis=1,
         )
-        if shift:
-            block = lax.ppermute(block, KV, [(j, (j + shift) % n_kv) for j in range(n_kv)])
-        scalars = jnp.stack([row_first, src * key_dev, jnp.int32(rows_dev)]).astype(jnp.int32)
-        total, summed = attend_kernel(scalars, q_block, block, total, summed)
+        moved = lax.ppermute(payload, "kx", [(k, (k + shift) % n_chip) for k in range(n_chip)])
+        arrived.append((moved, (src * n_core + core) * key_dev))
+        arrived.append((moved, (src * n_core + 1 - core) * key_dev))
+    for number, (block, key_first) in enumerate(arrived):
+        index = 0 if number < 2 else number % 2
+        scalars = jnp.stack([row_first, key_first, jnp.int32(rows_dev)]).astype(jnp.int32)
+        total, summed = attend_kernel(scalars, q_block, block, index, total, summed)
     mixed = (summed / total).astype(jnp.bfloat16)
-    return mixed.reshape(kv_local * group, rows_dev, HD).transpose(1, 0, 2).reshape(rows_dev, n_q // rows_dev * HD)
+    return mixed.reshape(group, rows_dev, HD).transpose(1, 0, 2).reshape(rows_dev, group * HD)
 
 
 def per_device(slab_start, queries, keys, values, out_weight):

time: 247 us -> 279 us (1.13)
  waiting for transfers between devices: 25 us -> 66.4 us
  local copies, waits for them, and re-layouts: 15.5 us -> 53.3 us
  starting transfers between devices: 42.9 us -> 10.5 us
  Pallas kernels: 86.2 us -> 77.5 us
  other arithmetic: 35.8 us -> 29 us
    ppermute x15 -> x8, waiting for transfers between devices: 16.8 us -> 58.5 us  [the longest x7 58.5 us: by_heads(): lax.ppermute(payload, 'kx', [(k, (k + shift) % n_chip) for k in range(n_c...]
    ppermute x15 -> x8, starting transfers between devices: 42.9 us -> 10.4 us  [the longest x7 10.4 us: by_heads(): lax.ppermute(payload, 'kx', [(k, (k + shift) % n_chip) for k in range(n_c...]
    dynamic_slice x0 -> x4, local copies, waits for them, and re-layouts: none -> 30.9 us  [the longest x3 27.1 us: heads_of(): lax.dynamic_index_in_dim(part, which, 2, keepdims=False)]
    another operation x32 -> x15, other arithmetic: 27.9 us -> 9.61 us  [by_heads(): jnp.stack([row_first, key_first, jnp.int32(rows_dev)]).astype(jnp.int32)]
    reshape x1 -> x3, local copies, waits for them, and re-layouts: 1.69 us -> 17.3 us  [the longest x1 7.91 us: by_heads(): keys.reshape(key_dev, n_chip, n_core, HD)]
    concatenate x0 -> x7, other arithmetic: none -> 10 us  [by_heads(): jnp.concatenate([lax.dynamic_slice_in_dim(own, dest, 1, 1), lax.dynamic_s...]
    pallas_call x16, Pallas kernels: 86.2 us -> 77.5 us  [attend_kernel(): pl.pallas_call(block_kernel, grid_spec=grid_spec, out_shape=(jax.ShapeDty...]
    another operation x1 -> x0, local copies, waits for them, and re-layouts: 6.65 us -> none  [by_heads(): jnp.stack((lax.dynamic_slice_in_dim(keys, dest * kv_feat, kv_feat, 1), la...]
  transfers between devices with their start and end apart: 16 -> 9, of which waited for: 3 -> 4; matrix products, arithmetic and copies ran while one was open for 12% -> 11% of each run, Pallas kernels for 33% -> 25%
where the time goes in v3:
time: 279 us; the launch traced here: 275 us
  Pallas kernels  77.5 us (28%)
  waiting for transfers between devices  66.4 us (24%)
  local copies, waits for them, and re-layouts  53.3 us (19%)
  blocking collectives  35.8 us (13%)
  other arithmetic  29 us (10%)
  starting transfers between devices  10.5 us (4%)
    pallas_call x16, Pallas kernels, attend_kernel(): pl.pallas_call(block_kernel, grid_spec=grid_spec, out_shape=(jax.ShapeDty...  77.5 us
    ppermute x7, waiting for transfers between devices, by_heads(): lax.ppermute(payload, 'kx', [(k, (k + shift) % n_chip) for k in range(n_c...  58.5 us
    all_to_all x1, blocking collectives, per_device(): lax.all_to_all(on_chip.astype(jnp.bfloat16), 'kx', split_axis=0, concat_a...  35.8 us
    dynamic_slice x3, local copies, waits for them, and re-layouts, heads_of(): lax.dynamic_index_in_dim(part, which, 2, keepdims=False)  27.1 us
    ppermute x7, starting transfers between devices, by_heads(): lax.ppermute(payload, 'kx', [(k, (k + shift) % n_chip) for k in range(n_c...  10.4 us
    concatenate x7, other arithmetic, by_heads(): jnp.concatenate([lax.dynamic_slice_in_dim(own, dest, 1, 1), lax.dynamic_s...  10 us
    another operation x15, other arithmetic, by_heads(): jnp.stack([row_first, key_first, jnp.int32(rows_dev)]).astype(jnp.int32)  9.61 us
    reshape x1, local copies, waits for them, and re-layouts, by_heads(): keys.reshape(key_dev, n_chip, n_core, HD)  7.91 us
  transfers between devices with their start and end apart: 9, of which 4 were waited for; matrix products, arithmetic and copies ran while one was open for 11% of the time, Pallas kernels for 25%

profile of v3, /device:TPU:120, one launch (start us, length us, event | category | flops | bytes accessed | tf_op | source)
XLA Modules:
  0.0 274.7 jit_solution(4886271090636669583)
XLA Ops:
  0.0 7.9 %reshape.33 = bf16[1024,8,2,128]{3,2,1,0:T(2,128)(2,1)} reshape(bf16[1024,2048]{1,0:T(8,128)(2,1)} %param.7) | data formatting | bytes 8388608 | tf_op jit(solution)/shard_map/reshape | solution.py:101
  7.9 7.7 %reshape.34 = bf16[1024,8,2,128]{3,2,1,0:T(2,128)(2,1)} reshape(bf16[1024,2048]{1,0:T(8,128)(2,1)} %param.8) | data formatting | bytes 8388608 | tf_op jit(solution)/shard_map/reshape | solution.py:101
  15.6 20.4 %constant_dynamic-slice_fusion.10 = (bf16[1024,8,1,128]{3,2,1,0:T(2,128)(2,1)}, bf16[1024,8,1,128]{3,2,1,0:T(2,128)(2,1)S(1)}, bf16[1024,8,1,128]{3,2,1,0:T(2,128)(2,1)S(1)}, bf16[1024,8,1,128]{3,2,1,0:T(2,128)(2,1)}) fusion(bf16[1024,8,2,128]{3,2,1,0:T(2,128)(2,1)} %reshape.34, s32[]{:T(128)S(6)} %select_n.104, s32[]{:T(128)S(6)} %select_n.107, ...), kind=kLoop, calls=%fused_computation.62 | loop fusion | bytes 16777224 | tf_op jit(solution)/shard_map/jit(dynamic_index_in_dim)/dynamic_slice | solution.py:105
  37.6 2.4 maximum_bitcast_fusion
  40.0 4.5 %copy.69 = bf16[1024,8,1,128]{3,0,1,2:T(8,128)(2,1)} copy(bf16[1024,8,1,128]{3,2,1,0:T(2,128)(2,1)} %get-tuple-element.87) | data formatting | bytes 4194304 | tf_op jit(solution)/shard_map/jit(dynamic_index_in_dim)/dynamic_slice | solution.py:105
  44.5 2.2 copy.70
  56.1 3.8 %constant_dynamic-slice_fusion = (bf16[2,1,1024,128]{3,2,1,0:T(8,128)(2,1)}, bf16[2,1,1024,128]{3,2,1,0:T(8,128)(2,1)S(1)}, bf16[2,1,1024,128]{3,2,1,0:T(8,128)(...) fusion(bf16[2,8,1024,128]{3,2,1,0:T(8,128)(2,1)} %collective-pe, ...), kind=kLoop, calls=%fused_computation.52 | loop fusion | bytes 8388640 | tf_op jit(solution)/shard_map/dynamic_slice | solution.py:114
  68.7 2.4 pad_maximum_fusion.4
  71.1 3.5 %collective-permute-start.5 = (bf16[2,2,1024,128]{3,2,1,0:T(8,128)(2,1)}, bf16[2,2,1024,128]{3,2,1,0:T(8,128)(2,1)}, u32[]{:S(2)}, u32[]{:S(2)}) collective-permute-start(bf16[2,2,1024,128]{3,2,1,0:T(8,128)(2,1)} %pad_maximum_fusion.4), channel_id=1, source_target_pairs={{0,6},{2,8},{4,10},{6,12},{8,14},{10,0},{12,2},{14,4},{1,7},{3,9},... | collective-permute-start | bytes 3145736 | tf_op jit(solution)/shard_map/ppermute | solution.py:123
  74.6 2.3 pad_maximum_fusion.3
  78.8 2.4 collective-permute-start.3
  83.4 23.6 %collective-permute-done.7.k_ref.v_ref = bf16[2,2,1024,128]{3,2,1,0:T(8,128)(2,1)} collective-permute-done((bf16[2,2,1024,128]{3,2,1,0:T(8,128)(2,1)}, bf16[2,2,1024,128]{3,2,1,0:T(8,128)(2,1)}, u32[]{:S(2)}, u32[]{:S(2)}) %collective-permute-start.7) | collective-permute-done | bytes 1048608 | tf_op jit(solution)/shard_map/ppermute | solution.py:123
  106.9 22.5 %collective-permute-done.6.k_ref.v_ref = bf16[2,2,1024,128]{3,2,1,0:T(8,128)(2,1)} collective-permute-done((bf16[2,2,1024,128]{3,2,1,0:T(8,128)(2,1)}, bf16[2,2,1024,128]{3,2,1,0:T(8,128)(2,1)}, u32[]{:S(2)}, u32[]{:S(2)}) %collective-permute-start.6) | collective-permute-done | bytes 1048608 | tf_op jit(solution)/shard_map/ppermute | solution.py:123
  131.7 5.6 %shard_map.55 = (f32[1024,1]{1,0:T(8,128)}, f32[1024,128]{1,0:T(8,128)}) custom-call(s32[3]{0:T(128)} %pad_add_fusion.sc_ref, bf16[1024,128]{1,0:T(8,128)(2,1)} %bitcast.79, bf16[2,1,1024,128]{3,2,1,0:T(8,128)(2,1)} %get-tuple-element.69.k_ref.v_ref, ...), custom_call_target="tpu_custom_call", output_to_operand_aliasing={{0}: (4, {}), {1}: (5, {})} | custom-call | flops 536870912 | bytes 1843200 | tf_op jit(solution)/shard_map/pallas_call | solution.py:73
  139.2 5.6 %shard_map.56 = (f32[1024,1]{1,0:T(8,128)}, f32[1024,128]{1,0:T(8,128)}) custom-call(s32[3]{0:T(128)} %pad_add_fusion.1.sc_ref, bf16[1024,128]{1,0:T(8,128)(2,1)} %bitcast.80, bf16[2,1,1024,128]{3,2,1,0:T(8,128)(2,1)} %get-tuple-element.75.k_ref.v_ref, ...), custom_call_target="tpu_custom_call", output_to_operand_aliasing={{0}: (4, {}), {1}: (5, {})} | custom-call | flops 536870912 | bytes 1843200 | tf_op jit(solution)/shard_map/pallas_call | solution.py:73
  144.9 5.6 %shard_map.57 = (f32[1024,1]{1,0:T(8,128)}, f32[1024,128]{1,0:T(8,128)}) custom-call(s32[3]{0:T(128)} %get-tuple-element.89.sc_ref, bf16[1024,128]{1,0:T(8,128)(2,1)} %bitcast.81, bf16[2,2,1024,128]{3,2,1,0:T(8,128)(2,1)} %collective-permute-done.7.k_ref.v_ref, ...), custom_call_target="tpu_custom_call", output_to_operand_aliasing={{0}: (4, {}), {1}: (5, {})} | custom-call | flops 536870912 | bytes 1843200 | tf_op jit(solution)/shard_map/pallas_call | solution.py:73
  150.5 5.6 %shard_map.58 = (f32[1024,1]{1,0:T(8,128)}, f32[1024,128]{1,0:T(8,128)}) custom-call(s32[3]{0:T(128)} %get-tuple-element.90.sc_ref, bf16[1024,128]{1,0:T(8,128)(2,1)} %bitcast.82, bf16[2,2,1024,128]{3,2,1,0:T(8,128)(2,1)} %collective-permute-done.7.k_ref.v_ref, ...), custom_call_target="tpu_custom_call", output_to_operand_aliasing={{0}: (4, {}), {1}: (5, {})} | custom-call | flops 536870912 | bytes 1843200 | tf_op jit(solution)/shard_map/pallas_call | solution.py:73
  156.1 4.5 %shard_map.59 = (f32[1024,1]{1,0:T(8,128)}, f32[1024,128]{1,0:T(8,128)}) custom-call(s32[3]{0:T(128)} %pad_add_fusion.4.sc_ref, bf16[1024,128]{1,0:T(8,128)(2,1)} %bitcast.83, bf16[2,2,1024,128]{3,2,1,0:T(8,128)(2,1)} %collective-permute-done.6.k_ref.v_ref, ...), custom_call_target="tpu_custom_call", output_to_operand_aliasing={{0}: (4, {}), {1}: (5, {})} | custom-call | flops 536870912 | bytes 1843200 | tf_op jit(solution)/shard_map/pallas_call | solution.py:73
  160.6 4.5 %shard_map.60 = (f32[1024,1]{1,0:T(8,128)}, f32[1024,128]{1,0:T(8,128)}) custom-call(s32[3]{0:T(128)} %pad_add_fusion.5.sc_ref, bf16[1024,128]{1,0:T(8,128)(2,1)} %bitcast.84, bf16[2,2,1024,128]{3,2,1,0:T(8,128)(2,1)} %collective-permute-done.6.k_ref.v_ref, ...), custom_call_target="tpu_custom_call", output_to_operand_aliasing={{0}: (4, {}), {1}: (5, {})} | custom-call | flops 536870912 | bytes 1843200 | tf_op jit(solution)/shard_map/pallas_call | solution.py:73
  165.0 4.5 %shard_map.61 = (f32[1024,1]{1,0:T(8,128)}, f32[1024,128]{1,0:T(8,128)}) custom-call(s32[3]{0:T(128)} %pad_add_fusion.6.sc_ref, bf16[1024,128]{1,0:T(8,128)(2,1)} %bitcast.85, bf16[2,2,1024,128]{3,2,1,0:T(8,128)(2,1)} %collective-permute-done.5.k_ref.v_ref, ...), custom_call_target="tpu_custom_call", output_to_operand_aliasing={{0}: (4, {}), {1}: (5, {})} | custom-call | flops 536870912 | bytes 1843200 | tf_op jit(solution)/shard_map/pallas_call | solution.py:73
  169.5 4.5 %shard_map.62 = (f32[1024,1]{1,0:T(8,128)}, f32[1024,128]{1,0:T(8,128)}) custom-call(s32[3]{0:T(128)} %pad_add_fusion.7.sc_ref, bf16[1024,128]{1,0:T(8,128)(2,1)} %bitcast.86, bf16[2,2,1024,128]{3,2,1,0:T(8,128)(2,1)} %collective-permute-done.5.k_ref.v_ref, ...), custom_call_target="tpu_custom_call", output_to_operand_aliasing={{0}: (4, {}), {1}: (5, {})} | custom-call | flops 536870912 | bytes 1843200 | tf_op jit(solution)/shard_map/pallas_call | solution.py:73
  174.0 12.4 %collective-permute-done.4.k_ref.v_ref = bf16[2,2,1024,128]{3,2,1,0:T(8,128)(2,1)} collective-permute-done((bf16[2,2,1024,128]{3,2,1,0:T(8,128)(2,1)}, bf16[2,2,1024,128]{3,2,1,0:T(8,128)(2,1)}, u32[]{:S(2)}, u32[]{:S(2)}) %collective-permute-start.4) | collective-permute-done | bytes 1048608 | tf_op jit(solution)/shard_map/ppermute | solution.py:123
  186.4 4.5 %shard_map.63 = (f32[1024,1]{1,0:T(8,128)}, f32[1024,128]{1,0:T(8,128)}) custom-call(s32[3]{0:T(128)} %pad_add_fusion.8.sc_ref, bf16[1024,128]{1,0:T(8,128)(2,1)} %bitcast.87, bf16[2,2,1024,128]{3,2,1,0:T(8,128)(2,1)} %collective-permute-done.4.k_ref.v_ref, ...), custom_call_target="tpu_custom_call", output_to_operand_aliasing={{0}: (4, {}), {1}: (5, {})} | custom-call | flops 536870912 | bytes 1843200 | tf_op jit(solution)/shard_map/pallas_call | solution.py:73
  190.8 4.5 %shard_map.64 = (f32[1024,1]{1,0:T(8,128)}, f32[1024,128]{1,0:T(8,128)}) custom-call(s32[3]{0:T(128)} %pad_add_fusion.9.sc_ref, bf16[1024,128]{1,0:T(8,128)(2,1)} %bitcast.88, bf16[2,2,1024,128]{3,2,1,0:T(8,128)(2,1)} %collective-permute-done.4.k_ref.v_ref, ...), custom_call_target="tpu_custom_call", output_to_operand_aliasing={{0}: (4, {}), {1}: (5, {})} | custom-call | flops 536870912 | bytes 1843200 | tf_op jit(solution)/shard_map/pallas_call | solution.py:73
  195.3 4.7 %shard_map.65 = (f32[1024,1]{1,0:T(8,128)}, f32[1024,128]{1,0:T(8,128)}) custom-call(s32[3]{0:T(128)} %pad_add_fusion.10.sc_ref, bf16[1024,128]{1,0:T(8,128)(2,1)} %bitcast.89, bf16[2,2,1024,128]{3,2,1,0:T(8,128)(2,1)} %collective-permute-done.3.k_ref.v_ref, ...), custom_call_target="tpu_custom_call", output_to_operand_aliasing={{0}: (4, {}), {1}: (5, {})} | custom-call | flops 536870912 | bytes 1843200 | tf_op jit(solution)/shard_map/pallas_call | solution.py:73
  200.0 4.5 %shard_map.66 = (f32[1024,1]{1,0:T(8,128)}, f32[1024,128]{1,0:T(8,128)}) custom-call(s32[3]{0:T(128)} %pad_add_fusion.11.sc_ref, bf16[1024,128]{1,0:T(8,128)(2,1)} %bitcast.90, bf16[2,2,1024,128]{3,2,1,0:T(8,128)(2,1)} %collective-permute-done.3.k_ref.v_ref, ...), custom_call_target="tpu_custom_call", output_to_operand_aliasing={{0}: (4, {}), {1}: (5, {})} | custom-call | flops 536870912 | bytes 1843200 | tf_op jit(solution)/shard_map/pallas_call | solution.py:73
  204.4 4.5 %shard_map.67 = (f32[1024,1]{1,0:T(8,128)}, f32[1024,128]{1,0:T(8,128)}) custom-call(s32[3]{0:T(128)} %pad_add_fusion.12.sc_ref, bf16[1024,128]{1,0:T(8,128)(2,1)} %bitcast.91, bf16[2,2,1024,128]{3,2,1,0:T(8,128)(2,1)} %collective-permute-done.2.k_ref.v_ref, ...), custom_call_target="tpu_custom_call", output_to_operand_aliasing={{0}: (4, {}), {1}: (5, {})} | custom-call | flops 536870912 | bytes 1843200 | tf_op jit(solution)/shard_map/pallas_call | solution.py:73
  208.9 4.5 %shard_map.68 = (f32[1024,1]{1,0:T(8,128)}, f32[1024,128]{1,0:T(8,128)}) custom-call(s32[3]{0:T(128)} %pad_add_fusion.13.sc_ref, bf16[1024,128]{1,0:T(8,128)(2,1)} %bitcast.92, bf16[2,2,1024,128]{3,2,1,0:T(8,128)(2,1)} %collective-permute-done.2.k_ref.v_ref, ...), custom_call_target="tpu_custom_call", output_to_operand_aliasing={{0}: (4, {}), {1}: (5, {})} | custom-call | flops 536870912 | bytes 1843200 | tf_op jit(solution)/shard_map/pallas_call | solution.py:73
  214.3 5.7 %shard_map.69 = (f32[1024,1]{1,0:T(8,128)}, f32[1024,128]{1,0:T(8,128)}) custom-call(s32[3]{0:T(128)} %pad_add_fusion.14.sc_ref, bf16[1024,128]{1,0:T(8,128)(2,1)} %bitcast.93, bf16[2,2,1024,128]{3,2,1,0:T(8,128)(2,1)} %copy-done.8, bf16[2,2,1024,128]{3,2,1,0:T(8,128)(2,1)} %copy-done.8, ...), custom_call_target="tpu_custom_call", output_to_operand_aliasing={{0}: (4, {}), {1}: (5, {})} | custom-call | flops 536870912 | bytes 1843200 | tf_op jit(solution)/shard_map/pallas_call | solution.py:73
  220.0 4.5 %shard_map.70 = (f32[1024,1]{1,0:T(8,128)}, f32[1024,128]{1,0:T(8,128)}) custom-call(s32[3]{0:T(128)} %pad_add_fusion.15.sc_ref, bf16[1024,128]{1,0:T(8,128)(2,1)} %bitcast.94, bf16[2,2,1024,128]{3,2,1,0:T(8,128)(2,1)} %copy-done.8, bf16[2,2,1024,128]{3,2,1,0:T(8,128)(2,1)} %copy-done.8, ...), custom_call_target="tpu_custom_call", output_to_operand_aliasing={{0}: (4, {}), {1}: (5, {})} | custom-call | flops 536870912 | bytes 1843200 | tf_op jit(solution)/shard_map/pallas_call | solution.py:73
  229.3 7.9 %collective-permute-done.8 = f32[8,32,4608]{2,1,0:T(8,128)S(1)} collective-permute-done((f32[8,32,4608]{2,1,0:T(8,128)S(1)}, f32[8,32,4608]{2,1,0:T(8,128)S(1)}, u32[]{:S(2)}, u32[]{:S(2)}) %collective-permute-start.8) | collective-permute-done | bytes 4718624 | tf_op jit(solution)/shard_map/ppermute | solution.py:145
  237.8 35.8 %all_to_all.5 = bf16[8,32,4608]{2,1,0:T(8,128)(2,1)S(1)} all-to-all(bf16[8,32,4608]{2,1,0:T(8,128)(2,1)S(1)} %fusion), channel_id=1, replica_groups=mesh['pb'=8,'kx'=8,'kc'=2] {'kx'}, dimensions={0} | all-to-all | bytes 4718592 | tf_op jit(solution)/shard_map/all_to_all | solution.py:146
  (65 shorter events, 34.7 us)
Async XLA Ops:
  0.0 227.5 %copy-start = (bf16[256,4608]{1,0:T(8,128)(2,1)S(1)}, bf16[256,4608]{1,0:T(8,128)(2,1)}, u32[]{:S(2)}) copy-start(bf16[256,4608]{1,0:T(8,128)(2,1)} %param.9) | copy-start | bytes 7077892
  40.0 16.1 %collective-permute-start = (bf16[2,8,1024,128]{3,2,1,0:T(8,128)(2,1)}, bf16[2,8,1024,128]{3,2,1,0:T(8,128)(2,1)}, u32[]{:S(2)}, u32[]{:S(2)}) collective-permute-start(bf16[2,8,1024,128]{3,2,1,0:T(8,128)(2,1)} %maximum_bitcast_fusion), channel_id=1, source_target_pairs={{0,1},{1,0},{2,3},{3,2},{4,5},{5,4},{6,7},{7,6},{8,9},{9,8},{10,11... | collective-permute-start | bytes 12582920 | tf_op jit(solution)/shard_map/ppermute | solution.py:109
  40.0 4.5 %copy-start.3 = (bf16[1024,8,1,128]{3,2,1,0:T(2,128)(2,1)S(1)}, bf16[1024,8,1,128]{3,2,1,0:T(2,128)(2,1)}, u32[]{:S(2)}) copy-start(bf16[1024,8,1,128]{3,2,1,0:T(2,128)(2,1)} %get-tuple-element.92) | copy-start | bytes 6291460
  47.4 7.2 %copy-start.1 = (bf16[1024,8,1,128]{3,0,1,2:T(8,128)(2,1)S(1)}, bf16[1024,8,1,128]{3,0,1,2:T(8,128)(2,1)}, u32[]{:S(2)}) copy-start(bf16[1024,8,1,128]{3,0,1,2:T(8,128)(2,1)} %copy.69) | copy-start | bytes 6291460
  47.4 7.2 %copy-start.2 = (bf16[1024,8,1,128]{3,0,1,2:T(8,128)(2,1)S(1)}, bf16[1024,8,1,128]{3,0,1,2:T(8,128)(2,1)}, u32[]{:S(2)}) copy-start(bf16[1024,8,1,128]{3,0,1,2:T(8,128)(2,1)} %copy.70) | copy-start | bytes 6291460
  61.0 45.9 %collective-permute-start.7 = (bf16[2,2,1024,128]{3,2,1,0:T(8,128)(2,1)}, bf16[2,2,1024,128]{3,2,1,0:T(8,128)(2,1)}, u32[]{:S(2)}, u32[]{:S(2)}) collective-permute-start(bf16[2,2,1024,128]{3,2,1,0:T(8,128)(2,1)} %pad_maximum_fusion.6), channel_id=1, source_target_pairs={{0,2},{2,4},{4,6},{6,8},{8,10},{10,12},{12,14},{14,0},{1,3},{3,5},... | collective-permute-start | bytes 3145736 | tf_op jit(solution)/shard_map/ppermute | solution.py:123
  64.3 65.1 %collective-permute-start.6 = (bf16[2,2,1024,128]{3,2,1,0:T(8,128)(2,1)}, bf16[2,2,1024,128]{3,2,1,0:T(8,128)(2,1)}, u32[]{:S(2)}, u32[]{:S(2)}) collective-permute-start(bf16[2,2,1024,128]{3,2,1,0:T(8,128)(2,1)} %pad_maximum_fusion.5), channel_id=1, source_target_pairs={{0,4},{2,6},{4,8},{6,10},{8,12},{10,14},{12,0},{14,2},{1,5},{3,7},... | collective-permute-start | bytes 3145736 | tf_op jit(solution)/shard_map/ppermute | solution.py:123
  66.4 11.3 %copy-start.4 = (bf16[2,1,1024,128]{3,2,1,0:T(8,128)(2,1)S(1)}, bf16[2,1,1024,128]{3,2,1,0:T(8,128)(2,1)}, u32[]{:S(2)}) copy-start(bf16[2,1,1024,128]{3,2,1,0:T(8,128)(2,1)} %get-tuple-element.72) | copy-start | bytes 1572868
  66.4 11.3 %copy-start.7 = (bf16[2,1,1024,128]{3,2,1,0:T(8,128)(2,1)S(1)}, bf16[2,1,1024,128]{3,2,1,0:T(8,128)(2,1)}, u32[]{:S(2)}) copy-start(bf16[2,1,1024,128]{3,2,1,0:T(8,128)(2,1)} %get-tuple-element.80) | copy-start | bytes 1572868
  66.4 14.8 %copy-start.6 = (bf16[2,1,1024,128]{3,2,1,0:T(8,128)(2,1)S(1)}, bf16[2,1,1024,128]{3,2,1,0:T(8,128)(2,1)}, u32[]{:S(2)}) copy-start(bf16[2,1,1024,128]{3,2,1,0:T(8,128)(2,1)} %get-tuple-element.81) | copy-start | bytes 1572868
  68.7 13.6 %copy-start.5 = (bf16[2,1,1024,128]{3,2,1,0:T(8,128)(2,1)S(1)}, bf16[2,1,1024,128]{3,2,1,0:T(8,128)(2,1)}, u32[]{:S(2)}) copy-start(bf16[2,1,1024,128]{3,2,1,0:T(8,128)(2,1)} %get-tuple-element.82) | copy-start | bytes 1572868
  71.1 94.0 %collective-permute-start.5 = (bf16[2,2,1024,128]{3,2,1,0:T(8,128)(2,1)}, bf16[2,2,1024,128]{3,2,1,0:T(8,128)(2,1)}, u32[]{:S(2)}, u32[]{:S(2)}) collective-permute-start(bf16[2,2,1024,128]{3,2,1,0:T(8,128)(2,1)} %pad_maximum_fusion.4), channel_id=1, source_target_pairs={{0,6},{2,8},{4,10},{6,12},{8,14},{10,0},{12,2},{14,4},{1,7},{3,9},... | collective-permute-start | bytes 3145736 | tf_op jit(solution)/shard_map/ppermute | solution.py:123
  76.9 109.5 %collective-permute-start.4 = (bf16[2,2,1024,128]{3,2,1,0:T(8,128)(2,1)}, bf16[2,2,1024,128]{3,2,1,0:T(8,128)(2,1)}, u32[]{:S(2)}, u32[]{:S(2)}) collective-permute-start(bf16[2,2,1024,128]{3,2,1,0:T(8,128)(2,1)} %pad_maximum_fusion.3), channel_id=1, source_target_pairs={{0,8},{2,10},{4,12},{6,14},{8,0},{10,2},{12,4},{14,6},{1,9},{3,11}... | collective-permute-start | bytes 3145736 | tf_op jit(solution)/shard_map/ppermute | solution.py:123
  78.8 116.5 %collective-permute-start.3 = (bf16[2,2,1024,128]{3,2,1,0:T(8,128)(2,1)}, bf16[2,2,1024,128]{3,2,1,0:T(8,128)(2,1)}, u32[]{:S(2)}, u32[]{:S(2)}) collective-permute-start(bf16[2,2,1024,128]{3,2,1,0:T(8,128)(2,1)} %pad_maximum_fusion.2), channel_id=1, source_target_pairs={{0,10},{2,12},{4,14},{6,0},{8,2},{10,4},{12,6},{14,8},{1,11},{3,13... | collective-permute-start | bytes 3145736 | tf_op jit(solution)/shard_map/ppermute | solution.py:123
  106.9 97.5 %collective-permute-start.2 = (bf16[2,2,1024,128]{3,2,1,0:T(8,128)(2,1)}, bf16[2,2,1024,128]{3,2,1,0:T(8,128)(2,1)}, u32[]{:S(2)}, u32[]{:S(2)}) collective-permute-start(bf16[2,2,1024,128]{3,2,1,0:T(8,128)(2,1)} %pad_maximum_fusion.1), channel_id=1, source_target_pairs={{0,12},{2,14},{4,0},{6,2},{8,4},{10,6},{12,8},{14,10},{1,13},{3,15... | collective-permute-start | bytes 3145736 | tf_op jit(solution)/shard_map/ppermute | solution.py:123
  129.4 84.0 %collective-permute-start.1 = (bf16[2,2,1024,128]{3,2,1,0:T(8,128)(2,1)}, bf16[2,2,1024,128]{3,2,1,0:T(8,128)(2,1)S(1)}, u32[]{:S(2)}, u32[]{:S(2)}) collective-permute-start(bf16[2,2,1024,128]{3,2,1,0:T(8,128)(2,1)} %pad_maximum_fusion), channel_id=1, source_target_pairs={{0,14},{2,0},{4,2},{6,4},{8,6},{10,8},{12,10},{14,12},{1,15},{3,1}... | collective-permute-start | bytes 3145736 | tf_op jit(solution)/shard_map/ppermute | solution.py:123
  213.4 1.0 copy-start.8
  229.2 8.0 %collective-permute-start.8 = (f32[8,32,4608]{2,1,0:T(8,128)S(1)}, f32[8,32,4608]{2,1,0:T(8,128)S(1)}, u32[]{:S(2)}, u32[]{:S(2)}) collective-permute-start(f32[8,32,4608]{2,1,0:T(8,128)S(1)} %dynamic-slice_bitcast_fusion), channel_id=1, source_target_pairs={{0,1},{1,0},{2,3},{3,2},{4,5},{5,4},{6,7},{7,6},{8,9},{9,8},{10,11... | collective-permute-start | bytes 14155784 | tf_op jit(solution)/shard_map/ppermute | solution.py:145

commit v4 on v0

--- a/solution.py
+++ b/solution.py
@@ -99,8 +99,8 @@
     total = jnp.zeros((n_q, 1), jnp.float32)
     summed = jnp.zeros((n_q, HD), jnp.float32)
     for shift in range(n_kv):
-        dest = (me + shift) % n_kv
-        src = (me - shift) % n_kv
+        dest = me ^ shift
+        src = dest
         block = jnp.stack(
             (
                 lax.dynamic_slice_in_dim(keys, dest * kv_feat, kv_feat, 1),
@@ -109,7 +109,7 @@
             axis=0,
         )
         if shift:
-            block = lax.ppermute(block, KV, [(j, (j + shift) % n_kv) for j in range(n_kv)])
+            block = lax.ppermute(block, KV, [(j, j ^ shift) for j in range(n_kv)])
         scalars = jnp.stack([row_first, src * key_dev, jnp.int32(rows_dev)]).astype(jnp.int32)
         total, summed = attend_kernel(scalars, q_block, block, total, summed)
     mixed = (summed / total).astype(jnp.bfloat16)

time: 247 us -> 236 us (0.955)
  starting transfers between devices: 42.9 us -> 24.7 us
  waiting for transfers between devices: 25 us -> 33.6 us
  blocking collectives: 37.6 us -> 40.4 us
    ppermute x15, starting transfers between devices: 42.9 us -> 24.4 us  [by_heads(): block = lax.ppermute(block, KV, [(j, j ^ shift) for j in range(n_kv)])]
    ppermute x15, waiting for transfers between devices: 16.8 us -> 25.7 us  [by_heads(): block = lax.ppermute(block, KV, [(j, j ^ shift) for j in range(n_kv)])]
    all_to_all x1, blocking collectives: 37.6 us -> 40.4 us  [per_device(): lax.all_to_all(on_chip.astype(jnp.bfloat16), 'kx', split_axis=0, concat_a...]
  transfers between devices with their start and end apart: 16 -> 16, of which waited for: 3 -> 5; matrix products, arithmetic and copies ran while one was open for 12% -> 12% of each run, Pallas kernels for 33% -> 34%
where the time goes in v4:
time: 236 us
  Pallas kernels  85 us (36%)
  blocking collectives  40.4 us (17%)
  other arithmetic  34.8 us (15%)
  waiting for transfers between devices  33.6 us (14%)
  starting transfers between devices  24.7 us (10%)
  local copies, waits for them, and re-layouts  15.5 us (7%)
    pallas_call x16, Pallas kernels, attend_kernel(): pl.pallas_call(block_kernel, grid_spec=grid_spec, out_shape=(jax.ShapeDty...  85 us
    all_to_all x1, blocking collectives, per_device(): lax.all_to_all(on_chip.astype(jnp.bfloat16), 'kx', split_axis=0, concat_a...  40.4 us
    ppermute x15, waiting for transfers between devices, by_heads(): block = lax.ppermute(block, KV, [(j, j ^ shift) for j in range(n_kv)])  25.7 us
    ppermute x15, starting transfers between devices, by_heads(): block = lax.ppermute(block, KV, [(j, j ^ shift) for j in range(n_kv)])  24.4 us
    another operation x16, other arithmetic, by_heads(): jnp.stack((lax.dynamic_slice_in_dim(keys, dest * kv_feat, kv_feat, 1), la...  17 us
    another operation x16, other arithmetic, by_heads(): jnp.stack([row_first, src * key_dev, jnp.int32(rows_dev)]).astype(jnp.int32)  9.82 us
    ppermute x1, waiting for transfers between devices, per_device(): on_chip = mine + lax.ppermute(theirs, 'kc', [(0, 1), (1, 0)])  7.91 us
    another operation x1, local copies, waits for them, and re-layouts, by_heads(): jnp.stack((lax.dynamic_slice_in_dim(keys, dest * kv_feat, kv_feat, 1), la...  6.65 us
  transfers between devices with their start and end apart: 16, of which 5 were waited for; matrix products, arithmetic and copies ran while one was open for 12% of the time, Pallas kernels for 34%

profile of v4, /device:TPU:120, one launch (start us, length us, event | category | flops | bytes accessed | tf_op | source)
XLA Modules:
  0.0 236.3 jit_solution(4348200446557256975)
XLA Ops:
  0.0 6.7 %dynamic-slice_bitcast_fusion.1 = (bf16[1,1024,128]{2,1,0:T(8,128)(2,1)}, bf16[1,1024,128]{2,1,0:T(8,128)(2,1)}, bf16[1,1024,128]{2,1,0:T(8,128)(2,1)}, bf16[1,1...) fusion(bf16[1024,2048]{1,0:T(8,128)(2,1)} %param.8, ...), kind=kLoop, calls=%fused_computation.24 | loop fusion | bytes 16777280 | tf_op jit(solution)/shard_map/stack | solution.py:104
  8.4 3.7 %collective-permute-start.5 = (bf16[2,1024,128]{2,1,0:T(8,128)(2,1)}, bf16[2,1024,128]{2,1,0:T(8,128)(2,1)}, u32[]{:S(2)}, u32[]{:S(2)}) collective-permute-start(bf16[2,1024,128]{2,1,0:T(8,128)(2,1)} %pad_maximum_fusion.5), channel_id=1, source_target_pairs={{0,10},{1,11},{2,8},{3,9},{4,14},{5,15},{6,12},{7,13},{8,2},{9,3},... | collective-permute-start | bytes 1572872 | tf_op jit(solution)/shard_map/ppermute | solution.py:112
  14.1 3.0 %collective-permute-start.7 = (bf16[2,1024,128]{2,1,0:T(8,128)(2,1)}, bf16[2,1024,128]{2,1,0:T(8,128)(2,1)}, u32[]{:S(2)}, u32[]{:S(2)}) collective-permute-start(bf16[2,1024,128]{2,1,0:T(8,128)(2,1)} %pad_maximum_fusion.7), channel_id=1, source_target_pairs={{0,8},{1,9},{2,10},{3,11},{4,12},{5,13},{6,14},{7,15},{8,0},{9,1},... | collective-permute-start | bytes 1572872 | tf_op jit(solution)/shard_map/ppermute | solution.py:112
  26.8 2.0 pad_maximum_fusion.15.k_ref.v_ref
  41.5 2.2 collective-permute-start.9
  44.7 2.2 collective-permute-start.12
  48.1 2.3 collective-permute-start.13
  51.0 9.4 %collective-permute-done.8.k_ref.v_ref = bf16[2,1024,128]{2,1,0:T(8,128)(2,1)} collective-permute-done((bf16[2,1024,128]{2,1,0:T(8,128)(2,1)}, bf16[2,1024,128]{2,1,0:T(8,128)(2,1)}, u32[]{:S(2)}, u32[]{:S(2)}) %collective-permute-start.8) | collective-permute-done | bytes 524320 | tf_op jit(solution)/shard_map/ppermute | solution.py:112
  64.1 8.2 %collective-permute-done.9.k_ref.v_ref = bf16[2,1024,128]{2,1,0:T(8,128)(2,1)S(1)} collective-permute-done((bf16[2,1024,128]{2,1,0:T(8,128)(2,1)}, bf16[2,1024,128]{2,1,0:T(8,128)(2,1)S(1)}, u32[]{:S(2)}, u32[]{:S(2)}) %collective-permute-start.9) | collective-permute-done | bytes 524320 | tf_op jit(solution)/shard_map/ppermute | solution.py:112
  75.5 5.6 %shard_map.55 = (f32[1024,1]{1,0:T(8,128)}, f32[1024,128]{1,0:T(8,128)}) custom-call(s32[3]{0:T(128)} %pad_add_fusion.sc_ref, bf16[1024,128]{1,0:T(8,128)(2,1)} %bitcast.107, bf16[2,1024,128]{2,1,0:T(8,128)(2,1)} %pad_maximum_fusion.15.k_ref.v_ref, ...), custom_call_target="tpu_custom_call", output_to_operand_aliasing={{0}: (4, {}), {1}: (5, {})} | custom-call | flops 536870912 | bytes 1843200 | tf_op jit(solution)/shard_map/pallas_call | solution.py:73
  82.1 5.6 %shard_map.56 = (f32[1024,1]{1,0:T(8,128)}, f32[1024,128]{1,0:T(8,128)}) custom-call(s32[3]{0:T(128)} %pad_add_fusion.1.sc_ref, bf16[1024,128]{1,0:T(8,128)(2,1)} %bitcast.108, bf16[2,1024,128]{2,1,0:T(8,128)(2,1)} %collective-permute-done.14.k_ref.v_ref, ...), custom_call_target="tpu_custom_call", output_to_operand_aliasing={{0}: (4, {}), {1}: (5, {})} | custom-call | flops 536870912 | bytes 1843200 | tf_op jit(solution)/shard_map/pallas_call | solution.py:73
  87.7 6.8 %collective-permute-done.13.k_ref.v_ref = bf16[2,1024,128]{2,1,0:T(8,128)(2,1)} collective-permute-done((bf16[2,1024,128]{2,1,0:T(8,128)(2,1)}, bf16[2,1024,128]{2,1,0:T(8,128)(2,1)}, u32[]{:S(2)}, u32[]{:S(2)}) %collective-permute-start.13) | collective-permute-done | bytes 524320 | tf_op jit(solution)/shard_map/ppermute | solution.py:112
  94.5 5.6 %shard_map.57 = (f32[1024,1]{1,0:T(8,128)}, f32[1024,128]{1,0:T(8,128)}) custom-call(s32[3]{0:T(128)} %pad_add_fusion.2.sc_ref, bf16[1024,128]{1,0:T(8,128)(2,1)} %bitcast.109, bf16[2,1024,128]{2,1,0:T(8,128)(2,1)} %collective-permute-done.13.k_ref.v_ref, ...), custom_call_target="tpu_custom_call", output_to_operand_aliasing={{0}: (4, {}), {1}: (5, {})} | custom-call | flops 536870912 | bytes 1843200 | tf_op jit(solution)/shard_map/pallas_call | solution.py:73
  100.1 2.9 %collective-permute-start.1 = (bf16[2,1024,128]{2,1,0:T(8,128)(2,1)}, bf16[2,1024,128]{2,1,0:T(8,128)(2,1)}, u32[]{:S(2)}, u32[]{:S(2)}) collective-permute-start(bf16[2,1024,128]{2,1,0:T(8,128)(2,1)} %pad_maximum_fusion.1), channel_id=1, source_target_pairs={{0,14},{1,15},{2,12},{3,13},{4,10},{5,11},{6,8},{7,9},{8,6},{9,7},... | collective-permute-start | bytes 1572872 | tf_op jit(solution)/shard_map/ppermute | solution.py:112
  103.0 5.6 %shard_map.58 = (f32[1024,1]{1,0:T(8,128)}, f32[1024,128]{1,0:T(8,128)}) custom-call(s32[3]{0:T(128)} %pad_add_fusion.3.sc_ref, bf16[1024,128]{1,0:T(8,128)(2,1)} %bitcast.110, bf16[2,1024,128]{2,1,0:T(8,128)(2,1)} %collective-permute-done.12.k_ref.v_ref, ...), custom_call_target="tpu_custom_call", output_to_operand_aliasing={{0}: (4, {}), {1}: (5, {})} | custom-call | flops 536870912 | bytes 1843200 | tf_op jit(solution)/shard_map/pallas_call | solution.py:73
  110.1 5.8 %shard_map.59 = (f32[1024,1]{1,0:T(8,128)}, f32[1024,128]{1,0:T(8,128)}) custom-call(s32[3]{0:T(128)} %pad_add_fusion.4.sc_ref, bf16[1024,128]{1,0:T(8,128)(2,1)} %bitcast.111, bf16[2,1024,128]{2,1,0:T(8,128)(2,1)} %collective-permute-done.11.k_ref.v_ref, ...), custom_call_target="tpu_custom_call", output_to_operand_aliasing={{0}: (4, {}), {1}: (5, {})} | custom-call | flops 536870912 | bytes 1843200 | tf_op jit(solution)/shard_map/pallas_call | solution.py:73
  115.8 5.6 %shard_map.60 = (f32[1024,1]{1,0:T(8,128)}, f32[1024,128]{1,0:T(8,128)}) custom-call(s32[3]{0:T(128)} %pad_add_fusion.5.sc_ref, bf16[1024,128]{1,0:T(8,128)(2,1)} %bitcast.112, bf16[2,1024,128]{2,1,0:T(8,128)(2,1)} %collective-permute-done.10.k_ref.v_ref, ...), custom_call_target="tpu_custom_call", output_to_operand_aliasing={{0}: (4, {}), {1}: (5, {})} | custom-call | flops 536870912 | bytes 1843200 | tf_op jit(solution)/shard_map/pallas_call | solution.py:73
  121.4 5.6 %shard_map.61 = (f32[1024,1]{1,0:T(8,128)}, f32[1024,128]{1,0:T(8,128)}) custom-call(s32[3]{0:T(128)} %pad_add_fusion.6.sc_ref, bf16[1024,128]{1,0:T(8,128)(2,1)} %bitcast.113, bf16[2,1024,128]{2,1,0:T(8,128)(2,1)} %copy-done.13, bf16[2,1024,128]{2,1,0:T(8,128)(2,1)} %copy-done.13, ...), custom_call_target="tpu_custom_call", output_to_operand_aliasing={{0}: (4, {}), {1}: (5, {})} | custom-call | flops 536870912 | bytes 1843200 | tf_op jit(solution)/shard_map/pallas_call | solution.py:73
  127.0 5.6 %shard_map.62 = (f32[1024,1]{1,0:T(8,128)}, f32[1024,128]{1,0:T(8,128)}) custom-call(s32[3]{0:T(128)} %pad_add_fusion.7.sc_ref, bf16[1024,128]{1,0:T(8,128)(2,1)} %bitcast.114, bf16[2,1024,128]{2,1,0:T(8,128)(2,1)} %collective-permute-done.8.k_ref.v_ref, ...), custom_call_target="tpu_custom_call", output_to_operand_aliasing={{0}: (4, {}), {1}: (5, {})} | custom-call | flops 536870912 | bytes 1843200 | tf_op jit(solution)/shard_map/pallas_call | solution.py:73
  132.6 5.6 %shard_map.63 = (f32[1024,1]{1,0:T(8,128)}, f32[1024,128]{1,0:T(8,128)}) custom-call(s32[3]{0:T(128)} %pad_add_fusion.8.sc_ref, bf16[1024,128]{1,0:T(8,128)(2,1)} %bitcast.115, bf16[2,1024,128]{2,1,0:T(8,128)(2,1)} %collective-permute-done.7.k_ref.v_ref, ...), custom_call_target="tpu_custom_call", output_to_operand_aliasing={{0}: (4, {}), {1}: (5, {})} | custom-call | flops 536870912 | bytes 1843200 | tf_op jit(solution)/shard_map/pallas_call | solution.py:73
  138.2 5.6 %shard_map.64 = (f32[1024,1]{1,0:T(8,128)}, f32[1024,128]{1,0:T(8,128)}) custom-call(s32[3]{0:T(128)} %pad_add_fusion.9.sc_ref, bf16[1024,128]{1,0:T(8,128)(2,1)} %bitcast.116, bf16[2,1024,128]{2,1,0:T(8,128)(2,1)} %collective-permute-done.6.k_ref.v_ref, ...), custom_call_target="tpu_custom_call", output_to_operand_aliasing={{0}: (4, {}), {1}: (5, {})} | custom-call | flops 536870912 | bytes 1843200 | tf_op jit(solution)/shard_map/pallas_call | solution.py:73
  143.8 5.6 %shard_map.65 = (f32[1024,1]{1,0:T(8,128)}, f32[1024,128]{1,0:T(8,128)}) custom-call(s32[3]{0:T(128)} %pad_add_fusion.10.sc_ref, bf16[1024,128]{1,0:T(8,128)(2,1)} %bitcast.117, bf16[2,1024,128]{2,1,0:T(8,128)(2,1)} %collective-permute-done.5.k_ref.v_ref, ...), custom_call_target="tpu_custom_call", output_to_operand_aliasing={{0}: (4, {}), {1}: (5, {})} | custom-call | flops 536870912 | bytes 1843200 | tf_op jit(solution)/shard_map/pallas_call | solution.py:73
  149.4 5.6 %shard_map.66 = (f32[1024,1]{1,0:T(8,128)}, f32[1024,128]{1,0:T(8,128)}) custom-call(s32[3]{0:T(128)} %pad_add_fusion.11.sc_ref, bf16[1024,128]{1,0:T(8,128)(2,1)} %bitcast.118, bf16[2,1024,128]{2,1,0:T(8,128)(2,1)} %collective-permute-done.4.k_ref.v_ref, ...), custom_call_target="tpu_custom_call", output_to_operand_aliasing={{0}: (4, {}), {1}: (5, {})} | custom-call | flops 536870912 | bytes 1843200 | tf_op jit(solution)/shard_map/pallas_call | solution.py:73
  155.0 4.4 %shard_map.67 = (f32[1024,1]{1,0:T(8,128)}, f32[1024,128]{1,0:T(8,128)}) custom-call(s32[3]{0:T(128)} %pad_add_fusion.12.sc_ref, bf16[1024,128]{1,0:T(8,128)(2,1)} %bitcast.119, bf16[2,1024,128]{2,1,0:T(8,128)(2,1)} %collective-permute-done.3.k_ref.v_ref, ...), custom_call_target="tpu_custom_call", output_to_operand_aliasing={{0}: (4, {}), {1}: (5, {})} | custom-call | flops 536870912 | bytes 1843200 | tf_op jit(solution)/shard_map/pallas_call | solution.py:73
  159.5 4.4 %shard_map.68 = (f32[1024,1]{1,0:T(8,128)}, f32[1024,128]{1,0:T(8,128)}) custom-call(s32[3]{0:T(128)} %pad_add_fusion.13.sc_ref, bf16[1024,128]{1,0:T(8,128)(2,1)} %bitcast.120, bf16[2,1024,128]{2,1,0:T(8,128)(2,1)} %collective-permute-done.2.k_ref.v_ref, ...), custom_call_target="tpu_custom_call", output_to_operand_aliasing={{0}: (4, {}), {1}: (5, {})} | custom-call | flops 536870912 | bytes 1843200 | tf_op jit(solution)/shard_map/pallas_call | solution.py:73
  163.9 4.4 %shard_map.69 = (f32[1024,1]{1,0:T(8,128)}, f32[1024,128]{1,0:T(8,128)}) custom-call(s32[3]{0:T(128)} %pad_add_fusion.14.sc_ref, bf16[1024,128]{1,0:T(8,128)(2,1)} %bitcast.121, bf16[2,1024,128]{2,1,0:T(8,128)(2,1)} %collective-permute-done.1.k_ref.v_ref, ...), custom_call_target="tpu_custom_call", output_to_operand_aliasing={{0}: (4, {}), {1}: (5, {})} | custom-call | flops 536870912 | bytes 1843200 | tf_op jit(solution)/shard_map/pallas_call | solution.py:73
  168.3 4.4 %shard_map.70 = (f32[1024,1]{1,0:T(8,128)}, f32[1024,128]{1,0:T(8,128)}) custom-call(s32[3]{0:T(128)} %pad_add_fusion.15.sc_ref, bf16[1024,128]{1,0:T(8,128)(2,1)} %bitcast.122, bf16[2,1024,128]{2,1,0:T(8,128)(2,1)} %collective-permute-done.k_ref.v_ref, ...), custom_call_target="tpu_custom_call", output_to_operand_aliasing={{0}: (4, {}), {1}: (5, {})} | custom-call | flops 536870912 | bytes 1843200 | tf_op jit(solution)/shard_map/pallas_call | solution.py:73
  177.2 2.9 %dynamic-slice_bitcast_fusion = f32[8,32,4608]{2,1,0:T(8,128)} fusion(f32[8,2,32,4608]{3,2,1,0:T(8,128)S(1)} %fusion.1, s32[]{:T(128)S(6)} %select_n.88), kind=kLoop, calls=%fused_computation.3 | loop fusion | bytes 9437188 | tf_op jit(solution)/shard_map/jit(dynamic_index_in_dim)/squeeze | solution.py:129
  180.0 2.2 copy-done.1
  182.5 7.9 %collective-permute-done.15 = f32[8,32,4608]{2,1,0:T(8,128)} collective-permute-done((f32[8,32,4608]{2,1,0:T(8,128)}, f32[8,32,4608]{2,1,0:T(8,128)}, u32[]{:S(2)}, u32[]{:S(2)}) %collective-permute-start.15) | collective-permute-done | bytes 4718624 | tf_op jit(solution)/shard_map/ppermute | solution.py:130
  190.4 4.3 %fusion = bf16[8,32,4608]{2,1,0:T(8,128)(2,1)S(1)} fusion(f32[8,32,4608]{2,1,0:T(8,128)} %collective-permute-done.15, f32[8,2,32,4608]{3,2,1,0:T(8,128)} %copy-done.1, s32[]{:T(128)S(6)} %select_n.87), kind=kLoop, calls=%fused_computation.1 | loop fusion | flops 2359296 | bytes 11796484 | tf_op jit(solution)/shard_map/convert_element_type | solution.py:132
  194.7 40.4 %all_to_all.5 = bf16[8,32,4608]{2,1,0:T(8,128)(2,1)S(1)} all-to-all(bf16[8,32,4608]{2,1,0:T(8,128)(2,1)S(1)} %fusion), channel_id=1, replica_groups=mesh['pb'=8,'kx'=8,'kc'=2] {'kx'}, dimensions={0} | all-to-all | bytes 4718592 | tf_op jit(solution)/shard_map/all_to_all | solution.py:131
  (89 shorter events, 43.4 us)
Async XLA Ops:
  0.0 175.7 %copy-start = (bf16[256,4608]{1,0:T(8,128)(2,1)S(1)}, bf16[256,4608]{1,0:T(8,128)(2,1)}, u32[]{:S(2)}) copy-start(bf16[256,4608]{1,0:T(8,128)(2,1)} %param.9) | copy-start | bytes 7077892
  7.5 33.9 %collective-permute-start.14 = (bf16[2,1024,128]{2,1,0:T(8,128)(2,1)}, bf16[2,1024,128]{2,1,0:T(8,128)(2,1)}, u32[]{:S(2)}, u32[]{:S(2)}) collective-permute-start(bf16[2,1024,128]{2,1,0:T(8,128)(2,1)} %pad_maximum_fusion.14), channel_id=1, source_target_pairs={{0,1},{1,0},{2,3},{3,2},{4,5},{5,4},{6,7},{7,6},{8,9},{9,8},{10,11... | collective-permute-start | bytes 1572872 | tf_op jit(solution)/shard_map/ppermute | solution.py:112
  8.4 35.3 %collective-permute-start.5 = (bf16[2,1024,128]{2,1,0:T(8,128)(2,1)}, bf16[2,1024,128]{2,1,0:T(8,128)(2,1)}, u32[]{:S(2)}, u32[]{:S(2)}) collective-permute-start(bf16[2,1024,128]{2,1,0:T(8,128)(2,1)} %pad_maximum_fusion.5), channel_id=1, source_target_pairs={{0,10},{1,11},{2,8},{3,9},{4,14},{5,15},{6,12},{7,13},{8,2},{9,3},... | collective-permute-start | bytes 1572872 | tf_op jit(solution)/shard_map/ppermute | solution.py:112
  12.9 31.8 %collective-permute-start.6 = (bf16[2,1024,128]{2,1,0:T(8,128)(2,1)}, bf16[2,1024,128]{2,1,0:T(8,128)(2,1)}, u32[]{:S(2)}, u32[]{:S(2)}) collective-permute-start(bf16[2,1024,128]{2,1,0:T(8,128)(2,1)} %pad_maximum_fusion.6), channel_id=1, source_target_pairs={{0,9},{1,8},{2,11},{3,10},{4,13},{5,12},{6,15},{7,14},{8,1},{9,0},... | collective-permute-start | bytes 1572872 | tf_op jit(solution)/shard_map/ppermute | solution.py:112
  14.1 34.1 %collective-permute-start.7 = (bf16[2,1024,128]{2,1,0:T(8,128)(2,1)}, bf16[2,1024,128]{2,1,0:T(8,128)(2,1)}, u32[]{:S(2)}, u32[]{:S(2)}) collective-permute-start(bf16[2,1024,128]{2,1,0:T(8,128)(2,1)} %pad_maximum_fusion.7), channel_id=1, source_target_pairs={{0,8},{1,9},{2,10},{3,11},{4,12},{5,13},{6,14},{7,15},{8,0},{9,1},... | collective-permute-start | bytes 1572872 | tf_op jit(solution)/shard_map/ppermute | solution.py:112
  18.0 42.4 %collective-permute-start.8 = (bf16[2,1024,128]{2,1,0:T(8,128)(2,1)}, bf16[2,1024,128]{2,1,0:T(8,128)(2,1)}, u32[]{:S(2)}, u32[]{:S(2)}) collective-permute-start(bf16[2,1024,128]{2,1,0:T(8,128)(2,1)} %pad_maximum_fusion.8), channel_id=1, source_target_pairs={{0,7},{1,6},{2,5},{3,4},{4,3},{5,2},{6,1},{7,0},{8,15},{9,14},{10,... | collective-permute-start | bytes 1572872 | tf_op jit(solution)/shard_map/ppermute | solution.py:112
  20.5 13.9 %copy-start.10 = (bf16[1,1024,128]{2,1,0:T(8,128)(2,1)S(1)}, bf16[1,1024,128]{2,1,0:T(8,128)(2,1)}, u32[]{:S(2)}) copy-start(bf16[1,1024,128]{2,1,0:T(8,128)(2,1)} %get-tuple-element.89) | copy-start | bytes 786436
  20.6 13.9 %copy-start.11 = (bf16[1,1024,128]{2,1,0:T(8,128)(2,1)S(1)}, bf16[1,1024,128]{2,1,0:T(8,128)(2,1)}, u32[]{:S(2)}) copy-start(bf16[1,1024,128]{2,1,0:T(8,128)(2,1)} %get-tuple-element.112) | copy-start | bytes 786436
  20.6 14.8 %copy-start.8 = (bf16[1,1024,128]{2,1,0:T(8,128)(2,1)S(1)}, bf16[1,1024,128]{2,1,0:T(8,128)(2,1)}, u32[]{:S(2)}) copy-start(bf16[1,1024,128]{2,1,0:T(8,128)(2,1)} %get-tuple-element.90) | copy-start | bytes 786436
  20.6 14.8 %copy-start.9 = (bf16[1,1024,128]{2,1,0:T(8,128)(2,1)S(1)}, bf16[1,1024,128]{2,1,0:T(8,128)(2,1)}, u32[]{:S(2)}) copy-start(bf16[1,1024,128]{2,1,0:T(8,128)(2,1)} %get-tuple-element.111) | copy-start | bytes 786436
  20.6 15.6 %copy-start.6 = (bf16[1,1024,128]{2,1,0:T(8,128)(2,1)S(1)}, bf16[1,1024,128]{2,1,0:T(8,128)(2,1)}, u32[]{:S(2)}) copy-start(bf16[1,1024,128]{2,1,0:T(8,128)(2,1)} %get-tuple-element.95) | copy-start | bytes 786436
  20.6 15.6 %copy-start.7 = (bf16[1,1024,128]{2,1,0:T(8,128)(2,1)S(1)}, bf16[1,1024,128]{2,1,0:T(8,128)(2,1)}, u32[]{:S(2)}) copy-start(bf16[1,1024,128]{2,1,0:T(8,128)(2,1)} %get-tuple-element.106) | copy-start | bytes 786436
  20.6 16.4 %copy-start.4 = (bf16[1,1024,128]{2,1,0:T(8,128)(2,1)S(1)}, bf16[1,1024,128]{2,1,0:T(8,128)(2,1)}, u32[]{:S(2)}) copy-start(bf16[1,1024,128]{2,1,0:T(8,128)(2,1)} %get-tuple-element.96) | copy-start | bytes 786436
  20.6 16.4 %copy-start.5 = (bf16[1,1024,128]{2,1,0:T(8,128)(2,1)S(1)}, bf16[1,1024,128]{2,1,0:T(8,128)(2,1)}, u32[]{:S(2)}) copy-start(bf16[1,1024,128]{2,1,0:T(8,128)(2,1)} %get-tuple-element.105) | copy-start | bytes 786436
  26.8 11.1 %copy-start.2 = (bf16[1,1024,128]{2,1,0:T(8,128)(2,1)S(1)}, bf16[1,1024,128]{2,1,0:T(8,128)(2,1)}, u32[]{:S(2)}) copy-start(bf16[1,1024,128]{2,1,0:T(8,128)(2,1)} %get-tuple-element.97) | copy-start | bytes 786436
  26.8 11.1 %copy-start.3 = (bf16[1,1024,128]{2,1,0:T(8,128)(2,1)S(1)}, bf16[1,1024,128]{2,1,0:T(8,128)(2,1)}, u32[]{:S(2)}) copy-start(bf16[1,1024,128]{2,1,0:T(8,128)(2,1)} %get-tuple-element.104) | copy-start | bytes 786436
  41.5 30.9 %collective-permute-start.9 = (bf16[2,1024,128]{2,1,0:T(8,128)(2,1)}, bf16[2,1024,128]{2,1,0:T(8,128)(2,1)S(1)}, u32[]{:S(2)}, u32[]{:S(2)}) collective-permute-start(bf16[2,1024,128]{2,1,0:T(8,128)(2,1)} %pad_maximum_fusion.9), channel_id=1, source_target_pairs={{0,6},{1,7},{2,4},{3,5},{4,2},{5,3},{6,0},{7,1},{8,14},{9,15},{10,... | collective-permute-start | bytes 1572872 | tf_op jit(solution)/shard_map/ppermute | solution.py:112
  43.7 37.4 %collective-permute-start.10 = (bf16[2,1024,128]{2,1,0:T(8,128)(2,1)}, bf16[2,1024,128]{2,1,0:T(8,128)(2,1)}, u32[]{:S(2)}, u32[]{:S(2)}) collective-permute-start(bf16[2,1024,128]{2,1,0:T(8,128)(2,1)} %pad_maximum_fusion.10), channel_id=1, source_target_pairs={{0,5},{1,4},{2,7},{3,6},{4,1},{5,0},{6,3},{7,2},{8,13},{9,12},{10,... | collective-permute-start | bytes 1572872 | tf_op jit(solution)/shard_map/ppermute | solution.py:112
  44.7 55.4 %collective-permute-start.12 = (bf16[2,1024,128]{2,1,0:T(8,128)(2,1)}, bf16[2,1024,128]{2,1,0:T(8,128)(2,1)}, u32[]{:S(2)}, u32[]{:S(2)}) collective-permute-start(bf16[2,1024,128]{2,1,0:T(8,128)(2,1)} %pad_maximum_fusion.12), channel_id=1, source_target_pairs={{0,3},{1,2},{2,1},{3,0},{4,7},{5,6},{6,5},{7,4},{8,11},{9,10},{10,... | collective-permute-start | bytes 1572872 | tf_op jit(solution)/shard_map/ppermute | solution.py:112
  48.1 46.3 %collective-permute-start.13 = (bf16[2,1024,128]{2,1,0:T(8,128)(2,1)}, bf16[2,1024,128]{2,1,0:T(8,128)(2,1)}, u32[]{:S(2)}, u32[]{:S(2)}) collective-permute-start(bf16[2,1024,128]{2,1,0:T(8,128)(2,1)} %pad_maximum_fusion.13), channel_id=1, source_target_pairs={{0,2},{1,3},{2,0},{3,1},{4,6},{5,7},{6,4},{7,5},{8,10},{9,11},{10,... | collective-permute-start | bytes 1572872 | tf_op jit(solution)/shard_map/ppermute | solution.py:112
  60.4 48.2 %collective-permute-start.11 = (bf16[2,1024,128]{2,1,0:T(8,128)(2,1)}, bf16[2,1024,128]{2,1,0:T(8,128)(2,1)}, u32[]{:S(2)}, u32[]{:S(2)}) collective-permute-start(bf16[2,1024,128]{2,1,0:T(8,128)(2,1)} %pad_maximum_fusion.11), channel_id=1, source_target_pairs={{0,4},{1,5},{2,6},{3,7},{4,0},{5,1},{6,2},{7,3},{8,12},{9,13},{10,... | collective-permute-start | bytes 1572872 | tf_op jit(solution)/shard_map/ppermute | solution.py:112
  72.4 1.5 copy-start.13
  72.4 77.1 %collective-permute-start.4 = (bf16[2,1024,128]{2,1,0:T(8,128)(2,1)}, bf16[2,1024,128]{2,1,0:T(8,128)(2,1)}, u32[]{:S(2)}, u32[]{:S(2)}) collective-permute-start(bf16[2,1024,128]{2,1,0:T(8,128)(2,1)} %pad_maximum_fusion.4), channel_id=1, source_target_pairs={{0,11},{1,10},{2,9},{3,8},{4,15},{5,14},{6,13},{7,12},{8,3},{9,2},... | collective-permute-start | bytes 1572872 | tf_op jit(solution)/shard_map/ppermute | solution.py:112
  74.7 19.8 %copy-start.12 = (bf16[2,1024,128]{2,1,0:T(8,128)(2,1)S(1)}, bf16[2,1024,128]{2,1,0:T(8,128)(2,1)}, u32[]{:S(2)}) copy-start(bf16[2,1024,128]{2,1,0:T(8,128)(2,1)} %pad_maximum_fusion.2) | copy-start | bytes 1572868
  81.1 73.9 %collective-permute-start.3 = (bf16[2,1024,128]{2,1,0:T(8,128)(2,1)}, bf16[2,1024,128]{2,1,0:T(8,128)(2,1)}, u32[]{:S(2)}, u32[]{:S(2)}) collective-permute-start(bf16[2,1024,128]{2,1,0:T(8,128)(2,1)} %pad_maximum_fusion.3), channel_id=1, source_target_pairs={{0,12},{1,13},{2,14},{3,15},{4,8},{5,9},{6,10},{7,11},{8,4},{9,5},... | collective-permute-start | bytes 1572872 | tf_op jit(solution)/shard_map/ppermute | solution.py:112
  94.5 65.0 %collective-permute-start.2 = (bf16[2,1024,128]{2,1,0:T(8,128)(2,1)S(1)}, bf16[2,1024,128]{2,1,0:T(8,128)(2,1)}, u32[]{:S(2)}, u32[]{:S(2)}) collective-permute-start(bf16[2,1024,128]{2,1,0:T(8,128)(2,1)S(1)} %copy-done.12), channel_id=1, source_target_pairs={{0,13},{1,12},{2,15},{3,14},{4,9},{5,8},{6,11},{7,10},{8,5},{9,4},... | collective-permute-start | bytes 1572872 | tf_op jit(solution)/shard_map/ppermute | solution.py:112
  100.1 63.8 %collective-permute-start.1 = (bf16[2,1024,128]{2,1,0:T(8,128)(2,1)}, bf16[2,1024,128]{2,1,0:T(8,128)(2,1)}, u32[]{:S(2)}, u32[]{:S(2)}) collective-permute-start(bf16[2,1024,128]{2,1,0:T(8,128)(2,1)} %pad_maximum_fusion.1), channel_id=1, source_target_pairs={{0,14},{1,15},{2,12},{3,13},{4,10},{5,11},{6,8},{7,9},{8,6},{9,7},... | collective-permute-start | bytes 1572872 | tf_op jit(solution)/shard_map/ppermute | solution.py:112
  108.6 59.8 %collective-permute-start = (bf16[2,1024,128]{2,1,0:T(8,128)(2,1)S(1)}, bf16[2,1024,128]{2,1,0:T(8,128)(2,1)}, u32[]{:S(2)}, u32[]{:S(2)}) collective-permute-start(bf16[2,1024,128]{2,1,0:T(8,128)(2,1)S(1)} %pad_maximum_fusion), channel_id=1, source_target_pairs={{0,15},{1,14},{2,13},{3,12},{4,11},{5,10},{6,9},{7,8},{8,7},{9,6},... | collective-permute-start | bytes 1572872 | tf_op jit(solution)/shard_map/ppermute | solution.py:112
  177.1 5.0 %copy-start.1 = (f32[8,2,32,4608]{3,2,1,0:T(8,128)}, f32[8,2,32,4608]{3,2,1,0:T(8,128)S(1)}, u32[]{:S(2)}) copy-start(f32[8,2,32,4608]{3,2,1,0:T(8,128)S(1)} %fusion.1) | copy-start | bytes 28311556
  182.2 8.3 %collective-permute-start.15 = (f32[8,32,4608]{2,1,0:T(8,128)}, f32[8,32,4608]{2,1,0:T(8,128)}, u32[]{:S(2)}, u32[]{:S(2)}) collective-permute-start(f32[8,32,4608]{2,1,0:T(8,128)} %dynamic-slice_bitcast_fusion), channel_id=1, source_target_pairs={{0,1},{1,0},{2,3},{3,2},{4,5},{5,4},{6,7},{7,6},{8,9},{9,8},{10,11... | collective-permute-start | bytes 14155784 | tf_op jit(solution)/shard_map/ppermute | solution.py:130

commit v5 on v4

--- a/solution.py
+++ b/solution.py
@@ -128,10 +128,13 @@
     mine = lax.dynamic_index_in_dim(partial, core, 1, keepdims=False)
     theirs = lax.dynamic_index_in_dim(partial, 1 - core, 1, keepdims=False)
     on_chip = mine + lax.ppermute(theirs, "kc", [(0, 1), (1, 0)])
-    parts = lax.all_to_all(
-        on_chip.astype(jnp.bfloat16), "kx", split_axis=0, concat_axis=0, tiled=True
-    )
-    return jnp.sum(parts.astype(jnp.float32), axis=0)
+    chip = lax.axis_index("kx")
+    result = lax.dynamic_index_in_dim(on_chip, chip, 0, keepdims=False)
+    for mask in range(1, n_chip):
+        part = lax.dynamic_index_in_dim(on_chip, chip ^ mask, 0, keepdims=False)
+        moved = lax.ppermute(part.astype(jnp.bfloat16), "kx", [(k, k ^ mask) for k in range(n_chip)])
+        result = result + moved.astype(jnp.float32)
+    return result
 
 
 def solution(mesh):

time: 236 us -> 240 us (1.017)
  blocking collectives: 40.4 us -> 0 us
  starting transfers between devices: 24.7 us -> 45.5 us
  waiting for transfers between devices: 33.6 us -> 50.9 us
  local copies, waits for them, and re-layouts: 15.5 us -> 19.5 us
  other arithmetic: 34.8 us -> 37.5 us
    all_to_all x1 -> x0, blocking collectives: 40.4 us -> none  [per_device(): lax.all_to_all(on_chip.astype(jnp.bfloat16), 'kx', split_axis=0, concat_a...]
    ppermute x0 -> x7, waiting for transfers between devices: none -> 24.3 us  [per_device(): lax.ppermute(part.astype(jnp.bfloat16), 'kx', [(k, k ^ mask) for k in ran...]
    ppermute x0 -> x7, starting transfers between devices: none -> 20.6 us  [per_device(): lax.ppermute(part.astype(jnp.bfloat16), 'kx', [(k, k ^ mask) for k in ran...]
    add x0 -> x2, other arithmetic: none -> 7.14 us  [the longest x1 4.37 us: per_device(): on_chip = mine + lax.ppermute(theirs, 'kc', [(0, 1), (1, 0)])]
    ppermute x15, waiting for transfers between devices: 25.7 us -> 18.7 us  [by_heads(): block = lax.ppermute(block, KV, [(j, j ^ shift) for j in range(n_kv)])]
    convert_element_type x1 -> x0, other arithmetic: 4.3 us -> none  [per_device(): on_chip.astype(jnp.bfloat16)]
    unnamed x28, local copies, waits for them, and re-layouts: 2.24 us -> 5.22 us
  transfers between devices with their start and end apart: 16 -> 23, of which waited for: 5 -> 10; matrix products, arithmetic and copies ran while one was open for 12% -> 13% of each run, Pallas kernels for 34% -> 33%
where the time goes in v5:
time: 240 us
  Pallas kernels  84.7 us (35%)
  waiting for transfers between devices  50.9 us (21%)
  starting transfers between devices  45.5 us (19%)
  other arithmetic  37.5 us (16%)
  local copies, waits for them, and re-layouts  19.5 us (8%)
    pallas_call x16, Pallas kernels, attend_kernel(): pl.pallas_call(block_kernel, grid_spec=grid_spec, out_shape=(jax.ShapeDty...  84.7 us
    ppermute x7, waiting for transfers between devices, per_device(): lax.ppermute(part.astype(jnp.bfloat16), 'kx', [(k, k ^ mask) for k in ran...  24.3 us
    ppermute x15, starting transfers between devices, by_heads(): block = lax.ppermute(block, KV, [(j, j ^ shift) for j in range(n_kv)])  23.6 us
    ppermute x7, starting transfers between devices, per_device(): lax.ppermute(part.astype(jnp.bfloat16), 'kx', [(k, k ^ mask) for k in ran...  20.6 us
    ppermute x15, waiting for transfers between devices, by_heads(): block = lax.ppermute(block, KV, [(j, j ^ shift) for j in range(n_kv)])  18.7 us
    another operation x16, other arithmetic, by_heads(): jnp.stack((lax.dynamic_slice_in_dim(keys, dest * kv_feat, kv_feat, 1), la...  18 us
    another operation x16, other arithmetic, by_heads(): jnp.stack([row_first, src * key_dev, jnp.int32(rows_dev)]).astype(jnp.int32)  9.85 us
    ppermute x1, waiting for transfers between devices, per_device(): on_chip = mine + lax.ppermute(theirs, 'kc', [(0, 1), (1, 0)])  7.88 us
  transfers between devices with their start and end apart: 23, of which 10 were waited for; matrix products, arithmetic and copies ran while one was open for 13% of the time, Pallas kernels for 33%

profile of v5, /device:TPU:120, one launch (start us, length us, event | category | flops | bytes accessed | tf_op | source)
XLA Modules:
  0.0 240.3 jit_solution(14795682663627945841)
XLA Ops:
  0.0 6.8 %dynamic-slice_bitcast_fusion.1 = (bf16[1,1024,128]{2,1,0:T(8,128)(2,1)}, bf16[1,1024,128]{2,1,0:T(8,128)(2,1)S(1)}, bf16[1,1024,128]{2,1,0:T(8,128)(2,1)S(1)}, ...) fusion(bf16[1024,2048]{1,0:T(8,128)(2,1)} %param.8, ...), kind=kLoop, calls=%fused_computation.43 | loop fusion | bytes 16777280 | tf_op jit(solution)/shard_map/stack | solution.py:104
  43.6 3.0 %collective-permute-start.7 = (bf16[2,1024,128]{2,1,0:T(8,128)(2,1)}, bf16[2,1024,128]{2,1,0:T(8,128)(2,1)}, u32[]{:S(2)}, u32[]{:S(2)}) collective-permute-start(bf16[2,1024,128]{2,1,0:T(8,128)(2,1)} %pad_maximum_fusion.7), channel_id=1, source_target_pairs={{0,8},{1,9},{2,10},{3,11},{4,12},{5,13},{6,14},{7,15},{8,0},{9,1},... | collective-permute-start | bytes 1572872 | tf_op jit(solution)/shard_map/ppermute | solution.py:112
  47.3 3.7 %collective-permute-start.5 = (bf16[2,1024,128]{2,1,0:T(8,128)(2,1)}, bf16[2,1024,128]{2,1,0:T(8,128)(2,1)}, u32[]{:S(2)}, u32[]{:S(2)}) collective-permute-start(bf16[2,1024,128]{2,1,0:T(8,128)(2,1)} %pad_maximum_fusion.5), channel_id=1, source_target_pairs={{0,10},{1,11},{2,8},{3,9},{4,14},{5,15},{6,12},{7,13},{8,2},{9,3},... | collective-permute-start | bytes 1572872 | tf_op jit(solution)/shard_map/ppermute | solution.py:112
  53.4 2.9 %collective-permute-done.9.k_ref.v_ref = bf16[2,1024,128]{2,1,0:T(8,128)(2,1)} collective-permute-done((bf16[2,1024,128]{2,1,0:T(8,128)(2,1)}, bf16[2,1024,128]{2,1,0:T(8,128)(2,1)}, u32[]{:S(2)}, u32[]{:S(2)}) %collective-permute-start.9) | collective-permute-done | bytes 524320 | tf_op jit(solution)/shard_map/ppermute | solution.py:112
  60.4 5.6 %shard_map.55 = (f32[1024,1]{1,0:T(8,128)}, f32[1024,128]{1,0:T(8,128)}) custom-call(s32[3]{0:T(128)} %pad_add_fusion.sc_ref, bf16[1024,128]{1,0:T(8,128)(2,1)} %bitcast.133, bf16[2,1024,128]{2,1,0:T(8,128)(2,1)} %pad_maximum_fusion.15.k_ref.v_ref, ...), custom_call_target="tpu_custom_call", output_to_operand_aliasing={{0}: (4, {}), {1}: (5, {})} | custom-call | flops 536870912 | bytes 1843200 | tf_op jit(solution)/shard_map/pallas_call | solution.py:73
  69.4 5.6 %shard_map.56 = (f32[1024,1]{1,0:T(8,128)}, f32[1024,128]{1,0:T(8,128)}) custom-call(s32[3]{0:T(128)} %pad_add_fusion.1.sc_ref, bf16[1024,128]{1,0:T(8,128)(2,1)} %bitcast.134, bf16[2,1024,128]{2,1,0:T(8,128)(2,1)} %collective-permute-done.14.k_ref.v_ref, ...), custom_call_target="tpu_custom_call", output_to_operand_aliasing={{0}: (4, {}), {1}: (5, {})} | custom-call | flops 536870912 | bytes 1843200 | tf_op jit(solution)/shard_map/pallas_call | solution.py:73
  74.9 4.4 %collective-permute-done.7.k_ref.v_ref = bf16[2,1024,128]{2,1,0:T(8,128)(2,1)} collective-permute-done((bf16[2,1024,128]{2,1,0:T(8,128)(2,1)}, bf16[2,1024,128]{2,1,0:T(8,128)(2,1)}, u32[]{:S(2)}, u32[]{:S(2)}) %collective-permute-start.7) | collective-permute-done | bytes 524320 | tf_op jit(solution)/shard_map/ppermute | solution.py:112
  79.3 5.6 %shard_map.57 = (f32[1024,1]{1,0:T(8,128)}, f32[1024,128]{1,0:T(8,128)}) custom-call(s32[3]{0:T(128)} %pad_add_fusion.2.sc_ref, bf16[1024,128]{1,0:T(8,128)(2,1)} %bitcast.135, bf16[2,1024,128]{2,1,0:T(8,128)(2,1)} %collective-permute-done.13.k_ref.v_ref, ...), custom_call_target="tpu_custom_call", output_to_operand_aliasing={{0}: (4, {}), {1}: (5, {})} | custom-call | flops 536870912 | bytes 1843200 | tf_op jit(solution)/shard_map/pallas_call | solution.py:73
  84.9 4.7 %collective-permute-done.6.k_ref.v_ref = bf16[2,1024,128]{2,1,0:T(8,128)(2,1)} collective-permute-done((bf16[2,1024,128]{2,1,0:T(8,128)(2,1)}, bf16[2,1024,128]{2,1,0:T(8,128)(2,1)}, u32[]{:S(2)}, u32[]{:S(2)}) %collective-permute-start.6) | collective-permute-done | bytes 524320 | tf_op jit(solution)/shard_map/ppermute | solution.py:112
  91.8 5.6 %shard_map.58 = (f32[1024,1]{1,0:T(8,128)}, f32[1024,128]{1,0:T(8,128)}) custom-call(s32[3]{0:T(128)} %pad_add_fusion.3.sc_ref, bf16[1024,128]{1,0:T(8,128)(2,1)} %bitcast.136, bf16[2,1024,128]{2,1,0:T(8,128)(2,1)} %collective-permute-done.12.k_ref.v_ref, ...), custom_call_target="tpu_custom_call", output_to_operand_aliasing={{0}: (4, {}), {1}: (5, {})} | custom-call | flops 536870912 | bytes 1843200 | tf_op jit(solution)/shard_map/pallas_call | solution.py:73
  97.4 6.1 %collective-permute-done.5.k_ref.v_ref = bf16[2,1024,128]{2,1,0:T(8,128)(2,1)} collective-permute-done((bf16[2,1024,128]{2,1,0:T(8,128)(2,1)}, bf16[2,1024,128]{2,1,0:T(8,128)(2,1)}, u32[]{:S(2)}, u32[]{:S(2)}) %collective-permute-start.5) | collective-permute-done | bytes 524320 | tf_op jit(solution)/shard_map/ppermute | solution.py:112
  103.5 5.8 %shard_map.59 = (f32[1024,1]{1,0:T(8,128)}, f32[1024,128]{1,0:T(8,128)}) custom-call(s32[3]{0:T(128)} %pad_add_fusion.4.sc_ref, bf16[1024,128]{1,0:T(8,128)(2,1)} %bitcast.137, bf16[2,1024,128]{2,1,0:T(8,128)(2,1)} %collective-permute-done.11.k_ref.v_ref, ...), custom_call_target="tpu_custom_call", output_to_operand_aliasing={{0}: (4, {}), {1}: (5, {})} | custom-call | flops 536870912 | bytes 1843200 | tf_op jit(solution)/shard_map/pallas_call | solution.py:73
  109.3 5.6 %shard_map.60 = (f32[1024,1]{1,0:T(8,128)}, f32[1024,128]{1,0:T(8,128)}) custom-call(s32[3]{0:T(128)} %pad_add_fusion.5.sc_ref, bf16[1024,128]{1,0:T(8,128)(2,1)} %bitcast.138, bf16[2,1024,128]{2,1,0:T(8,128)(2,1)} %collective-permute-done.10.k_ref.v_ref, ...), custom_call_target="tpu_custom_call", output_to_operand_aliasing={{0}: (4, {}), {1}: (5, {})} | custom-call | flops 536870912 | bytes 1843200 | tf_op jit(solution)/shard_map/pallas_call | solution.py:73
  114.9 5.6 %shard_map.61 = (f32[1024,1]{1,0:T(8,128)}, f32[1024,128]{1,0:T(8,128)}) custom-call(s32[3]{0:T(128)} %pad_add_fusion.6.sc_ref, bf16[1024,128]{1,0:T(8,128)(2,1)} %bitcast.139, bf16[2,1024,128]{2,1,0:T(8,128)(2,1)} %collective-permute-done.9.k_ref.v_ref, ...), custom_call_target="tpu_custom_call", output_to_operand_aliasing={{0}: (4, {}), {1}: (5, {})} | custom-call | flops 536870912 | bytes 1843200 | tf_op jit(solution)/shard_map/pallas_call | solution.py:73
  120.5 5.6 %shard_map.62 = (f32[1024,1]{1,0:T(8,128)}, f32[1024,128]{1,0:T(8,128)}) custom-call(s32[3]{0:T(128)} %pad_add_fusion.7.sc_ref, bf16[1024,128]{1,0:T(8,128)(2,1)} %bitcast.140, bf16[2,1024,128]{2,1,0:T(8,128)(2,1)} %collective-permute-done.8.k_ref.v_ref, ...), custom_call_target="tpu_custom_call", output_to_operand_aliasing={{0}: (4, {}), {1}: (5, {})} | custom-call | flops 536870912 | bytes 1843200 | tf_op jit(solution)/shard_map/pallas_call | solution.py:73
  126.1 5.7 %shard_map.63 = (f32[1024,1]{1,0:T(8,128)}, f32[1024,128]{1,0:T(8,128)}) custom-call(s32[3]{0:T(128)} %pad_add_fusion.8.sc_ref, bf16[1024,128]{1,0:T(8,128)(2,1)} %bitcast.141, bf16[2,1024,128]{2,1,0:T(8,128)(2,1)} %collective-permute-done.7.k_ref.v_ref, ...), custom_call_target="tpu_custom_call", output_to_operand_aliasing={{0}: (4, {}), {1}: (5, {})} | custom-call | flops 536870912 | bytes 1843200 | tf_op jit(solution)/shard_map/pallas_call | solution.py:73
  131.8 5.1 %shard_map.64 = (f32[1024,1]{1,0:T(8,128)}, f32[1024,128]{1,0:T(8,128)}) custom-call(s32[3]{0:T(128)} %pad_add_fusion.9.sc_ref, bf16[1024,128]{1,0:T(8,128)(2,1)} %bitcast.142, bf16[2,1024,128]{2,1,0:T(8,128)(2,1)} %collective-permute-done.6.k_ref.v_ref, ...), custom_call_target="tpu_custom_call", output_to_operand_aliasing={{0}: (4, {}), {1}: (5, {})} | custom-call | flops 536870912 | bytes 1843200 | tf_op jit(solution)/shard_map/pallas_call | solution.py:73
  136.8 5.6 %shard_map.65 = (f32[1024,1]{1,0:T(8,128)}, f32[1024,128]{1,0:T(8,128)}) custom-call(s32[3]{0:T(128)} %pad_add_fusion.10.sc_ref, bf16[1024,128]{1,0:T(8,128)(2,1)} %bitcast.143, bf16[2,1024,128]{2,1,0:T(8,128)(2,1)} %collective-permute-done.5.k_ref.v_ref, ...), custom_call_target="tpu_custom_call", output_to_operand_aliasing={{0}: (4, {}), {1}: (5, {})} | custom-call | flops 536870912 | bytes 1843200 | tf_op jit(solution)/shard_map/pallas_call | solution.py:73
  142.4 5.6 %shard_map.66 = (f32[1024,1]{1,0:T(8,128)}, f32[1024,128]{1,0:T(8,128)}) custom-call(s32[3]{0:T(128)} %pad_add_fusion.11.sc_ref, bf16[1024,128]{1,0:T(8,128)(2,1)} %bitcast.144, bf16[2,1024,128]{2,1,0:T(8,128)(2,1)} %collective-permute-done.4.k_ref.v_ref, ...), custom_call_target="tpu_custom_call", output_to_operand_aliasing={{0}: (4, {}), {1}: (5, {})} | custom-call | flops 536870912 | bytes 1843200 | tf_op jit(solution)/shard_map/pallas_call | solution.py:73
  148.0 4.4 %shard_map.67 = (f32[1024,1]{1,0:T(8,128)}, f32[1024,128]{1,0:T(8,128)}) custom-call(s32[3]{0:T(128)} %pad_add_fusion.12.sc_ref, bf16[1024,128]{1,0:T(8,128)(2,1)} %bitcast.145, bf16[2,1024,128]{2,1,0:T(8,128)(2,1)} %collective-permute-done.3.k_ref.v_ref, ...), custom_call_target="tpu_custom_call", output_to_operand_aliasing={{0}: (4, {}), {1}: (5, {})} | custom-call | flops 536870912 | bytes 1843200 | tf_op jit(solution)/shard_map/pallas_call | solution.py:73
  152.5 4.4 %shard_map.68 = (f32[1024,1]{1,0:T(8,128)}, f32[1024,128]{1,0:T(8,128)}) custom-call(s32[3]{0:T(128)} %pad_add_fusion.13.sc_ref, bf16[1024,128]{1,0:T(8,128)(2,1)} %bitcast.146, bf16[2,1024,128]{2,1,0:T(8,128)(2,1)} %collective-permute-done.2.k_ref.v_ref, ...), custom_call_target="tpu_custom_call", output_to_operand_aliasing={{0}: (4, {}), {1}: (5, {})} | custom-call | flops 536870912 | bytes 1843200 | tf_op jit(solution)/shard_map/pallas_call | solution.py:73
  156.9 4.4 %shard_map.69 = (f32[1024,1]{1,0:T(8,128)}, f32[1024,128]{1,0:T(8,128)}) custom-call(s32[3]{0:T(128)} %pad_add_fusion.14.sc_ref, bf16[1024,128]{1,0:T(8,128)(2,1)} %bitcast.147, bf16[2,1024,128]{2,1,0:T(8,128)(2,1)} %collective-permute-done.1.k_ref.v_ref, ...), custom_call_target="tpu_custom_call", output_to_operand_aliasing={{0}: (4, {}), {1}: (5, {})} | custom-call | flops 536870912 | bytes 1843200 | tf_op jit(solution)/shard_map/pallas_call | solution.py:73
  161.4 4.4 %shard_map.70 = (f32[1024,1]{1,0:T(8,128)}, f32[1024,128]{1,0:T(8,128)}) custom-call(s32[3]{0:T(128)} %pad_add_fusion.15.sc_ref, bf16[1024,128]{1,0:T(8,128)(2,1)} %bitcast.148, bf16[2,1024,128]{2,1,0:T(8,128)(2,1)} %collective-permute-done.k_ref.v_ref, ...), custom_call_target="tpu_custom_call", output_to_operand_aliasing={{0}: (4, {}), {1}: (5, {})} | custom-call | flops 536870912 | bytes 1843200 | tf_op jit(solution)/shard_map/pallas_call | solution.py:73
  170.2 2.8 %dynamic-slice_bitcast_fusion = f32[8,32,4608]{2,1,0:T(8,128)} fusion(f32[8,2,32,4608]{3,2,1,0:T(8,128)S(1)} %fusion, s32[]{:T(128)S(6)} %select_n.113), kind=kLoop, calls=%fused_computation.1 | loop fusion | bytes 9437188 | tf_op jit(solution)/shard_map/jit(dynamic_index_in_dim)/squeeze | solution.py:129
  176.5 7.9 %collective-permute-done.15 = f32[8,32,4608]{2,1,0:T(8,128)} collective-permute-done((f32[8,32,4608]{2,1,0:T(8,128)}, f32[8,32,4608]{2,1,0:T(8,128)}, u32[]{:S(2)}, u32[]{:S(2)}) %collective-permute-start.15) | collective-permute-done | bytes 4718624 | tf_op jit(solution)/shard_map/ppermute | solution.py:130
  184.4 4.4 %bitcast_add_fusion = f32[8,32,4608]{2,1,0:T(8,128)S(1)} fusion(f32[8,32,4608]{2,1,0:T(8,128)} %collective-permute-done.15, f32[8,2,32,4608]{3,2,1,0:T(8,128)} %copy-done.1, s32[]{:T(128)S(6)} %select_n.112), kind=kLoop, calls=%fused_computation | loop fusion | flops 1179648 | bytes 14155780 | tf_op jit(solution)/shard_map/add | solution.py:130
  196.9 6.8 %collective-permute-start.19 = (bf16[32,4608]{1,0:T(8,128)(2,1)S(1)}, bf16[32,4608]{1,0:T(8,128)(2,1)}, u32[]{:S(2)}, u32[]{:S(2)}) collective-permute-start(bf16[32,4608]{1,0:T(8,128)(2,1)S(1)} %get-tuple-element.73), channel_id=1, source_target_pairs={{0,8},{2,10},{4,12},{6,14},{8,0},{10,2},{12,4},{14,6},{1,9},{3,11}... | collective-permute-start | bytes 884744 | tf_op jit(solution)/shard_map/ppermute | solution.py:135
  205.4 4.6 %collective-permute-start.21 = (bf16[32,4608]{1,0:T(8,128)(2,1)S(1)}, bf16[32,4608]{1,0:T(8,128)(2,1)}, u32[]{:S(2)}, u32[]{:S(2)}) collective-permute-start(bf16[32,4608]{1,0:T(8,128)(2,1)S(1)} %get-tuple-element.71), channel_id=1, source_target_pairs={{0,12},{2,14},{4,8},{6,10},{8,4},{10,6},{12,0},{14,2},{1,13},{3,15... | collective-permute-start | bytes 884744 | tf_op jit(solution)/shard_map/ppermute | solution.py:135
  213.2 10.5 %collective-permute-done.19 = bf16[32,4608]{1,0:T(8,128)(2,1)} collective-permute-done((bf16[32,4608]{1,0:T(8,128)(2,1)S(1)}, bf16[32,4608]{1,0:T(8,128)(2,1)}, u32[]{:S(2)}, u32[]{:S(2)}) %collective-permute-start.19) | collective-permute-done | bytes 294944 | tf_op jit(solution)/shard_map/ppermute | solution.py:135
  223.7 6.1 %collective-permute-done.20 = bf16[32,4608]{1,0:T(8,128)(2,1)} collective-permute-done((bf16[32,4608]{1,0:T(8,128)(2,1)S(1)}, bf16[32,4608]{1,0:T(8,128)(2,1)}, u32[]{:S(2)}, u32[]{:S(2)}) %collective-permute-start.20) | collective-permute-done | bytes 294944 | tf_op jit(solution)/shard_map/ppermute | solution.py:135
  230.7 6.9 %collective-permute-done.22 = bf16[32,4608]{1,0:T(8,128)(2,1)} collective-permute-done((bf16[32,4608]{1,0:T(8,128)(2,1)S(1)}, bf16[32,4608]{1,0:T(8,128)(2,1)}, u32[]{:S(2)}, u32[]{:S(2)}) %collective-permute-start.22) | collective-permute-done | bytes 294944 | tf_op jit(solution)/shard_map/ppermute | solution.py:135
  237.6 2.8 %fusion.7 = f32[32,4608]{1,0:T(8,128)} fusion(bf16[32,4608]{1,0:T(8,128)(2,1)} %collective-permute-done.22, bf16[32,4608]{1,0:T(8,128)(2,1)} %collective-permute-done.21, bf16[32,4608]{1,0:T(8,128)(2,1)} %collective-permute-done.20, bf16[32,4608]{1,0:T(8,128)(2,1)} %collective-permute-done.19, bf16[32,4608]{1,0:T(8,128)(2,1)} %collective-permute-done.18, ...), kind=kLoop, calls=%fused_computation.10 | loop fusion | flops 2064384 | bytes 3244036 | tf_op jit(solution)/shard_map/add | solution.py:136
  (103 shorter events, 70.5 us)
Async XLA Ops:
  0.0 168.8 %copy-start = (bf16[256,4608]{1,0:T(8,128)(2,1)S(1)}, bf16[256,4608]{1,0:T(8,128)(2,1)}, u32[]{:S(2)}) copy-start(bf16[256,4608]{1,0:T(8,128)(2,1)} %param.9) | copy-start | bytes 7077892
  7.6 31.1 %collective-permute-start.14 = (bf16[2,1024,128]{2,1,0:T(8,128)(2,1)}, bf16[2,1024,128]{2,1,0:T(8,128)(2,1)}, u32[]{:S(2)}, u32[]{:S(2)}) collective-permute-start(bf16[2,1024,128]{2,1,0:T(8,128)(2,1)} %pad_maximum_fusion.14), channel_id=1, source_target_pairs={{0,1},{1,0},{2,3},{3,2},{4,5},{5,4},{6,7},{7,6},{8,9},{9,8},{10,11... | collective-permute-start | bytes 1572872 | tf_op jit(solution)/shard_map/ppermute | solution.py:112
  8.5 32.5 %collective-permute-start.13 = (bf16[2,1024,128]{2,1,0:T(8,128)(2,1)}, bf16[2,1024,128]{2,1,0:T(8,128)(2,1)}, u32[]{:S(2)}, u32[]{:S(2)}) collective-permute-start(bf16[2,1024,128]{2,1,0:T(8,128)(2,1)} %pad_maximum_fusion.13), channel_id=1, source_target_pairs={{0,2},{1,3},{2,0},{3,1},{4,6},{5,7},{6,4},{7,5},{8,10},{9,11},{10,... | collective-permute-start | bytes 1572872 | tf_op jit(solution)/shard_map/ppermute | solution.py:112
  10.6 33.0 %collective-permute-start.12 = (bf16[2,1024,128]{2,1,0:T(8,128)(2,1)}, bf16[2,1024,128]{2,1,0:T(8,128)(2,1)}, u32[]{:S(2)}, u32[]{:S(2)}) collective-permute-start(bf16[2,1024,128]{2,1,0:T(8,128)(2,1)} %pad_maximum_fusion.12), channel_id=1, source_target_pairs={{0,3},{1,2},{2,1},{3,0},{4,7},{5,6},{6,5},{7,4},{8,11},{9,10},{10,... | collective-permute-start | bytes 1572872 | tf_op jit(solution)/shard_map/ppermute | solution.py:112
  13.5 33.1 %collective-permute-start.11 = (bf16[2,1024,128]{2,1,0:T(8,128)(2,1)}, bf16[2,1024,128]{2,1,0:T(8,128)(2,1)}, u32[]{:S(2)}, u32[]{:S(2)}) collective-permute-start(bf16[2,1024,128]{2,1,0:T(8,128)(2,1)} %pad_maximum_fusion.11), channel_id=1, source_target_pairs={{0,4},{1,5},{2,6},{3,7},{4,0},{5,1},{6,2},{7,3},{8,12},{9,13},{10,... | collective-permute-start | bytes 1572872 | tf_op jit(solution)/shard_map/ppermute | solution.py:112
  15.9 31.4 %collective-permute-start.10 = (bf16[2,1024,128]{2,1,0:T(8,128)(2,1)}, bf16[2,1024,128]{2,1,0:T(8,128)(2,1)}, u32[]{:S(2)}, u32[]{:S(2)}) collective-permute-start(bf16[2,1024,128]{2,1,0:T(8,128)(2,1)} %pad_maximum_fusion.10), channel_id=1, source_target_pairs={{0,5},{1,4},{2,7},{3,6},{4,1},{5,0},{6,3},{7,2},{8,13},{9,12},{10,... | collective-permute-start | bytes 1572872 | tf_op jit(solution)/shard_map/ppermute | solution.py:112
  16.7 15.8 %copy-start.9 = (bf16[1,1024,128]{2,1,0:T(8,128)(2,1)S(1)}, bf16[1,1024,128]{2,1,0:T(8,128)(2,1)}, u32[]{:S(2)}) copy-start(bf16[1,1024,128]{2,1,0:T(8,128)(2,1)} %get-tuple-element.101) | copy-start | bytes 786436
  16.7 16.7 %copy-start.7 = (bf16[1,1024,128]{2,1,0:T(8,128)(2,1)S(1)}, bf16[1,1024,128]{2,1,0:T(8,128)(2,1)}, u32[]{:S(2)}) copy-start(bf16[1,1024,128]{2,1,0:T(8,128)(2,1)} %get-tuple-element.102) | copy-start | bytes 786436
  16.7 16.7 %copy-start.8 = (bf16[1,1024,128]{2,1,0:T(8,128)(2,1)S(1)}, bf16[1,1024,128]{2,1,0:T(8,128)(2,1)}, u32[]{:S(2)}) copy-start(bf16[1,1024,128]{2,1,0:T(8,128)(2,1)} %get-tuple-element.113) | copy-start | bytes 786436
  16.7 17.5 %copy-start.5 = (bf16[1,1024,128]{2,1,0:T(8,128)(2,1)S(1)}, bf16[1,1024,128]{2,1,0:T(8,128)(2,1)}, u32[]{:S(2)}) copy-start(bf16[1,1024,128]{2,1,0:T(8,128)(2,1)} %get-tuple-element.103) | copy-start | bytes 786436
  16.7 17.5 %copy-start.6 = (bf16[1,1024,128]{2,1,0:T(8,128)(2,1)S(1)}, bf16[1,1024,128]{2,1,0:T(8,128)(2,1)}, u32[]{:S(2)}) copy-start(bf16[1,1024,128]{2,1,0:T(8,128)(2,1)} %get-tuple-element.112) | copy-start | bytes 786436
  16.7 18.3 %copy-start.3 = (bf16[1,1024,128]{2,1,0:T(8,128)(2,1)S(1)}, bf16[1,1024,128]{2,1,0:T(8,128)(2,1)}, u32[]{:S(2)}) copy-start(bf16[1,1024,128]{2,1,0:T(8,128)(2,1)} %get-tuple-element.104) | copy-start | bytes 786436
  16.7 18.3 %copy-start.4 = (bf16[1,1024,128]{2,1,0:T(8,128)(2,1)S(1)}, bf16[1,1024,128]{2,1,0:T(8,128)(2,1)}, u32[]{:S(2)}) copy-start(bf16[1,1024,128]{2,1,0:T(8,128)(2,1)} %get-tuple-element.111) | copy-start | bytes 786436
  38.7 17.6 %collective-permute-start.9 = (bf16[2,1024,128]{2,1,0:T(8,128)(2,1)}, bf16[2,1024,128]{2,1,0:T(8,128)(2,1)}, u32[]{:S(2)}, u32[]{:S(2)}) collective-permute-start(bf16[2,1024,128]{2,1,0:T(8,128)(2,1)} %pad_maximum_fusion.9), channel_id=1, source_target_pairs={{0,6},{1,7},{2,4},{3,5},{4,2},{5,3},{6,0},{7,1},{8,14},{9,15},{10,... | collective-permute-start | bytes 1572872 | tf_op jit(solution)/shard_map/ppermute | solution.py:112
  40.9 25.7 %collective-permute-start.8 = (bf16[2,1024,128]{2,1,0:T(8,128)(2,1)}, bf16[2,1024,128]{2,1,0:T(8,128)(2,1)}, u32[]{:S(2)}, u32[]{:S(2)}) collective-permute-start(bf16[2,1024,128]{2,1,0:T(8,128)(2,1)} %pad_maximum_fusion.8), channel_id=1, source_target_pairs={{0,7},{1,6},{2,5},{3,4},{4,3},{5,2},{6,1},{7,0},{8,15},{9,14},{10,... | collective-permute-start | bytes 1572872 | tf_op jit(solution)/shard_map/ppermute | solution.py:112
  43.6 35.7 %collective-permute-start.7 = (bf16[2,1024,128]{2,1,0:T(8,128)(2,1)}, bf16[2,1024,128]{2,1,0:T(8,128)(2,1)}, u32[]{:S(2)}, u32[]{:S(2)}) collective-permute-start(bf16[2,1024,128]{2,1,0:T(8,128)(2,1)} %pad_maximum_fusion.7), channel_id=1, source_target_pairs={{0,8},{1,9},{2,10},{3,11},{4,12},{5,13},{6,14},{7,15},{8,0},{9,1},... | collective-permute-start | bytes 1572872 | tf_op jit(solution)/shard_map/ppermute | solution.py:112
  46.6 43.0 %collective-permute-start.6 = (bf16[2,1024,128]{2,1,0:T(8,128)(2,1)}, bf16[2,1024,128]{2,1,0:T(8,128)(2,1)}, u32[]{:S(2)}, u32[]{:S(2)}) collective-permute-start(bf16[2,1024,128]{2,1,0:T(8,128)(2,1)} %pad_maximum_fusion.6), channel_id=1, source_target_pairs={{0,9},{1,8},{2,11},{3,10},{4,13},{5,12},{6,15},{7,14},{8,1},{9,0},... | collective-permute-start | bytes 1572872 | tf_op jit(solution)/shard_map/ppermute | solution.py:112
  47.3 56.2 %collective-permute-start.5 = (bf16[2,1024,128]{2,1,0:T(8,128)(2,1)}, bf16[2,1024,128]{2,1,0:T(8,128)(2,1)}, u32[]{:S(2)}, u32[]{:S(2)}) collective-permute-start(bf16[2,1024,128]{2,1,0:T(8,128)(2,1)} %pad_maximum_fusion.5), channel_id=1, source_target_pairs={{0,10},{1,11},{2,8},{3,9},{4,14},{5,15},{6,12},{7,13},{8,2},{9,3},... | collective-permute-start | bytes 1572872 | tf_op jit(solution)/shard_map/ppermute | solution.py:112
  51.6 27.7 %copy-start.11 = (bf16[2,1024,128]{2,1,0:T(8,128)(2,1)S(1)}, bf16[2,1024,128]{2,1,0:T(8,128)(2,1)}, u32[]{:S(2)}) copy-start(bf16[2,1024,128]{2,1,0:T(8,128)(2,1)} %pad_maximum_fusion.2) | copy-start | bytes 1572868
  56.3 86.2 %collective-permute-start.4 = (bf16[2,1024,128]{2,1,0:T(8,128)(2,1)}, bf16[2,1024,128]{2,1,0:T(8,128)(2,1)}, u32[]{:S(2)}, u32[]{:S(2)}) collective-permute-start(bf16[2,1024,128]{2,1,0:T(8,128)(2,1)} %pad_maximum_fusion.4), channel_id=1, source_target_pairs={{0,11},{1,10},{2,9},{3,8},{4,15},{5,14},{6,13},{7,12},{8,3},{9,2},... | collective-permute-start | bytes 1572872 | tf_op jit(solution)/shard_map/ppermute | solution.py:112
  66.6 81.5 %collective-permute-start.3 = (bf16[2,1024,128]{2,1,0:T(8,128)(2,1)}, bf16[2,1024,128]{2,1,0:T(8,128)(2,1)}, u32[]{:S(2)}, u32[]{:S(2)}) collective-permute-start(bf16[2,1024,128]{2,1,0:T(8,128)(2,1)} %pad_maximum_fusion.3), channel_id=1, source_target_pairs={{0,12},{1,13},{2,14},{3,15},{4,8},{5,9},{6,10},{7,11},{8,4},{9,5},... | collective-permute-start | bytes 1572872 | tf_op jit(solution)/shard_map/ppermute | solution.py:112
  79.3 73.2 %collective-permute-start.2 = (bf16[2,1024,128]{2,1,0:T(8,128)(2,1)S(1)}, bf16[2,1024,128]{2,1,0:T(8,128)(2,1)}, u32[]{:S(2)}, u32[]{:S(2)}) collective-permute-start(bf16[2,1024,128]{2,1,0:T(8,128)(2,1)S(1)} %copy-done.11), channel_id=1, source_target_pairs={{0,13},{1,12},{2,15},{3,14},{4,9},{5,8},{6,11},{7,10},{8,5},{9,4},... | collective-permute-start | bytes 1572872 | tf_op jit(solution)/shard_map/ppermute | solution.py:112
  89.6 67.3 %collective-permute-start.1 = (bf16[2,1024,128]{2,1,0:T(8,128)(2,1)}, bf16[2,1024,128]{2,1,0:T(8,128)(2,1)}, u32[]{:S(2)}, u32[]{:S(2)}) collective-permute-start(bf16[2,1024,128]{2,1,0:T(8,128)(2,1)} %pad_maximum_fusion.1), channel_id=1, source_target_pairs={{0,14},{1,15},{2,12},{3,13},{4,10},{5,11},{6,8},{7,9},{8,6},{9,7},... | collective-permute-start | bytes 1572872 | tf_op jit(solution)/shard_map/ppermute | solution.py:112
  103.5 57.8 %collective-permute-start = (bf16[2,1024,128]{2,1,0:T(8,128)(2,1)S(1)}, bf16[2,1024,128]{2,1,0:T(8,128)(2,1)}, u32[]{:S(2)}, u32[]{:S(2)}) collective-permute-start(bf16[2,1024,128]{2,1,0:T(8,128)(2,1)S(1)} %pad_maximum_fusion), channel_id=1, source_target_pairs={{0,15},{1,14},{2,13},{3,12},{4,11},{5,10},{6,9},{7,8},{8,7},{9,6},... | collective-permute-start | bytes 1572872 | tf_op jit(solution)/shard_map/ppermute | solution.py:112
  175.3 9.1 %collective-permute-start.15 = (f32[8,32,4608]{2,1,0:T(8,128)}, f32[8,32,4608]{2,1,0:T(8,128)}, u32[]{:S(2)}, u32[]{:S(2)}) collective-permute-start(f32[8,32,4608]{2,1,0:T(8,128)} %dynamic-slice_bitcast_fusion), channel_id=1, source_target_pairs={{0,1},{1,0},{2,3},{3,2},{4,5},{5,4},{6,7},{7,6},{8,9},{9,8},{10,11... | collective-permute-start | bytes 14155784 | tf_op jit(solution)/shard_map/ppermute | solution.py:130
  191.9 13.6 %collective-permute-start.16 = (bf16[32,4608]{1,0:T(8,128)(2,1)S(1)}, bf16[32,4608]{1,0:T(8,128)(2,1)S(1)}, u32[]{:S(2)}, u32[]{:S(2)}) collective-permute-start(bf16[32,4608]{1,0:T(8,128)(2,1)S(1)} %get-tuple-element.69), channel_id=1, source_target_pairs={{0,2},{2,0},{4,6},{6,4},{8,10},{10,8},{12,14},{14,12},{1,3},{3,1},... | collective-permute-start | bytes 884744 | tf_op jit(solution)/shard_map/ppermute | solution.py:135
  194.2 15.9 %collective-permute-start.17 = (bf16[32,4608]{1,0:T(8,128)(2,1)S(1)}, bf16[32,4608]{1,0:T(8,128)(2,1)S(1)}, u32[]{:S(2)}, u32[]{:S(2)}) collective-permute-start(bf16[32,4608]{1,0:T(8,128)(2,1)S(1)} %get-tuple-element.75), channel_id=1, source_target_pairs={{0,4},{2,6},{4,0},{6,2},{8,12},{10,14},{12,8},{14,10},{1,5},{3,7},... | collective-permute-start | bytes 884744 | tf_op jit(solution)/shard_map/ppermute | solution.py:135
  194.4 18.8 %collective-permute-start.18 = (bf16[32,4608]{1,0:T(8,128)(2,1)}, bf16[32,4608]{1,0:T(8,128)(2,1)}, u32[]{:S(2)}, u32[]{:S(2)}) collective-permute-start(bf16[32,4608]{1,0:T(8,128)(2,1)} %get-tuple-element.74), channel_id=1, source_target_pairs={{0,6},{2,4},{4,2},{6,0},{8,14},{10,12},{12,10},{14,8},{1,7},{3,5},... | collective-permute-start | bytes 884744 | tf_op jit(solution)/shard_map/ppermute | solution.py:135
  196.9 26.9 %collective-permute-start.19 = (bf16[32,4608]{1,0:T(8,128)(2,1)S(1)}, bf16[32,4608]{1,0:T(8,128)(2,1)}, u32[]{:S(2)}, u32[]{:S(2)}) collective-permute-start(bf16[32,4608]{1,0:T(8,128)(2,1)S(1)} %get-tuple-element.73), channel_id=1, source_target_pairs={{0,8},{2,10},{4,12},{6,14},{8,0},{10,2},{12,4},{14,6},{1,9},{3,11}... | collective-permute-start | bytes 884744 | tf_op jit(solution)/shard_map/ppermute | solution.py:135
  203.7 26.1 %collective-permute-start.20 = (bf16[32,4608]{1,0:T(8,128)(2,1)S(1)}, bf16[32,4608]{1,0:T(8,128)(2,1)}, u32[]{:S(2)}, u32[]{:S(2)}) collective-permute-start(bf16[32,4608]{1,0:T(8,128)(2,1)S(1)} %get-tuple-element.72), channel_id=1, source_target_pairs={{0,10},{2,8},{4,14},{6,12},{8,2},{10,0},{12,6},{14,4},{1,11},{3,9}... | collective-permute-start | bytes 884744 | tf_op jit(solution)/shard_map/ppermute | solution.py:135
  205.4 25.2 %collective-permute-start.21 = (bf16[32,4608]{1,0:T(8,128)(2,1)S(1)}, bf16[32,4608]{1,0:T(8,128)(2,1)}, u32[]{:S(2)}, u32[]{:S(2)}) collective-permute-start(bf16[32,4608]{1,0:T(8,128)(2,1)S(1)} %get-tuple-element.71), channel_id=1, source_target_pairs={{0,12},{2,14},{4,8},{6,10},{8,4},{10,6},{12,0},{14,2},{1,13},{3,15... | collective-permute-start | bytes 884744 | tf_op jit(solution)/shard_map/ppermute | solution.py:135
  210.8 26.8 %collective-permute-start.22 = (bf16[32,4608]{1,0:T(8,128)(2,1)S(1)}, bf16[32,4608]{1,0:T(8,128)(2,1)}, u32[]{:S(2)}, u32[]{:S(2)}) collective-permute-start(bf16[32,4608]{1,0:T(8,128)(2,1)S(1)} %get-tuple-element.70), channel_id=1, source_target_pairs={{0,14},{2,12},{4,10},{6,8},{8,6},{10,4},{12,2},{14,0},{1,15},{3,13... | collective-permute-start | bytes 884744 | tf_op jit(solution)/shard_map/ppermute | solution.py:135
  (5 other events, 28.4 us)

commit v6 on v4

--- a/solution.py
+++ b/solution.py
@@ -1,3 +1,5 @@
+import functools
+
 import jax
 import jax.numpy as jnp
 from jax import lax
@@ -14,12 +16,12 @@
 TQ = 256
 
 
-def block_kernel(sc_ref, q_ref, k_ref, v_ref, l_ref, acc_ref, l_out, acc_out):
+def block_kernel(sc_ref, q_ref, k_ref, v_ref, l_ref, acc_ref, l_out, acc_out, *, slot, rows):
     tq = q_ref.shape[0]
     tk = k_ref.shape[0]
-    row_first = sc_ref[0] + (pl.program_id(0) * tq) % sc_ref[2]
+    row_first = sc_ref[0] + (pl.program_id(0) * tq) % rows
     row_last = row_first + tq - 1
-    key_first = sc_ref[1]
+    key_first = sc_ref[1 + slot]
     key_last = key_first + tk - 1
 
     def update(masked):
@@ -50,7 +52,7 @@
         update(True)
 
 
-def attend_kernel(scalars, q, block, total, summed):
+def attend_kernel(scalars, slot, rows, q, block, total, summed):
     n_q, hd = q.shape
     n_k = block.shape[1]
     tq = min(TQ, n_q)
@@ -71,7 +73,7 @@
         ],
     )
     return pl.pallas_call(
-        block_kernel,
+        functools.partial(block_kernel, slot=slot, rows=rows),
         grid_spec=grid_spec,
         out_shape=(
             jax.ShapeDtypeStruct(total.shape, jnp.float32),
@@ -98,20 +100,17 @@
     q_block = queries.reshape(rows_dev, kv_local * group, HD).transpose(1, 0, 2).reshape(n_q, HD)
     total = jnp.zeros((n_q, 1), jnp.float32)
     summed = jnp.zeros((n_q, HD), jnp.float32)
+    table = jnp.stack(
+        (keys.reshape(key_dev, n_kv, kv_feat), values.reshape(key_dev, n_kv, kv_feat)), axis=0
+    ).transpose(2, 0, 1, 3)
+    sources = me ^ jnp.arange(n_kv, dtype=jnp.int32)
+    scalars = jnp.concatenate([row_first[None], sources * key_dev]).astype(jnp.int32)
     for shift in range(n_kv):
-        dest = me ^ shift
-        src = dest
-        block = jnp.stack(
-            (
-                lax.dynamic_slice_in_dim(keys, dest * kv_feat, kv_feat, 1),
-                lax.dynamic_slice_in_dim(values, dest * kv_feat, kv_feat, 1),
-            ),
-            axis=0,
-        )
+        block = lax.dynamic_index_in_dim(table, me ^ shift, 0, keepdims=False)
         if shift:
             block = lax.ppermute(block, KV, [(j, j ^ shift) for j in range(n_kv)])
-        scalars = jnp.stack([row_first, src * key_dev, jnp.int32(rows_dev)]).astype(jnp.int32)
-        total, summed = attend_kernel(scalars, q_block, block, total, summed)
+        block = block.reshape(2, key_dev, kv_feat)
+        total, summed = attend_kernel(scalars, shift, rows_dev, q_block, block, total, summed)
     mixed = (summed / total).astype(jnp.bfloat16)
     return mixed.reshape(kv_local * group, rows_dev, HD).transpose(1, 0, 2).reshape(rows_dev, n_q // rows_dev * HD)
 

time: 236 us -> 239 us (1.013)
  other arithmetic: 34.8 us -> 8.51 us
  local copies, waits for them, and re-layouts: 15.5 us -> 31.7 us
  waiting for transfers between devices: 33.6 us -> 46.9 us
    another operation x32 -> x0, other arithmetic: 26.8 us -> none  [the longest x16 17 us: by_heads(): jnp.stack((lax.dynamic_slice_in_dim(keys, dest * kv_feat, kv_feat, 1), la...]
    ppermute x15, waiting for transfers between devices: 25.7 us -> 39.1 us  [by_heads(): block = lax.ppermute(block, KV, [(j, j ^ shift) for j in range(n_kv)])]
    unnamed x28 -> x17, local copies, waits for them, and re-layouts: 2.24 us -> 13.3 us
    squeeze x0 -> x1, local copies, waits for them, and re-layouts: none -> 6.51 us  [by_heads(): block = lax.dynamic_index_in_dim(table, me ^ shift, 0, keepdims=False)]
  transfers between devices with their start and end apart: 16 -> 16, of which waited for: 5 -> 7; matrix products, arithmetic and copies ran while one was open for 12% -> 2% of each run, Pallas kernels for 34% -> 34%
where the time goes in v6:
time: 239 us
  Pallas kernels  86.6 us (36%)
  waiting for transfers between devices  46.9 us (20%)
  blocking collectives  39.2 us (16%)
  local copies, waits for them, and re-layouts  31.7 us (13%)
  starting transfers between devices  24.1 us (10%)
  other arithmetic  8.51 us (4%)
    pallas_call x16, Pallas kernels, attend_kernel(): pl.pallas_call(functools.partial(block_kernel, slot=slot, rows=rows), gri...  86.6 us
    all_to_all x1, blocking collectives, per_device(): lax.all_to_all(on_chip.astype(jnp.bfloat16), 'kx', split_axis=0, concat_a...  39.2 us
    ppermute x15, waiting for transfers between devices, by_heads(): block = lax.ppermute(block, KV, [(j, j ^ shift) for j in range(n_kv)])  39.1 us
    ppermute x15, starting transfers between devices, by_heads(): block = lax.ppermute(block, KV, [(j, j ^ shift) for j in range(n_kv)])  22.4 us
    unnamed x17, local copies, waits for them, and re-layouts  13.3 us
    ppermute x1, waiting for transfers between devices, per_device(): on_chip = mine + lax.ppermute(theirs, 'kc', [(0, 1), (1, 0)])  7.88 us
    squeeze x1, local copies, waits for them, and re-layouts, by_heads(): block = lax.dynamic_index_in_dim(table, me ^ shift, 0, keepdims=False)  6.51 us
    another operation x1, local copies, waits for them, and re-layouts, by_heads(): jnp.stack((keys.reshape(key_dev, n_kv, kv_feat), values.reshape(key_dev,...  5.27 us
  transfers between devices with their start and end apart: 16, of which 7 were waited for; matrix products, arithmetic and copies ran while one was open for 2% of the time, Pallas kernels for 34%

profile of v6, /device:TPU:120, one launch (start us, length us, event | category | flops | bytes accessed | tf_op | source)
XLA Modules:
  0.0 239.2 jit_solution(2313331830145232310)
XLA Ops:
  0.0 3.7 %copy.54 = bf16[128,8,16,128]{3,2,1,0:T(8,128)(2,1)S(1)} copy(bf16[128,8,16,128]{3,1,2,0:T(8,128)(2,1)} %bitcast.66) | data formatting | bytes 8388608
  3.8 3.1 %copy_dynamic-update-slice_fusion.1 = bf16[2,1024,16,128]{3,1,0,2:T(8,128)(2,1)} fusion(bf16[1,1024,16,128]{3,2,1,0:T(8,128)(2,1)S(1)} %bitcast.65), kind=kLoop, calls=%fused_computation.5 | loop fusion | bytes 8388608
  6.8 3.4 %copy.55 = bf16[128,8,16,128]{3,2,1,0:T(8,128)(2,1)} copy(bf16[128,8,16,128]{3,1,2,0:T(8,128)(2,1)S(1)} %bitcast.67) | data formatting | bytes 8388608
  10.2 5.3 %copy_dynamic-update-slice_fusion = bf16[2,1024,16,128]{3,1,0,2:T(8,128)(2,1)} fusion(bf16[2,1024,16,128]{3,1,0,2:T(8,128)(2,1)} %copy_dynamic-update-slice_fusion.1, bf16[1,1024,16,128]{3,2,1,0:T(8,128)(2,1)} %bitcast.64), kind=kLoop, calls=%fused_computation.4 | loop fusion | bytes 8388608 | tf_op jit(solution)/shard_map/stack | solution.py:103
  15.5 6.5 %dynamic-slice_bitcast_fusion.1 = (bf16[2,1024,128]{2,1,0:T(8,128)(2,1)}, bf16[2,1024,128]{2,1,0:T(8,128)(2,1)S(1)}, bf16[2,1024,128]{2,1,0:T(8,128)(2,1)S(1)}, ...) fusion(bf16[2,1024,16,128]{3,1,0,2:T(8,128)(2,1)} %copy_dynamic, ...), kind=kLoop, calls=%fused_computation.9 | loop fusion | bytes 16777280 | tf_op jit(solution)/shard_map/jit(dynamic_index_in_dim)/squeeze | solution.py:109
  29.3 9.1 %collective-permute-done.13.k_ref.v_ref = bf16[2,1024,128]{2,1,0:T(8,128)(2,1)S(1)} collective-permute-done((bf16[2,1024,128]{2,1,0:T(8,128)(2,1)S(1)}, bf16[2,1024,128]{2,1,0:T(8,128)(2,1)S(1)}, u32[]{:S(2)}, u32[]{:S(2)}) %collective-permute-start.13) | collective-permute-done | bytes 524320 | tf_op jit(solution)/shard_map/ppermute | solution.py:111
  39.2 9.3 %collective-permute-done.12.k_ref.v_ref = bf16[2,1024,128]{2,1,0:T(8,128)(2,1)S(1)} collective-permute-done((bf16[2,1024,128]{2,1,0:T(8,128)(2,1)S(1)}, bf16[2,1024,128]{2,1,0:T(8,128)(2,1)S(1)}, u32[]{:S(2)}, u32[]{:S(2)}) %collective-permute-start.12) | collective-permute-done | bytes 524320 | tf_op jit(solution)/shard_map/ppermute | solution.py:111
  53.3 3.8 %collective-permute-start.5 = (bf16[2,1024,128]{2,1,0:T(8,128)(2,1)}, bf16[2,1024,128]{2,1,0:T(8,128)(2,1)}, u32[]{:S(2)}, u32[]{:S(2)}) collective-permute-start(bf16[2,1024,128]{2,1,0:T(8,128)(2,1)} %get-tuple-element.79), channel_id=1, source_target_pairs={{0,10},{1,11},{2,8},{3,9},{4,14},{5,15},{6,12},{7,13},{8,2},{9,3},... | collective-permute-start | bytes 1572872 | tf_op jit(solution)/shard_map/ppermute | solution.py:111
  59.3 4.1 %collective-permute-done.9.k_ref.v_ref = bf16[2,1024,128]{2,1,0:T(8,128)(2,1)} collective-permute-done((bf16[2,1024,128]{2,1,0:T(8,128)(2,1)}, bf16[2,1024,128]{2,1,0:T(8,128)(2,1)}, u32[]{:S(2)}, u32[]{:S(2)}) %collective-permute-start.9) | collective-permute-done | bytes 524320 | tf_op jit(solution)/shard_map/ppermute | solution.py:111
  63.4 3.3 %collective-permute-start.4 = (bf16[2,1024,128]{2,1,0:T(8,128)(2,1)}, bf16[2,1024,128]{2,1,0:T(8,128)(2,1)}, u32[]{:S(2)}, u32[]{:S(2)}) collective-permute-start(bf16[2,1024,128]{2,1,0:T(8,128)(2,1)} %get-tuple-element.80), channel_id=1, source_target_pairs={{0,11},{1,10},{2,9},{3,8},{4,15},{5,14},{6,13},{7,12},{8,3},{9,2},... | collective-permute-start | bytes 1572872 | tf_op jit(solution)/shard_map/ppermute | solution.py:111
  68.4 5.6 %shard_map.55 = (f32[1024,1]{1,0:T(8,128)}, f32[1024,128]{1,0:T(8,128)}) custom-call(s32[17]{0:T(128)} %pad_add_fusion.sc_ref, bf16[1024,128]{1,0:T(8,128)(2,1)} %bitcast.69, bf16[2,1024,128]{2,1,0:T(8,128)(2,1)} %get-tuple-element.69.k_ref.v_ref, bf16[2,1024,128]{2,1,0:T(8,128)(2,1)} %get-tuple-element.69.k_ref.v_ref, ...), custom_call_target="tpu_custom_call", output_to_operand_aliasing={{0}: (4, {}), {1}: (5, {})} | custom-call | flops 536870912 | bytes 1843200 | tf_op jit(solution)/shard_map/pallas_call | solution.py:75
  76.3 5.6 %shard_map.56 = (f32[1024,1]{1,0:T(8,128)}, f32[1024,128]{1,0:T(8,128)}) custom-call(s32[17]{0:T(128)} %pad_add_fusion.sc_ref, bf16[1024,128]{1,0:T(8,128)(2,1)} %bitcast.70, bf16[2,1024,128]{2,1,0:T(8,128)(2,1)} %copy-done.6, bf16[2,1024,128]{2,1,0:T(8,128)(2,1)} %copy-done.6, ...), custom_call_target="tpu_custom_call", output_to_operand_aliasing={{0}: (4, {}), {1}: (5, {})} | custom-call | flops 536870912 | bytes 1843200 | tf_op jit(solution)/shard_map/pallas_call | solution.py:75
  81.9 5.7 %collective-permute-done.7.k_ref.v_ref = bf16[2,1024,128]{2,1,0:T(8,128)(2,1)} collective-permute-done((bf16[2,1024,128]{2,1,0:T(8,128)(2,1)}, bf16[2,1024,128]{2,1,0:T(8,128)(2,1)}, u32[]{:S(2)}, u32[]{:S(2)}) %collective-permute-start.7) | collective-permute-done | bytes 524320 | tf_op jit(solution)/shard_map/ppermute | solution.py:111
  87.5 5.6 %shard_map.57 = (f32[1024,1]{1,0:T(8,128)}, f32[1024,128]{1,0:T(8,128)}) custom-call(s32[17]{0:T(128)} %pad_add_fusion.sc_ref, bf16[1024,128]{1,0:T(8,128)(2,1)} %bitcast.71, bf16[2,1024,128]{2,1,0:T(8,128)(2,1)} %copy-done.5, bf16[2,1024,128]{2,1,0:T(8,128)(2,1)} %copy-done.5, ...), custom_call_target="tpu_custom_call", output_to_operand_aliasing={{0}: (4, {}), {1}: (5, {})} | custom-call | flops 536870912 | bytes 1843200 | tf_op jit(solution)/shard_map/pallas_call | solution.py:75
  93.2 4.4 %collective-permute-done.6.k_ref.v_ref = bf16[2,1024,128]{2,1,0:T(8,128)(2,1)} collective-permute-done((bf16[2,1024,128]{2,1,0:T(8,128)(2,1)}, bf16[2,1024,128]{2,1,0:T(8,128)(2,1)}, u32[]{:S(2)}, u32[]{:S(2)}) %collective-permute-start.6) | collective-permute-done | bytes 524320 | tf_op jit(solution)/shard_map/ppermute | solution.py:111
  98.7 5.6 %shard_map.58 = (f32[1024,1]{1,0:T(8,128)}, f32[1024,128]{1,0:T(8,128)}) custom-call(s32[17]{0:T(128)} %pad_add_fusion.sc_ref, bf16[1024,128]{1,0:T(8,128)(2,1)} %bitcast.72, bf16[2,1024,128]{2,1,0:T(8,128)(2,1)} %copy-done.4, bf16[2,1024,128]{2,1,0:T(8,128)(2,1)} %copy-done.4, ...), custom_call_target="tpu_custom_call", output_to_operand_aliasing={{0}: (4, {}), {1}: (5, {})} | custom-call | flops 536870912 | bytes 1843200 | tf_op jit(solution)/shard_map/pallas_call | solution.py:75
  104.3 6.3 %collective-permute-done.5.k_ref.v_ref = bf16[2,1024,128]{2,1,0:T(8,128)(2,1)} collective-permute-done((bf16[2,1024,128]{2,1,0:T(8,128)(2,1)}, bf16[2,1024,128]{2,1,0:T(8,128)(2,1)}, u32[]{:S(2)}, u32[]{:S(2)}) %collective-permute-start.5) | collective-permute-done | bytes 524320 | tf_op jit(solution)/shard_map/ppermute | solution.py:111
  111.4 5.6 %shard_map.59 = (f32[1024,1]{1,0:T(8,128)}, f32[1024,128]{1,0:T(8,128)}) custom-call(s32[17]{0:T(128)} %pad_add_fusion.sc_ref, bf16[1024,128]{1,0:T(8,128)(2,1)} %bitcast.73, bf16[2,1024,128]{2,1,0:T(8,128)(2,1)} %copy-done.3, bf16[2,1024,128]{2,1,0:T(8,128)(2,1)} %copy-done.3, ...), custom_call_target="tpu_custom_call", output_to_operand_aliasing={{0}: (4, {}), {1}: (5, {})} | custom-call | flops 536870912 | bytes 1843200 | tf_op jit(solution)/shard_map/pallas_call | solution.py:75
  117.0 5.6 %shard_map.60 = (f32[1024,1]{1,0:T(8,128)}, f32[1024,128]{1,0:T(8,128)}) custom-call(s32[17]{0:T(128)} %pad_add_fusion.sc_ref, bf16[1024,128]{1,0:T(8,128)(2,1)} %bitcast.74, bf16[2,1024,128]{2,1,0:T(8,128)(2,1)} %collective-permute-done.10.k_ref.v_ref, ...), custom_call_target="tpu_custom_call", output_to_operand_aliasing={{0}: (4, {}), {1}: (5, {})} | custom-call | flops 536870912 | bytes 1843200 | tf_op jit(solution)/shard_map/pallas_call | solution.py:75
  122.6 5.6 %shard_map.61 = (f32[1024,1]{1,0:T(8,128)}, f32[1024,128]{1,0:T(8,128)}) custom-call(s32[17]{0:T(128)} %pad_add_fusion.sc_ref, bf16[1024,128]{1,0:T(8,128)(2,1)} %bitcast.75, bf16[2,1024,128]{2,1,0:T(8,128)(2,1)} %collective-permute-done.9.k_ref.v_ref, ...), custom_call_target="tpu_custom_call", output_to_operand_aliasing={{0}: (4, {}), {1}: (5, {})} | custom-call | flops 536870912 | bytes 1843200 | tf_op jit(solution)/shard_map/pallas_call | solution.py:75
  128.2 5.6 %shard_map.62 = (f32[1024,1]{1,0:T(8,128)}, f32[1024,128]{1,0:T(8,128)}) custom-call(s32[17]{0:T(128)} %pad_add_fusion.sc_ref, bf16[1024,128]{1,0:T(8,128)(2,1)} %bitcast.76, bf16[2,1024,128]{2,1,0:T(8,128)(2,1)} %collective-permute-done.8.k_ref.v_ref, ...), custom_call_target="tpu_custom_call", output_to_operand_aliasing={{0}: (4, {}), {1}: (5, {})} | custom-call | flops 536870912 | bytes 1843200 | tf_op jit(solution)/shard_map/pallas_call | solution.py:75
  133.8 5.6 %shard_map.63 = (f32[1024,1]{1,0:T(8,128)}, f32[1024,128]{1,0:T(8,128)}) custom-call(s32[17]{0:T(128)} %pad_add_fusion.sc_ref, bf16[1024,128]{1,0:T(8,128)(2,1)} %bitcast.77, bf16[2,1024,128]{2,1,0:T(8,128)(2,1)} %collective-permute-done.7.k_ref.v_ref, ...), custom_call_target="tpu_custom_call", output_to_operand_aliasing={{0}: (4, {}), {1}: (5, {})} | custom-call | flops 536870912 | bytes 1843200 | tf_op jit(solution)/shard_map/pallas_call | solution.py:75
  139.4 5.6 %shard_map.64 = (f32[1024,1]{1,0:T(8,128)}, f32[1024,128]{1,0:T(8,128)}) custom-call(s32[17]{0:T(128)} %pad_add_fusion.sc_ref, bf16[1024,128]{1,0:T(8,128)(2,1)} %bitcast.78, bf16[2,1024,128]{2,1,0:T(8,128)(2,1)} %collective-permute-done.6.k_ref.v_ref, ...), custom_call_target="tpu_custom_call", output_to_operand_aliasing={{0}: (4, {}), {1}: (5, {})} | custom-call | flops 536870912 | bytes 1843200 | tf_op jit(solution)/shard_map/pallas_call | solution.py:75
  145.0 5.6 %shard_map.65 = (f32[1024,1]{1,0:T(8,128)}, f32[1024,128]{1,0:T(8,128)}) custom-call(s32[17]{0:T(128)} %pad_add_fusion.sc_ref, bf16[1024,128]{1,0:T(8,128)(2,1)} %bitcast.79, bf16[2,1024,128]{2,1,0:T(8,128)(2,1)} %collective-permute-done.5.k_ref.v_ref, ...), custom_call_target="tpu_custom_call", output_to_operand_aliasing={{0}: (4, {}), {1}: (5, {})} | custom-call | flops 536870912 | bytes 1843200 | tf_op jit(solution)/shard_map/pallas_call | solution.py:75
  150.6 5.6 %shard_map.66 = (f32[1024,1]{1,0:T(8,128)}, f32[1024,128]{1,0:T(8,128)}) custom-call(s32[17]{0:T(128)} %pad_add_fusion.sc_ref, bf16[1024,128]{1,0:T(8,128)(2,1)} %bitcast.80, bf16[2,1024,128]{2,1,0:T(8,128)(2,1)} %collective-permute-done.4.k_ref.v_ref, ...), custom_call_target="tpu_custom_call", output_to_operand_aliasing={{0}: (4, {}), {1}: (5, {})} | custom-call | flops 536870912 | bytes 1843200 | tf_op jit(solution)/shard_map/pallas_call | solution.py:75
  156.2 4.5 %shard_map.67 = (f32[1024,1]{1,0:T(8,128)}, f32[1024,128]{1,0:T(8,128)}) custom-call(s32[17]{0:T(128)} %pad_add_fusion.sc_ref, bf16[1024,128]{1,0:T(8,128)(2,1)} %bitcast.81, bf16[2,1024,128]{2,1,0:T(8,128)(2,1)} %collective-permute-done.3.k_ref.v_ref, ...), custom_call_target="tpu_custom_call", output_to_operand_aliasing={{0}: (4, {}), {1}: (5, {})} | custom-call | flops 536870912 | bytes 1843200 | tf_op jit(solution)/shard_map/pallas_call | solution.py:75
  160.7 4.5 %shard_map.68 = (f32[1024,1]{1,0:T(8,128)}, f32[1024,128]{1,0:T(8,128)}) custom-call(s32[17]{0:T(128)} %pad_add_fusion.sc_ref, bf16[1024,128]{1,0:T(8,128)(2,1)} %bitcast.82, bf16[2,1024,128]{2,1,0:T(8,128)(2,1)} %collective-permute-done.2.k_ref.v_ref, ...), custom_call_target="tpu_custom_call", output_to_operand_aliasing={{0}: (4, {}), {1}: (5, {})} | custom-call | flops 536870912 | bytes 1843200 | tf_op jit(solution)/shard_map/pallas_call | solution.py:75
  165.2 5.7 %shard_map.69 = (f32[1024,1]{1,0:T(8,128)}, f32[1024,128]{1,0:T(8,128)}) custom-call(s32[17]{0:T(128)} %pad_add_fusion.sc_ref, bf16[1024,128]{1,0:T(8,128)(2,1)} %bitcast.83, bf16[2,1024,128]{2,1,0:T(8,128)(2,1)} %collective-permute-done.1.k_ref.v_ref, ...), custom_call_target="tpu_custom_call", output_to_operand_aliasing={{0}: (4, {}), {1}: (5, {})} | custom-call | flops 536870912 | bytes 1843200 | tf_op jit(solution)/shard_map/pallas_call | solution.py:75
  170.9 4.7 %shard_map.70 = (f32[1024,1]{1,0:T(8,128)}, f32[1024,128]{1,0:T(8,128)}) custom-call(s32[17]{0:T(128)} %pad_add_fusion.sc_ref, bf16[1024,128]{1,0:T(8,128)(2,1)} %bitcast.84, bf16[2,1024,128]{2,1,0:T(8,128)(2,1)} %collective-permute-done.k_ref.v_ref, ...), custom_call_target="tpu_custom_call", output_to_operand_aliasing={{0}: (4, {}), {1}: (5, {})} | custom-call | flops 536870912 | bytes 1843200 | tf_op jit(solution)/shard_map/pallas_call | solution.py:75
  186.7 7.9 %collective-permute-done.15 = f32[8,32,4608]{2,1,0:T(8,128)} collective-permute-done((f32[8,32,4608]{2,1,0:T(8,128)}, f32[8,32,4608]{2,1,0:T(8,128)}, u32[]{:S(2)}, u32[]{:S(2)}) %collective-permute-start.15) | collective-permute-done | bytes 4718624 | tf_op jit(solution)/shard_map/ppermute | solution.py:129
  194.6 4.3 %fusion = bf16[8,32,4608]{2,1,0:T(8,128)(2,1)S(1)} fusion(f32[8,32,4608]{2,1,0:T(8,128)} %collective-permute-done.15, f32[8,2,32,4608]{3,2,1,0:T(8,128)} %copy-done.1, s32[]{:T(128)S(6)} %select_n.72), kind=kLoop, calls=%fused_computation.1 | loop fusion | flops 2359296 | bytes 11796484 | tf_op jit(solution)/shard_map/convert_element_type | solution.py:131
  198.9 39.2 %all_to_all.5 = bf16[8,32,4608]{2,1,0:T(8,128)(2,1)S(1)} all-to-all(bf16[8,32,4608]{2,1,0:T(8,128)(2,1)S(1)} %fusion), channel_id=1, replica_groups=mesh['pb'=8,'kx'=8,'kc'=2] {'kx'}, dimensions={0} | all-to-all | bytes 4718592 | tf_op jit(solution)/shard_map/all_to_all | solution.py:130
  (49 shorter events, 32.3 us)
Async XLA Ops:
  0.0 178.6 %copy-start = (bf16[256,4608]{1,0:T(8,128)(2,1)S(1)}, bf16[256,4608]{1,0:T(8,128)(2,1)}, u32[]{:S(2)}) copy-start(bf16[256,4608]{1,0:T(8,128)(2,1)} %param.9) | copy-start | bytes 7077892
  3.7 3.1 %copy-start.2 = (bf16[1024,2048]{1,0:T(8,128)(2,1)S(1)}, bf16[1024,2048]{1,0:T(8,128)(2,1)}, u32[]{:S(2)}) copy-start(bf16[1024,2048]{1,0:T(8,128)(2,1)} %param.8) | copy-start | bytes 12582916
  22.0 5.1 %collective-permute-start.14 = (bf16[2,1024,128]{2,1,0:T(8,128)(2,1)S(1)}, bf16[2,1024,128]{2,1,0:T(8,128)(2,1)S(1)}, u32[]{:S(2)}, u32[]{:S(2)}) collective-permute-start(bf16[2,1024,128]{2,1,0:T(8,128)(2,1)S(1)} %get-tuple-element.70), channel_id=1, source_target_pairs={{0,1},{1,0},{2,3},{3,2},{4,5},{5,4},{6,7},{7,6},{8,9},{9,8},{10,11... | collective-permute-start | bytes 1572872 | tf_op jit(solution)/shard_map/ppermute | solution.py:111
  22.1 16.4 %collective-permute-start.13 = (bf16[2,1024,128]{2,1,0:T(8,128)(2,1)S(1)}, bf16[2,1024,128]{2,1,0:T(8,128)(2,1)S(1)}, u32[]{:S(2)}, u32[]{:S(2)}) collective-permute-start(bf16[2,1024,128]{2,1,0:T(8,128)(2,1)S(1)} %get-tuple-element.71), channel_id=1, source_target_pairs={{0,2},{1,3},{2,0},{3,1},{4,6},{5,7},{6,4},{7,5},{8,10},{9,11},{10,... | collective-permute-start | bytes 1572872 | tf_op jit(solution)/shard_map/ppermute | solution.py:111
  23.4 25.2 %collective-permute-start.12 = (bf16[2,1024,128]{2,1,0:T(8,128)(2,1)S(1)}, bf16[2,1024,128]{2,1,0:T(8,128)(2,1)S(1)}, u32[]{:S(2)}, u32[]{:S(2)}) collective-permute-start(bf16[2,1024,128]{2,1,0:T(8,128)(2,1)S(1)} %get-tuple-element.72), channel_id=1, source_target_pairs={{0,3},{1,2},{2,1},{3,0},{4,7},{5,6},{6,5},{7,4},{8,11},{9,10},{10,... | collective-permute-start | bytes 1572872 | tf_op jit(solution)/shard_map/ppermute | solution.py:111
  25.4 26.2 %collective-permute-start.11 = (bf16[2,1024,128]{2,1,0:T(8,128)(2,1)S(1)}, bf16[2,1024,128]{2,1,0:T(8,128)(2,1)S(1)}, u32[]{:S(2)}, u32[]{:S(2)}) collective-permute-start(bf16[2,1024,128]{2,1,0:T(8,128)(2,1)S(1)} %get-tuple-element.73), channel_id=1, source_target_pairs={{0,4},{1,5},{2,6},{3,7},{4,0},{5,1},{6,2},{7,3},{8,12},{9,13},{10,... | collective-permute-start | bytes 1572872 | tf_op jit(solution)/shard_map/ppermute | solution.py:111
  26.9 26.4 %collective-permute-start.10 = (bf16[2,1024,128]{2,1,0:T(8,128)(2,1)}, bf16[2,1024,128]{2,1,0:T(8,128)(2,1)}, u32[]{:S(2)}, u32[]{:S(2)}) collective-permute-start(bf16[2,1024,128]{2,1,0:T(8,128)(2,1)} %get-tuple-element.74), channel_id=1, source_target_pairs={{0,5},{1,4},{2,7},{3,6},{4,1},{5,0},{6,3},{7,2},{8,13},{9,12},{10,... | collective-permute-start | bytes 1572872 | tf_op jit(solution)/shard_map/ppermute | solution.py:111
  27.1 25.5 %copy-start.6 = (bf16[2,1024,128]{2,1,0:T(8,128)(2,1)}, bf16[2,1024,128]{2,1,0:T(8,128)(2,1)S(1)}, u32[]{:S(2)}) copy-start(bf16[2,1024,128]{2,1,0:T(8,128)(2,1)S(1)} %collective-permute-done.14.k_ref.v_ref) | copy-start | bytes 1572868
  27.1 36.3 %collective-permute-start.9 = (bf16[2,1024,128]{2,1,0:T(8,128)(2,1)}, bf16[2,1024,128]{2,1,0:T(8,128)(2,1)}, u32[]{:S(2)}, u32[]{:S(2)}) collective-permute-start(bf16[2,1024,128]{2,1,0:T(8,128)(2,1)} %get-tuple-element.75), channel_id=1, source_target_pairs={{0,6},{1,7},{2,4},{3,5},{4,2},{5,3},{6,0},{7,1},{8,14},{9,15},{10,... | collective-permute-start | bytes 1572872 | tf_op jit(solution)/shard_map/ppermute | solution.py:111
  38.4 14.2 %copy-start.5 = (bf16[2,1024,128]{2,1,0:T(8,128)(2,1)}, bf16[2,1024,128]{2,1,0:T(8,128)(2,1)S(1)}, u32[]{:S(2)}) copy-start(bf16[2,1024,128]{2,1,0:T(8,128)(2,1)S(1)} %collective-permute-done.13.k_ref.v_ref) | copy-start | bytes 1572868
  38.4 35.6 %collective-permute-start.8 = (bf16[2,1024,128]{2,1,0:T(8,128)(2,1)}, bf16[2,1024,128]{2,1,0:T(8,128)(2,1)}, u32[]{:S(2)}, u32[]{:S(2)}) collective-permute-start(bf16[2,1024,128]{2,1,0:T(8,128)(2,1)} %get-tuple-element.76), channel_id=1, source_target_pairs={{0,7},{1,6},{2,5},{3,4},{4,3},{5,2},{6,1},{7,0},{8,15},{9,14},{10,... | collective-permute-start | bytes 1572872 | tf_op jit(solution)/shard_map/ppermute | solution.py:111
  48.6 3.8 %copy-start.4 = (bf16[2,1024,128]{2,1,0:T(8,128)(2,1)}, bf16[2,1024,128]{2,1,0:T(8,128)(2,1)S(1)}, u32[]{:S(2)}) copy-start(bf16[2,1024,128]{2,1,0:T(8,128)(2,1)S(1)} %collective-permute-done.12.k_ref.v_ref) | copy-start | bytes 1572868
  48.6 39.0 %collective-permute-start.7 = (bf16[2,1024,128]{2,1,0:T(8,128)(2,1)}, bf16[2,1024,128]{2,1,0:T(8,128)(2,1)}, u32[]{:S(2)}, u32[]{:S(2)}) collective-permute-start(bf16[2,1024,128]{2,1,0:T(8,128)(2,1)} %get-tuple-element.77), channel_id=1, source_target_pairs={{0,8},{1,9},{2,10},{3,11},{4,12},{5,13},{6,14},{7,15},{8,0},{9,1},... | collective-permute-start | bytes 1572872 | tf_op jit(solution)/shard_map/ppermute | solution.py:111
  51.6 0.8 copy-start.3
  52.4 45.2 %collective-permute-start.6 = (bf16[2,1024,128]{2,1,0:T(8,128)(2,1)}, bf16[2,1024,128]{2,1,0:T(8,128)(2,1)}, u32[]{:S(2)}, u32[]{:S(2)}) collective-permute-start(bf16[2,1024,128]{2,1,0:T(8,128)(2,1)} %get-tuple-element.78), channel_id=1, source_target_pairs={{0,9},{1,8},{2,11},{3,10},{4,13},{5,12},{6,15},{7,14},{8,1},{9,0},... | collective-permute-start | bytes 1572872 | tf_op jit(solution)/shard_map/ppermute | solution.py:111
  53.3 57.4 %collective-permute-start.5 = (bf16[2,1024,128]{2,1,0:T(8,128)(2,1)}, bf16[2,1024,128]{2,1,0:T(8,128)(2,1)}, u32[]{:S(2)}, u32[]{:S(2)}) collective-permute-start(bf16[2,1024,128]{2,1,0:T(8,128)(2,1)} %get-tuple-element.79), channel_id=1, source_target_pairs={{0,10},{1,11},{2,8},{3,9},{4,14},{5,15},{6,12},{7,13},{8,2},{9,3},... | collective-permute-start | bytes 1572872 | tf_op jit(solution)/shard_map/ppermute | solution.py:111
  63.4 87.2 %collective-permute-start.4 = (bf16[2,1024,128]{2,1,0:T(8,128)(2,1)}, bf16[2,1024,128]{2,1,0:T(8,128)(2,1)}, u32[]{:S(2)}, u32[]{:S(2)}) collective-permute-start(bf16[2,1024,128]{2,1,0:T(8,128)(2,1)} %get-tuple-element.80), channel_id=1, source_target_pairs={{0,11},{1,10},{2,9},{3,8},{4,15},{5,14},{6,13},{7,12},{8,3},{9,2},... | collective-permute-start | bytes 1572872 | tf_op jit(solution)/shard_map/ppermute | solution.py:111
  74.0 82.2 %collective-permute-start.3 = (bf16[2,1024,128]{2,1,0:T(8,128)(2,1)}, bf16[2,1024,128]{2,1,0:T(8,128)(2,1)}, u32[]{:S(2)}, u32[]{:S(2)}) collective-permute-start(bf16[2,1024,128]{2,1,0:T(8,128)(2,1)} %get-tuple-element.81), channel_id=1, source_target_pairs={{0,12},{1,13},{2,14},{3,15},{4,8},{5,9},{6,10},{7,11},{8,4},{9,5},... | collective-permute-start | bytes 1572872 | tf_op jit(solution)/shard_map/ppermute | solution.py:111
  87.5 73.2 %collective-permute-start.2 = (bf16[2,1024,128]{2,1,0:T(8,128)(2,1)}, bf16[2,1024,128]{2,1,0:T(8,128)(2,1)}, u32[]{:S(2)}, u32[]{:S(2)}) collective-permute-start(bf16[2,1024,128]{2,1,0:T(8,128)(2,1)} %get-tuple-element.82), channel_id=1, source_target_pairs={{0,13},{1,12},{2,15},{3,14},{4,9},{5,8},{6,11},{7,10},{8,5},{9,4},... | collective-permute-start | bytes 1572872 | tf_op jit(solution)/shard_map/ppermute | solution.py:111
  97.6 67.6 %collective-permute-start.1 = (bf16[2,1024,128]{2,1,0:T(8,128)(2,1)S(1)}, bf16[2,1024,128]{2,1,0:T(8,128)(2,1)}, u32[]{:S(2)}, u32[]{:S(2)}) collective-permute-start(bf16[2,1024,128]{2,1,0:T(8,128)(2,1)S(1)} %get-tuple-element.83), channel_id=1, source_target_pairs={{0,14},{1,15},{2,12},{3,13},{4,10},{5,11},{6,8},{7,9},{8,6},{9,7},... | collective-permute-start | bytes 1572872 | tf_op jit(solution)/shard_map/ppermute | solution.py:111
  110.7 60.2 %collective-permute-start = (bf16[2,1024,128]{2,1,0:T(8,128)(2,1)S(1)}, bf16[2,1024,128]{2,1,0:T(8,128)(2,1)}, u32[]{:S(2)}, u32[]{:S(2)}) collective-permute-start(bf16[2,1024,128]{2,1,0:T(8,128)(2,1)S(1)} %get-tuple-element.84), channel_id=1, source_target_pairs={{0,15},{1,14},{2,13},{3,12},{4,11},{5,10},{6,9},{7,8},{8,7},{9,6},... | collective-permute-start | bytes 1572872 | tf_op jit(solution)/shard_map/ppermute | solution.py:111
  180.0 5.1 %copy-start.1 = (f32[8,2,32,4608]{3,2,1,0:T(8,128)}, f32[8,2,32,4608]{3,2,1,0:T(8,128)S(1)}, u32[]{:S(2)}) copy-start(f32[8,2,32,4608]{3,2,1,0:T(8,128)S(1)} %fusion.1) | copy-start | bytes 28311556
  185.0 9.5 %collective-permute-start.15 = (f32[8,32,4608]{2,1,0:T(8,128)}, f32[8,32,4608]{2,1,0:T(8,128)}, u32[]{:S(2)}, u32[]{:S(2)}) collective-permute-start(f32[8,32,4608]{2,1,0:T(8,128)} %dynamic-slice_bitcast_fusion), channel_id=1, source_target_pairs={{0,1},{1,0},{2,3},{3,2},{4,5},{5,4},{6,7},{7,6},{8,9},{9,8},{10,11... | collective-permute-start | bytes 14155784 | tf_op jit(solution)/shard_map/ppermute | solution.py:129

commit v7 on v4

--- a/solution.py
+++ b/solution.py
@@ -126,8 +126,8 @@
     partial = partial.reshape(n_chip, n_core, rows_dev // (n_chip * n_core), partial.shape[1])
     core = lax.axis_index("kc")
     mine = lax.dynamic_index_in_dim(partial, core, 1, keepdims=False)
-    theirs = lax.dynamic_index_in_dim(partial, 1 - core, 1, keepdims=False)
-    on_chip = mine + lax.ppermute(theirs, "kc", [(0, 1), (1, 0)])
+    theirs = lax.dynamic_index_in_dim(partial, 1 - core, 1, keepdims=False).astype(jnp.bfloat16)
+    on_chip = mine + lax.ppermute(theirs, "kc", [(0, 1), (1, 0)]).astype(jnp.float32)
     parts = lax.all_to_all(
         on_chip.astype(jnp.bfloat16), "kx", split_axis=0, concat_axis=0, tiled=True
     )

time: 236 us -> 234 us (level)
  waiting for transfers between devices: 33.6 us -> 30.2 us
    ppermute x1, waiting for transfers between devices: 7.91 us -> 4.54 us  [per_device(): lax.ppermute(theirs, 'kc', [(0, 1), (1, 0)]).astype(jnp.float32)]
    squeeze x1 -> x0, local copies, waits for them, and re-layouts: 2.85 us -> none  [per_device(): theirs = lax.dynamic_index_in_dim(partial, 1 - core, 1, keepdims=False)]
  transfers between devices with their start and end apart: 16 -> 16, of which waited for: 5 -> 5; matrix products, arithmetic and copies ran while one was open for 12% -> 13% of each run, Pallas kernels for 34% -> 35%
where the time goes in v7:
time: 234 us; the launch traced here: 233 us
  Pallas kernels  85 us (36%)
  blocking collectives  40.4 us (17%)
  other arithmetic  34.1 us (15%)
  waiting for transfers between devices  30.2 us (13%)
  starting transfers between devices  24.7 us (11%)
  local copies, waits for them, and re-layouts  15.8 us (7%)
    pallas_call x16, Pallas kernels, attend_kernel(): pl.pallas_call(block_kernel, grid_spec=grid_spec, out_shape=(jax.ShapeDty...  85 us
    all_to_all x1, blocking collectives, per_device(): lax.all_to_all(on_chip.astype(jnp.bfloat16), 'kx', split_axis=0, concat_a...  40.4 us
    ppermute x15, waiting for transfers between devices, by_heads(): block = lax.ppermute(block, KV, [(j, j ^ shift) for j in range(n_kv)])  25.7 us
    ppermute x15, starting transfers between devices, by_heads(): block = lax.ppermute(block, KV, [(j, j ^ shift) for j in range(n_kv)])  24.4 us
    another operation x16, other arithmetic, by_heads(): jnp.stack((lax.dynamic_slice_in_dim(keys, dest * kv_feat, kv_feat, 1), la...  17 us
    another operation x16, other arithmetic, by_heads(): jnp.stack([row_first, src * key_dev, jnp.int32(rows_dev)]).astype(jnp.int32)  9.82 us
    another operation x1, local copies, waits for them, and re-layouts, by_heads(): jnp.stack((lax.dynamic_slice_in_dim(keys, dest * kv_feat, kv_feat, 1), la...  6.65 us
  transfers between devices with their start and end apart: 16, of which 5 were waited for; matrix products, arithmetic and copies ran while one was open for 13% of the time, Pallas kernels for 35%

profile of v7, /device:TPU:120, one launch (start us, length us, event | category | flops | bytes accessed | tf_op | source)
XLA Modules:
  0.0 232.5 jit_solution(17269614349288898436)
XLA Ops:
  0.0 6.7 %dynamic-slice_bitcast_fusion = (bf16[1,1024,128]{2,1,0:T(8,128)(2,1)}, bf16[1,1024,128]{2,1,0:T(8,128)(2,1)}, bf16[1,1024,128]{2,1,0:T(8,128)(2,1)}, bf16[1,102...) fusion(bf16[1024,2048]{1,0:T(8,128)(2,1)} %param.8, ...), kind=kLoop, calls=%fused_computation.25 | loop fusion | bytes 16777280 | tf_op jit(solution)/shard_map/stack | solution.py:104
  8.4 3.7 %collective-permute-start.5 = (bf16[2,1024,128]{2,1,0:T(8,128)(2,1)}, bf16[2,1024,128]{2,1,0:T(8,128)(2,1)}, u32[]{:S(2)}, u32[]{:S(2)}) collective-permute-start(bf16[2,1024,128]{2,1,0:T(8,128)(2,1)} %pad_maximum_fusion.5), channel_id=1, source_target_pairs={{0,10},{1,11},{2,8},{3,9},{4,14},{5,15},{6,12},{7,13},{8,2},{9,3},... | collective-permute-start | bytes 1572872 | tf_op jit(solution)/shard_map/ppermute | solution.py:112
  14.1 3.0 %collective-permute-start.7 = (bf16[2,1024,128]{2,1,0:T(8,128)(2,1)}, bf16[2,1024,128]{2,1,0:T(8,128)(2,1)}, u32[]{:S(2)}, u32[]{:S(2)}) collective-permute-start(bf16[2,1024,128]{2,1,0:T(8,128)(2,1)} %pad_maximum_fusion.7), channel_id=1, source_target_pairs={{0,8},{1,9},{2,10},{3,11},{4,12},{5,13},{6,14},{7,15},{8,0},{9,1},... | collective-permute-start | bytes 1572872 | tf_op jit(solution)/shard_map/ppermute | solution.py:112
  18.0 1.9 collective-permute-start.8
  26.8 2.0 pad_maximum_fusion.15.k_ref.v_ref
  41.5 2.2 collective-permute-start.9
  44.7 2.2 collective-permute-start.12
  48.1 2.3 collective-permute-start.13
  51.0 9.4 %collective-permute-done.8.k_ref.v_ref = bf16[2,1024,128]{2,1,0:T(8,128)(2,1)} collective-permute-done((bf16[2,1024,128]{2,1,0:T(8,128)(2,1)}, bf16[2,1024,128]{2,1,0:T(8,128)(2,1)}, u32[]{:S(2)}, u32[]{:S(2)}) %collective-permute-start.8) | collective-permute-done | bytes 524320 | tf_op jit(solution)/shard_map/ppermute | solution.py:112
  64.1 8.2 %collective-permute-done.9.k_ref.v_ref = bf16[2,1024,128]{2,1,0:T(8,128)(2,1)S(1)} collective-permute-done((bf16[2,1024,128]{2,1,0:T(8,128)(2,1)}, bf16[2,1024,128]{2,1,0:T(8,128)(2,1)S(1)}, u32[]{:S(2)}, u32[]{:S(2)}) %collective-permute-start.9) | collective-permute-done | bytes 524320 | tf_op jit(solution)/shard_map/ppermute | solution.py:112
  75.5 5.6 %shard_map.55 = (f32[1024,1]{1,0:T(8,128)}, f32[1024,128]{1,0:T(8,128)}) custom-call(s32[3]{0:T(128)} %pad_add_fusion.sc_ref, bf16[1024,128]{1,0:T(8,128)(2,1)} %bitcast.107, bf16[2,1024,128]{2,1,0:T(8,128)(2,1)} %pad_maximum_fusion.15.k_ref.v_ref, ...), custom_call_target="tpu_custom_call", output_to_operand_aliasing={{0}: (4, {}), {1}: (5, {})} | custom-call | flops 536870912 | bytes 1843200 | tf_op jit(solution)/shard_map/pallas_call | solution.py:73
  82.1 5.6 %shard_map.56 = (f32[1024,1]{1,0:T(8,128)}, f32[1024,128]{1,0:T(8,128)}) custom-call(s32[3]{0:T(128)} %pad_add_fusion.1.sc_ref, bf16[1024,128]{1,0:T(8,128)(2,1)} %bitcast.108, bf16[2,1024,128]{2,1,0:T(8,128)(2,1)} %collective-permute-done.14.k_ref.v_ref, ...), custom_call_target="tpu_custom_call", output_to_operand_aliasing={{0}: (4, {}), {1}: (5, {})} | custom-call | flops 536870912 | bytes 1843200 | tf_op jit(solution)/shard_map/pallas_call | solution.py:73
  87.7 6.8 %collective-permute-done.13.k_ref.v_ref = bf16[2,1024,128]{2,1,0:T(8,128)(2,1)} collective-permute-done((bf16[2,1024,128]{2,1,0:T(8,128)(2,1)}, bf16[2,1024,128]{2,1,0:T(8,128)(2,1)}, u32[]{:S(2)}, u32[]{:S(2)}) %collective-permute-start.13) | collective-permute-done | bytes 524320 | tf_op jit(solution)/shard_map/ppermute | solution.py:112
  94.5 5.6 %shard_map.57 = (f32[1024,1]{1,0:T(8,128)}, f32[1024,128]{1,0:T(8,128)}) custom-call(s32[3]{0:T(128)} %pad_add_fusion.2.sc_ref, bf16[1024,128]{1,0:T(8,128)(2,1)} %bitcast.109, bf16[2,1024,128]{2,1,0:T(8,128)(2,1)} %collective-permute-done.13.k_ref.v_ref, ...), custom_call_target="tpu_custom_call", output_to_operand_aliasing={{0}: (4, {}), {1}: (5, {})} | custom-call | flops 536870912 | bytes 1843200 | tf_op jit(solution)/shard_map/pallas_call | solution.py:73
  100.1 2.9 %collective-permute-start.1 = (bf16[2,1024,128]{2,1,0:T(8,128)(2,1)}, bf16[2,1024,128]{2,1,0:T(8,128)(2,1)}, u32[]{:S(2)}, u32[]{:S(2)}) collective-permute-start(bf16[2,1024,128]{2,1,0:T(8,128)(2,1)} %pad_maximum_fusion.1), channel_id=1, source_target_pairs={{0,14},{1,15},{2,12},{3,13},{4,10},{5,11},{6,8},{7,9},{8,6},{9,7},... | collective-permute-start | bytes 1572872 | tf_op jit(solution)/shard_map/ppermute | solution.py:112
  103.0 5.6 %shard_map.58 = (f32[1024,1]{1,0:T(8,128)}, f32[1024,128]{1,0:T(8,128)}) custom-call(s32[3]{0:T(128)} %pad_add_fusion.3.sc_ref, bf16[1024,128]{1,0:T(8,128)(2,1)} %bitcast.110, bf16[2,1024,128]{2,1,0:T(8,128)(2,1)} %collective-permute-done.12.k_ref.v_ref, ...), custom_call_target="tpu_custom_call", output_to_operand_aliasing={{0}: (4, {}), {1}: (5, {})} | custom-call | flops 536870912 | bytes 1843200 | tf_op jit(solution)/shard_map/pallas_call | solution.py:73
  110.1 5.8 %shard_map.59 = (f32[1024,1]{1,0:T(8,128)}, f32[1024,128]{1,0:T(8,128)}) custom-call(s32[3]{0:T(128)} %pad_add_fusion.4.sc_ref, bf16[1024,128]{1,0:T(8,128)(2,1)} %bitcast.111, bf16[2,1024,128]{2,1,0:T(8,128)(2,1)} %collective-permute-done.11.k_ref.v_ref, ...), custom_call_target="tpu_custom_call", output_to_operand_aliasing={{0}: (4, {}), {1}: (5, {})} | custom-call | flops 536870912 | bytes 1843200 | tf_op jit(solution)/shard_map/pallas_call | solution.py:73
  115.8 5.6 %shard_map.60 = (f32[1024,1]{1,0:T(8,128)}, f32[1024,128]{1,0:T(8,128)}) custom-call(s32[3]{0:T(128)} %pad_add_fusion.5.sc_ref, bf16[1024,128]{1,0:T(8,128)(2,1)} %bitcast.112, bf16[2,1024,128]{2,1,0:T(8,128)(2,1)} %collective-permute-done.10.k_ref.v_ref, ...), custom_call_target="tpu_custom_call", output_to_operand_aliasing={{0}: (4, {}), {1}: (5, {})} | custom-call | flops 536870912 | bytes 1843200 | tf_op jit(solution)/shard_map/pallas_call | solution.py:73
  121.4 5.6 %shard_map.61 = (f32[1024,1]{1,0:T(8,128)}, f32[1024,128]{1,0:T(8,128)}) custom-call(s32[3]{0:T(128)} %pad_add_fusion.6.sc_ref, bf16[1024,128]{1,0:T(8,128)(2,1)} %bitcast.113, bf16[2,1024,128]{2,1,0:T(8,128)(2,1)} %copy-done.13, bf16[2,1024,128]{2,1,0:T(8,128)(2,1)} %copy-done.13, ...), custom_call_target="tpu_custom_call", output_to_operand_aliasing={{0}: (4, {}), {1}: (5, {})} | custom-call | flops 536870912 | bytes 1843200 | tf_op jit(solution)/shard_map/pallas_call | solution.py:73
  127.0 5.6 %shard_map.62 = (f32[1024,1]{1,0:T(8,128)}, f32[1024,128]{1,0:T(8,128)}) custom-call(s32[3]{0:T(128)} %pad_add_fusion.7.sc_ref, bf16[1024,128]{1,0:T(8,128)(2,1)} %bitcast.114, bf16[2,1024,128]{2,1,0:T(8,128)(2,1)} %collective-permute-done.8.k_ref.v_ref, ...), custom_call_target="tpu_custom_call", output_to_operand_aliasing={{0}: (4, {}), {1}: (5, {})} | custom-call | flops 536870912 | bytes 1843200 | tf_op jit(solution)/shard_map/pallas_call | solution.py:73
  132.6 5.6 %shard_map.63 = (f32[1024,1]{1,0:T(8,128)}, f32[1024,128]{1,0:T(8,128)}) custom-call(s32[3]{0:T(128)} %pad_add_fusion.8.sc_ref, bf16[1024,128]{1,0:T(8,128)(2,1)} %bitcast.115, bf16[2,1024,128]{2,1,0:T(8,128)(2,1)} %collective-permute-done.7.k_ref.v_ref, ...), custom_call_target="tpu_custom_call", output_to_operand_aliasing={{0}: (4, {}), {1}: (5, {})} | custom-call | flops 536870912 | bytes 1843200 | tf_op jit(solution)/shard_map/pallas_call | solution.py:73
  138.2 5.6 %shard_map.64 = (f32[1024,1]{1,0:T(8,128)}, f32[1024,128]{1,0:T(8,128)}) custom-call(s32[3]{0:T(128)} %pad_add_fusion.9.sc_ref, bf16[1024,128]{1,0:T(8,128)(2,1)} %bitcast.116, bf16[2,1024,128]{2,1,0:T(8,128)(2,1)} %collective-permute-done.6.k_ref.v_ref, ...), custom_call_target="tpu_custom_call", output_to_operand_aliasing={{0}: (4, {}), {1}: (5, {})} | custom-call | flops 536870912 | bytes 1843200 | tf_op jit(solution)/shard_map/pallas_call | solution.py:73
  143.8 5.6 %shard_map.65 = (f32[1024,1]{1,0:T(8,128)}, f32[1024,128]{1,0:T(8,128)}) custom-call(s32[3]{0:T(128)} %pad_add_fusion.10.sc_ref, bf16[1024,128]{1,0:T(8,128)(2,1)} %bitcast.117, bf16[2,1024,128]{2,1,0:T(8,128)(2,1)} %collective-permute-done.5.k_ref.v_ref, ...), custom_call_target="tpu_custom_call", output_to_operand_aliasing={{0}: (4, {}), {1}: (5, {})} | custom-call | flops 536870912 | bytes 1843200 | tf_op jit(solution)/shard_map/pallas_call | solution.py:73
  149.4 5.6 %shard_map.66 = (f32[1024,1]{1,0:T(8,128)}, f32[1024,128]{1,0:T(8,128)}) custom-call(s32[3]{0:T(128)} %pad_add_fusion.11.sc_ref, bf16[1024,128]{1,0:T(8,128)(2,1)} %bitcast.118, bf16[2,1024,128]{2,1,0:T(8,128)(2,1)} %collective-permute-done.4.k_ref.v_ref, ...), custom_call_target="tpu_custom_call", output_to_operand_aliasing={{0}: (4, {}), {1}: (5, {})} | custom-call | flops 536870912 | bytes 1843200 | tf_op jit(solution)/shard_map/pallas_call | solution.py:73
  155.0 4.4 %shard_map.67 = (f32[1024,1]{1,0:T(8,128)}, f32[1024,128]{1,0:T(8,128)}) custom-call(s32[3]{0:T(128)} %pad_add_fusion.12.sc_ref, bf16[1024,128]{1,0:T(8,128)(2,1)} %bitcast.119, bf16[2,1024,128]{2,1,0:T(8,128)(2,1)} %collective-permute-done.3.k_ref.v_ref, ...), custom_call_target="tpu_custom_call", output_to_operand_aliasing={{0}: (4, {}), {1}: (5, {})} | custom-call | flops 536870912 | bytes 1843200 | tf_op jit(solution)/shard_map/pallas_call | solution.py:73
  159.5 4.4 %shard_map.68 = (f32[1024,1]{1,0:T(8,128)}, f32[1024,128]{1,0:T(8,128)}) custom-call(s32[3]{0:T(128)} %pad_add_fusion.13.sc_ref, bf16[1024,128]{1,0:T(8,128)(2,1)} %bitcast.120, bf16[2,1024,128]{2,1,0:T(8,128)(2,1)} %collective-permute-done.2.k_ref.v_ref, ...), custom_call_target="tpu_custom_call", output_to_operand_aliasing={{0}: (4, {}), {1}: (5, {})} | custom-call | flops 536870912 | bytes 1843200 | tf_op jit(solution)/shard_map/pallas_call | solution.py:73
  163.9 4.4 %shard_map.69 = (f32[1024,1]{1,0:T(8,128)}, f32[1024,128]{1,0:T(8,128)}) custom-call(s32[3]{0:T(128)} %pad_add_fusion.14.sc_ref, bf16[1024,128]{1,0:T(8,128)(2,1)} %bitcast.121, bf16[2,1024,128]{2,1,0:T(8,128)(2,1)} %collective-permute-done.1.k_ref.v_ref, ...), custom_call_target="tpu_custom_call", output_to_operand_aliasing={{0}: (4, {}), {1}: (5, {})} | custom-call | flops 536870912 | bytes 1843200 | tf_op jit(solution)/shard_map/pallas_call | solution.py:73
  168.3 4.4 %shard_map.70 = (f32[1024,1]{1,0:T(8,128)}, f32[1024,128]{1,0:T(8,128)}) custom-call(s32[3]{0:T(128)} %pad_add_fusion.15.sc_ref, bf16[1024,128]{1,0:T(8,128)(2,1)} %bitcast.122, bf16[2,1024,128]{2,1,0:T(8,128)(2,1)} %collective-permute-done.k_ref.v_ref, ...), custom_call_target="tpu_custom_call", output_to_operand_aliasing={{0}: (4, {}), {1}: (5, {})} | custom-call | flops 536870912 | bytes 1843200 | tf_op jit(solution)/shard_map/pallas_call | solution.py:73
  177.2 3.6 %copy-done.1 = f32[8,2,32,4608]{3,2,1,0:T(8,128)} copy-done((f32[8,2,32,4608]{3,2,1,0:T(8,128)}, f32[8,2,32,4608]{3,2,1,0:T(8,128)S(1)}, u32[]{:S(2)}) %copy-start.1) | copy-done | bytes 9437208
  182.8 4.5 %collective-permute-done.15 = bf16[8,32,4608]{2,1,0:T(8,128)(2,1)} collective-permute-done((bf16[8,32,4608]{2,1,0:T(8,128)(2,1)}, bf16[8,32,4608]{2,1,0:T(8,128)(2,1)}, u32[]{:S(2)}, u32[]{:S(2)}) %collective-permute-start.15) | collective-permute-done | bytes 2359328 | tf_op jit(solution)/shard_map/ppermute | solution.py:130
  187.3 3.6 %fusion = bf16[8,32,4608]{2,1,0:T(8,128)(2,1)S(1)} fusion(bf16[8,32,4608]{2,1,0:T(8,128)(2,1)} %collective-permute-done.15, f32[8,2,32,4608]{3,2,1,0:T(8,128)} %copy-done.1, s32[]{:T(128)S(6)} %select_n.87), kind=kLoop, calls=%fused_computation.1 | loop fusion | flops 3538944 | bytes 9437188 | tf_op jit(solution)/shard_map/convert_element_type | solution.py:132
  190.9 40.4 %all_to_all.5 = bf16[8,32,4608]{2,1,0:T(8,128)(2,1)S(1)} all-to-all(bf16[8,32,4608]{2,1,0:T(8,128)(2,1)S(1)} %fusion), channel_id=1, replica_groups=mesh['pb'=8,'kx'=8,'kc'=2] {'kx'}, dimensions={0} | all-to-all | bytes 4718592 | tf_op jit(solution)/shard_map/all_to_all | solution.py:131
  (89 shorter events, 43.2 us)
Async XLA Ops:
  0.0 175.7 %copy-start = (bf16[256,4608]{1,0:T(8,128)(2,1)S(1)}, bf16[256,4608]{1,0:T(8,128)(2,1)}, u32[]{:S(2)}) copy-start(bf16[256,4608]{1,0:T(8,128)(2,1)} %param.9) | copy-start | bytes 7077892
  7.5 33.9 %collective-permute-start.14 = (bf16[2,1024,128]{2,1,0:T(8,128)(2,1)}, bf16[2,1024,128]{2,1,0:T(8,128)(2,1)}, u32[]{:S(2)}, u32[]{:S(2)}) collective-permute-start(bf16[2,1024,128]{2,1,0:T(8,128)(2,1)} %pad_maximum_fusion.14), channel_id=1, source_target_pairs={{0,1},{1,0},{2,3},{3,2},{4,5},{5,4},{6,7},{7,6},{8,9},{9,8},{10,11... | collective-permute-start | bytes 1572872 | tf_op jit(solution)/shard_map/ppermute | solution.py:112
  8.4 35.3 %collective-permute-start.5 = (bf16[2,1024,128]{2,1,0:T(8,128)(2,1)}, bf16[2,1024,128]{2,1,0:T(8,128)(2,1)}, u32[]{:S(2)}, u32[]{:S(2)}) collective-permute-start(bf16[2,1024,128]{2,1,0:T(8,128)(2,1)} %pad_maximum_fusion.5), channel_id=1, source_target_pairs={{0,10},{1,11},{2,8},{3,9},{4,14},{5,15},{6,12},{7,13},{8,2},{9,3},... | collective-permute-start | bytes 1572872 | tf_op jit(solution)/shard_map/ppermute | solution.py:112
  12.9 31.8 %collective-permute-start.6 = (bf16[2,1024,128]{2,1,0:T(8,128)(2,1)}, bf16[2,1024,128]{2,1,0:T(8,128)(2,1)}, u32[]{:S(2)}, u32[]{:S(2)}) collective-permute-start(bf16[2,1024,128]{2,1,0:T(8,128)(2,1)} %pad_maximum_fusion.6), channel_id=1, source_target_pairs={{0,9},{1,8},{2,11},{3,10},{4,13},{5,12},{6,15},{7,14},{8,1},{9,0},... | collective-permute-start | bytes 1572872 | tf_op jit(solution)/shard_map/ppermute | solution.py:112
  14.1 34.1 %collective-permute-start.7 = (bf16[2,1024,128]{2,1,0:T(8,128)(2,1)}, bf16[2,1024,128]{2,1,0:T(8,128)(2,1)}, u32[]{:S(2)}, u32[]{:S(2)}) collective-permute-start(bf16[2,1024,128]{2,1,0:T(8,128)(2,1)} %pad_maximum_fusion.7), channel_id=1, source_target_pairs={{0,8},{1,9},{2,10},{3,11},{4,12},{5,13},{6,14},{7,15},{8,0},{9,1},... | collective-permute-start | bytes 1572872 | tf_op jit(solution)/shard_map/ppermute | solution.py:112
  18.0 42.4 %collective-permute-start.8 = (bf16[2,1024,128]{2,1,0:T(8,128)(2,1)}, bf16[2,1024,128]{2,1,0:T(8,128)(2,1)}, u32[]{:S(2)}, u32[]{:S(2)}) collective-permute-start(bf16[2,1024,128]{2,1,0:T(8,128)(2,1)} %pad_maximum_fusion.8), channel_id=1, source_target_pairs={{0,7},{1,6},{2,5},{3,4},{4,3},{5,2},{6,1},{7,0},{8,15},{9,14},{10,... | collective-permute-start | bytes 1572872 | tf_op jit(solution)/shard_map/ppermute | solution.py:112
  20.5 13.9 %copy-start.10 = (bf16[1,1024,128]{2,1,0:T(8,128)(2,1)S(1)}, bf16[1,1024,128]{2,1,0:T(8,128)(2,1)}, u32[]{:S(2)}) copy-start(bf16[1,1024,128]{2,1,0:T(8,128)(2,1)} %get-tuple-element.89) | copy-start | bytes 786436
  20.6 13.9 %copy-start.11 = (bf16[1,1024,128]{2,1,0:T(8,128)(2,1)S(1)}, bf16[1,1024,128]{2,1,0:T(8,128)(2,1)}, u32[]{:S(2)}) copy-start(bf16[1,1024,128]{2,1,0:T(8,128)(2,1)} %get-tuple-element.112) | copy-start | bytes 786436
  20.6 14.8 %copy-start.8 = (bf16[1,1024,128]{2,1,0:T(8,128)(2,1)S(1)}, bf16[1,1024,128]{2,1,0:T(8,128)(2,1)}, u32[]{:S(2)}) copy-start(bf16[1,1024,128]{2,1,0:T(8,128)(2,1)} %get-tuple-element.90) | copy-start | bytes 786436
  20.6 14.8 %copy-start.9 = (bf16[1,1024,128]{2,1,0:T(8,128)(2,1)S(1)}, bf16[1,1024,128]{2,1,0:T(8,128)(2,1)}, u32[]{:S(2)}) copy-start(bf16[1,1024,128]{2,1,0:T(8,128)(2,1)} %get-tuple-element.111) | copy-start | bytes 786436
  20.6 15.6 %copy-start.6 = (bf16[1,1024,128]{2,1,0:T(8,128)(2,1)S(1)}, bf16[1,1024,128]{2,1,0:T(8,128)(2,1)}, u32[]{:S(2)}) copy-start(bf16[1,1024,128]{2,1,0:T(8,128)(2,1)} %get-tuple-element.95) | copy-start | bytes 786436
  20.6 15.6 %copy-start.7 = (bf16[1,1024,128]{2,1,0:T(8,128)(2,1)S(1)}, bf16[1,1024,128]{2,1,0:T(8,128)(2,1)}, u32[]{:S(2)}) copy-start(bf16[1,1024,128]{2,1,0:T(8,128)(2,1)} %get-tuple-element.106) | copy-start | bytes 786436
  20.6 16.4 %copy-start.4 = (bf16[1,1024,128]{2,1,0:T(8,128)(2,1)S(1)}, bf16[1,1024,128]{2,1,0:T(8,128)(2,1)}, u32[]{:S(2)}) copy-start(bf16[1,1024,128]{2,1,0:T(8,128)(2,1)} %get-tuple-element.96) | copy-start | bytes 786436
  20.6 16.4 %copy-start.5 = (bf16[1,1024,128]{2,1,0:T(8,128)(2,1)S(1)}, bf16[1,1024,128]{2,1,0:T(8,128)(2,1)}, u32[]{:S(2)}) copy-start(bf16[1,1024,128]{2,1,0:T(8,128)(2,1)} %get-tuple-element.105) | copy-start | bytes 786436
  26.8 11.1 %copy-start.2 = (bf16[1,1024,128]{2,1,0:T(8,128)(2,1)S(1)}, bf16[1,1024,128]{2,1,0:T(8,128)(2,1)}, u32[]{:S(2)}) copy-start(bf16[1,1024,128]{2,1,0:T(8,128)(2,1)} %get-tuple-element.97) | copy-start | bytes 786436
  26.8 11.1 %copy-start.3 = (bf16[1,1024,128]{2,1,0:T(8,128)(2,1)S(1)}, bf16[1,1024,128]{2,1,0:T(8,128)(2,1)}, u32[]{:S(2)}) copy-start(bf16[1,1024,128]{2,1,0:T(8,128)(2,1)} %get-tuple-element.104) | copy-start | bytes 786436
  41.5 30.9 %collective-permute-start.9 = (bf16[2,1024,128]{2,1,0:T(8,128)(2,1)}, bf16[2,1024,128]{2,1,0:T(8,128)(2,1)S(1)}, u32[]{:S(2)}, u32[]{:S(2)}) collective-permute-start(bf16[2,1024,128]{2,1,0:T(8,128)(2,1)} %pad_maximum_fusion.9), channel_id=1, source_target_pairs={{0,6},{1,7},{2,4},{3,5},{4,2},{5,3},{6,0},{7,1},{8,14},{9,15},{10,... | collective-permute-start | bytes 1572872 | tf_op jit(solution)/shard_map/ppermute | solution.py:112
  43.7 37.4 %collective-permute-start.10 = (bf16[2,1024,128]{2,1,0:T(8,128)(2,1)}, bf16[2,1024,128]{2,1,0:T(8,128)(2,1)}, u32[]{:S(2)}, u32[]{:S(2)}) collective-permute-start(bf16[2,1024,128]{2,1,0:T(8,128)(2,1)} %pad_maximum_fusion.10), channel_id=1, source_target_pairs={{0,5},{1,4},{2,7},{3,6},{4,1},{5,0},{6,3},{7,2},{8,13},{9,12},{10,... | collective-permute-start | bytes 1572872 | tf_op jit(solution)/shard_map/ppermute | solution.py:112
  44.7 55.4 %collective-permute-start.12 = (bf16[2,1024,128]{2,1,0:T(8,128)(2,1)}, bf16[2,1024,128]{2,1,0:T(8,128)(2,1)}, u32[]{:S(2)}, u32[]{:S(2)}) collective-permute-start(bf16[2,1024,128]{2,1,0:T(8,128)(2,1)} %pad_maximum_fusion.12), channel_id=1, source_target_pairs={{0,3},{1,2},{2,1},{3,0},{4,7},{5,6},{6,5},{7,4},{8,11},{9,10},{10,... | collective-permute-start | bytes 1572872 | tf_op jit(solution)/shard_map/ppermute | solution.py:112
  48.1 46.3 %collective-permute-start.13 = (bf16[2,1024,128]{2,1,0:T(8,128)(2,1)}, bf16[2,1024,128]{2,1,0:T(8,128)(2,1)}, u32[]{:S(2)}, u32[]{:S(2)}) collective-permute-start(bf16[2,1024,128]{2,1,0:T(8,128)(2,1)} %pad_maximum_fusion.13), channel_id=1, source_target_pairs={{0,2},{1,3},{2,0},{3,1},{4,6},{5,7},{6,4},{7,5},{8,10},{9,11},{10,... | collective-permute-start | bytes 1572872 | tf_op jit(solution)/shard_map/ppermute | solution.py:112
  60.4 48.2 %collective-permute-start.11 = (bf16[2,1024,128]{2,1,0:T(8,128)(2,1)}, bf16[2,1024,128]{2,1,0:T(8,128)(2,1)}, u32[]{:S(2)}, u32[]{:S(2)}) collective-permute-start(bf16[2,1024,128]{2,1,0:T(8,128)(2,1)} %pad_maximum_fusion.11), channel_id=1, source_target_pairs={{0,4},{1,5},{2,6},{3,7},{4,0},{5,1},{6,2},{7,3},{8,12},{9,13},{10,... | collective-permute-start | bytes 1572872 | tf_op jit(solution)/shard_map/ppermute | solution.py:112
  72.4 1.5 copy-start.13
  72.4 77.1 %collective-permute-start.4 = (bf16[2,1024,128]{2,1,0:T(8,128)(2,1)}, bf16[2,1024,128]{2,1,0:T(8,128)(2,1)}, u32[]{:S(2)}, u32[]{:S(2)}) collective-permute-start(bf16[2,1024,128]{2,1,0:T(8,128)(2,1)} %pad_maximum_fusion.4), channel_id=1, source_target_pairs={{0,11},{1,10},{2,9},{3,8},{4,15},{5,14},{6,13},{7,12},{8,3},{9,2},... | collective-permute-start | bytes 1572872 | tf_op jit(solution)/shard_map/ppermute | solution.py:112
  74.7 19.8 %copy-start.12 = (bf16[2,1024,128]{2,1,0:T(8,128)(2,1)S(1)}, bf16[2,1024,128]{2,1,0:T(8,128)(2,1)}, u32[]{:S(2)}) copy-start(bf16[2,1024,128]{2,1,0:T(8,128)(2,1)} %pad_maximum_fusion.2) | copy-start | bytes 1572868
  81.1 73.9 %collective-permute-start.3 = (bf16[2,1024,128]{2,1,0:T(8,128)(2,1)}, bf16[2,1024,128]{2,1,0:T(8,128)(2,1)}, u32[]{:S(2)}, u32[]{:S(2)}) collective-permute-start(bf16[2,1024,128]{2,1,0:T(8,128)(2,1)} %pad_maximum_fusion.3), channel_id=1, source_target_pairs={{0,12},{1,13},{2,14},{3,15},{4,8},{5,9},{6,10},{7,11},{8,4},{9,5},... | collective-permute-start | bytes 1572872 | tf_op jit(solution)/shard_map/ppermute | solution.py:112
  94.5 65.0 %collective-permute-start.2 = (bf16[2,1024,128]{2,1,0:T(8,128)(2,1)S(1)}, bf16[2,1024,128]{2,1,0:T(8,128)(2,1)}, u32[]{:S(2)}, u32[]{:S(2)}) collective-permute-start(bf16[2,1024,128]{2,1,0:T(8,128)(2,1)S(1)} %copy-done.12), channel_id=1, source_target_pairs={{0,13},{1,12},{2,15},{3,14},{4,9},{5,8},{6,11},{7,10},{8,5},{9,4},... | collective-permute-start | bytes 1572872 | tf_op jit(solution)/shard_map/ppermute | solution.py:112
  100.1 63.8 %collective-permute-start.1 = (bf16[2,1024,128]{2,1,0:T(8,128)(2,1)}, bf16[2,1024,128]{2,1,0:T(8,128)(2,1)}, u32[]{:S(2)}, u32[]{:S(2)}) collective-permute-start(bf16[2,1024,128]{2,1,0:T(8,128)(2,1)} %pad_maximum_fusion.1), channel_id=1, source_target_pairs={{0,14},{1,15},{2,12},{3,13},{4,10},{5,11},{6,8},{7,9},{8,6},{9,7},... | collective-permute-start | bytes 1572872 | tf_op jit(solution)/shard_map/ppermute | solution.py:112
  108.6 59.8 %collective-permute-start = (bf16[2,1024,128]{2,1,0:T(8,128)(2,1)S(1)}, bf16[2,1024,128]{2,1,0:T(8,128)(2,1)}, u32[]{:S(2)}, u32[]{:S(2)}) collective-permute-start(bf16[2,1024,128]{2,1,0:T(8,128)(2,1)S(1)} %pad_maximum_fusion), channel_id=1, source_target_pairs={{0,15},{1,14},{2,13},{3,12},{4,11},{5,10},{6,9},{7,8},{8,7},{9,6},... | collective-permute-start | bytes 1572872 | tf_op jit(solution)/shard_map/ppermute | solution.py:112
  177.1 3.6 %copy-start.1 = (f32[8,2,32,4608]{3,2,1,0:T(8,128)}, f32[8,2,32,4608]{3,2,1,0:T(8,128)S(1)}, u32[]{:S(2)}) copy-start(f32[8,2,32,4608]{3,2,1,0:T(8,128)S(1)} %fusion.2) | copy-start | bytes 28311556
  182.5 4.9 %collective-permute-start.15 = (bf16[8,32,4608]{2,1,0:T(8,128)(2,1)}, bf16[8,32,4608]{2,1,0:T(8,128)(2,1)}, u32[]{:S(2)}, u32[]{:S(2)}) collective-permute-start(bf16[8,32,4608]{2,1,0:T(8,128)(2,1)} %fusion.1), channel_id=1, source_target_pairs={{0,1},{1,0},{2,3},{3,2},{4,5},{5,4},{6,7},{7,6},{8,9},{9,8},{10,11... | collective-permute-start | bytes 7077896 | tf_op jit(solution)/shard_map/ppermute | solution.py:130

commit v8 on v7

--- a/solution.py
+++ b/solution.py
@@ -128,10 +128,9 @@
     mine = lax.dynamic_index_in_dim(partial, core, 1, keepdims=False)
     theirs = lax.dynamic_index_in_dim(partial, 1 - core, 1, keepdims=False).astype(jnp.bfloat16)
     on_chip = mine + lax.ppermute(theirs, "kc", [(0, 1), (1, 0)]).astype(jnp.float32)
-    parts = lax.all_to_all(
-        on_chip.astype(jnp.bfloat16), "kx", split_axis=0, concat_axis=0, tiled=True
-    )
-    return jnp.sum(parts.astype(jnp.float32), axis=0)
+    return lax.psum_scatter(
+        on_chip.astype(jnp.bfloat16), "kx", scatter_dimension=0, tiled=True
+    ).reshape(on_chip.shape[1:]).astype(jnp.float32)
 
 
 def solution(mesh):

time: 234 us -> 286 us (1.22); the launches traced: 233 us -> 281 us
  waiting for transfers between devices: 30.2 us -> 112 us
  blocking collectives: 40.4 us -> 0 us
  between operations: 0.84 us -> 14.2 us
  Pallas kernels: 85 us -> 76.8 us
    reduce_scatter x0 -> x1, waiting for transfers between devices: none -> 81.8 us  [per_device(): lax.psum_scatter(on_chip.astype(jnp.bfloat16), 'kx', scatter_dimension=0,...]
    all_to_all x1 -> x0, blocking collectives: 40.4 us -> none  [per_device(): lax.all_to_all(on_chip.astype(jnp.bfloat16), 'kx', split_axis=0, concat_a...]
    pallas_call x16, Pallas kernels: 85 us -> 76.8 us  [attend_kernel(): pl.pallas_call(block_kernel, grid_spec=grid_spec, out_shape=(jax.ShapeDty...]
  transfers between devices with their start and end apart: 16 -> 17, of which waited for: 5 -> 6; matrix products, arithmetic and copies ran while one was open for 13% -> 10% of each run, Pallas kernels for 35% -> 26%
where the time goes in v8:
time: 286 us; the launch traced here: 281 us
  waiting for transfers between devices  112 us (39%)
  Pallas kernels  76.8 us (27%)
  other arithmetic  36.3 us (13%)
  starting transfers between devices  24.8 us (9%)
  local copies, waits for them, and re-layouts  15.8 us (6%)
  between operations  14.2 us (5%)
    reduce_scatter x1, waiting for transfers between devices, per_device(): lax.psum_scatter(on_chip.astype(jnp.bfloat16), 'kx', scatter_dimension=0,...  81.8 us
    pallas_call x16, Pallas kernels, attend_kernel(): pl.pallas_call(block_kernel, grid_spec=grid_spec, out_shape=(jax.ShapeDty...  76.8 us
    ppermute x15, waiting for transfers between devices, by_heads(): block = lax.ppermute(block, KV, [(j, j ^ shift) for j in range(n_kv)])  25.5 us
    ppermute x15, starting transfers between devices, by_heads(): block = lax.ppermute(block, KV, [(j, j ^ shift) for j in range(n_kv)])  24.4 us
    another operation x16, other arithmetic, by_heads(): jnp.stack((lax.dynamic_slice_in_dim(keys, dest * kv_feat, kv_feat, 1), la...  17.1 us
    another operation x16, other arithmetic, by_heads(): jnp.stack([row_first, src * key_dev, jnp.int32(rows_dev)]).astype(jnp.int32)  9.91 us
    another operation x1, local copies, waits for them, and re-layouts, by_heads(): jnp.stack((lax.dynamic_slice_in_dim(keys, dest * kv_feat, kv_feat, 1), la...  6.67 us
  transfers between devices with their start and end apart: 17, of which 6 were waited for; matrix products, arithmetic and copies ran while one was open for 10% of the time, Pallas kernels for 26%

profile of v8, /device:TPU:120, one launch (start us, length us, event | category | flops | bytes accessed | tf_op | source)
XLA Modules:
  0.0 281.1 jit_solution(10222980102889809705)
XLA Ops:
  6.5 6.7 %dynamic-slice_bitcast_fusion = (bf16[1,1024,128]{2,1,0:T(8,128)(2,1)}, bf16[1,1024,128]{2,1,0:T(8,128)(2,1)}, bf16[1,1024,128]{2,1,0:T(8,128)(2,1)}, bf16[1,102...) fusion(bf16[1024,2048]{1,0:T(8,128)(2,1)} %param.8, ...), kind=kLoop, calls=%fused_computation.25 | loop fusion | bytes 16777280 | tf_op jit(solution)/shard_map/stack | solution.py:104
  14.9 3.7 %collective-permute-start.5 = (bf16[2,1024,128]{2,1,0:T(8,128)(2,1)}, bf16[2,1024,128]{2,1,0:T(8,128)(2,1)}, u32[]{:S(2)}, u32[]{:S(2)}) collective-permute-start(bf16[2,1024,128]{2,1,0:T(8,128)(2,1)} %pad_maximum_fusion.5), channel_id=1, source_target_pairs={{0,10},{1,11},{2,8},{3,9},{4,14},{5,15},{6,12},{7,13},{8,2},{9,3},... | collective-permute-start | bytes 1572872 | tf_op jit(solution)/shard_map/ppermute | solution.py:112
  20.6 3.0 %collective-permute-start.7 = (bf16[2,1024,128]{2,1,0:T(8,128)(2,1)}, bf16[2,1024,128]{2,1,0:T(8,128)(2,1)}, u32[]{:S(2)}, u32[]{:S(2)}) collective-permute-start(bf16[2,1024,128]{2,1,0:T(8,128)(2,1)} %pad_maximum_fusion.7), channel_id=1, source_target_pairs={{0,8},{1,9},{2,10},{3,11},{4,12},{5,13},{6,14},{7,15},{8,0},{9,1},... | collective-permute-start | bytes 1572872 | tf_op jit(solution)/shard_map/ppermute | solution.py:112
  24.5 1.9 collective-permute-start.8
  33.5 2.0 pad_maximum_fusion.15.k_ref.v_ref
  48.2 2.2 collective-permute-start.9
  51.3 2.2 collective-permute-start.12
  54.7 2.3 collective-permute-start.13
  57.6 9.3 %collective-permute-done.8.k_ref.v_ref = bf16[2,1024,128]{2,1,0:T(8,128)(2,1)} collective-permute-done((bf16[2,1024,128]{2,1,0:T(8,128)(2,1)}, bf16[2,1024,128]{2,1,0:T(8,128)(2,1)}, u32[]{:S(2)}, u32[]{:S(2)}) %collective-permute-start.8) | collective-permute-done | bytes 524320 | tf_op jit(solution)/shard_map/ppermute | solution.py:112
  70.6 8.3 %collective-permute-done.9.k_ref.v_ref = bf16[2,1024,128]{2,1,0:T(8,128)(2,1)S(1)} collective-permute-done((bf16[2,1024,128]{2,1,0:T(8,128)(2,1)}, bf16[2,1024,128]{2,1,0:T(8,128)(2,1)S(1)}, u32[]{:S(2)}, u32[]{:S(2)}) %collective-permute-start.9) | collective-permute-done | bytes 524320 | tf_op jit(solution)/shard_map/ppermute | solution.py:112
  82.0 5.6 %shard_map.55 = (f32[1024,1]{1,0:T(8,128)}, f32[1024,128]{1,0:T(8,128)}) custom-call(s32[3]{0:T(128)} %pad_add_fusion.sc_ref, bf16[1024,128]{1,0:T(8,128)(2,1)} %bitcast.110, bf16[2,1024,128]{2,1,0:T(8,128)(2,1)} %pad_maximum_fusion.15.k_ref.v_ref, ...), custom_call_target="tpu_custom_call", output_to_operand_aliasing={{0}: (4, {}), {1}: (5, {})} | custom-call | flops 536870912 | bytes 1843200 | tf_op jit(solution)/shard_map/pallas_call | solution.py:73
  88.7 5.7 %shard_map.56 = (f32[1024,1]{1,0:T(8,128)}, f32[1024,128]{1,0:T(8,128)}) custom-call(s32[3]{0:T(128)} %pad_add_fusion.1.sc_ref, bf16[1024,128]{1,0:T(8,128)(2,1)} %bitcast.111, bf16[2,1024,128]{2,1,0:T(8,128)(2,1)} %collective-permute-done.14.k_ref.v_ref, ...), custom_call_target="tpu_custom_call", output_to_operand_aliasing={{0}: (4, {}), {1}: (5, {})} | custom-call | flops 536870912 | bytes 1843200 | tf_op jit(solution)/shard_map/pallas_call | solution.py:73
  94.3 6.8 %collective-permute-done.13.k_ref.v_ref = bf16[2,1024,128]{2,1,0:T(8,128)(2,1)} collective-permute-done((bf16[2,1024,128]{2,1,0:T(8,128)(2,1)}, bf16[2,1024,128]{2,1,0:T(8,128)(2,1)}, u32[]{:S(2)}, u32[]{:S(2)}) %collective-permute-start.13) | collective-permute-done | bytes 524320 | tf_op jit(solution)/shard_map/ppermute | solution.py:112
  101.1 5.6 %shard_map.57 = (f32[1024,1]{1,0:T(8,128)}, f32[1024,128]{1,0:T(8,128)}) custom-call(s32[3]{0:T(128)} %pad_add_fusion.2.sc_ref, bf16[1024,128]{1,0:T(8,128)(2,1)} %bitcast.112, bf16[2,1024,128]{2,1,0:T(8,128)(2,1)} %collective-permute-done.13.k_ref.v_ref, ...), custom_call_target="tpu_custom_call", output_to_operand_aliasing={{0}: (4, {}), {1}: (5, {})} | custom-call | flops 536870912 | bytes 1843200 | tf_op jit(solution)/shard_map/pallas_call | solution.py:73
  106.7 2.8 %collective-permute-start.1 = (bf16[2,1024,128]{2,1,0:T(8,128)(2,1)}, bf16[2,1024,128]{2,1,0:T(8,128)(2,1)}, u32[]{:S(2)}, u32[]{:S(2)}) collective-permute-start(bf16[2,1024,128]{2,1,0:T(8,128)(2,1)} %pad_maximum_fusion.1), channel_id=1, source_target_pairs={{0,14},{1,15},{2,12},{3,13},{4,10},{5,11},{6,8},{7,9},{8,6},{9,7},... | collective-permute-start | bytes 1572872 | tf_op jit(solution)/shard_map/ppermute | solution.py:112
  109.5 5.6 %shard_map.58 = (f32[1024,1]{1,0:T(8,128)}, f32[1024,128]{1,0:T(8,128)}) custom-call(s32[3]{0:T(128)} %pad_add_fusion.3.sc_ref, bf16[1024,128]{1,0:T(8,128)(2,1)} %bitcast.113, bf16[2,1024,128]{2,1,0:T(8,128)(2,1)} %collective-permute-done.12.k_ref.v_ref, ...), custom_call_target="tpu_custom_call", output_to_operand_aliasing={{0}: (4, {}), {1}: (5, {})} | custom-call | flops 536870912 | bytes 1843200 | tf_op jit(solution)/shard_map/pallas_call | solution.py:73
  116.7 4.6 %shard_map.59 = (f32[1024,1]{1,0:T(8,128)}, f32[1024,128]{1,0:T(8,128)}) custom-call(s32[3]{0:T(128)} %pad_add_fusion.4.sc_ref, bf16[1024,128]{1,0:T(8,128)(2,1)} %bitcast.114, bf16[2,1024,128]{2,1,0:T(8,128)(2,1)} %collective-permute-done.11.k_ref.v_ref, ...), custom_call_target="tpu_custom_call", output_to_operand_aliasing={{0}: (4, {}), {1}: (5, {})} | custom-call | flops 536870912 | bytes 1843200 | tf_op jit(solution)/shard_map/pallas_call | solution.py:73
  121.3 4.5 %shard_map.60 = (f32[1024,1]{1,0:T(8,128)}, f32[1024,128]{1,0:T(8,128)}) custom-call(s32[3]{0:T(128)} %pad_add_fusion.5.sc_ref, bf16[1024,128]{1,0:T(8,128)(2,1)} %bitcast.115, bf16[2,1024,128]{2,1,0:T(8,128)(2,1)} %collective-permute-done.10.k_ref.v_ref, ...), custom_call_target="tpu_custom_call", output_to_operand_aliasing={{0}: (4, {}), {1}: (5, {})} | custom-call | flops 536870912 | bytes 1843200 | tf_op jit(solution)/shard_map/pallas_call | solution.py:73
  125.8 5.1 %shard_map.61 = (f32[1024,1]{1,0:T(8,128)}, f32[1024,128]{1,0:T(8,128)}) custom-call(s32[3]{0:T(128)} %pad_add_fusion.6.sc_ref, bf16[1024,128]{1,0:T(8,128)(2,1)} %bitcast.116, bf16[2,1024,128]{2,1,0:T(8,128)(2,1)} %copy-done.13, bf16[2,1024,128]{2,1,0:T(8,128)(2,1)} %copy-done.13, ...), custom_call_target="tpu_custom_call", output_to_operand_aliasing={{0}: (4, {}), {1}: (5, {})} | custom-call | flops 536870912 | bytes 1843200 | tf_op jit(solution)/shard_map/pallas_call | solution.py:73
  130.9 4.5 %shard_map.62 = (f32[1024,1]{1,0:T(8,128)}, f32[1024,128]{1,0:T(8,128)}) custom-call(s32[3]{0:T(128)} %pad_add_fusion.7.sc_ref, bf16[1024,128]{1,0:T(8,128)(2,1)} %bitcast.117, bf16[2,1024,128]{2,1,0:T(8,128)(2,1)} %collective-permute-done.8.k_ref.v_ref, ...), custom_call_target="tpu_custom_call", output_to_operand_aliasing={{0}: (4, {}), {1}: (5, {})} | custom-call | flops 536870912 | bytes 1843200 | tf_op jit(solution)/shard_map/pallas_call | solution.py:73
  135.3 4.5 %shard_map.63 = (f32[1024,1]{1,0:T(8,128)}, f32[1024,128]{1,0:T(8,128)}) custom-call(s32[3]{0:T(128)} %pad_add_fusion.8.sc_ref, bf16[1024,128]{1,0:T(8,128)(2,1)} %bitcast.118, bf16[2,1024,128]{2,1,0:T(8,128)(2,1)} %collective-permute-done.7.k_ref.v_ref, ...), custom_call_target="tpu_custom_call", output_to_operand_aliasing={{0}: (4, {}), {1}: (5, {})} | custom-call | flops 536870912 | bytes 1843200 | tf_op jit(solution)/shard_map/pallas_call | solution.py:73
  139.8 4.5 %shard_map.64 = (f32[1024,1]{1,0:T(8,128)}, f32[1024,128]{1,0:T(8,128)}) custom-call(s32[3]{0:T(128)} %pad_add_fusion.9.sc_ref, bf16[1024,128]{1,0:T(8,128)(2,1)} %bitcast.119, bf16[2,1024,128]{2,1,0:T(8,128)(2,1)} %collective-permute-done.6.k_ref.v_ref, ...), custom_call_target="tpu_custom_call", output_to_operand_aliasing={{0}: (4, {}), {1}: (5, {})} | custom-call | flops 536870912 | bytes 1843200 | tf_op jit(solution)/shard_map/pallas_call | solution.py:73
  144.3 4.5 %shard_map.65 = (f32[1024,1]{1,0:T(8,128)}, f32[1024,128]{1,0:T(8,128)}) custom-call(s32[3]{0:T(128)} %pad_add_fusion.10.sc_ref, bf16[1024,128]{1,0:T(8,128)(2,1)} %bitcast.120, bf16[2,1024,128]{2,1,0:T(8,128)(2,1)} %collective-permute-done.5.k_ref.v_ref, ...), custom_call_target="tpu_custom_call", output_to_operand_aliasing={{0}: (4, {}), {1}: (5, {})} | custom-call | flops 536870912 | bytes 1843200 | tf_op jit(solution)/shard_map/pallas_call | solution.py:73
  148.7 4.5 %shard_map.66 = (f32[1024,1]{1,0:T(8,128)}, f32[1024,128]{1,0:T(8,128)}) custom-call(s32[3]{0:T(128)} %pad_add_fusion.11.sc_ref, bf16[1024,128]{1,0:T(8,128)(2,1)} %bitcast.121, bf16[2,1024,128]{2,1,0:T(8,128)(2,1)} %collective-permute-done.4.k_ref.v_ref, ...), custom_call_target="tpu_custom_call", output_to_operand_aliasing={{0}: (4, {}), {1}: (5, {})} | custom-call | flops 536870912 | bytes 1843200 | tf_op jit(solution)/shard_map/pallas_call | solution.py:73
  153.2 4.5 %shard_map.67 = (f32[1024,1]{1,0:T(8,128)}, f32[1024,128]{1,0:T(8,128)}) custom-call(s32[3]{0:T(128)} %pad_add_fusion.12.sc_ref, bf16[1024,128]{1,0:T(8,128)(2,1)} %bitcast.122, bf16[2,1024,128]{2,1,0:T(8,128)(2,1)} %collective-permute-done.3.k_ref.v_ref, ...), custom_call_target="tpu_custom_call", output_to_operand_aliasing={{0}: (4, {}), {1}: (5, {})} | custom-call | flops 536870912 | bytes 1843200 | tf_op jit(solution)/shard_map/pallas_call | solution.py:73
  157.6 4.5 %shard_map.68 = (f32[1024,1]{1,0:T(8,128)}, f32[1024,128]{1,0:T(8,128)}) custom-call(s32[3]{0:T(128)} %pad_add_fusion.13.sc_ref, bf16[1024,128]{1,0:T(8,128)(2,1)} %bitcast.123, bf16[2,1024,128]{2,1,0:T(8,128)(2,1)} %collective-permute-done.2.k_ref.v_ref, ...), custom_call_target="tpu_custom_call", output_to_operand_aliasing={{0}: (4, {}), {1}: (5, {})} | custom-call | flops 536870912 | bytes 1843200 | tf_op jit(solution)/shard_map/pallas_call | solution.py:73
  162.1 4.5 %shard_map.69 = (f32[1024,1]{1,0:T(8,128)}, f32[1024,128]{1,0:T(8,128)}) custom-call(s32[3]{0:T(128)} %pad_add_fusion.14.sc_ref, bf16[1024,128]{1,0:T(8,128)(2,1)} %bitcast.124, bf16[2,1024,128]{2,1,0:T(8,128)(2,1)} %collective-permute-done.1.k_ref.v_ref, ...), custom_call_target="tpu_custom_call", output_to_operand_aliasing={{0}: (4, {}), {1}: (5, {})} | custom-call | flops 536870912 | bytes 1843200 | tf_op jit(solution)/shard_map/pallas_call | solution.py:73
  166.6 4.5 %shard_map.70 = (f32[1024,1]{1,0:T(8,128)}, f32[1024,128]{1,0:T(8,128)}) custom-call(s32[3]{0:T(128)} %pad_add_fusion.15.sc_ref, bf16[1024,128]{1,0:T(8,128)(2,1)} %bitcast.125, bf16[2,1024,128]{2,1,0:T(8,128)(2,1)} %collective-permute-done.k_ref.v_ref, ...), custom_call_target="tpu_custom_call", output_to_operand_aliasing={{0}: (4, {}), {1}: (5, {})} | custom-call | flops 536870912 | bytes 1843200 | tf_op jit(solution)/shard_map/pallas_call | solution.py:73
  175.4 3.6 %copy-done.1 = f32[8,2,32,4608]{3,2,1,0:T(8,128)} copy-done((f32[8,2,32,4608]{3,2,1,0:T(8,128)}, f32[8,2,32,4608]{3,2,1,0:T(8,128)S(1)}, u32[]{:S(2)}) %copy-start.1) | copy-done | bytes 9437208
  181.1 4.5 %collective-permute-done.15 = bf16[8,32,4608]{2,1,0:T(8,128)(2,1)} collective-permute-done((bf16[8,32,4608]{2,1,0:T(8,128)(2,1)}, bf16[8,32,4608]{2,1,0:T(8,128)(2,1)}, u32[]{:S(2)}, u32[]{:S(2)}) %collective-permute-start.15) | collective-permute-done | bytes 2359328 | tf_op jit(solution)/shard_map/ppermute | solution.py:130
  185.6 5.0 %fusion = bf16[8,32,4608]{2,1,0:T(8,128)(2,1)} fusion(bf16[8,32,4608]{2,1,0:T(8,128)(2,1)} %collective-permute-done.15, f32[8,2,32,4608]{3,2,1,0:T(8,128)} %copy-done.1, s32[]{:T(128)S(6)} %select_n.87), kind=kLoop, calls=%fused_computation.1 | loop fusion | flops 3538944 | bytes 9437188 | tf_op jit(solution)/shard_map/convert_element_type | solution.py:132
  190.6 81.8 %reduce-scatter.2.cloned.1.call-done = bf16[1,32,4608]{2,1,0:T(8,128)(2,1)} async-done(((bf16[8,32,4608]{2,1,0:T(8,128)(2,1)}), bf16[1,32,4608]{2,1,0:T(8,128)(2,1)}) %reduce-scatter.2.cloned.1.call-update) | async-done | bytes 294928 | tf_op jit(solution)/shard_map/reduce_scatter | solution.py:131
  (91 shorter events, 44.1 us)
Async XLA Ops:
  6.5 167.5 %copy-start = (bf16[256,4608]{1,0:T(8,128)(2,1)S(1)}, bf16[256,4608]{1,0:T(8,128)(2,1)}, u32[]{:S(2)}) copy-start(bf16[256,4608]{1,0:T(8,128)(2,1)} %param.9) | copy-start | bytes 7077892
  6.5 265.9 %reduce-scatter.2.cloned.1.call-start = ((), (), s32[]{:S(2)}) async-start(), calls=%async_computation.1 | async-start | bytes 2654208 | tf_op jit(solution)/shard_map/reduce_scatter | solution.py:131
  14.1 34.1 %collective-permute-start.14 = (bf16[2,1024,128]{2,1,0:T(8,128)(2,1)}, bf16[2,1024,128]{2,1,0:T(8,128)(2,1)}, u32[]{:S(2)}, u32[]{:S(2)}) collective-permute-start(bf16[2,1024,128]{2,1,0:T(8,128)(2,1)} %pad_maximum_fusion.14), channel_id=1, source_target_pairs={{0,1},{1,0},{2,3},{3,2},{4,5},{5,4},{6,7},{7,6},{8,9},{9,8},{10,11... | collective-permute-start | bytes 1572872 | tf_op jit(solution)/shard_map/ppermute | solution.py:112
  14.9 35.4 %collective-permute-start.5 = (bf16[2,1024,128]{2,1,0:T(8,128)(2,1)}, bf16[2,1024,128]{2,1,0:T(8,128)(2,1)}, u32[]{:S(2)}, u32[]{:S(2)}) collective-permute-start(bf16[2,1024,128]{2,1,0:T(8,128)(2,1)} %pad_maximum_fusion.5), channel_id=1, source_target_pairs={{0,10},{1,11},{2,8},{3,9},{4,14},{5,15},{6,12},{7,13},{8,2},{9,3},... | collective-permute-start | bytes 1572872 | tf_op jit(solution)/shard_map/ppermute | solution.py:112
  19.4 31.9 %collective-permute-start.6 = (bf16[2,1024,128]{2,1,0:T(8,128)(2,1)}, bf16[2,1024,128]{2,1,0:T(8,128)(2,1)}, u32[]{:S(2)}, u32[]{:S(2)}) collective-permute-start(bf16[2,1024,128]{2,1,0:T(8,128)(2,1)} %pad_maximum_fusion.6), channel_id=1, source_target_pairs={{0,9},{1,8},{2,11},{3,10},{4,13},{5,12},{6,15},{7,14},{8,1},{9,0},... | collective-permute-start | bytes 1572872 | tf_op jit(solution)/shard_map/ppermute | solution.py:112
  20.6 34.0 %collective-permute-start.7 = (bf16[2,1024,128]{2,1,0:T(8,128)(2,1)}, bf16[2,1024,128]{2,1,0:T(8,128)(2,1)}, u32[]{:S(2)}, u32[]{:S(2)}) collective-permute-start(bf16[2,1024,128]{2,1,0:T(8,128)(2,1)} %pad_maximum_fusion.7), channel_id=1, source_target_pairs={{0,8},{1,9},{2,10},{3,11},{4,12},{5,13},{6,14},{7,15},{8,0},{9,1},... | collective-permute-start | bytes 1572872 | tf_op jit(solution)/shard_map/ppermute | solution.py:112
  24.5 42.4 %collective-permute-start.8 = (bf16[2,1024,128]{2,1,0:T(8,128)(2,1)}, bf16[2,1024,128]{2,1,0:T(8,128)(2,1)}, u32[]{:S(2)}, u32[]{:S(2)}) collective-permute-start(bf16[2,1024,128]{2,1,0:T(8,128)(2,1)} %pad_maximum_fusion.8), channel_id=1, source_target_pairs={{0,7},{1,6},{2,5},{3,4},{4,3},{5,2},{6,1},{7,0},{8,15},{9,14},{10,... | collective-permute-start | bytes 1572872 | tf_op jit(solution)/shard_map/ppermute | solution.py:112
  27.1 14.1 %copy-start.10 = (bf16[1,1024,128]{2,1,0:T(8,128)(2,1)S(1)}, bf16[1,1024,128]{2,1,0:T(8,128)(2,1)}, u32[]{:S(2)}) copy-start(bf16[1,1024,128]{2,1,0:T(8,128)(2,1)} %get-tuple-element.89) | copy-start | bytes 786436
  27.1 14.1 %copy-start.11 = (bf16[1,1024,128]{2,1,0:T(8,128)(2,1)S(1)}, bf16[1,1024,128]{2,1,0:T(8,128)(2,1)}, u32[]{:S(2)}) copy-start(bf16[1,1024,128]{2,1,0:T(8,128)(2,1)} %get-tuple-element.112) | copy-start | bytes 786436
  27.1 14.9 %copy-start.8 = (bf16[1,1024,128]{2,1,0:T(8,128)(2,1)S(1)}, bf16[1,1024,128]{2,1,0:T(8,128)(2,1)}, u32[]{:S(2)}) copy-start(bf16[1,1024,128]{2,1,0:T(8,128)(2,1)} %get-tuple-element.90) | copy-start | bytes 786436
  27.1 14.9 %copy-start.9 = (bf16[1,1024,128]{2,1,0:T(8,128)(2,1)S(1)}, bf16[1,1024,128]{2,1,0:T(8,128)(2,1)}, u32[]{:S(2)}) copy-start(bf16[1,1024,128]{2,1,0:T(8,128)(2,1)} %get-tuple-element.111) | copy-start | bytes 786436
  27.1 15.8 %copy-start.6 = (bf16[1,1024,128]{2,1,0:T(8,128)(2,1)S(1)}, bf16[1,1024,128]{2,1,0:T(8,128)(2,1)}, u32[]{:S(2)}) copy-start(bf16[1,1024,128]{2,1,0:T(8,128)(2,1)} %get-tuple-element.95) | copy-start | bytes 786436
  27.1 15.8 %copy-start.7 = (bf16[1,1024,128]{2,1,0:T(8,128)(2,1)S(1)}, bf16[1,1024,128]{2,1,0:T(8,128)(2,1)}, u32[]{:S(2)}) copy-start(bf16[1,1024,128]{2,1,0:T(8,128)(2,1)} %get-tuple-element.106) | copy-start | bytes 786436
  27.1 16.6 %copy-start.4 = (bf16[1,1024,128]{2,1,0:T(8,128)(2,1)S(1)}, bf16[1,1024,128]{2,1,0:T(8,128)(2,1)}, u32[]{:S(2)}) copy-start(bf16[1,1024,128]{2,1,0:T(8,128)(2,1)} %get-tuple-element.96) | copy-start | bytes 786436
  27.1 16.6 %copy-start.5 = (bf16[1,1024,128]{2,1,0:T(8,128)(2,1)S(1)}, bf16[1,1024,128]{2,1,0:T(8,128)(2,1)}, u32[]{:S(2)}) copy-start(bf16[1,1024,128]{2,1,0:T(8,128)(2,1)} %get-tuple-element.105) | copy-start | bytes 786436
  33.5 11.1 %copy-start.2 = (bf16[1,1024,128]{2,1,0:T(8,128)(2,1)S(1)}, bf16[1,1024,128]{2,1,0:T(8,128)(2,1)}, u32[]{:S(2)}) copy-start(bf16[1,1024,128]{2,1,0:T(8,128)(2,1)} %get-tuple-element.97) | copy-start | bytes 786436
  33.5 11.1 %copy-start.3 = (bf16[1,1024,128]{2,1,0:T(8,128)(2,1)S(1)}, bf16[1,1024,128]{2,1,0:T(8,128)(2,1)}, u32[]{:S(2)}) copy-start(bf16[1,1024,128]{2,1,0:T(8,128)(2,1)} %get-tuple-element.104) | copy-start | bytes 786436
  48.2 30.7 %collective-permute-start.9 = (bf16[2,1024,128]{2,1,0:T(8,128)(2,1)}, bf16[2,1024,128]{2,1,0:T(8,128)(2,1)S(1)}, u32[]{:S(2)}, u32[]{:S(2)}) collective-permute-start(bf16[2,1024,128]{2,1,0:T(8,128)(2,1)} %pad_maximum_fusion.9), channel_id=1, source_target_pairs={{0,6},{1,7},{2,4},{3,5},{4,2},{5,3},{6,0},{7,1},{8,14},{9,15},{10,... | collective-permute-start | bytes 1572872 | tf_op jit(solution)/shard_map/ppermute | solution.py:112
  50.3 37.3 %collective-permute-start.10 = (bf16[2,1024,128]{2,1,0:T(8,128)(2,1)}, bf16[2,1024,128]{2,1,0:T(8,128)(2,1)}, u32[]{:S(2)}, u32[]{:S(2)}) collective-permute-start(bf16[2,1024,128]{2,1,0:T(8,128)(2,1)} %pad_maximum_fusion.10), channel_id=1, source_target_pairs={{0,5},{1,4},{2,7},{3,6},{4,1},{5,0},{6,3},{7,2},{8,13},{9,12},{10,... | collective-permute-start | bytes 1572872 | tf_op jit(solution)/shard_map/ppermute | solution.py:112
  51.3 55.4 %collective-permute-start.12 = (bf16[2,1024,128]{2,1,0:T(8,128)(2,1)}, bf16[2,1024,128]{2,1,0:T(8,128)(2,1)}, u32[]{:S(2)}, u32[]{:S(2)}) collective-permute-start(bf16[2,1024,128]{2,1,0:T(8,128)(2,1)} %pad_maximum_fusion.12), channel_id=1, source_target_pairs={{0,3},{1,2},{2,1},{3,0},{4,7},{5,6},{6,5},{7,4},{8,11},{9,10},{10,... | collective-permute-start | bytes 1572872 | tf_op jit(solution)/shard_map/ppermute | solution.py:112
  54.7 46.4 %collective-permute-start.13 = (bf16[2,1024,128]{2,1,0:T(8,128)(2,1)}, bf16[2,1024,128]{2,1,0:T(8,128)(2,1)}, u32[]{:S(2)}, u32[]{:S(2)}) collective-permute-start(bf16[2,1024,128]{2,1,0:T(8,128)(2,1)} %pad_maximum_fusion.13), channel_id=1, source_target_pairs={{0,2},{1,3},{2,0},{3,1},{4,6},{5,7},{6,4},{7,5},{8,10},{9,11},{10,... | collective-permute-start | bytes 1572872 | tf_op jit(solution)/shard_map/ppermute | solution.py:112
  66.9 48.3 %collective-permute-start.11 = (bf16[2,1024,128]{2,1,0:T(8,128)(2,1)}, bf16[2,1024,128]{2,1,0:T(8,128)(2,1)}, u32[]{:S(2)}, u32[]{:S(2)}) collective-permute-start(bf16[2,1024,128]{2,1,0:T(8,128)(2,1)} %pad_maximum_fusion.11), channel_id=1, source_target_pairs={{0,4},{1,5},{2,6},{3,7},{4,0},{5,1},{6,2},{7,3},{8,12},{9,13},{10,... | collective-permute-start | bytes 1572872 | tf_op jit(solution)/shard_map/ppermute | solution.py:112
  78.9 1.5 copy-start.13
  78.9 69.8 %collective-permute-start.4 = (bf16[2,1024,128]{2,1,0:T(8,128)(2,1)}, bf16[2,1024,128]{2,1,0:T(8,128)(2,1)}, u32[]{:S(2)}, u32[]{:S(2)}) collective-permute-start(bf16[2,1024,128]{2,1,0:T(8,128)(2,1)} %pad_maximum_fusion.4), channel_id=1, source_target_pairs={{0,11},{1,10},{2,9},{3,8},{4,15},{5,14},{6,13},{7,12},{8,3},{9,2},... | collective-permute-start | bytes 1572872 | tf_op jit(solution)/shard_map/ppermute | solution.py:112
  81.2 19.9 %copy-start.12 = (bf16[2,1024,128]{2,1,0:T(8,128)(2,1)S(1)}, bf16[2,1024,128]{2,1,0:T(8,128)(2,1)}, u32[]{:S(2)}) copy-start(bf16[2,1024,128]{2,1,0:T(8,128)(2,1)} %pad_maximum_fusion.2) | copy-start | bytes 1572868
  87.6 65.6 %collective-permute-start.3 = (bf16[2,1024,128]{2,1,0:T(8,128)(2,1)}, bf16[2,1024,128]{2,1,0:T(8,128)(2,1)}, u32[]{:S(2)}, u32[]{:S(2)}) collective-permute-start(bf16[2,1024,128]{2,1,0:T(8,128)(2,1)} %pad_maximum_fusion.3), channel_id=1, source_target_pairs={{0,12},{1,13},{2,14},{3,15},{4,8},{5,9},{6,10},{7,11},{8,4},{9,5},... | collective-permute-start | bytes 1572872 | tf_op jit(solution)/shard_map/ppermute | solution.py:112
  101.1 56.5 %collective-permute-start.2 = (bf16[2,1024,128]{2,1,0:T(8,128)(2,1)S(1)}, bf16[2,1024,128]{2,1,0:T(8,128)(2,1)}, u32[]{:S(2)}, u32[]{:S(2)}) collective-permute-start(bf16[2,1024,128]{2,1,0:T(8,128)(2,1)S(1)} %copy-done.12), channel_id=1, source_target_pairs={{0,13},{1,12},{2,15},{3,14},{4,9},{5,8},{6,11},{7,10},{8,5},{9,4},... | collective-permute-start | bytes 1572872 | tf_op jit(solution)/shard_map/ppermute | solution.py:112
  106.7 55.4 %collective-permute-start.1 = (bf16[2,1024,128]{2,1,0:T(8,128)(2,1)}, bf16[2,1024,128]{2,1,0:T(8,128)(2,1)}, u32[]{:S(2)}, u32[]{:S(2)}) collective-permute-start(bf16[2,1024,128]{2,1,0:T(8,128)(2,1)} %pad_maximum_fusion.1), channel_id=1, source_target_pairs={{0,14},{1,15},{2,12},{3,13},{4,10},{5,11},{6,8},{7,9},{8,6},{9,7},... | collective-permute-start | bytes 1572872 | tf_op jit(solution)/shard_map/ppermute | solution.py:112
  115.1 51.4 %collective-permute-start = (bf16[2,1024,128]{2,1,0:T(8,128)(2,1)S(1)}, bf16[2,1024,128]{2,1,0:T(8,128)(2,1)}, u32[]{:S(2)}, u32[]{:S(2)}) collective-permute-start(bf16[2,1024,128]{2,1,0:T(8,128)(2,1)S(1)} %pad_maximum_fusion), channel_id=1, source_target_pairs={{0,15},{1,14},{2,13},{3,12},{4,11},{5,10},{6,9},{7,8},{8,7},{9,6},... | collective-permute-start | bytes 1572872 | tf_op jit(solution)/shard_map/ppermute | solution.py:112
  175.4 3.6 %copy-start.1 = (f32[8,2,32,4608]{3,2,1,0:T(8,128)}, f32[8,2,32,4608]{3,2,1,0:T(8,128)S(1)}, u32[]{:S(2)}) copy-start(f32[8,2,32,4608]{3,2,1,0:T(8,128)S(1)} %fusion.2) | copy-start | bytes 28311556
  180.7 4.9 %collective-permute-start.15 = (bf16[8,32,4608]{2,1,0:T(8,128)(2,1)}, bf16[8,32,4608]{2,1,0:T(8,128)(2,1)}, u32[]{:S(2)}, u32[]{:S(2)}) collective-permute-start(bf16[8,32,4608]{2,1,0:T(8,128)(2,1)} %fusion.1), channel_id=1, source_target_pairs={{0,1},{1,0},{2,3},{3,2},{4,5},{5,4},{6,7},{7,6},{8,9},{9,8},{10,11... | collective-permute-start | bytes 7077896 | tf_op jit(solution)/shard_map/ppermute | solution.py:130
Sparse Core Ops, SparseCore 0:
  190.8 81.6 reduce-scatter.1

commit v9 on v4

--- a/solution.py
+++ b/solution.py
@@ -31,9 +31,12 @@
             q_pos = row_first + lax.broadcasted_iota(jnp.int32, (tq, tk), 0)
             k_pos = key_first + lax.broadcasted_iota(jnp.int32, (tq, tk), 1)
             prob = jnp.where(k_pos <= q_pos, prob, 0.0)
-        l_out[...] = l_ref[...] + jnp.sum(prob, axis=1, keepdims=True)
+        weights = prob.astype(jnp.bfloat16)
+        ones = jnp.ones((tk, v_ref.shape[1]), jnp.bfloat16)
+        sums = jnp.dot(weights, ones, preferred_element_type=jnp.float32)
+        l_out[...] = l_ref[...] + sums[:, :1]
         acc_out[...] = acc_ref[...] + jnp.dot(
-            prob.astype(jnp.bfloat16), v_ref[...], preferred_element_type=jnp.float32
+            weights, v_ref[...], preferred_element_type=jnp.float32
         )
 
     @pl.when(key_first > row_last)

time: 236 us -> 244 us (1.034)
  Pallas kernels: 85 us -> 93.4 us
    pallas_call x16, Pallas kernels: 85 us -> 93.4 us  [attend_kernel(): pl.pallas_call(block_kernel, grid_spec=grid_spec, out_shape=(jax.ShapeDty...]
  transfers between devices with their start and end apart: 16 -> 16, of which waited for: 5 -> 5; matrix products, arithmetic and copies ran while one was open for 12% -> 12% of each run, Pallas kernels for 34% -> 36%
where the time goes in v9:
time: 244 us
  Pallas kernels  93.4 us (38%)
  blocking collectives  40.6 us (17%)
  other arithmetic  34.8 us (14%)
  waiting for transfers between devices  33.2 us (14%)
  starting transfers between devices  24.1 us (10%)
  local copies, waits for them, and re-layouts  15.5 us (6%)
    pallas_call x16, Pallas kernels, attend_kernel(): pl.pallas_call(block_kernel, grid_spec=grid_spec, out_shape=(jax.ShapeDty...  93.4 us
    all_to_all x1, blocking collectives, per_device(): lax.all_to_all(on_chip.astype(jnp.bfloat16), 'kx', split_axis=0, concat_a...  40.6 us
    ppermute x15, waiting for transfers between devices, by_heads(): block = lax.ppermute(block, KV, [(j, j ^ shift) for j in range(n_kv)])  25.3 us
    ppermute x15, starting transfers between devices, by_heads(): block = lax.ppermute(block, KV, [(j, j ^ shift) for j in range(n_kv)])  23.7 us
    another operation x16, other arithmetic, by_heads(): jnp.stack((lax.dynamic_slice_in_dim(keys, dest * kv_feat, kv_feat, 1), la...  17 us
    another operation x16, other arithmetic, by_heads(): jnp.stack([row_first, src * key_dev, jnp.int32(rows_dev)]).astype(jnp.int32)  9.82 us
    ppermute x1, waiting for transfers between devices, per_device(): on_chip = mine + lax.ppermute(theirs, 'kc', [(0, 1), (1, 0)])  7.9 us
    another operation x1, local copies, waits for them, and re-layouts, by_heads(): jnp.stack((lax.dynamic_slice_in_dim(keys, dest * kv_feat, kv_feat, 1), la...  6.65 us
  transfers between devices with their start and end apart: 16, of which 5 were waited for; matrix products, arithmetic and copies ran while one was open for 12% of the time, Pallas kernels for 36%

profile of v9, /device:TPU:120, one launch (start us, length us, event | category | flops | bytes accessed | tf_op | source)
XLA Modules:
  0.0 243.7 jit_solution(7147412152126807919)
XLA Ops:
  0.0 6.7 %dynamic-slice_bitcast_fusion.1 = (bf16[1,1024,128]{2,1,0:T(8,128)(2,1)}, bf16[1,1024,128]{2,1,0:T(8,128)(2,1)}, bf16[1,1024,128]{2,1,0:T(8,128)(2,1)}, bf16[1,1...) fusion(bf16[1024,2048]{1,0:T(8,128)(2,1)} %param.8, ...), kind=kLoop, calls=%fused_computation.24 | loop fusion | bytes 16777280 | tf_op jit(solution)/shard_map/stack | solution.py:107
  8.4 3.7 %collective-permute-start.5 = (bf16[2,1024,128]{2,1,0:T(8,128)(2,1)}, bf16[2,1024,128]{2,1,0:T(8,128)(2,1)}, u32[]{:S(2)}, u32[]{:S(2)}) collective-permute-start(bf16[2,1024,128]{2,1,0:T(8,128)(2,1)} %pad_maximum_fusion.5), channel_id=1, source_target_pairs={{0,10},{1,11},{2,8},{3,9},{4,14},{5,15},{6,12},{7,13},{8,2},{9,3},... | collective-permute-start | bytes 1572872 | tf_op jit(solution)/shard_map/ppermute | solution.py:115
  14.1 3.0 %collective-permute-start.7 = (bf16[2,1024,128]{2,1,0:T(8,128)(2,1)}, bf16[2,1024,128]{2,1,0:T(8,128)(2,1)}, u32[]{:S(2)}, u32[]{:S(2)}) collective-permute-start(bf16[2,1024,128]{2,1,0:T(8,128)(2,1)} %pad_maximum_fusion.7), channel_id=1, source_target_pairs={{0,8},{1,9},{2,10},{3,11},{4,12},{5,13},{6,14},{7,15},{8,0},{9,1},... | collective-permute-start | bytes 1572872 | tf_op jit(solution)/shard_map/ppermute | solution.py:115
  26.8 2.0 pad_maximum_fusion.15.k_ref.v_ref
  41.5 2.2 collective-permute-start.9
  44.7 2.2 collective-permute-start.12
  48.1 2.3 collective-permute-start.13
  51.0 9.4 %collective-permute-done.8.k_ref.v_ref = bf16[2,1024,128]{2,1,0:T(8,128)(2,1)} collective-permute-done((bf16[2,1024,128]{2,1,0:T(8,128)(2,1)}, bf16[2,1024,128]{2,1,0:T(8,128)(2,1)}, u32[]{:S(2)}, u32[]{:S(2)}) %collective-permute-start.8) | collective-permute-done | bytes 524320 | tf_op jit(solution)/shard_map/ppermute | solution.py:115
  64.1 8.2 %collective-permute-done.9.k_ref.v_ref = bf16[2,1024,128]{2,1,0:T(8,128)(2,1)S(1)} collective-permute-done((bf16[2,1024,128]{2,1,0:T(8,128)(2,1)}, bf16[2,1024,128]{2,1,0:T(8,128)(2,1)S(1)}, u32[]{:S(2)}, u32[]{:S(2)}) %collective-permute-start.9) | collective-permute-done | bytes 524320 | tf_op jit(solution)/shard_map/ppermute | solution.py:115
  75.5 6.0 %shard_map.55 = (f32[1024,1]{1,0:T(8,128)}, f32[1024,128]{1,0:T(8,128)}) custom-call(s32[3]{0:T(128)} %pad_add_fusion.sc_ref, bf16[1024,128]{1,0:T(8,128)(2,1)} %bitcast.107, bf16[2,1024,128]{2,1,0:T(8,128)(2,1)} %pad_maximum_fusion.15.k_ref.v_ref, ...), custom_call_target="tpu_custom_call", output_to_operand_aliasing={{0}: (4, {}), {1}: (5, {})} | custom-call | flops 536870912 | bytes 1843200 | tf_op jit(solution)/shard_map/pallas_call | solution.py:76
  82.1 6.0 %shard_map.56 = (f32[1024,1]{1,0:T(8,128)}, f32[1024,128]{1,0:T(8,128)}) custom-call(s32[3]{0:T(128)} %pad_add_fusion.1.sc_ref, bf16[1024,128]{1,0:T(8,128)(2,1)} %bitcast.108, bf16[2,1024,128]{2,1,0:T(8,128)(2,1)} %collective-permute-done.14.k_ref.v_ref, ...), custom_call_target="tpu_custom_call", output_to_operand_aliasing={{0}: (4, {}), {1}: (5, {})} | custom-call | flops 536870912 | bytes 1843200 | tf_op jit(solution)/shard_map/pallas_call | solution.py:76
  88.1 6.4 %collective-permute-done.13.k_ref.v_ref = bf16[2,1024,128]{2,1,0:T(8,128)(2,1)} collective-permute-done((bf16[2,1024,128]{2,1,0:T(8,128)(2,1)}, bf16[2,1024,128]{2,1,0:T(8,128)(2,1)}, u32[]{:S(2)}, u32[]{:S(2)}) %collective-permute-start.13) | collective-permute-done | bytes 524320 | tf_op jit(solution)/shard_map/ppermute | solution.py:115
  94.5 6.0 %shard_map.57 = (f32[1024,1]{1,0:T(8,128)}, f32[1024,128]{1,0:T(8,128)}) custom-call(s32[3]{0:T(128)} %pad_add_fusion.2.sc_ref, bf16[1024,128]{1,0:T(8,128)(2,1)} %bitcast.109, bf16[2,1024,128]{2,1,0:T(8,128)(2,1)} %collective-permute-done.13.k_ref.v_ref, ...), custom_call_target="tpu_custom_call", output_to_operand_aliasing={{0}: (4, {}), {1}: (5, {})} | custom-call | flops 536870912 | bytes 1843200 | tf_op jit(solution)/shard_map/pallas_call | solution.py:76
  100.5 2.5 %collective-permute-start.1 = (bf16[2,1024,128]{2,1,0:T(8,128)(2,1)}, bf16[2,1024,128]{2,1,0:T(8,128)(2,1)}, u32[]{:S(2)}, u32[]{:S(2)}) collective-permute-start(bf16[2,1024,128]{2,1,0:T(8,128)(2,1)} %pad_maximum_fusion.1), channel_id=1, source_target_pairs={{0,14},{1,15},{2,12},{3,13},{4,10},{5,11},{6,8},{7,9},{8,6},{9,7},... | collective-permute-start | bytes 1572872 | tf_op jit(solution)/shard_map/ppermute | solution.py:115
  103.0 6.0 %shard_map.58 = (f32[1024,1]{1,0:T(8,128)}, f32[1024,128]{1,0:T(8,128)}) custom-call(s32[3]{0:T(128)} %pad_add_fusion.3.sc_ref, bf16[1024,128]{1,0:T(8,128)(2,1)} %bitcast.110, bf16[2,1024,128]{2,1,0:T(8,128)(2,1)} %collective-permute-done.12.k_ref.v_ref, ...), custom_call_target="tpu_custom_call", output_to_operand_aliasing={{0}: (4, {}), {1}: (5, {})} | custom-call | flops 536870912 | bytes 1843200 | tf_op jit(solution)/shard_map/pallas_call | solution.py:76
  110.7 6.0 %shard_map.59 = (f32[1024,1]{1,0:T(8,128)}, f32[1024,128]{1,0:T(8,128)}) custom-call(s32[3]{0:T(128)} %pad_add_fusion.4.sc_ref, bf16[1024,128]{1,0:T(8,128)(2,1)} %bitcast.111, bf16[2,1024,128]{2,1,0:T(8,128)(2,1)} %collective-permute-done.11.k_ref.v_ref, ...), custom_call_target="tpu_custom_call", output_to_operand_aliasing={{0}: (4, {}), {1}: (5, {})} | custom-call | flops 536870912 | bytes 1843200 | tf_op jit(solution)/shard_map/pallas_call | solution.py:76
  116.7 6.0 %shard_map.60 = (f32[1024,1]{1,0:T(8,128)}, f32[1024,128]{1,0:T(8,128)}) custom-call(s32[3]{0:T(128)} %pad_add_fusion.5.sc_ref, bf16[1024,128]{1,0:T(8,128)(2,1)} %bitcast.112, bf16[2,1024,128]{2,1,0:T(8,128)(2,1)} %collective-permute-done.10.k_ref.v_ref, ...), custom_call_target="tpu_custom_call", output_to_operand_aliasing={{0}: (4, {}), {1}: (5, {})} | custom-call | flops 536870912 | bytes 1843200 | tf_op jit(solution)/shard_map/pallas_call | solution.py:76
  122.7 6.0 %shard_map.61 = (f32[1024,1]{1,0:T(8,128)}, f32[1024,128]{1,0:T(8,128)}) custom-call(s32[3]{0:T(128)} %pad_add_fusion.6.sc_ref, bf16[1024,128]{1,0:T(8,128)(2,1)} %bitcast.113, bf16[2,1024,128]{2,1,0:T(8,128)(2,1)} %copy-done.13, bf16[2,1024,128]{2,1,0:T(8,128)(2,1)} %copy-done.13, ...), custom_call_target="tpu_custom_call", output_to_operand_aliasing={{0}: (4, {}), {1}: (5, {})} | custom-call | flops 536870912 | bytes 1843200 | tf_op jit(solution)/shard_map/pallas_call | solution.py:76
  128.7 6.0 %shard_map.62 = (f32[1024,1]{1,0:T(8,128)}, f32[1024,128]{1,0:T(8,128)}) custom-call(s32[3]{0:T(128)} %pad_add_fusion.7.sc_ref, bf16[1024,128]{1,0:T(8,128)(2,1)} %bitcast.114, bf16[2,1024,128]{2,1,0:T(8,128)(2,1)} %collective-permute-done.8.k_ref.v_ref, ...), custom_call_target="tpu_custom_call", output_to_operand_aliasing={{0}: (4, {}), {1}: (5, {})} | custom-call | flops 536870912 | bytes 1843200 | tf_op jit(solution)/shard_map/pallas_call | solution.py:76
  134.7 6.0 %shard_map.63 = (f32[1024,1]{1,0:T(8,128)}, f32[1024,128]{1,0:T(8,128)}) custom-call(s32[3]{0:T(128)} %pad_add_fusion.8.sc_ref, bf16[1024,128]{1,0:T(8,128)(2,1)} %bitcast.115, bf16[2,1024,128]{2,1,0:T(8,128)(2,1)} %collective-permute-done.7.k_ref.v_ref, ...), custom_call_target="tpu_custom_call", output_to_operand_aliasing={{0}: (4, {}), {1}: (5, {})} | custom-call | flops 536870912 | bytes 1843200 | tf_op jit(solution)/shard_map/pallas_call | solution.py:76
  140.7 6.0 %shard_map.64 = (f32[1024,1]{1,0:T(8,128)}, f32[1024,128]{1,0:T(8,128)}) custom-call(s32[3]{0:T(128)} %pad_add_fusion.9.sc_ref, bf16[1024,128]{1,0:T(8,128)(2,1)} %bitcast.116, bf16[2,1024,128]{2,1,0:T(8,128)(2,1)} %collective-permute-done.6.k_ref.v_ref, ...), custom_call_target="tpu_custom_call", output_to_operand_aliasing={{0}: (4, {}), {1}: (5, {})} | custom-call | flops 536870912 | bytes 1843200 | tf_op jit(solution)/shard_map/pallas_call | solution.py:76
  146.8 6.0 %shard_map.65 = (f32[1024,1]{1,0:T(8,128)}, f32[1024,128]{1,0:T(8,128)}) custom-call(s32[3]{0:T(128)} %pad_add_fusion.10.sc_ref, bf16[1024,128]{1,0:T(8,128)(2,1)} %bitcast.117, bf16[2,1024,128]{2,1,0:T(8,128)(2,1)} %collective-permute-done.5.k_ref.v_ref, ...), custom_call_target="tpu_custom_call", output_to_operand_aliasing={{0}: (4, {}), {1}: (5, {})} | custom-call | flops 536870912 | bytes 1843200 | tf_op jit(solution)/shard_map/pallas_call | solution.py:76
  152.8 6.0 %shard_map.66 = (f32[1024,1]{1,0:T(8,128)}, f32[1024,128]{1,0:T(8,128)}) custom-call(s32[3]{0:T(128)} %pad_add_fusion.11.sc_ref, bf16[1024,128]{1,0:T(8,128)(2,1)} %bitcast.118, bf16[2,1024,128]{2,1,0:T(8,128)(2,1)} %collective-permute-done.4.k_ref.v_ref, ...), custom_call_target="tpu_custom_call", output_to_operand_aliasing={{0}: (4, {}), {1}: (5, {})} | custom-call | flops 536870912 | bytes 1843200 | tf_op jit(solution)/shard_map/pallas_call | solution.py:76
  158.8 4.4 %shard_map.67 = (f32[1024,1]{1,0:T(8,128)}, f32[1024,128]{1,0:T(8,128)}) custom-call(s32[3]{0:T(128)} %pad_add_fusion.12.sc_ref, bf16[1024,128]{1,0:T(8,128)(2,1)} %bitcast.119, bf16[2,1024,128]{2,1,0:T(8,128)(2,1)} %collective-permute-done.3.k_ref.v_ref, ...), custom_call_target="tpu_custom_call", output_to_operand_aliasing={{0}: (4, {}), {1}: (5, {})} | custom-call | flops 536870912 | bytes 1843200 | tf_op jit(solution)/shard_map/pallas_call | solution.py:76
  163.2 4.7 %shard_map.68 = (f32[1024,1]{1,0:T(8,128)}, f32[1024,128]{1,0:T(8,128)}) custom-call(s32[3]{0:T(128)} %pad_add_fusion.13.sc_ref, bf16[1024,128]{1,0:T(8,128)(2,1)} %bitcast.120, bf16[2,1024,128]{2,1,0:T(8,128)(2,1)} %collective-permute-done.2.k_ref.v_ref, ...), custom_call_target="tpu_custom_call", output_to_operand_aliasing={{0}: (4, {}), {1}: (5, {})} | custom-call | flops 536870912 | bytes 1843200 | tf_op jit(solution)/shard_map/pallas_call | solution.py:76
  167.9 6.0 %shard_map.69 = (f32[1024,1]{1,0:T(8,128)}, f32[1024,128]{1,0:T(8,128)}) custom-call(s32[3]{0:T(128)} %pad_add_fusion.14.sc_ref, bf16[1024,128]{1,0:T(8,128)(2,1)} %bitcast.121, bf16[2,1024,128]{2,1,0:T(8,128)(2,1)} %collective-permute-done.1.k_ref.v_ref, ...), custom_call_target="tpu_custom_call", output_to_operand_aliasing={{0}: (4, {}), {1}: (5, {})} | custom-call | flops 536870912 | bytes 1843200 | tf_op jit(solution)/shard_map/pallas_call | solution.py:76
  173.9 6.1 %shard_map.70 = (f32[1024,1]{1,0:T(8,128)}, f32[1024,128]{1,0:T(8,128)}) custom-call(s32[3]{0:T(128)} %pad_add_fusion.15.sc_ref, bf16[1024,128]{1,0:T(8,128)(2,1)} %bitcast.122, bf16[2,1024,128]{2,1,0:T(8,128)(2,1)} %collective-permute-done.k_ref.v_ref, ...), custom_call_target="tpu_custom_call", output_to_operand_aliasing={{0}: (4, {}), {1}: (5, {})} | custom-call | flops 536870912 | bytes 1843200 | tf_op jit(solution)/shard_map/pallas_call | solution.py:76
  184.4 2.9 %dynamic-slice_bitcast_fusion = f32[8,32,4608]{2,1,0:T(8,128)} fusion(f32[8,2,32,4608]{3,2,1,0:T(8,128)S(1)} %fusion.1, s32[]{:T(128)S(6)} %select_n.88), kind=kLoop, calls=%fused_computation.3 | loop fusion | bytes 9437188 | tf_op jit(solution)/shard_map/jit(dynamic_index_in_dim)/squeeze | solution.py:132
  187.2 2.2 copy-done.1
  189.8 7.9 %collective-permute-done.15 = f32[8,32,4608]{2,1,0:T(8,128)} collective-permute-done((f32[8,32,4608]{2,1,0:T(8,128)}, f32[8,32,4608]{2,1,0:T(8,128)}, u32[]{:S(2)}, u32[]{:S(2)}) %collective-permute-start.15) | collective-permute-done | bytes 4718624 | tf_op jit(solution)/shard_map/ppermute | solution.py:133
  197.7 4.3 %fusion = bf16[8,32,4608]{2,1,0:T(8,128)(2,1)S(1)} fusion(f32[8,32,4608]{2,1,0:T(8,128)} %collective-permute-done.15, f32[8,2,32,4608]{3,2,1,0:T(8,128)} %copy-done.1, s32[]{:T(128)S(6)} %select_n.87), kind=kLoop, calls=%fused_computation.1 | loop fusion | flops 2359296 | bytes 11796484 | tf_op jit(solution)/shard_map/convert_element_type | solution.py:135
  202.0 40.6 %all_to_all.5 = bf16[8,32,4608]{2,1,0:T(8,128)(2,1)S(1)} all-to-all(bf16[8,32,4608]{2,1,0:T(8,128)(2,1)S(1)} %fusion), channel_id=1, replica_groups=mesh['pb'=8,'kx'=8,'kc'=2] {'kx'}, dimensions={0} | all-to-all | bytes 4718592 | tf_op jit(solution)/shard_map/all_to_all | solution.py:134
  (89 shorter events, 43.2 us)
Async XLA Ops:
  0.0 183.0 %copy-start = (bf16[256,4608]{1,0:T(8,128)(2,1)S(1)}, bf16[256,4608]{1,0:T(8,128)(2,1)}, u32[]{:S(2)}) copy-start(bf16[256,4608]{1,0:T(8,128)(2,1)} %param.9) | copy-start | bytes 7077892
  7.5 33.9 %collective-permute-start.14 = (bf16[2,1024,128]{2,1,0:T(8,128)(2,1)}, bf16[2,1024,128]{2,1,0:T(8,128)(2,1)}, u32[]{:S(2)}, u32[]{:S(2)}) collective-permute-start(bf16[2,1024,128]{2,1,0:T(8,128)(2,1)} %pad_maximum_fusion.14), channel_id=1, source_target_pairs={{0,1},{1,0},{2,3},{3,2},{4,5},{5,4},{6,7},{7,6},{8,9},{9,8},{10,11... | collective-permute-start | bytes 1572872 | tf_op jit(solution)/shard_map/ppermute | solution.py:115
  8.4 35.3 %collective-permute-start.5 = (bf16[2,1024,128]{2,1,0:T(8,128)(2,1)}, bf16[2,1024,128]{2,1,0:T(8,128)(2,1)}, u32[]{:S(2)}, u32[]{:S(2)}) collective-permute-start(bf16[2,1024,128]{2,1,0:T(8,128)(2,1)} %pad_maximum_fusion.5), channel_id=1, source_target_pairs={{0,10},{1,11},{2,8},{3,9},{4,14},{5,15},{6,12},{7,13},{8,2},{9,3},... | collective-permute-start | bytes 1572872 | tf_op jit(solution)/shard_map/ppermute | solution.py:115
  12.9 31.8 %collective-permute-start.6 = (bf16[2,1024,128]{2,1,0:T(8,128)(2,1)}, bf16[2,1024,128]{2,1,0:T(8,128)(2,1)}, u32[]{:S(2)}, u32[]{:S(2)}) collective-permute-start(bf16[2,1024,128]{2,1,0:T(8,128)(2,1)} %pad_maximum_fusion.6), channel_id=1, source_target_pairs={{0,9},{1,8},{2,11},{3,10},{4,13},{5,12},{6,15},{7,14},{8,1},{9,0},... | collective-permute-start | bytes 1572872 | tf_op jit(solution)/shard_map/ppermute | solution.py:115
  14.1 34.1 %collective-permute-start.7 = (bf16[2,1024,128]{2,1,0:T(8,128)(2,1)}, bf16[2,1024,128]{2,1,0:T(8,128)(2,1)}, u32[]{:S(2)}, u32[]{:S(2)}) collective-permute-start(bf16[2,1024,128]{2,1,0:T(8,128)(2,1)} %pad_maximum_fusion.7), channel_id=1, source_target_pairs={{0,8},{1,9},{2,10},{3,11},{4,12},{5,13},{6,14},{7,15},{8,0},{9,1},... | collective-permute-start | bytes 1572872 | tf_op jit(solution)/shard_map/ppermute | solution.py:115
  18.0 42.4 %collective-permute-start.8 = (bf16[2,1024,128]{2,1,0:T(8,128)(2,1)}, bf16[2,1024,128]{2,1,0:T(8,128)(2,1)}, u32[]{:S(2)}, u32[]{:S(2)}) collective-permute-start(bf16[2,1024,128]{2,1,0:T(8,128)(2,1)} %pad_maximum_fusion.8), channel_id=1, source_target_pairs={{0,7},{1,6},{2,5},{3,4},{4,3},{5,2},{6,1},{7,0},{8,15},{9,14},{10,... | collective-permute-start | bytes 1572872 | tf_op jit(solution)/shard_map/ppermute | solution.py:115
  20.5 13.9 %copy-start.10 = (bf16[1,1024,128]{2,1,0:T(8,128)(2,1)S(1)}, bf16[1,1024,128]{2,1,0:T(8,128)(2,1)}, u32[]{:S(2)}) copy-start(bf16[1,1024,128]{2,1,0:T(8,128)(2,1)} %get-tuple-element.89) | copy-start | bytes 786436
  20.6 13.9 %copy-start.11 = (bf16[1,1024,128]{2,1,0:T(8,128)(2,1)S(1)}, bf16[1,1024,128]{2,1,0:T(8,128)(2,1)}, u32[]{:S(2)}) copy-start(bf16[1,1024,128]{2,1,0:T(8,128)(2,1)} %get-tuple-element.112) | copy-start | bytes 786436
  20.6 14.8 %copy-start.8 = (bf16[1,1024,128]{2,1,0:T(8,128)(2,1)S(1)}, bf16[1,1024,128]{2,1,0:T(8,128)(2,1)}, u32[]{:S(2)}) copy-start(bf16[1,1024,128]{2,1,0:T(8,128)(2,1)} %get-tuple-element.90) | copy-start | bytes 786436
  20.6 14.8 %copy-start.9 = (bf16[1,1024,128]{2,1,0:T(8,128)(2,1)S(1)}, bf16[1,1024,128]{2,1,0:T(8,128)(2,1)}, u32[]{:S(2)}) copy-start(bf16[1,1024,128]{2,1,0:T(8,128)(2,1)} %get-tuple-element.111) | copy-start | bytes 786436
  20.6 15.6 %copy-start.6 = (bf16[1,1024,128]{2,1,0:T(8,128)(2,1)S(1)}, bf16[1,1024,128]{2,1,0:T(8,128)(2,1)}, u32[]{:S(2)}) copy-start(bf16[1,1024,128]{2,1,0:T(8,128)(2,1)} %get-tuple-element.95) | copy-start | bytes 786436
  20.6 15.6 %copy-start.7 = (bf16[1,1024,128]{2,1,0:T(8,128)(2,1)S(1)}, bf16[1,1024,128]{2,1,0:T(8,128)(2,1)}, u32[]{:S(2)}) copy-start(bf16[1,1024,128]{2,1,0:T(8,128)(2,1)} %get-tuple-element.106) | copy-start | bytes 786436
  20.6 16.4 %copy-start.4 = (bf16[1,1024,128]{2,1,0:T(8,128)(2,1)S(1)}, bf16[1,1024,128]{2,1,0:T(8,128)(2,1)}, u32[]{:S(2)}) copy-start(bf16[1,1024,128]{2,1,0:T(8,128)(2,1)} %get-tuple-element.96) | copy-start | bytes 786436
  20.6 16.4 %copy-start.5 = (bf16[1,1024,128]{2,1,0:T(8,128)(2,1)S(1)}, bf16[1,1024,128]{2,1,0:T(8,128)(2,1)}, u32[]{:S(2)}) copy-start(bf16[1,1024,128]{2,1,0:T(8,128)(2,1)} %get-tuple-element.105) | copy-start | bytes 786436
  26.8 11.1 %copy-start.2 = (bf16[1,1024,128]{2,1,0:T(8,128)(2,1)S(1)}, bf16[1,1024,128]{2,1,0:T(8,128)(2,1)}, u32[]{:S(2)}) copy-start(bf16[1,1024,128]{2,1,0:T(8,128)(2,1)} %get-tuple-element.97) | copy-start | bytes 786436
  26.8 11.1 %copy-start.3 = (bf16[1,1024,128]{2,1,0:T(8,128)(2,1)S(1)}, bf16[1,1024,128]{2,1,0:T(8,128)(2,1)}, u32[]{:S(2)}) copy-start(bf16[1,1024,128]{2,1,0:T(8,128)(2,1)} %get-tuple-element.104) | copy-start | bytes 786436
  41.5 30.9 %collective-permute-start.9 = (bf16[2,1024,128]{2,1,0:T(8,128)(2,1)}, bf16[2,1024,128]{2,1,0:T(8,128)(2,1)S(1)}, u32[]{:S(2)}, u32[]{:S(2)}) collective-permute-start(bf16[2,1024,128]{2,1,0:T(8,128)(2,1)} %pad_maximum_fusion.9), channel_id=1, source_target_pairs={{0,6},{1,7},{2,4},{3,5},{4,2},{5,3},{6,0},{7,1},{8,14},{9,15},{10,... | collective-permute-start | bytes 1572872 | tf_op jit(solution)/shard_map/ppermute | solution.py:115
  43.7 37.9 %collective-permute-start.10 = (bf16[2,1024,128]{2,1,0:T(8,128)(2,1)}, bf16[2,1024,128]{2,1,0:T(8,128)(2,1)}, u32[]{:S(2)}, u32[]{:S(2)}) collective-permute-start(bf16[2,1024,128]{2,1,0:T(8,128)(2,1)} %pad_maximum_fusion.10), channel_id=1, source_target_pairs={{0,5},{1,4},{2,7},{3,6},{4,1},{5,0},{6,3},{7,2},{8,13},{9,12},{10,... | collective-permute-start | bytes 1572872 | tf_op jit(solution)/shard_map/ppermute | solution.py:115
  44.7 55.8 %collective-permute-start.12 = (bf16[2,1024,128]{2,1,0:T(8,128)(2,1)}, bf16[2,1024,128]{2,1,0:T(8,128)(2,1)}, u32[]{:S(2)}, u32[]{:S(2)}) collective-permute-start(bf16[2,1024,128]{2,1,0:T(8,128)(2,1)} %pad_maximum_fusion.12), channel_id=1, source_target_pairs={{0,3},{1,2},{2,1},{3,0},{4,7},{5,6},{6,5},{7,4},{8,11},{9,10},{10,... | collective-permute-start | bytes 1572872 | tf_op jit(solution)/shard_map/ppermute | solution.py:115
  48.1 46.3 %collective-permute-start.13 = (bf16[2,1024,128]{2,1,0:T(8,128)(2,1)}, bf16[2,1024,128]{2,1,0:T(8,128)(2,1)}, u32[]{:S(2)}, u32[]{:S(2)}) collective-permute-start(bf16[2,1024,128]{2,1,0:T(8,128)(2,1)} %pad_maximum_fusion.13), channel_id=1, source_target_pairs={{0,2},{1,3},{2,0},{3,1},{4,6},{5,7},{6,4},{7,5},{8,10},{9,11},{10,... | collective-permute-start | bytes 1572872 | tf_op jit(solution)/shard_map/ppermute | solution.py:115
  60.4 48.6 %collective-permute-start.11 = (bf16[2,1024,128]{2,1,0:T(8,128)(2,1)}, bf16[2,1024,128]{2,1,0:T(8,128)(2,1)}, u32[]{:S(2)}, u32[]{:S(2)}) collective-permute-start(bf16[2,1024,128]{2,1,0:T(8,128)(2,1)} %pad_maximum_fusion.11), channel_id=1, source_target_pairs={{0,4},{1,5},{2,6},{3,7},{4,0},{5,1},{6,2},{7,3},{8,12},{9,13},{10,... | collective-permute-start | bytes 1572872 | tf_op jit(solution)/shard_map/ppermute | solution.py:115
  72.4 1.5 copy-start.13
  72.4 80.4 %collective-permute-start.4 = (bf16[2,1024,128]{2,1,0:T(8,128)(2,1)}, bf16[2,1024,128]{2,1,0:T(8,128)(2,1)}, u32[]{:S(2)}, u32[]{:S(2)}) collective-permute-start(bf16[2,1024,128]{2,1,0:T(8,128)(2,1)} %pad_maximum_fusion.4), channel_id=1, source_target_pairs={{0,11},{1,10},{2,9},{3,8},{4,15},{5,14},{6,13},{7,12},{8,3},{9,2},... | collective-permute-start | bytes 1572872 | tf_op jit(solution)/shard_map/ppermute | solution.py:115
  74.7 19.8 %copy-start.12 = (bf16[2,1024,128]{2,1,0:T(8,128)(2,1)S(1)}, bf16[2,1024,128]{2,1,0:T(8,128)(2,1)}, u32[]{:S(2)}) copy-start(bf16[2,1024,128]{2,1,0:T(8,128)(2,1)} %pad_maximum_fusion.2) | copy-start | bytes 1572868
  81.5 77.3 %collective-permute-start.3 = (bf16[2,1024,128]{2,1,0:T(8,128)(2,1)}, bf16[2,1024,128]{2,1,0:T(8,128)(2,1)}, u32[]{:S(2)}, u32[]{:S(2)}) collective-permute-start(bf16[2,1024,128]{2,1,0:T(8,128)(2,1)} %pad_maximum_fusion.3), channel_id=1, source_target_pairs={{0,12},{1,13},{2,14},{3,15},{4,8},{5,9},{6,10},{7,11},{8,4},{9,5},... | collective-permute-start | bytes 1572872 | tf_op jit(solution)/shard_map/ppermute | solution.py:115
  94.5 68.8 %collective-permute-start.2 = (bf16[2,1024,128]{2,1,0:T(8,128)(2,1)S(1)}, bf16[2,1024,128]{2,1,0:T(8,128)(2,1)}, u32[]{:S(2)}, u32[]{:S(2)}) collective-permute-start(bf16[2,1024,128]{2,1,0:T(8,128)(2,1)S(1)} %copy-done.12), channel_id=1, source_target_pairs={{0,13},{1,12},{2,15},{3,14},{4,9},{5,8},{6,11},{7,10},{8,5},{9,4},... | collective-permute-start | bytes 1572872 | tf_op jit(solution)/shard_map/ppermute | solution.py:115
  100.5 67.4 %collective-permute-start.1 = (bf16[2,1024,128]{2,1,0:T(8,128)(2,1)}, bf16[2,1024,128]{2,1,0:T(8,128)(2,1)}, u32[]{:S(2)}, u32[]{:S(2)}) collective-permute-start(bf16[2,1024,128]{2,1,0:T(8,128)(2,1)} %pad_maximum_fusion.1), channel_id=1, source_target_pairs={{0,14},{1,15},{2,12},{3,13},{4,10},{5,11},{6,8},{7,9},{8,6},{9,7},... | collective-permute-start | bytes 1572872 | tf_op jit(solution)/shard_map/ppermute | solution.py:115
  109.0 64.9 %collective-permute-start = (bf16[2,1024,128]{2,1,0:T(8,128)(2,1)S(1)}, bf16[2,1024,128]{2,1,0:T(8,128)(2,1)}, u32[]{:S(2)}, u32[]{:S(2)}) collective-permute-start(bf16[2,1024,128]{2,1,0:T(8,128)(2,1)S(1)} %pad_maximum_fusion), channel_id=1, source_target_pairs={{0,15},{1,14},{2,13},{3,12},{4,11},{5,10},{6,9},{7,8},{8,7},{9,6},... | collective-permute-start | bytes 1572872 | tf_op jit(solution)/shard_map/ppermute | solution.py:115
  184.4 5.0 %copy-start.1 = (f32[8,2,32,4608]{3,2,1,0:T(8,128)}, f32[8,2,32,4608]{3,2,1,0:T(8,128)S(1)}, u32[]{:S(2)}) copy-start(f32[8,2,32,4608]{3,2,1,0:T(8,128)S(1)} %fusion.1) | copy-start | bytes 28311556
  189.4 8.3 %collective-permute-start.15 = (f32[8,32,4608]{2,1,0:T(8,128)}, f32[8,32,4608]{2,1,0:T(8,128)}, u32[]{:S(2)}, u32[]{:S(2)}) collective-permute-start(f32[8,32,4608]{2,1,0:T(8,128)} %dynamic-slice_bitcast_fusion), channel_id=1, source_target_pairs={{0,1},{1,0},{2,3},{3,2},{4,5},{5,4},{6,7},{7,6},{8,9},{9,8},{10,11... | collective-permute-start | bytes 14155784 | tf_op jit(solution)/shard_map/ppermute | solution.py:133

commit v10 on v7

--- a/solution.py
+++ b/solution.py
@@ -120,14 +120,18 @@
     rows_dev = queries.shape[0]
     row_first = slab_start[0] + lax.axis_index("pb") * rows_dev
     attended = by_heads(queries, keys, values, row_first)
-    partial = jnp.dot(attended, out_weight, preferred_element_type=jnp.float32)
     n_chip = lax.axis_size("kx")
     n_core = lax.axis_size("kc")
-    partial = partial.reshape(n_chip, n_core, rows_dev // (n_chip * n_core), partial.shape[1])
+    by_core = attended.reshape(n_chip, n_core, rows_dev // (n_chip * n_core), attended.shape[1])
     core = lax.axis_index("kc")
-    mine = lax.dynamic_index_in_dim(partial, core, 1, keepdims=False)
-    theirs = lax.dynamic_index_in_dim(partial, 1 - core, 1, keepdims=False).astype(jnp.bfloat16)
-    on_chip = mine + lax.ppermute(theirs, "kc", [(0, 1), (1, 0)]).astype(jnp.float32)
+
+    def project(which):
+        rows = lax.dynamic_index_in_dim(by_core, which, 1, keepdims=False)
+        return jnp.einsum("cra,ad->crd", rows, out_weight, preferred_element_type=jnp.float32)
+
+    theirs = project(1 - core)
+    moved = lax.ppermute(theirs, "kc", [(0, 1), (1, 0)])
+    on_chip = project(core) + moved
     parts = lax.all_to_all(
         on_chip.astype(jnp.bfloat16), "kx", split_axis=0, concat_axis=0, tiled=True
     )

time: 234 us -> 239 us (1.021)
  waiting for transfers between devices: 30.2 us -> 36.5 us
  blocking collectives: 40.4 us -> 34.9 us
  Pallas kernels: 85 us -> 90.3 us
  local copies, waits for them, and re-layouts: 15.8 us -> 10.6 us
  matrix products: 1.39 us -> 6.04 us
  starting transfers between devices: 24.7 us -> 28.2 us
  other arithmetic: 34.1 us -> 31.1 us
    all_to_all x1, blocking collectives: 40.4 us -> 34.9 us  [per_device(): lax.all_to_all(on_chip.astype(jnp.bfloat16), 'kx', split_axis=0, concat_a...]
    pallas_call x16, Pallas kernels: 85 us -> 90.3 us  [attend_kernel(): pl.pallas_call(block_kernel, grid_spec=grid_spec, out_shape=(jax.ShapeDty...]
    dot_general x1 -> x2, matrix products: 1.39 us -> 6.04 us  [project(): jnp.einsum('cra,ad->crd', rows, out_weight, preferred_element_type=jnp.fl...]
    ppermute x15, starting transfers between devices: 24.4 us -> 28.2 us  [by_heads(): block = lax.ppermute(block, KV, [(j, j ^ shift) for j in range(n_kv)])]
    ppermute x1, waiting for transfers between devices: 4.54 us -> 8.25 us  [per_device(): moved = lax.ppermute(theirs, 'kc', [(0, 1), (1, 0)])]
    unnamed x28, local copies, waits for them, and re-layouts: 3.69 us -> 0.06 us
    convert_element_type x1 -> x0, other arithmetic: 3.59 us -> none  [per_device(): on_chip.astype(jnp.bfloat16)]
    ppermute x15, waiting for transfers between devices: 25.7 us -> 28.3 us  [by_heads(): block = lax.ppermute(block, KV, [(j, j ^ shift) for j in range(n_kv)])]
  transfers between devices with their start and end apart: 16 -> 16, of which waited for: 5 -> 5; matrix products, arithmetic and copies ran while one was open for 13% -> 13% of each run, Pallas kernels for 35% -> 36%
where the time goes in v10:
time: 239 us
  Pallas kernels  90.3 us (38%)
  waiting for transfers between devices  36.5 us (15%)
  blocking collectives  34.9 us (15%)
  other arithmetic  31.1 us (13%)
  starting transfers between devices  28.2 us (12%)
  local copies, waits for them, and re-layouts  10.6 us (4%)
  matrix products  6.04 us (3%)
    pallas_call x16, Pallas kernels, attend_kernel(): pl.pallas_call(block_kernel, grid_spec=grid_spec, out_shape=(jax.ShapeDty...  90.3 us
    all_to_all x1, blocking collectives, per_device(): lax.all_to_all(on_chip.astype(jnp.bfloat16), 'kx', split_axis=0, concat_a...  34.9 us
    ppermute x15, waiting for transfers between devices, by_heads(): block = lax.ppermute(block, KV, [(j, j ^ shift) for j in range(n_kv)])  28.3 us
    ppermute x15, starting transfers between devices, by_heads(): block = lax.ppermute(block, KV, [(j, j ^ shift) for j in range(n_kv)])  28.2 us
    another operation x16, other arithmetic, by_heads(): jnp.stack((lax.dynamic_slice_in_dim(keys, dest * kv_feat, kv_feat, 1), la...  17.8 us
    another operation x16, other arithmetic, by_heads(): jnp.stack([row_first, src * key_dev, jnp.int32(rows_dev)]).astype(jnp.int32)  9.65 us
    ppermute x1, waiting for transfers between devices, per_device(): moved = lax.ppermute(theirs, 'kc', [(0, 1), (1, 0)])  8.25 us
    another operation x1, local copies, waits for them, and re-layouts, by_heads(): jnp.stack((lax.dynamic_slice_in_dim(keys, dest * kv_feat, kv_feat, 1), la...  6.7 us
  transfers between devices with their start and end apart: 16, of which 5 were waited for; matrix products, arithmetic and copies ran while one was open for 13% of the time, Pallas kernels for 36%

profile of v10, /device:TPU:120, one launch (start us, length us, event | category | flops | bytes accessed | tf_op | source)
XLA Modules:
  0.0 238.5 jit_solution(11504492827631758556)
XLA Ops:
  0.0 6.7 %dynamic-slice_bitcast_fusion = (bf16[1,1024,128]{2,1,0:T(8,128)(2,1)S(1)}, bf16[1,1024,128]{2,1,0:T(8,128)(2,1)}, bf16[1,1024,128]{2,1,0:T(8,128)(2,1)}, bf16[1...) fusion(bf16[1024,2048]{1,0:T(8,128)(2,1)} %param.8, ...), kind=kLoop, calls=%fused_computation.25 | loop fusion | bytes 16777280 | tf_op jit(solution)/shard_map/stack | solution.py:104
  7.5 3.7 %collective-permute-start.5 = (bf16[2,1024,128]{2,1,0:T(8,128)(2,1)}, bf16[2,1024,128]{2,1,0:T(8,128)(2,1)}, u32[]{:S(2)}, u32[]{:S(2)}) collective-permute-start(bf16[2,1024,128]{2,1,0:T(8,128)(2,1)} %pad_maximum_fusion.5), channel_id=1, source_target_pairs={{0,10},{1,11},{2,8},{3,9},{4,14},{5,15},{6,12},{7,13},{8,2},{9,3},... | collective-permute-start | bytes 1572872 | tf_op jit(solution)/shard_map/ppermute | solution.py:112
  13.0 2.7 %collective-permute-start.7 = (bf16[2,1024,128]{2,1,0:T(8,128)(2,1)}, bf16[2,1024,128]{2,1,0:T(8,128)(2,1)}, u32[]{:S(2)}, u32[]{:S(2)}) collective-permute-start(bf16[2,1024,128]{2,1,0:T(8,128)(2,1)} %pad_maximum_fusion.7), channel_id=1, source_target_pairs={{0,8},{1,9},{2,10},{3,11},{4,12},{5,13},{6,14},{7,15},{8,0},{9,1},... | collective-permute-start | bytes 1572872 | tf_op jit(solution)/shard_map/ppermute | solution.py:112
  16.5 2.6 %collective-permute-start.8 = (bf16[2,1024,128]{2,1,0:T(8,128)(2,1)}, bf16[2,1024,128]{2,1,0:T(8,128)(2,1)}, u32[]{:S(2)}, u32[]{:S(2)}) collective-permute-start(bf16[2,1024,128]{2,1,0:T(8,128)(2,1)} %pad_maximum_fusion.8), channel_id=1, source_target_pairs={{0,7},{1,6},{2,5},{3,4},{4,3},{5,2},{6,1},{7,0},{8,15},{9,14},{10,... | collective-permute-start | bytes 1572872 | tf_op jit(solution)/shard_map/ppermute | solution.py:112
  20.0 2.1 collective-permute-start.9
  29.0 1.9 pad_maximum_fusion
  47.5 10.7 %collective-permute-done.8.k_ref.v_ref = bf16[2,1024,128]{2,1,0:T(8,128)(2,1)} collective-permute-done((bf16[2,1024,128]{2,1,0:T(8,128)(2,1)}, bf16[2,1024,128]{2,1,0:T(8,128)(2,1)}, u32[]{:S(2)}, u32[]{:S(2)}) %collective-permute-start.8) | collective-permute-done | bytes 524320 | tf_op jit(solution)/shard_map/ppermute | solution.py:112
  60.6 11.1 %collective-permute-done.9.k_ref.v_ref = bf16[2,1024,128]{2,1,0:T(8,128)(2,1)} collective-permute-done((bf16[2,1024,128]{2,1,0:T(8,128)(2,1)}, bf16[2,1024,128]{2,1,0:T(8,128)(2,1)}, u32[]{:S(2)}, u32[]{:S(2)}) %collective-permute-start.9) | collective-permute-done | bytes 524320 | tf_op jit(solution)/shard_map/ppermute | solution.py:112
  75.3 4.7 %collective-permute-done.10.k_ref.v_ref = bf16[2,1024,128]{2,1,0:T(8,128)(2,1)S(1)} collective-permute-done((bf16[2,1024,128]{2,1,0:T(8,128)(2,1)}, bf16[2,1024,128]{2,1,0:T(8,128)(2,1)S(1)}, u32[]{:S(2)}, u32[]{:S(2)}) %collective-permute-start.10) | collective-permute-done | bytes 524320 | tf_op jit(solution)/shard_map/ppermute | solution.py:112
  80.1 4.5 %collective-permute-start.4 = (bf16[2,1024,128]{2,1,0:T(8,128)(2,1)}, bf16[2,1024,128]{2,1,0:T(8,128)(2,1)}, u32[]{:S(2)}, u32[]{:S(2)}) collective-permute-start(bf16[2,1024,128]{2,1,0:T(8,128)(2,1)} %pad_maximum_fusion.4), channel_id=1, source_target_pairs={{0,11},{1,10},{2,9},{3,8},{4,15},{5,14},{6,13},{7,12},{8,3},{9,2},... | collective-permute-start | bytes 1572872 | tf_op jit(solution)/shard_map/ppermute | solution.py:112
  86.3 5.6 %shard_map.55 = (f32[1024,1]{1,0:T(8,128)}, f32[1024,128]{1,0:T(8,128)}) custom-call(s32[3]{0:T(128)} %pad_add_fusion.sc_ref, bf16[1024,128]{1,0:T(8,128)(2,1)} %bitcast.108, bf16[2,1024,128]{2,1,0:T(8,128)(2,1)} %pad_maximum_fusion.15.k_ref.v_ref, ...), custom_call_target="tpu_custom_call", output_to_operand_aliasing={{0}: (4, {}), {1}: (5, {})} | custom-call | flops 536870912 | bytes 1843200 | tf_op jit(solution)/shard_map/pallas_call | solution.py:73
  91.9 2.2 collective-permute-start.3
  94.1 5.6 %shard_map.56 = (f32[1024,1]{1,0:T(8,128)}, f32[1024,128]{1,0:T(8,128)}) custom-call(s32[3]{0:T(128)} %pad_add_fusion.1.sc_ref, bf16[1024,128]{1,0:T(8,128)(2,1)} %bitcast.109, bf16[2,1024,128]{2,1,0:T(8,128)(2,1)} %collective-permute-done.14.k_ref.v_ref, ...), custom_call_target="tpu_custom_call", output_to_operand_aliasing={{0}: (4, {}), {1}: (5, {})} | custom-call | flops 536870912 | bytes 1843200 | tf_op jit(solution)/shard_map/pallas_call | solution.py:73
  99.8 5.8 %shard_map.57 = (f32[1024,1]{1,0:T(8,128)}, f32[1024,128]{1,0:T(8,128)}) custom-call(s32[3]{0:T(128)} %pad_add_fusion.2.sc_ref, bf16[1024,128]{1,0:T(8,128)(2,1)} %bitcast.110, bf16[2,1024,128]{2,1,0:T(8,128)(2,1)} %collective-permute-done.13.k_ref.v_ref, ...), custom_call_target="tpu_custom_call", output_to_operand_aliasing={{0}: (4, {}), {1}: (5, {})} | custom-call | flops 536870912 | bytes 1843200 | tf_op jit(solution)/shard_map/pallas_call | solution.py:73
  107.5 5.6 %shard_map.58 = (f32[1024,1]{1,0:T(8,128)}, f32[1024,128]{1,0:T(8,128)}) custom-call(s32[3]{0:T(128)} %pad_add_fusion.3.sc_ref, bf16[1024,128]{1,0:T(8,128)(2,1)} %bitcast.111, bf16[2,1024,128]{2,1,0:T(8,128)(2,1)} %collective-permute-done.12.k_ref.v_ref, ...), custom_call_target="tpu_custom_call", output_to_operand_aliasing={{0}: (4, {}), {1}: (5, {})} | custom-call | flops 536870912 | bytes 1843200 | tf_op jit(solution)/shard_map/pallas_call | solution.py:73
  113.1 4.4 %collective-permute-start = (bf16[2,1024,128]{2,1,0:T(8,128)(2,1)S(1)}, bf16[2,1024,128]{2,1,0:T(8,128)(2,1)}, u32[]{:S(2)}, u32[]{:S(2)}) collective-permute-start(bf16[2,1024,128]{2,1,0:T(8,128)(2,1)S(1)} %copy-done.11), channel_id=1, source_target_pairs={{0,15},{1,14},{2,13},{3,12},{4,11},{5,10},{6,9},{7,8},{8,7},{9,6},... | collective-permute-start | bytes 1572872 | tf_op jit(solution)/shard_map/ppermute | solution.py:112
  117.5 5.8 %shard_map.59 = (f32[1024,1]{1,0:T(8,128)}, f32[1024,128]{1,0:T(8,128)}) custom-call(s32[3]{0:T(128)} %pad_add_fusion.4.sc_ref, bf16[1024,128]{1,0:T(8,128)(2,1)} %bitcast.112, bf16[2,1024,128]{2,1,0:T(8,128)(2,1)} %collective-permute-done.11.k_ref.v_ref, ...), custom_call_target="tpu_custom_call", output_to_operand_aliasing={{0}: (4, {}), {1}: (5, {})} | custom-call | flops 536870912 | bytes 1843200 | tf_op jit(solution)/shard_map/pallas_call | solution.py:73
  123.3 5.6 %shard_map.60 = (f32[1024,1]{1,0:T(8,128)}, f32[1024,128]{1,0:T(8,128)}) custom-call(s32[3]{0:T(128)} %pad_add_fusion.5.sc_ref, bf16[1024,128]{1,0:T(8,128)(2,1)} %bitcast.113, bf16[2,1024,128]{2,1,0:T(8,128)(2,1)} %copy-done.13, bf16[2,1024,128]{2,1,0:T(8,128)(2,1)} %copy-done.13, ...), custom_call_target="tpu_custom_call", output_to_operand_aliasing={{0}: (4, {}), {1}: (5, {})} | custom-call | flops 536870912 | bytes 1843200 | tf_op jit(solution)/shard_map/pallas_call | solution.py:73
  128.9 5.6 %shard_map.61 = (f32[1024,1]{1,0:T(8,128)}, f32[1024,128]{1,0:T(8,128)}) custom-call(s32[3]{0:T(128)} %pad_add_fusion.6.sc_ref, bf16[1024,128]{1,0:T(8,128)(2,1)} %bitcast.114, bf16[2,1024,128]{2,1,0:T(8,128)(2,1)} %collective-permute-done.9.k_ref.v_ref, ...), custom_call_target="tpu_custom_call", output_to_operand_aliasing={{0}: (4, {}), {1}: (5, {})} | custom-call | flops 536870912 | bytes 1843200 | tf_op jit(solution)/shard_map/pallas_call | solution.py:73
  134.5 5.6 %shard_map.62 = (f32[1024,1]{1,0:T(8,128)}, f32[1024,128]{1,0:T(8,128)}) custom-call(s32[3]{0:T(128)} %pad_add_fusion.7.sc_ref, bf16[1024,128]{1,0:T(8,128)(2,1)} %bitcast.115, bf16[2,1024,128]{2,1,0:T(8,128)(2,1)} %collective-permute-done.8.k_ref.v_ref, ...), custom_call_target="tpu_custom_call", output_to_operand_aliasing={{0}: (4, {}), {1}: (5, {})} | custom-call | flops 536870912 | bytes 1843200 | tf_op jit(solution)/shard_map/pallas_call | solution.py:73
  140.2 5.6 %shard_map.63 = (f32[1024,1]{1,0:T(8,128)}, f32[1024,128]{1,0:T(8,128)}) custom-call(s32[3]{0:T(128)} %pad_add_fusion.8.sc_ref, bf16[1024,128]{1,0:T(8,128)(2,1)} %bitcast.116, bf16[2,1024,128]{2,1,0:T(8,128)(2,1)} %collective-permute-done.7.k_ref.v_ref, ...), custom_call_target="tpu_custom_call", output_to_operand_aliasing={{0}: (4, {}), {1}: (5, {})} | custom-call | flops 536870912 | bytes 1843200 | tf_op jit(solution)/shard_map/pallas_call | solution.py:73
  145.8 5.6 %shard_map.64 = (f32[1024,1]{1,0:T(8,128)}, f32[1024,128]{1,0:T(8,128)}) custom-call(s32[3]{0:T(128)} %pad_add_fusion.9.sc_ref, bf16[1024,128]{1,0:T(8,128)(2,1)} %bitcast.117, bf16[2,1024,128]{2,1,0:T(8,128)(2,1)} %collective-permute-done.6.k_ref.v_ref, ...), custom_call_target="tpu_custom_call", output_to_operand_aliasing={{0}: (4, {}), {1}: (5, {})} | custom-call | flops 536870912 | bytes 1843200 | tf_op jit(solution)/shard_map/pallas_call | solution.py:73
  151.4 5.6 %shard_map.65 = (f32[1024,1]{1,0:T(8,128)}, f32[1024,128]{1,0:T(8,128)}) custom-call(s32[3]{0:T(128)} %pad_add_fusion.10.sc_ref, bf16[1024,128]{1,0:T(8,128)(2,1)} %bitcast.118, bf16[2,1024,128]{2,1,0:T(8,128)(2,1)} %collective-permute-done.5.k_ref.v_ref, ...), custom_call_target="tpu_custom_call", output_to_operand_aliasing={{0}: (4, {}), {1}: (5, {})} | custom-call | flops 536870912 | bytes 1843200 | tf_op jit(solution)/shard_map/pallas_call | solution.py:73
  157.0 5.6 %shard_map.66 = (f32[1024,1]{1,0:T(8,128)}, f32[1024,128]{1,0:T(8,128)}) custom-call(s32[3]{0:T(128)} %pad_add_fusion.11.sc_ref, bf16[1024,128]{1,0:T(8,128)(2,1)} %bitcast.119, bf16[2,1024,128]{2,1,0:T(8,128)(2,1)} %collective-permute-done.4.k_ref.v_ref, ...), custom_call_target="tpu_custom_call", output_to_operand_aliasing={{0}: (4, {}), {1}: (5, {})} | custom-call | flops 536870912 | bytes 1843200 | tf_op jit(solution)/shard_map/pallas_call | solution.py:73
  162.7 5.6 %shard_map.67 = (f32[1024,1]{1,0:T(8,128)}, f32[1024,128]{1,0:T(8,128)}) custom-call(s32[3]{0:T(128)} %pad_add_fusion.12.sc_ref, bf16[1024,128]{1,0:T(8,128)(2,1)} %bitcast.120, bf16[2,1024,128]{2,1,0:T(8,128)(2,1)} %collective-permute-done.3.k_ref.v_ref, ...), custom_call_target="tpu_custom_call", output_to_operand_aliasing={{0}: (4, {}), {1}: (5, {})} | custom-call | flops 536870912 | bytes 1843200 | tf_op jit(solution)/shard_map/pallas_call | solution.py:73
  168.3 5.7 %shard_map.68 = (f32[1024,1]{1,0:T(8,128)}, f32[1024,128]{1,0:T(8,128)}) custom-call(s32[3]{0:T(128)} %pad_add_fusion.13.sc_ref, bf16[1024,128]{1,0:T(8,128)(2,1)} %bitcast.121, bf16[2,1024,128]{2,1,0:T(8,128)(2,1)} %collective-permute-done.2.k_ref.v_ref, ...), custom_call_target="tpu_custom_call", output_to_operand_aliasing={{0}: (4, {}), {1}: (5, {})} | custom-call | flops 536870912 | bytes 1843200 | tf_op jit(solution)/shard_map/pallas_call | solution.py:73
  174.0 5.6 %shard_map.69 = (f32[1024,1]{1,0:T(8,128)}, f32[1024,128]{1,0:T(8,128)}) custom-call(s32[3]{0:T(128)} %pad_add_fusion.14.sc_ref, bf16[1024,128]{1,0:T(8,128)(2,1)} %bitcast.122, bf16[2,1024,128]{2,1,0:T(8,128)(2,1)} %collective-permute-done.1.k_ref.v_ref, ...), custom_call_target="tpu_custom_call", output_to_operand_aliasing={{0}: (4, {}), {1}: (5, {})} | custom-call | flops 536870912 | bytes 1843200 | tf_op jit(solution)/shard_map/pallas_call | solution.py:73
  179.6 5.6 %shard_map.70 = (f32[1024,1]{1,0:T(8,128)}, f32[1024,128]{1,0:T(8,128)}) custom-call(s32[3]{0:T(128)} %pad_add_fusion.15.sc_ref, bf16[1024,128]{1,0:T(8,128)(2,1)} %bitcast.123, bf16[2,1024,128]{2,1,0:T(8,128)(2,1)} %collective-permute-done.k_ref.v_ref, ...), custom_call_target="tpu_custom_call", output_to_operand_aliasing={{0}: (4, {}), {1}: (5, {})} | custom-call | flops 536870912 | bytes 1843200 | tf_op jit(solution)/shard_map/pallas_call | solution.py:73
  188.2 2.9 %fusion.1 = f32[8,32,4608]{2,1,0:T(8,128)} fusion(bf16[256,4608]{1,0:T(8,128)(2,1)S(1)} %copy-done, bf16[8,2,32,256]{3,2,1,0:T(8,128)(2,1)S(1)} %reshape_reshape.3, s32[]{:T(128)S(6)} %select_n.88), kind=kOutput, calls=%fused_computation.3 | convolution fusion | flops 603979776 | bytes 7208964 | tf_op jit(solution)/shard_map/cra,ad->crd/dot_general | solution.py:130
  191.1 8.2 %collective-permute-done.15 = f32[8,32,4608]{2,1,0:T(8,128)} collective-permute-done((f32[8,32,4608]{2,1,0:T(8,128)}, f32[8,32,4608]{2,1,0:T(8,128)}, u32[]{:S(2)}, u32[]{:S(2)}) %collective-permute-start.15) | collective-permute-done | bytes 4718624 | tf_op jit(solution)/shard_map/ppermute | solution.py:133
  199.4 3.1 %fusion = bf16[8,32,4608]{2,1,0:T(8,128)(2,1)S(1)} fusion(f32[8,32,4608]{2,1,0:T(8,128)} %collective-permute-done.15, bf16[256,4608]{1,0:T(8,128)(2,1)S(1)} %copy-done, bf16[8,2,32,256]{3,2,1,0:T(8,128)(2,1)S(1)} %reshape_reshape.3, s32[]{:T(128)S(6)} %select_n.87), kind=kOutput, calls=%fused_computation.1 | convolution fusion | flops 606339072 | bytes 9568260 | tf_op jit(solution)/shard_map/cra,ad->crd/dot_general | solution.py:130
  202.5 34.9 %all_to_all.5 = bf16[8,32,4608]{2,1,0:T(8,128)(2,1)S(1)} all-to-all(bf16[8,32,4608]{2,1,0:T(8,128)(2,1)S(1)} %fusion), channel_id=1, replica_groups=mesh['pb'=8,'kx'=8,'kc'=2] {'kx'}, dimensions={0} | all-to-all | bytes 4718592 | tf_op jit(solution)/shard_map/all_to_all | solution.py:135
  (88 shorter events, 40.9 us)
Async XLA Ops:
  0.0 188.2 %copy-start = (bf16[256,4608]{1,0:T(8,128)(2,1)S(1)}, bf16[256,4608]{1,0:T(8,128)(2,1)}, u32[]{:S(2)}) copy-start(bf16[256,4608]{1,0:T(8,128)(2,1)} %param.9) | copy-start | bytes 7077892
  7.5 36.7 %collective-permute-start.5 = (bf16[2,1024,128]{2,1,0:T(8,128)(2,1)}, bf16[2,1024,128]{2,1,0:T(8,128)(2,1)}, u32[]{:S(2)}, u32[]{:S(2)}) collective-permute-start(bf16[2,1024,128]{2,1,0:T(8,128)(2,1)} %pad_maximum_fusion.5), channel_id=1, source_target_pairs={{0,10},{1,11},{2,8},{3,9},{4,14},{5,15},{6,12},{7,13},{8,2},{9,3},... | collective-permute-start | bytes 1572872 | tf_op jit(solution)/shard_map/ppermute | solution.py:112
  12.1 32.1 %collective-permute-start.6 = (bf16[2,1024,128]{2,1,0:T(8,128)(2,1)}, bf16[2,1024,128]{2,1,0:T(8,128)(2,1)}, u32[]{:S(2)}, u32[]{:S(2)}) collective-permute-start(bf16[2,1024,128]{2,1,0:T(8,128)(2,1)} %pad_maximum_fusion.6), channel_id=1, source_target_pairs={{0,9},{1,8},{2,11},{3,10},{4,13},{5,12},{6,15},{7,14},{8,1},{9,0},... | collective-permute-start | bytes 1572872 | tf_op jit(solution)/shard_map/ppermute | solution.py:112
  13.0 34.3 %collective-permute-start.7 = (bf16[2,1024,128]{2,1,0:T(8,128)(2,1)}, bf16[2,1024,128]{2,1,0:T(8,128)(2,1)}, u32[]{:S(2)}, u32[]{:S(2)}) collective-permute-start(bf16[2,1024,128]{2,1,0:T(8,128)(2,1)} %pad_maximum_fusion.7), channel_id=1, source_target_pairs={{0,8},{1,9},{2,10},{3,11},{4,12},{5,13},{6,14},{7,15},{8,0},{9,1},... | collective-permute-start | bytes 1572872 | tf_op jit(solution)/shard_map/ppermute | solution.py:112
  16.5 41.6 %collective-permute-start.8 = (bf16[2,1024,128]{2,1,0:T(8,128)(2,1)}, bf16[2,1024,128]{2,1,0:T(8,128)(2,1)}, u32[]{:S(2)}, u32[]{:S(2)}) collective-permute-start(bf16[2,1024,128]{2,1,0:T(8,128)(2,1)} %pad_maximum_fusion.8), channel_id=1, source_target_pairs={{0,7},{1,6},{2,5},{3,4},{4,3},{5,2},{6,1},{7,0},{8,15},{9,14},{10,... | collective-permute-start | bytes 1572872 | tf_op jit(solution)/shard_map/ppermute | solution.py:112
  20.0 51.6 %collective-permute-start.9 = (bf16[2,1024,128]{2,1,0:T(8,128)(2,1)}, bf16[2,1024,128]{2,1,0:T(8,128)(2,1)}, u32[]{:S(2)}, u32[]{:S(2)}) collective-permute-start(bf16[2,1024,128]{2,1,0:T(8,128)(2,1)} %pad_maximum_fusion.9), channel_id=1, source_target_pairs={{0,6},{1,7},{2,4},{3,5},{4,2},{5,3},{6,0},{7,1},{8,14},{9,15},{10,... | collective-permute-start | bytes 1572872 | tf_op jit(solution)/shard_map/ppermute | solution.py:112
  22.8 13.8 %copy-start.9 = (bf16[1,1024,128]{2,1,0:T(8,128)(2,1)S(1)}, bf16[1,1024,128]{2,1,0:T(8,128)(2,1)}, u32[]{:S(2)}) copy-start(bf16[1,1024,128]{2,1,0:T(8,128)(2,1)} %get-tuple-element.95) | copy-start | bytes 786436
  22.8 13.8 %copy-start.10 = (bf16[1,1024,128]{2,1,0:T(8,128)(2,1)S(1)}, bf16[1,1024,128]{2,1,0:T(8,128)(2,1)}, u32[]{:S(2)}) copy-start(bf16[1,1024,128]{2,1,0:T(8,128)(2,1)} %get-tuple-element.106) | copy-start | bytes 786436
  22.8 14.6 %copy-start.7 = (bf16[1,1024,128]{2,1,0:T(8,128)(2,1)S(1)}, bf16[1,1024,128]{2,1,0:T(8,128)(2,1)}, u32[]{:S(2)}) copy-start(bf16[1,1024,128]{2,1,0:T(8,128)(2,1)} %get-tuple-element.89) | copy-start | bytes 786436
  22.8 14.6 %copy-start.8 = (bf16[1,1024,128]{2,1,0:T(8,128)(2,1)S(1)}, bf16[1,1024,128]{2,1,0:T(8,128)(2,1)}, u32[]{:S(2)}) copy-start(bf16[1,1024,128]{2,1,0:T(8,128)(2,1)} %get-tuple-element.112) | copy-start | bytes 786436
  22.8 15.4 %copy-start.5 = (bf16[1,1024,128]{2,1,0:T(8,128)(2,1)S(1)}, bf16[1,1024,128]{2,1,0:T(8,128)(2,1)}, u32[]{:S(2)}) copy-start(bf16[1,1024,128]{2,1,0:T(8,128)(2,1)} %get-tuple-element.88) | copy-start | bytes 786436
  22.8 15.4 %copy-start.6 = (bf16[1,1024,128]{2,1,0:T(8,128)(2,1)S(1)}, bf16[1,1024,128]{2,1,0:T(8,128)(2,1)}, u32[]{:S(2)}) copy-start(bf16[1,1024,128]{2,1,0:T(8,128)(2,1)} %get-tuple-element.113) | copy-start | bytes 786436
  22.8 16.3 %copy-start.3 = (bf16[1,1024,128]{2,1,0:T(8,128)(2,1)S(1)}, bf16[1,1024,128]{2,1,0:T(8,128)(2,1)}, u32[]{:S(2)}) copy-start(bf16[1,1024,128]{2,1,0:T(8,128)(2,1)} %get-tuple-element.87) | copy-start | bytes 786436
  22.8 16.3 %copy-start.4 = (bf16[1,1024,128]{2,1,0:T(8,128)(2,1)S(1)}, bf16[1,1024,128]{2,1,0:T(8,128)(2,1)}, u32[]{:S(2)}) copy-start(bf16[1,1024,128]{2,1,0:T(8,128)(2,1)} %get-tuple-element.114) | copy-start | bytes 786436
  29.0 11.0 %copy-start.1 = (bf16[1,1024,128]{2,1,0:T(8,128)(2,1)S(1)}, bf16[1,1024,128]{2,1,0:T(8,128)(2,1)}, u32[]{:S(2)}) copy-start(bf16[1,1024,128]{2,1,0:T(8,128)(2,1)} %get-tuple-element.86) | copy-start | bytes 786436
  29.0 11.0 %copy-start.2 = (bf16[1,1024,128]{2,1,0:T(8,128)(2,1)S(1)}, bf16[1,1024,128]{2,1,0:T(8,128)(2,1)}, u32[]{:S(2)}) copy-start(bf16[1,1024,128]{2,1,0:T(8,128)(2,1)} %get-tuple-element.115) | copy-start | bytes 786436
  44.2 35.8 %collective-permute-start.10 = (bf16[2,1024,128]{2,1,0:T(8,128)(2,1)}, bf16[2,1024,128]{2,1,0:T(8,128)(2,1)S(1)}, u32[]{:S(2)}, u32[]{:S(2)}) collective-permute-start(bf16[2,1024,128]{2,1,0:T(8,128)(2,1)} %pad_maximum_fusion.10), channel_id=1, source_target_pairs={{0,5},{1,4},{2,7},{3,6},{4,1},{5,0},{6,3},{7,2},{8,13},{9,12},{10,... | collective-permute-start | bytes 1572872 | tf_op jit(solution)/shard_map/ppermute | solution.py:112
  44.2 47.7 %collective-permute-start.14 = (bf16[2,1024,128]{2,1,0:T(8,128)(2,1)}, bf16[2,1024,128]{2,1,0:T(8,128)(2,1)}, u32[]{:S(2)}, u32[]{:S(2)}) collective-permute-start(bf16[2,1024,128]{2,1,0:T(8,128)(2,1)} %pad_maximum_fusion.14), channel_id=1, source_target_pairs={{0,1},{1,0},{2,3},{3,2},{4,5},{5,4},{6,7},{7,6},{8,9},{9,8},{10,11... | collective-permute-start | bytes 1572872 | tf_op jit(solution)/shard_map/ppermute | solution.py:112
  47.3 58.3 %collective-permute-start.12 = (bf16[2,1024,128]{2,1,0:T(8,128)(2,1)}, bf16[2,1024,128]{2,1,0:T(8,128)(2,1)}, u32[]{:S(2)}, u32[]{:S(2)}) collective-permute-start(bf16[2,1024,128]{2,1,0:T(8,128)(2,1)} %pad_maximum_fusion.12), channel_id=1, source_target_pairs={{0,3},{1,2},{2,1},{3,0},{4,7},{5,6},{6,5},{7,4},{8,11},{9,10},{10,... | collective-permute-start | bytes 1572872 | tf_op jit(solution)/shard_map/ppermute | solution.py:112
  58.2 41.6 %collective-permute-start.13 = (bf16[2,1024,128]{2,1,0:T(8,128)(2,1)}, bf16[2,1024,128]{2,1,0:T(8,128)(2,1)}, u32[]{:S(2)}, u32[]{:S(2)}) collective-permute-start(bf16[2,1024,128]{2,1,0:T(8,128)(2,1)} %pad_maximum_fusion.13), channel_id=1, source_target_pairs={{0,2},{1,3},{2,0},{3,1},{4,6},{5,7},{6,4},{7,5},{8,10},{9,11},{10,... | collective-permute-start | bytes 1572872 | tf_op jit(solution)/shard_map/ppermute | solution.py:112
  71.6 41.5 %collective-permute-start.11 = (bf16[2,1024,128]{2,1,0:T(8,128)(2,1)}, bf16[2,1024,128]{2,1,0:T(8,128)(2,1)}, u32[]{:S(2)}, u32[]{:S(2)}) collective-permute-start(bf16[2,1024,128]{2,1,0:T(8,128)(2,1)} %pad_maximum_fusion.11), channel_id=1, source_target_pairs={{0,4},{1,5},{2,6},{3,7},{4,0},{5,1},{6,2},{7,3},{8,12},{9,13},{10,... | collective-permute-start | bytes 1572872 | tf_op jit(solution)/shard_map/ppermute | solution.py:112
  80.1 14.0 %copy-start.13 = (bf16[2,1024,128]{2,1,0:T(8,128)(2,1)}, bf16[2,1024,128]{2,1,0:T(8,128)(2,1)S(1)}, u32[]{:S(2)}) copy-start(bf16[2,1024,128]{2,1,0:T(8,128)(2,1)S(1)} %collective-permute-done.10.k_ref.v_ref) | copy-start | bytes 1572868
  80.1 77.0 %collective-permute-start.4 = (bf16[2,1024,128]{2,1,0:T(8,128)(2,1)}, bf16[2,1024,128]{2,1,0:T(8,128)(2,1)}, u32[]{:S(2)}, u32[]{:S(2)}) collective-permute-start(bf16[2,1024,128]{2,1,0:T(8,128)(2,1)} %pad_maximum_fusion.4), channel_id=1, source_target_pairs={{0,11},{1,10},{2,9},{3,8},{4,15},{5,14},{6,13},{7,12},{8,3},{9,2},... | collective-permute-start | bytes 1572872 | tf_op jit(solution)/shard_map/ppermute | solution.py:112
  91.9 13.7 %copy-start.12 = (bf16[2,1024,128]{2,1,0:T(8,128)(2,1)S(1)}, bf16[2,1024,128]{2,1,0:T(8,128)(2,1)}, u32[]{:S(2)}) copy-start(bf16[2,1024,128]{2,1,0:T(8,128)(2,1)} %pad_maximum_fusion.1) | copy-start | bytes 1572868
  91.9 70.7 %collective-permute-start.3 = (bf16[2,1024,128]{2,1,0:T(8,128)(2,1)}, bf16[2,1024,128]{2,1,0:T(8,128)(2,1)}, u32[]{:S(2)}, u32[]{:S(2)}) collective-permute-start(bf16[2,1024,128]{2,1,0:T(8,128)(2,1)} %pad_maximum_fusion.3), channel_id=1, source_target_pairs={{0,12},{1,13},{2,14},{3,15},{4,8},{5,9},{6,10},{7,11},{8,4},{9,5},... | collective-permute-start | bytes 1572872 | tf_op jit(solution)/shard_map/ppermute | solution.py:112
  99.7 13.4 %copy-start.11 = (bf16[2,1024,128]{2,1,0:T(8,128)(2,1)S(1)}, bf16[2,1024,128]{2,1,0:T(8,128)(2,1)}, u32[]{:S(2)}) copy-start(bf16[2,1024,128]{2,1,0:T(8,128)(2,1)} %pad_maximum_fusion) | copy-start | bytes 1572868
  99.7 68.6 %collective-permute-start.2 = (bf16[2,1024,128]{2,1,0:T(8,128)(2,1)}, bf16[2,1024,128]{2,1,0:T(8,128)(2,1)}, u32[]{:S(2)}, u32[]{:S(2)}) collective-permute-start(bf16[2,1024,128]{2,1,0:T(8,128)(2,1)} %pad_maximum_fusion.2), channel_id=1, source_target_pairs={{0,13},{1,12},{2,15},{3,14},{4,9},{5,8},{6,11},{7,10},{8,5},{9,4},... | collective-permute-start | bytes 1572872 | tf_op jit(solution)/shard_map/ppermute | solution.py:112
  105.6 68.4 %collective-permute-start.1 = (bf16[2,1024,128]{2,1,0:T(8,128)(2,1)S(1)}, bf16[2,1024,128]{2,1,0:T(8,128)(2,1)}, u32[]{:S(2)}, u32[]{:S(2)}) collective-permute-start(bf16[2,1024,128]{2,1,0:T(8,128)(2,1)S(1)} %copy-done.12), channel_id=1, source_target_pairs={{0,14},{1,15},{2,12},{3,13},{4,10},{5,11},{6,8},{7,9},{8,6},{9,7},... | collective-permute-start | bytes 1572872 | tf_op jit(solution)/shard_map/ppermute | solution.py:112
  113.1 66.5 %collective-permute-start = (bf16[2,1024,128]{2,1,0:T(8,128)(2,1)S(1)}, bf16[2,1024,128]{2,1,0:T(8,128)(2,1)}, u32[]{:S(2)}, u32[]{:S(2)}) collective-permute-start(bf16[2,1024,128]{2,1,0:T(8,128)(2,1)S(1)} %copy-done.11), channel_id=1, source_target_pairs={{0,15},{1,14},{2,13},{3,12},{4,11},{5,10},{6,9},{7,8},{8,7},{9,6},... | collective-permute-start | bytes 1572872 | tf_op jit(solution)/shard_map/ppermute | solution.py:112
  191.1 8.3 %collective-permute-start.15 = (f32[8,32,4608]{2,1,0:T(8,128)}, f32[8,32,4608]{2,1,0:T(8,128)}, u32[]{:S(2)}, u32[]{:S(2)}) collective-permute-start(f32[8,32,4608]{2,1,0:T(8,128)} %fusion.1), channel_id=1, source_target_pairs={{0,1},{1,0},{2,3},{3,2},{4,5},{5,4},{6,7},{7,6},{8,9},{9,8},{10,11... | collective-permute-start | bytes 14155784 | tf_op jit(solution)/shard_map/ppermute | solution.py:133

commit v11 on v4

--- a/solution.py
+++ b/solution.py
@@ -50,9 +50,9 @@
         update(True)
 
 
-def attend_kernel(scalars, q, block, total, summed):
+def attend_kernel(scalars, q, key_part, value_part, total, summed):
     n_q, hd = q.shape
-    n_k = block.shape[1]
+    n_k = key_part.shape[0]
     tq = min(TQ, n_q)
     row = lambda i, sc: (i, 0)
     grid_spec = pltpu.PrefetchScalarGridSpec(
@@ -60,8 +60,8 @@
         grid=(n_q // tq,),
         in_specs=[
             pl.BlockSpec((tq, hd), row),
-            pl.BlockSpec((None, n_k, hd), lambda i, sc: (0, 0, 0)),
-            pl.BlockSpec((None, n_k, hd), lambda i, sc: (1, 0, 0)),
+            pl.BlockSpec((n_k, hd), lambda i, sc: (0, 0)),
+            pl.BlockSpec((n_k, hd), lambda i, sc: (0, 0)),
             pl.BlockSpec((tq, 1), row),
             pl.BlockSpec((tq, hd), row),
         ],
@@ -83,7 +83,7 @@
             transcendentals=2 * n_q * n_k,
             bytes_accessed=2 * (n_q + 2 * n_k) * hd + 8 * n_q * (hd + 1),
         ),
-    )(scalars, q, block, block, total, summed)
+    )(scalars, q, key_part, value_part, total, summed)
 
 
 def by_heads(queries, keys, values, row_first):
@@ -101,17 +101,14 @@
     for shift in range(n_kv):
         dest = me ^ shift
         src = dest
-        block = jnp.stack(
-            (
-                lax.dynamic_slice_in_dim(keys, dest * kv_feat, kv_feat, 1),
-                lax.dynamic_slice_in_dim(values, dest * kv_feat, kv_feat, 1),
-            ),
-            axis=0,
+        block = (
+            lax.dynamic_slice_in_dim(keys, dest * kv_feat, kv_feat, 1),
+            lax.dynamic_slice_in_dim(values, dest * kv_feat, kv_feat, 1),
         )
         if shift:
             block = lax.ppermute(block, KV, [(j, j ^ shift) for j in range(n_kv)])
         scalars = jnp.stack([row_first, src * key_dev, jnp.int32(rows_dev)]).astype(jnp.int32)
-        total, summed = attend_kernel(scalars, q_block, block, total, summed)
+        total, summed = attend_kernel(scalars, q_block, *block, total, summed)
     mixed = (summed / total).astype(jnp.bfloat16)
     return mixed.reshape(kv_local * group, rows_dev, HD).transpose(1, 0, 2).reshape(rows_dev, n_q // rows_dev * HD)
 

time: 236 us -> 250 us (1.059); the launches traced: 236 us -> 246 us
  starting transfers between devices: 24.7 us -> 50.6 us
  other arithmetic: 34.8 us -> 17.8 us
  Pallas kernels: 85 us -> 81.4 us
  blocking collectives: 40.4 us -> 43.8 us
    ppermute x15 -> x30, starting transfers between devices: 24.4 us -> 50.5 us  [by_heads(): block = lax.ppermute(block, KV, [(j, j ^ shift) for j in range(n_kv)])]
    another operation x16 -> x0, other arithmetic: 17 us -> none  [by_heads(): jnp.stack((lax.dynamic_slice_in_dim(keys, dest * kv_feat, kv_feat, 1), la...]
    dynamic_slice x0 -> x2, local copies, waits for them, and re-layouts: none -> 8.65 us  [the longest x1 4.34 us: by_heads(): lax.dynamic_slice_in_dim(keys, dest * kv_feat, kv_feat, 1)]
    another operation x1 -> x0, local copies, waits for them, and re-layouts: 6.65 us -> none  [by_heads(): jnp.stack((lax.dynamic_slice_in_dim(keys, dest * kv_feat, kv_feat, 1), la...]
    pallas_call x16, Pallas kernels: 85 us -> 81.4 us  [attend_kernel(): pl.pallas_call(block_kernel, grid_spec=grid_spec, out_shape=(jax.ShapeDty...]
    all_to_all x1, blocking collectives: 40.4 us -> 43.8 us  [per_device(): lax.all_to_all(on_chip.astype(jnp.bfloat16), 'kx', split_axis=0, concat_a...]
    ppermute x15 -> x30, waiting for transfers between devices: 25.7 us -> 25.8 us  [by_heads(): block = lax.ppermute(block, KV, [(j, j ^ shift) for j in range(n_kv)])]
  transfers between devices with their start and end apart: 16 -> 31, of which waited for: 5 -> 7; matrix products, arithmetic and copies ran while one was open for 12% -> 7% of each run, Pallas kernels for 34% -> 31%
where the time goes in v11:
time: 250 us; the launch traced here: 246 us
  Pallas kernels  81.4 us (33%)
  starting transfers between devices  50.6 us (20%)
  blocking collectives  43.8 us (18%)
  waiting for transfers between devices  34 us (14%)
  other arithmetic  17.8 us (7%)
  local copies, waits for them, and re-layouts  16.5 us (7%)
    pallas_call x16, Pallas kernels, attend_kernel(): pl.pallas_call(block_kernel, grid_spec=grid_spec, out_shape=(jax.ShapeDty...  81.4 us
    ppermute x30, starting transfers between devices, by_heads(): block = lax.ppermute(block, KV, [(j, j ^ shift) for j in range(n_kv)])  50.5 us
    all_to_all x1, blocking collectives, per_device(): lax.all_to_all(on_chip.astype(jnp.bfloat16), 'kx', split_axis=0, concat_a...  43.8 us
    ppermute x30, waiting for transfers between devices, by_heads(): block = lax.ppermute(block, KV, [(j, j ^ shift) for j in range(n_kv)])  25.8 us
    another operation x16, other arithmetic, by_heads(): jnp.stack([row_first, src * key_dev, jnp.int32(rows_dev)]).astype(jnp.int32)  9.86 us
    ppermute x1, waiting for transfers between devices, per_device(): on_chip = mine + lax.ppermute(theirs, 'kc', [(0, 1), (1, 0)])  8.16 us
  transfers between devices with their start and end apart: 31, of which 7 were waited for; matrix products, arithmetic and copies ran while one was open for 7% of the time, Pallas kernels for 31%

profile of v11, /device:TPU:120, one launch (start us, length us, event | category | flops | bytes accessed | tf_op | source)
XLA Modules:
  0.0 246.3 jit_solution(10881346411922114271)
XLA Ops:
  0.0 4.3 %constant_dynamic-slice_fusion.1 = (bf16[1024,128]{1,0:T(8,128)(2,1)}, bf16[1024,128]{1,0:T(8,128)(2,1)}, bf16[1024,128]{1,0:T(8,128)(2,1)}, bf16[1024,128]{1,0:...) fusion(bf16[1024,2048]{1,0:T(8,128)(2,1)} %param.7, ...), kind=kLoop, calls=%fused_computation.9 | loop fusion | bytes 8388672 | tf_op jit(solution)/shard_map/dynamic_slice | solution.py:105
  16.1 4.3 %constant_dynamic-slice_fusion = (bf16[1024,128]{1,0:T(8,128)(2,1)}, bf16[1024,128]{1,0:T(8,128)(2,1)}, bf16[1024,128]{1,0:T(8,128)(2,1)}, bf16[1024,128]{1,0:T(...) fusion(bf16[1024,2048]{1,0:T(8,128)(2,1)} %param.8, ...), kind=kLoop, calls=%fused_computation.8 | loop fusion | bytes 8388672 | tf_op jit(solution)/shard_map/dynamic_slice | solution.py:106
  23.8 3.0 %collective-permute-start.14 = (bf16[1024,128]{1,0:T(8,128)(2,1)}, bf16[1024,128]{1,0:T(8,128)(2,1)}, u32[]{:S(2)}, u32[]{:S(2)}) collective-permute-start(bf16[1024,128]{1,0:T(8,128)(2,1)} %get-tuple-element.92), channel_id=1, source_target_pairs={{0,8},{1,9},{2,10},{3,11},{4,12},{5,13},{6,14},{7,15},{8,0},{9,1},... | collective-permute-start | bytes 786440 | tf_op jit(solution)/shard_map/ppermute | solution.py:109
  28.1 3.7 %collective-permute-start.10 = (bf16[1024,128]{1,0:T(8,128)(2,1)}, bf16[1024,128]{1,0:T(8,128)(2,1)}, u32[]{:S(2)}, u32[]{:S(2)}) collective-permute-start(bf16[1024,128]{1,0:T(8,128)(2,1)} %get-tuple-element.94), channel_id=1, source_target_pairs={{0,10},{1,11},{2,8},{3,9},{4,14},{5,15},{6,12},{7,13},{8,2},{9,3},... | collective-permute-start | bytes 786440 | tf_op jit(solution)/shard_map/ppermute | solution.py:109
  37.3 4.1 %collective-permute-done.14.k_ref = bf16[1024,128]{1,0:T(8,128)(2,1)} collective-permute-done((bf16[1024,128]{1,0:T(8,128)(2,1)}, bf16[1024,128]{1,0:T(8,128)(2,1)}, u32[]{:S(2)}, u32[]{:S(2)}) %collective-permute-start.14) | collective-permute-done | bytes 262176 | tf_op jit(solution)/shard_map/ppermute | solution.py:109
  41.5 5.5 %collective-permute-done.12.k_ref = bf16[1024,128]{1,0:T(8,128)(2,1)} collective-permute-done((bf16[1024,128]{1,0:T(8,128)(2,1)}, bf16[1024,128]{1,0:T(8,128)(2,1)}, u32[]{:S(2)}, u32[]{:S(2)}) %collective-permute-start.12) | collective-permute-done | bytes 262176 | tf_op jit(solution)/shard_map/ppermute | solution.py:109
  47.7 5.6 %collective-permute-done.10.k_ref = bf16[1024,128]{1,0:T(8,128)(2,1)} collective-permute-done((bf16[1024,128]{1,0:T(8,128)(2,1)}, bf16[1024,128]{1,0:T(8,128)(2,1)}, u32[]{:S(2)}, u32[]{:S(2)}) %collective-permute-start.10) | collective-permute-done | bytes 262176 | tf_op jit(solution)/shard_map/ppermute | solution.py:109
  55.6 3.4 %collective-permute-done.8.k_ref = bf16[1024,128]{1,0:T(8,128)(2,1)} collective-permute-done((bf16[1024,128]{1,0:T(8,128)(2,1)}, bf16[1024,128]{1,0:T(8,128)(2,1)}, u32[]{:S(2)}, u32[]{:S(2)}) %collective-permute-start.8) | collective-permute-done | bytes 262176 | tf_op jit(solution)/shard_map/ppermute | solution.py:109
  64.0 5.4 %collective-permute-done.4.k_ref = bf16[1024,128]{1,0:T(8,128)(2,1)} collective-permute-done((bf16[1024,128]{1,0:T(8,128)(2,1)}, bf16[1024,128]{1,0:T(8,128)(2,1)}, u32[]{:S(2)}, u32[]{:S(2)}) %collective-permute-start.4) | collective-permute-done | bytes 262176 | tf_op jit(solution)/shard_map/ppermute | solution.py:109
  75.9 5.6 %shard_map.55 = (f32[1024,1]{1,0:T(8,128)}, f32[1024,128]{1,0:T(8,128)}) custom-call(s32[3]{0:T(128)} %pad_add_fusion.sc_ref, bf16[1024,128]{1,0:T(8,128)(2,1)} %bitcast.43, bf16[1024,128]{1,0:T(8,128)(2,1)} %get-tuple-element.85.k_ref, bf16[1024,128]{1,0:T(8,128)(2,1)} %get-tuple-element.69.v_ref, ...), custom_call_target="tpu_custom_call", output_to_operand_aliasing={{0}: (4, {}), {1}: (5, {})} | custom-call | flops 536870912 | bytes 1843200 | tf_op jit(solution)/shard_map/pallas_call | solution.py:73
  82.6 5.6 %shard_map.56 = (f32[1024,1]{1,0:T(8,128)}, f32[1024,128]{1,0:T(8,128)}) custom-call(s32[3]{0:T(128)} %pad_add_fusion.1.sc_ref, bf16[1024,128]{1,0:T(8,128)(2,1)} %bitcast.44, bf16[1024,128]{1,0:T(8,128)(2,1)} %collective-permute-done.28.k_ref, bf16[1024,128]{1,0:T(8,128)(2,1)} %collective-permute-done.29.v_ref, ...), custom_call_target="tpu_custom_call", output_to_operand_aliasing={{0}: (4, {}), {1}: (5, {})} | custom-call | flops 536870912 | bytes 1843200 | tf_op jit(solution)/shard_map/pallas_call | solution.py:73
  92.4 5.6 %shard_map.57 = (f32[1024,1]{1,0:T(8,128)}, f32[1024,128]{1,0:T(8,128)}) custom-call(s32[3]{0:T(128)} %pad_add_fusion.2.sc_ref, bf16[1024,128]{1,0:T(8,128)(2,1)} %bitcast.45, bf16[1024,128]{1,0:T(8,128)(2,1)} %collective-permute-done.26.k_ref, bf16[1024,128]{1,0:T(8,128)(2,1)} %collective-permute-done.27.v_ref, ...), custom_call_target="tpu_custom_call", output_to_operand_aliasing={{0}: (4, {}), {1}: (5, {})} | custom-call | flops 536870912 | bytes 1843200 | tf_op jit(solution)/shard_map/pallas_call | solution.py:73
  100.2 3.3 %collective-permute-start.7 = (bf16[1024,128]{1,0:T(8,128)(2,1)}, bf16[1024,128]{1,0:T(8,128)(2,1)}, u32[]{:S(2)}, u32[]{:S(2)}) collective-permute-start(bf16[1024,128]{1,0:T(8,128)(2,1)} %get-tuple-element.80), channel_id=1, source_target_pairs={{0,12},{1,13},{2,14},{3,15},{4,8},{5,9},{6,10},{7,11},{8,4},{9,5},... | collective-permute-start | bytes 786440 | tf_op jit(solution)/shard_map/ppermute | solution.py:109
  103.5 5.6 %shard_map.58 = (f32[1024,1]{1,0:T(8,128)}, f32[1024,128]{1,0:T(8,128)}) custom-call(s32[3]{0:T(128)} %pad_add_fusion.3.sc_ref, bf16[1024,128]{1,0:T(8,128)(2,1)} %bitcast.46, bf16[1024,128]{1,0:T(8,128)(2,1)} %collective-permute-done.24.k_ref, bf16[1024,128]{1,0:T(8,128)(2,1)} %collective-permute-done.25.v_ref, ...), custom_call_target="tpu_custom_call", output_to_operand_aliasing={{0}: (4, {}), {1}: (5, {})} | custom-call | flops 536870912 | bytes 1843200 | tf_op jit(solution)/shard_map/pallas_call | solution.py:73
  109.1 5.6 %shard_map.59 = (f32[1024,1]{1,0:T(8,128)}, f32[1024,128]{1,0:T(8,128)}) custom-call(s32[3]{0:T(128)} %pad_add_fusion.4.sc_ref, bf16[1024,128]{1,0:T(8,128)(2,1)} %bitcast.47, bf16[1024,128]{1,0:T(8,128)(2,1)} %collective-permute-done.22.k_ref, bf16[1024,128]{1,0:T(8,128)(2,1)} %collective-permute-done.23.v_ref, ...), custom_call_target="tpu_custom_call", output_to_operand_aliasing={{0}: (4, {}), {1}: (5, {})} | custom-call | flops 536870912 | bytes 1843200 | tf_op jit(solution)/shard_map/pallas_call | solution.py:73
  114.7 5.6 %shard_map.60 = (f32[1024,1]{1,0:T(8,128)}, f32[1024,128]{1,0:T(8,128)}) custom-call(s32[3]{0:T(128)} %pad_add_fusion.5.sc_ref, bf16[1024,128]{1,0:T(8,128)(2,1)} %bitcast.48, bf16[1024,128]{1,0:T(8,128)(2,1)} %collective-permute-done.20.k_ref, bf16[1024,128]{1,0:T(8,128)(2,1)} %collective-permute-done.21.v_ref, ...), custom_call_target="tpu_custom_call", output_to_operand_aliasing={{0}: (4, {}), {1}: (5, {})} | custom-call | flops 536870912 | bytes 1843200 | tf_op jit(solution)/shard_map/pallas_call | solution.py:73
  120.3 5.6 %shard_map.61 = (f32[1024,1]{1,0:T(8,128)}, f32[1024,128]{1,0:T(8,128)}) custom-call(s32[3]{0:T(128)} %pad_add_fusion.6.sc_ref, bf16[1024,128]{1,0:T(8,128)(2,1)} %bitcast.49, bf16[1024,128]{1,0:T(8,128)(2,1)} %collective-permute-done.18.k_ref, bf16[1024,128]{1,0:T(8,128)(2,1)} %collective-permute-done.19.v_ref, ...), custom_call_target="tpu_custom_call", output_to_operand_aliasing={{0}: (4, {}), {1}: (5, {})} | custom-call | flops 536870912 | bytes 1843200 | tf_op jit(solution)/shard_map/pallas_call | solution.py:73
  126.0 5.6 %shard_map.62 = (f32[1024,1]{1,0:T(8,128)}, f32[1024,128]{1,0:T(8,128)}) custom-call(s32[3]{0:T(128)} %pad_add_fusion.7.sc_ref, bf16[1024,128]{1,0:T(8,128)(2,1)} %bitcast.50, bf16[1024,128]{1,0:T(8,128)(2,1)} %collective-permute-done.16.k_ref, bf16[1024,128]{1,0:T(8,128)(2,1)} %collective-permute-done.17.v_ref, ...), custom_call_target="tpu_custom_call", output_to_operand_aliasing={{0}: (4, {}), {1}: (5, {})} | custom-call | flops 536870912 | bytes 1843200 | tf_op jit(solution)/shard_map/pallas_call | solution.py:73
  131.6 3.0 %collective-permute-start.2 = (bf16[1024,128]{1,0:T(8,128)(2,1)S(1)}, bf16[1024,128]{1,0:T(8,128)(2,1)}, u32[]{:S(2)}, u32[]{:S(2)}) collective-permute-start(bf16[1024,128]{1,0:T(8,128)(2,1)S(1)} %get-tuple-element.98), channel_id=1, source_target_pairs={{0,14},{1,15},{2,12},{3,13},{4,10},{5,11},{6,8},{7,9},{8,6},{9,7},... | collective-permute-start | bytes 786440 | tf_op jit(solution)/shard_map/ppermute | solution.py:109
  137.3 4.4 %shard_map.63 = (f32[1024,1]{1,0:T(8,128)}, f32[1024,128]{1,0:T(8,128)}) custom-call(s32[3]{0:T(128)} %pad_add_fusion.8.sc_ref, bf16[1024,128]{1,0:T(8,128)(2,1)} %bitcast.51, bf16[1024,128]{1,0:T(8,128)(2,1)} %collective-permute-done.14.k_ref, bf16[1024,128]{1,0:T(8,128)(2,1)} %collective-permute-done.15.v_ref, ...), custom_call_target="tpu_custom_call", output_to_operand_aliasing={{0}: (4, {}), {1}: (5, {})} | custom-call | flops 536870912 | bytes 1843200 | tf_op jit(solution)/shard_map/pallas_call | solution.py:73
  141.7 3.0 %collective-permute-start = (bf16[1024,128]{1,0:T(8,128)(2,1)S(1)}, bf16[1024,128]{1,0:T(8,128)(2,1)}, u32[]{:S(2)}, u32[]{:S(2)}) collective-permute-start(bf16[1024,128]{1,0:T(8,128)(2,1)S(1)} %get-tuple-element.99), channel_id=1, source_target_pairs={{0,15},{1,14},{2,13},{3,12},{4,11},{5,10},{6,9},{7,8},{8,7},{9,6},... | collective-permute-start | bytes 786440 | tf_op jit(solution)/shard_map/ppermute | solution.py:109
  147.2 4.4 %shard_map.64 = (f32[1024,1]{1,0:T(8,128)}, f32[1024,128]{1,0:T(8,128)}) custom-call(s32[3]{0:T(128)} %pad_add_fusion.9.sc_ref, bf16[1024,128]{1,0:T(8,128)(2,1)} %bitcast.52, bf16[1024,128]{1,0:T(8,128)(2,1)} %collective-permute-done.12.k_ref, bf16[1024,128]{1,0:T(8,128)(2,1)} %collective-permute-done.13.v_ref, ...), custom_call_target="tpu_custom_call", output_to_operand_aliasing={{0}: (4, {}), {1}: (5, {})} | custom-call | flops 536870912 | bytes 1843200 | tf_op jit(solution)/shard_map/pallas_call | solution.py:73
  151.6 5.7 %shard_map.65 = (f32[1024,1]{1,0:T(8,128)}, f32[1024,128]{1,0:T(8,128)}) custom-call(s32[3]{0:T(128)} %pad_add_fusion.10.sc_ref, bf16[1024,128]{1,0:T(8,128)(2,1)} %bitcast.53, bf16[1024,128]{1,0:T(8,128)(2,1)} %collective-permute-done.10.k_ref, bf16[1024,128]{1,0:T(8,128)(2,1)} %collective-permute-done.11.v_ref, ...), custom_call_target="tpu_custom_call", output_to_operand_aliasing={{0}: (4, {}), {1}: (5, {})} | custom-call | flops 536870912 | bytes 1843200 | tf_op jit(solution)/shard_map/pallas_call | solution.py:73
  157.2 4.4 %shard_map.66 = (f32[1024,1]{1,0:T(8,128)}, f32[1024,128]{1,0:T(8,128)}) custom-call(s32[3]{0:T(128)} %pad_add_fusion.11.sc_ref, bf16[1024,128]{1,0:T(8,128)(2,1)} %bitcast.54, bf16[1024,128]{1,0:T(8,128)(2,1)} %collective-permute-done.8.k_ref, bf16[1024,128]{1,0:T(8,128)(2,1)} %collective-permute-done.9.v_ref, ...), custom_call_target="tpu_custom_call", output_to_operand_aliasing={{0}: (4, {}), {1}: (5, {})} | custom-call | flops 536870912 | bytes 1843200 | tf_op jit(solution)/shard_map/pallas_call | solution.py:73
  161.7 4.4 %shard_map.67 = (f32[1024,1]{1,0:T(8,128)}, f32[1024,128]{1,0:T(8,128)}) custom-call(s32[3]{0:T(128)} %pad_add_fusion.12.sc_ref, bf16[1024,128]{1,0:T(8,128)(2,1)} %bitcast.55, bf16[1024,128]{1,0:T(8,128)(2,1)} %collective-permute-done.6.k_ref, bf16[1024,128]{1,0:T(8,128)(2,1)} %collective-permute-done.7.v_ref, ...), custom_call_target="tpu_custom_call", output_to_operand_aliasing={{0}: (4, {}), {1}: (5, {})} | custom-call | flops 536870912 | bytes 1843200 | tf_op jit(solution)/shard_map/pallas_call | solution.py:73
  166.1 4.4 %shard_map.68 = (f32[1024,1]{1,0:T(8,128)}, f32[1024,128]{1,0:T(8,128)}) custom-call(s32[3]{0:T(128)} %pad_add_fusion.13.sc_ref, bf16[1024,128]{1,0:T(8,128)(2,1)} %bitcast.56, bf16[1024,128]{1,0:T(8,128)(2,1)} %collective-permute-done.4.k_ref, bf16[1024,128]{1,0:T(8,128)(2,1)} %collective-permute-done.5.v_ref, ...), custom_call_target="tpu_custom_call", output_to_operand_aliasing={{0}: (4, {}), {1}: (5, {})} | custom-call | flops 536870912 | bytes 1843200 | tf_op jit(solution)/shard_map/pallas_call | solution.py:73
  170.5 4.4 %shard_map.69 = (f32[1024,1]{1,0:T(8,128)}, f32[1024,128]{1,0:T(8,128)}) custom-call(s32[3]{0:T(128)} %pad_add_fusion.14.sc_ref, bf16[1024,128]{1,0:T(8,128)(2,1)} %bitcast.57, bf16[1024,128]{1,0:T(8,128)(2,1)} %collective-permute-done.2.k_ref, bf16[1024,128]{1,0:T(8,128)(2,1)} %collective-permute-done.3.v_ref, ...), custom_call_target="tpu_custom_call", output_to_operand_aliasing={{0}: (4, {}), {1}: (5, {})} | custom-call | flops 536870912 | bytes 1843200 | tf_op jit(solution)/shard_map/pallas_call | solution.py:73
  175.0 4.4 %shard_map.70 = (f32[1024,1]{1,0:T(8,128)}, f32[1024,128]{1,0:T(8,128)}) custom-call(s32[3]{0:T(128)} %pad_add_fusion.15.sc_ref, bf16[1024,128]{1,0:T(8,128)(2,1)} %bitcast.58, bf16[1024,128]{1,0:T(8,128)(2,1)} %collective-permute-done.k_ref, bf16[1024,128]{1,0:T(8,128)(2,1)} %collective-permute-done.1.v_ref, ...), custom_call_target="tpu_custom_call", output_to_operand_aliasing={{0}: (4, {}), {1}: (5, {})} | custom-call | flops 536870912 | bytes 1843200 | tf_op jit(solution)/shard_map/pallas_call | solution.py:73
  183.8 2.8 %dynamic-slice_bitcast_fusion = f32[8,32,4608]{2,1,0:T(8,128)} fusion(f32[8,2,32,4608]{3,2,1,0:T(8,128)S(1)} %fusion.1, s32[]{:T(128)S(6)} %select_n.88), kind=kLoop, calls=%fused_computation.3 | loop fusion | bytes 9437188 | tf_op jit(solution)/shard_map/jit(dynamic_index_in_dim)/squeeze | solution.py:126
  188.9 8.2 %collective-permute-done.30 = f32[8,32,4608]{2,1,0:T(8,128)} collective-permute-done((f32[8,32,4608]{2,1,0:T(8,128)}, f32[8,32,4608]{2,1,0:T(8,128)}, u32[]{:S(2)}, u32[]{:S(2)}) %collective-permute-start.30) | collective-permute-done | bytes 4718624 | tf_op jit(solution)/shard_map/ppermute | solution.py:127
  197.1 4.3 %fusion = bf16[8,32,4608]{2,1,0:T(8,128)(2,1)S(1)} fusion(f32[8,32,4608]{2,1,0:T(8,128)} %collective-permute-done.30, f32[8,2,32,4608]{3,2,1,0:T(8,128)} %copy-done.1, s32[]{:T(128)S(6)} %select_n.87), kind=kLoop, calls=%fused_computation.1 | loop fusion | flops 2359296 | bytes 11796484 | tf_op jit(solution)/shard_map/convert_element_type | solution.py:129
  201.4 43.8 %all_to_all.5 = bf16[8,32,4608]{2,1,0:T(8,128)(2,1)S(1)} all-to-all(bf16[8,32,4608]{2,1,0:T(8,128)(2,1)S(1)} %fusion), channel_id=1, replica_groups=mesh['pb'=8,'kx'=8,'kc'=2] {'kx'}, dimensions={0} | all-to-all | bytes 4718592 | tf_op jit(solution)/shard_map/all_to_all | solution.py:128
  (82 shorter events, 56.4 us)
Async XLA Ops:
  0.0 182.4 %copy-start = (bf16[256,4608]{1,0:T(8,128)(2,1)S(1)}, bf16[256,4608]{1,0:T(8,128)(2,1)}, u32[]{:S(2)}) copy-start(bf16[256,4608]{1,0:T(8,128)(2,1)} %param.9) | copy-start | bytes 7077892
  4.3 17.9 %collective-permute-start.26 = (bf16[1024,128]{1,0:T(8,128)(2,1)}, bf16[1024,128]{1,0:T(8,128)(2,1)}, u32[]{:S(2)}, u32[]{:S(2)}) collective-permute-start(bf16[1024,128]{1,0:T(8,128)(2,1)} %get-tuple-element.86), channel_id=1, source_target_pairs={{0,2},{1,3},{2,0},{3,1},{4,6},{5,7},{6,4},{7,5},{8,10},{9,11},{10,... | collective-permute-start | bytes 786440 | tf_op jit(solution)/shard_map/ppermute | solution.py:109
  5.7 18.1 %collective-permute-start.24 = (bf16[1024,128]{1,0:T(8,128)(2,1)}, bf16[1024,128]{1,0:T(8,128)(2,1)}, u32[]{:S(2)}, u32[]{:S(2)}) collective-permute-start(bf16[1024,128]{1,0:T(8,128)(2,1)} %get-tuple-element.87), channel_id=1, source_target_pairs={{0,3},{1,2},{2,1},{3,0},{4,7},{5,6},{6,5},{7,4},{8,11},{9,10},{10,... | collective-permute-start | bytes 786440 | tf_op jit(solution)/shard_map/ppermute | solution.py:109
  7.1 19.6 %collective-permute-start.22 = (bf16[1024,128]{1,0:T(8,128)(2,1)}, bf16[1024,128]{1,0:T(8,128)(2,1)}, u32[]{:S(2)}, u32[]{:S(2)}) collective-permute-start(bf16[1024,128]{1,0:T(8,128)(2,1)} %get-tuple-element.88), channel_id=1, source_target_pairs={{0,4},{1,5},{2,6},{3,7},{4,0},{5,1},{6,2},{7,3},{8,12},{9,13},{10,... | collective-permute-start | bytes 786440 | tf_op jit(solution)/shard_map/ppermute | solution.py:109
  8.6 19.5 %collective-permute-start.20 = (bf16[1024,128]{1,0:T(8,128)(2,1)}, bf16[1024,128]{1,0:T(8,128)(2,1)}, u32[]{:S(2)}, u32[]{:S(2)}) collective-permute-start(bf16[1024,128]{1,0:T(8,128)(2,1)} %get-tuple-element.89), channel_id=1, source_target_pairs={{0,5},{1,4},{2,7},{3,6},{4,1},{5,0},{6,3},{7,2},{8,13},{9,12},{10,... | collective-permute-start | bytes 786440 | tf_op jit(solution)/shard_map/ppermute | solution.py:109
  9.4 22.4 %collective-permute-start.18 = (bf16[1024,128]{1,0:T(8,128)(2,1)}, bf16[1024,128]{1,0:T(8,128)(2,1)}, u32[]{:S(2)}, u32[]{:S(2)}) collective-permute-start(bf16[1024,128]{1,0:T(8,128)(2,1)} %get-tuple-element.90), channel_id=1, source_target_pairs={{0,6},{1,7},{2,4},{3,5},{4,2},{5,3},{6,0},{7,1},{8,14},{9,15},{10,... | collective-permute-start | bytes 786440 | tf_op jit(solution)/shard_map/ppermute | solution.py:109
  22.3 12.3 %collective-permute-start.16 = (bf16[1024,128]{1,0:T(8,128)(2,1)}, bf16[1024,128]{1,0:T(8,128)(2,1)}, u32[]{:S(2)}, u32[]{:S(2)}) collective-permute-start(bf16[1024,128]{1,0:T(8,128)(2,1)} %get-tuple-element.91), channel_id=1, source_target_pairs={{0,7},{1,6},{2,5},{3,4},{4,3},{5,2},{6,1},{7,0},{8,15},{9,14},{10,... | collective-permute-start | bytes 786440 | tf_op jit(solution)/shard_map/ppermute | solution.py:109
  23.8 17.6 %collective-permute-start.14 = (bf16[1024,128]{1,0:T(8,128)(2,1)}, bf16[1024,128]{1,0:T(8,128)(2,1)}, u32[]{:S(2)}, u32[]{:S(2)}) collective-permute-start(bf16[1024,128]{1,0:T(8,128)(2,1)} %get-tuple-element.92), channel_id=1, source_target_pairs={{0,8},{1,9},{2,10},{3,11},{4,12},{5,13},{6,14},{7,15},{8,0},{9,1},... | collective-permute-start | bytes 786440 | tf_op jit(solution)/shard_map/ppermute | solution.py:109
  26.8 20.2 %collective-permute-start.12 = (bf16[1024,128]{1,0:T(8,128)(2,1)}, bf16[1024,128]{1,0:T(8,128)(2,1)}, u32[]{:S(2)}, u32[]{:S(2)}) collective-permute-start(bf16[1024,128]{1,0:T(8,128)(2,1)} %get-tuple-element.93), channel_id=1, source_target_pairs={{0,9},{1,8},{2,11},{3,10},{4,13},{5,12},{6,15},{7,14},{8,1},{9,0},... | collective-permute-start | bytes 786440 | tf_op jit(solution)/shard_map/ppermute | solution.py:109
  28.1 25.2 %collective-permute-start.10 = (bf16[1024,128]{1,0:T(8,128)(2,1)}, bf16[1024,128]{1,0:T(8,128)(2,1)}, u32[]{:S(2)}, u32[]{:S(2)}) collective-permute-start(bf16[1024,128]{1,0:T(8,128)(2,1)} %get-tuple-element.94), channel_id=1, source_target_pairs={{0,10},{1,11},{2,8},{3,9},{4,14},{5,15},{6,12},{7,13},{8,2},{9,3},... | collective-permute-start | bytes 786440 | tf_op jit(solution)/shard_map/ppermute | solution.py:109
  31.8 27.1 %collective-permute-start.8 = (bf16[1024,128]{1,0:T(8,128)(2,1)}, bf16[1024,128]{1,0:T(8,128)(2,1)}, u32[]{:S(2)}, u32[]{:S(2)}) collective-permute-start(bf16[1024,128]{1,0:T(8,128)(2,1)} %get-tuple-element.95), channel_id=1, source_target_pairs={{0,11},{1,10},{2,9},{3,8},{4,15},{5,14},{6,13},{7,12},{8,3},{9,2},... | collective-permute-start | bytes 786440 | tf_op jit(solution)/shard_map/ppermute | solution.py:109
  34.6 29.2 %collective-permute-start.6 = (bf16[1024,128]{1,0:T(8,128)(2,1)}, bf16[1024,128]{1,0:T(8,128)(2,1)}, u32[]{:S(2)}, u32[]{:S(2)}) collective-permute-start(bf16[1024,128]{1,0:T(8,128)(2,1)} %get-tuple-element.96), channel_id=1, source_target_pairs={{0,12},{1,13},{2,14},{3,15},{4,8},{5,9},{6,10},{7,11},{8,4},{9,5},... | collective-permute-start | bytes 786440 | tf_op jit(solution)/shard_map/ppermute | solution.py:109
  41.4 28.0 %collective-permute-start.4 = (bf16[1024,128]{1,0:T(8,128)(2,1)}, bf16[1024,128]{1,0:T(8,128)(2,1)}, u32[]{:S(2)}, u32[]{:S(2)}) collective-permute-start(bf16[1024,128]{1,0:T(8,128)(2,1)} %get-tuple-element.97), channel_id=1, source_target_pairs={{0,13},{1,12},{2,15},{3,14},{4,9},{5,8},{6,11},{7,10},{8,5},{9,4},... | collective-permute-start | bytes 786440 | tf_op jit(solution)/shard_map/ppermute | solution.py:109
  47.0 22.4 %collective-permute-start.28 = (bf16[1024,128]{1,0:T(8,128)(2,1)}, bf16[1024,128]{1,0:T(8,128)(2,1)}, u32[]{:S(2)}, u32[]{:S(2)}) collective-permute-start(bf16[1024,128]{1,0:T(8,128)(2,1)} %get-tuple-element.100), channel_id=1, source_target_pairs={{0,1},{1,0},{2,3},{3,2},{4,5},{5,4},{6,7},{7,6},{8,9},{9,8},{10,11... | collective-permute-start | bytes 786440 | tf_op jit(solution)/shard_map/ppermute | solution.py:109
  53.3 17.1 %collective-permute-start.27 = (bf16[1024,128]{1,0:T(8,128)(2,1)}, bf16[1024,128]{1,0:T(8,128)(2,1)}, u32[]{:S(2)}, u32[]{:S(2)}) collective-permute-start(bf16[1024,128]{1,0:T(8,128)(2,1)} %get-tuple-element.70), channel_id=1, source_target_pairs={{0,2},{1,3},{2,0},{3,1},{4,6},{5,7},{6,4},{7,5},{8,10},{9,11},{10,... | collective-permute-start | bytes 786440 | tf_op jit(solution)/shard_map/ppermute | solution.py:109
  59.0 13.8 %collective-permute-start.25 = (bf16[1024,128]{1,0:T(8,128)(2,1)}, bf16[1024,128]{1,0:T(8,128)(2,1)}, u32[]{:S(2)}, u32[]{:S(2)}) collective-permute-start(bf16[1024,128]{1,0:T(8,128)(2,1)} %get-tuple-element.71), channel_id=1, source_target_pairs={{0,3},{1,2},{2,1},{3,0},{4,7},{5,6},{6,5},{7,4},{8,11},{9,10},{10,... | collective-permute-start | bytes 786440 | tf_op jit(solution)/shard_map/ppermute | solution.py:109
  63.7 24.4 %collective-permute-start.23 = (bf16[1024,128]{1,0:T(8,128)(2,1)}, bf16[1024,128]{1,0:T(8,128)(2,1)}, u32[]{:S(2)}, u32[]{:S(2)}) collective-permute-start(bf16[1024,128]{1,0:T(8,128)(2,1)} %get-tuple-element.72), channel_id=1, source_target_pairs={{0,4},{1,5},{2,6},{3,7},{4,0},{5,1},{6,2},{7,3},{8,12},{9,13},{10,... | collective-permute-start | bytes 786440 | tf_op jit(solution)/shard_map/ppermute | solution.py:109
  69.4 20.7 %collective-permute-start.21 = (bf16[1024,128]{1,0:T(8,128)(2,1)}, bf16[1024,128]{1,0:T(8,128)(2,1)}, u32[]{:S(2)}, u32[]{:S(2)}) collective-permute-start(bf16[1024,128]{1,0:T(8,128)(2,1)} %get-tuple-element.73), channel_id=1, source_target_pairs={{0,5},{1,4},{2,7},{3,6},{4,1},{5,0},{6,3},{7,2},{8,13},{9,12},{10,... | collective-permute-start | bytes 786440 | tf_op jit(solution)/shard_map/ppermute | solution.py:109
  69.4 12.7 %collective-permute-start.29 = (bf16[1024,128]{1,0:T(8,128)(2,1)}, bf16[1024,128]{1,0:T(8,128)(2,1)}, u32[]{:S(2)}, u32[]{:S(2)}) collective-permute-start(bf16[1024,128]{1,0:T(8,128)(2,1)} %get-tuple-element.84), channel_id=1, source_target_pairs={{0,1},{1,0},{2,3},{3,2},{4,5},{5,4},{6,7},{7,6},{8,9},{9,8},{10,11... | collective-permute-start | bytes 786440 | tf_op jit(solution)/shard_map/ppermute | solution.py:109
  70.4 27.7 %collective-permute-start.19 = (bf16[1024,128]{1,0:T(8,128)(2,1)}, bf16[1024,128]{1,0:T(8,128)(2,1)}, u32[]{:S(2)}, u32[]{:S(2)}) collective-permute-start(bf16[1024,128]{1,0:T(8,128)(2,1)} %get-tuple-element.74), channel_id=1, source_target_pairs={{0,6},{1,7},{2,4},{3,5},{4,2},{5,3},{6,0},{7,1},{8,14},{9,15},{10,... | collective-permute-start | bytes 786440 | tf_op jit(solution)/shard_map/ppermute | solution.py:109
  72.8 27.4 %collective-permute-start.17 = (bf16[1024,128]{1,0:T(8,128)(2,1)}, bf16[1024,128]{1,0:T(8,128)(2,1)}, u32[]{:S(2)}, u32[]{:S(2)}) collective-permute-start(bf16[1024,128]{1,0:T(8,128)(2,1)} %get-tuple-element.75), channel_id=1, source_target_pairs={{0,7},{1,6},{2,5},{3,4},{4,3},{5,2},{6,1},{7,0},{8,15},{9,14},{10,... | collective-permute-start | bytes 786440 | tf_op jit(solution)/shard_map/ppermute | solution.py:109
  82.1 43.8 %collective-permute-start.15 = (bf16[1024,128]{1,0:T(8,128)(2,1)}, bf16[1024,128]{1,0:T(8,128)(2,1)}, u32[]{:S(2)}, u32[]{:S(2)}) collective-permute-start(bf16[1024,128]{1,0:T(8,128)(2,1)} %get-tuple-element.76), channel_id=1, source_target_pairs={{0,8},{1,9},{2,10},{3,11},{4,12},{5,13},{6,14},{7,15},{8,0},{9,1},... | collective-permute-start | bytes 786440 | tf_op jit(solution)/shard_map/ppermute | solution.py:109
  88.2 43.4 %collective-permute-start.13 = (bf16[1024,128]{1,0:T(8,128)(2,1)}, bf16[1024,128]{1,0:T(8,128)(2,1)}, u32[]{:S(2)}, u32[]{:S(2)}) collective-permute-start(bf16[1024,128]{1,0:T(8,128)(2,1)} %get-tuple-element.77), channel_id=1, source_target_pairs={{0,9},{1,8},{2,11},{3,10},{4,13},{5,12},{6,15},{7,14},{8,1},{9,0},... | collective-permute-start | bytes 786440 | tf_op jit(solution)/shard_map/ppermute | solution.py:109
  90.1 44.5 %collective-permute-start.11 = (bf16[1024,128]{1,0:T(8,128)(2,1)}, bf16[1024,128]{1,0:T(8,128)(2,1)}, u32[]{:S(2)}, u32[]{:S(2)}) collective-permute-start(bf16[1024,128]{1,0:T(8,128)(2,1)} %get-tuple-element.78), channel_id=1, source_target_pairs={{0,10},{1,11},{2,8},{3,9},{4,14},{5,15},{6,12},{7,13},{8,2},{9,3},... | collective-permute-start | bytes 786440 | tf_op jit(solution)/shard_map/ppermute | solution.py:109
  98.0 43.7 %collective-permute-start.9 = (bf16[1024,128]{1,0:T(8,128)(2,1)}, bf16[1024,128]{1,0:T(8,128)(2,1)}, u32[]{:S(2)}, u32[]{:S(2)}) collective-permute-start(bf16[1024,128]{1,0:T(8,128)(2,1)} %get-tuple-element.79), channel_id=1, source_target_pairs={{0,11},{1,10},{2,9},{3,8},{4,15},{5,14},{6,13},{7,12},{8,3},{9,2},... | collective-permute-start | bytes 786440 | tf_op jit(solution)/shard_map/ppermute | solution.py:109
  100.2 44.5 %collective-permute-start.7 = (bf16[1024,128]{1,0:T(8,128)(2,1)}, bf16[1024,128]{1,0:T(8,128)(2,1)}, u32[]{:S(2)}, u32[]{:S(2)}) collective-permute-start(bf16[1024,128]{1,0:T(8,128)(2,1)} %get-tuple-element.80), channel_id=1, source_target_pairs={{0,12},{1,13},{2,14},{3,15},{4,8},{5,9},{6,10},{7,11},{8,4},{9,5},... | collective-permute-start | bytes 786440 | tf_op jit(solution)/shard_map/ppermute | solution.py:109
  125.9 40.2 %collective-permute-start.5 = (bf16[1024,128]{1,0:T(8,128)(2,1)}, bf16[1024,128]{1,0:T(8,128)(2,1)}, u32[]{:S(2)}, u32[]{:S(2)}) collective-permute-start(bf16[1024,128]{1,0:T(8,128)(2,1)} %get-tuple-element.81), channel_id=1, source_target_pairs={{0,13},{1,12},{2,15},{3,14},{4,9},{5,8},{6,11},{7,10},{8,5},{9,4},... | collective-permute-start | bytes 786440 | tf_op jit(solution)/shard_map/ppermute | solution.py:109
  131.6 38.9 %collective-permute-start.2 = (bf16[1024,128]{1,0:T(8,128)(2,1)S(1)}, bf16[1024,128]{1,0:T(8,128)(2,1)}, u32[]{:S(2)}, u32[]{:S(2)}) collective-permute-start(bf16[1024,128]{1,0:T(8,128)(2,1)S(1)} %get-tuple-element.98), channel_id=1, source_target_pairs={{0,14},{1,15},{2,12},{3,13},{4,10},{5,11},{6,8},{7,9},{8,6},{9,7},... | collective-permute-start | bytes 786440 | tf_op jit(solution)/shard_map/ppermute | solution.py:109
  134.5 36.0 %collective-permute-start.3 = (bf16[1024,128]{1,0:T(8,128)(2,1)S(1)}, bf16[1024,128]{1,0:T(8,128)(2,1)}, u32[]{:S(2)}, u32[]{:S(2)}) collective-permute-start(bf16[1024,128]{1,0:T(8,128)(2,1)S(1)} %get-tuple-element.82), channel_id=1, source_target_pairs={{0,14},{1,15},{2,12},{3,13},{4,10},{5,11},{6,8},{7,9},{8,6},{9,7},... | collective-permute-start | bytes 786440 | tf_op jit(solution)/shard_map/ppermute | solution.py:109
  141.7 33.2 %collective-permute-start = (bf16[1024,128]{1,0:T(8,128)(2,1)S(1)}, bf16[1024,128]{1,0:T(8,128)(2,1)}, u32[]{:S(2)}, u32[]{:S(2)}) collective-permute-start(bf16[1024,128]{1,0:T(8,128)(2,1)S(1)} %get-tuple-element.99), channel_id=1, source_target_pairs={{0,15},{1,14},{2,13},{3,12},{4,11},{5,10},{6,9},{7,8},{8,7},{9,6},... | collective-permute-start | bytes 786440 | tf_op jit(solution)/shard_map/ppermute | solution.py:109
  144.7 30.2 %collective-permute-start.1 = (bf16[1024,128]{1,0:T(8,128)(2,1)S(1)}, bf16[1024,128]{1,0:T(8,128)(2,1)}, u32[]{:S(2)}, u32[]{:S(2)}) collective-permute-start(bf16[1024,128]{1,0:T(8,128)(2,1)S(1)} %get-tuple-element.83), channel_id=1, source_target_pairs={{0,15},{1,14},{2,13},{3,12},{4,11},{5,10},{6,9},{7,8},{8,7},{9,6},... | collective-permute-start | bytes 786440 | tf_op jit(solution)/shard_map/ppermute | solution.py:109
  188.8 8.3 %collective-permute-start.30 = (f32[8,32,4608]{2,1,0:T(8,128)}, f32[8,32,4608]{2,1,0:T(8,128)}, u32[]{:S(2)}, u32[]{:S(2)}) collective-permute-start(f32[8,32,4608]{2,1,0:T(8,128)} %dynamic-slice_bitcast_fusion), channel_id=1, source_target_pairs={{0,1},{1,0},{2,3},{3,2},{4,5},{5,4},{6,7},{7,6},{8,9},{9,8},{10,11... | collective-permute-start | bytes 14155784 | tf_op jit(solution)/shard_map/ppermute | solution.py:127
  (2 other events, 20.4 us)

commit v12 on v4

--- a/solution.py
+++ b/solution.py
@@ -12,6 +12,7 @@
 SCALAR = 144
 KV = ("kx", "kc")
 TQ = 256
+LAG = 4
 
 
 def block_kernel(sc_ref, q_ref, k_ref, v_ref, l_ref, acc_ref, l_out, acc_out):
@@ -98,20 +99,29 @@
     q_block = queries.reshape(rows_dev, kv_local * group, HD).transpose(1, 0, 2).reshape(n_q, HD)
     total = jnp.zeros((n_q, 1), jnp.float32)
     summed = jnp.zeros((n_q, HD), jnp.float32)
+    sends = []
     for shift in range(n_kv):
         dest = me ^ shift
-        src = dest
-        block = jnp.stack(
-            (
-                lax.dynamic_slice_in_dim(keys, dest * kv_feat, kv_feat, 1),
-                lax.dynamic_slice_in_dim(values, dest * kv_feat, kv_feat, 1),
-            ),
-            axis=0,
+        sends.append(
+            jnp.stack(
+                (
+                    lax.dynamic_slice_in_dim(keys, dest * kv_feat, kv_feat, 1),
+                    lax.dynamic_slice_in_dim(values, dest * kv_feat, kv_feat, 1),
+                ),
+                axis=0,
+            )
         )
-        if shift:
-            block = lax.ppermute(block, KV, [(j, j ^ shift) for j in range(n_kv)])
+    received = [sends[0]]
+    for shift in range(1, min(LAG + 1, n_kv)):
+        received.append(lax.ppermute(sends[shift], KV, [(j, j ^ shift) for j in range(n_kv)]))
+    for shift in range(n_kv):
+        src = me ^ shift
         scalars = jnp.stack([row_first, src * key_dev, jnp.int32(rows_dev)]).astype(jnp.int32)
-        total, summed = attend_kernel(scalars, q_block, block, total, summed)
+        total, summed = attend_kernel(scalars, q_block, received[shift], total, summed)
+        nxt = shift + LAG + 1
+        if nxt < n_kv:
+            payload, total = lax.optimization_barrier((sends[nxt], total))
+            received.append(lax.ppermute(payload, KV, [(j, j ^ nxt) for j in range(n_kv)]))
     mixed = (summed / total).astype(jnp.bfloat16)
     return mixed.reshape(kv_local * group, rows_dev, HD).transpose(1, 0, 2).reshape(rows_dev, n_q // rows_dev * HD)
 

time: 236 us -> 243 us (1.030); the launches traced: 236 us -> 240 us
  other arithmetic: 34.8 us -> 42.1 us
  blocking collectives: 40.4 us -> 37.2 us
  Pallas kernels: 85 us -> 82.5 us
    another operation x16, other arithmetic: 17 us -> 23.9 us  [by_heads(): jnp.stack((lax.dynamic_slice_in_dim(keys, dest * kv_feat, kv_feat, 1), la...]
    all_to_all x1, blocking collectives: 40.4 us -> 37.2 us  [per_device(): lax.all_to_all(on_chip.astype(jnp.bfloat16), 'kx', split_axis=0, concat_a...]
    pallas_call x16, Pallas kernels: 85 us -> 82.5 us  [attend_kernel(): pl.pallas_call(block_kernel, grid_spec=grid_spec, out_shape=(jax.ShapeDty...]
  transfers between devices with their start and end apart: 16 -> 16, of which waited for: 5 -> 5; matrix products, arithmetic and copies ran while one was open for 12% -> 13% of each run, Pallas kernels for 34% -> 30%
where the time goes in v12:
time: 243 us; the launch traced here: 240 us
  Pallas kernels  82.5 us (34%)
  other arithmetic  42.1 us (17%)
  blocking collectives  37.2 us (15%)
  waiting for transfers between devices  34.3 us (14%)
  starting transfers between devices  25.6 us (11%)
  local copies, waits for them, and re-layouts  15.7 us (6%)
    pallas_call x16, Pallas kernels, attend_kernel(): pl.pallas_call(block_kernel, grid_spec=grid_spec, out_shape=(jax.ShapeDty...  82.5 us
    all_to_all x1, blocking collectives, per_device(): lax.all_to_all(on_chip.astype(jnp.bfloat16), 'kx', split_axis=0, concat_a...  37.2 us
    ppermute x11, waiting for transfers between devices, by_heads(): lax.ppermute(payload, KV, [(j, j ^ nxt) for j in range(n_kv)])  26.1 us
    another operation x16, other arithmetic, by_heads(): jnp.stack((lax.dynamic_slice_in_dim(keys, dest * kv_feat, kv_feat, 1), la...  23.9 us
    ppermute x11, starting transfers between devices, by_heads(): lax.ppermute(payload, KV, [(j, j ^ nxt) for j in range(n_kv)])  21.4 us
    another operation x16, other arithmetic, by_heads(): jnp.stack([row_first, src * key_dev, jnp.int32(rows_dev)]).astype(jnp.int32)  10.3 us
    ppermute x1, waiting for transfers between devices, per_device(): on_chip = mine + lax.ppermute(theirs, 'kc', [(0, 1), (1, 0)])  8.14 us
    another operation x1, local copies, waits for them, and re-layouts, by_heads(): jnp.stack((lax.dynamic_slice_in_dim(keys, dest * kv_feat, kv_feat, 1), la...  6.86 us
  transfers between devices with their start and end apart: 16, of which 5 were waited for; matrix products, arithmetic and copies ran while one was open for 13% of the time, Pallas kernels for 30%

profile of v12, /device:TPU:120, one launch (start us, length us, event | category | flops | bytes accessed | tf_op | source)
XLA Modules:
  0.0 239.8 jit_solution(6433354489528697151)
XLA Ops:
  2.5 6.9 %dynamic-slice_bitcast_fusion.1 = (bf16[1,1024,128]{2,1,0:T(8,128)(2,1)}, bf16[1,1024,128]{2,1,0:T(8,128)(2,1)}, bf16[1,1024,128]{2,1,0:T(8,128)(2,1)}, bf16[1,1...) fusion(bf16[1024,2048]{1,0:T(8,128)(2,1)} %param.8, ...), kind=kLoop, calls=%fused_computation.24 | loop fusion | bytes 16777280 | tf_op jit(solution)/shard_map/stack | solution.py:106
  13.3 5.6 %shard_map.55 = (f32[1024,1]{1,0:T(8,128)}, f32[1024,128]{1,0:T(8,128)}) custom-call(s32[3]{0:T(128)} %pad_add_fusion.12.sc_ref, bf16[1024,128]{1,0:T(8,128)(2,1)} %bitcast.107, bf16[2,1024,128]{2,1,0:T(8,128)(2,1)} %pad_maximum_fusion.3.k_ref.v_ref, ...), custom_call_target="tpu_custom_call", output_to_operand_aliasing={{0}: (4, {}), {1}: (5, {})} | custom-call | flops 536870912 | bytes 1843200 | tf_op jit(solution)/shard_map/pallas_call | solution.py:74
  27.2 2.3 collective-permute-start.3
  51.5 5.6 %shard_map.56 = (f32[1024,1]{1,0:T(8,128)}, f32[1024,128]{1,0:T(8,128)}) custom-call(s32[3]{0:T(128)} %pad_add_fusion.8.sc_ref, bf16[1024,128]{1,0:T(8,128)(2,1)} %bitcast.108, bf16[2,1024,128]{2,1,0:T(8,128)(2,1)} %collective-permute-done.4.k_ref.v_ref, ...), custom_call_target="tpu_custom_call", output_to_operand_aliasing={{0}: (4, {}), {1}: (5, {})} | custom-call | flops 536870912 | bytes 1843200 | tf_op jit(solution)/shard_map/pallas_call | solution.py:74
  57.1 2.2 collective-permute-start.9
  59.2 5.6 %shard_map.57 = (f32[1024,1]{1,0:T(8,128)}, f32[1024,128]{1,0:T(8,128)}) custom-call(s32[3]{0:T(128)} %pad_add_fusion.9.sc_ref, bf16[1024,128]{1,0:T(8,128)(2,1)} %bitcast.109, bf16[2,1024,128]{2,1,0:T(8,128)(2,1)} %collective-permute-done.3.k_ref.v_ref, ...), custom_call_target="tpu_custom_call", output_to_operand_aliasing={{0}: (4, {}), {1}: (5, {})} | custom-call | flops 536870912 | bytes 1843200 | tf_op jit(solution)/shard_map/pallas_call | solution.py:74
  64.8 2.1 collective-permute-start.8
  66.9 5.6 %shard_map.58 = (f32[1024,1]{1,0:T(8,128)}, f32[1024,128]{1,0:T(8,128)}) custom-call(s32[3]{0:T(128)} %pad_add_fusion.10.sc_ref, bf16[1024,128]{1,0:T(8,128)(2,1)} %bitcast.110, bf16[2,1024,128]{2,1,0:T(8,128)(2,1)} %collective-permute-done.2.k_ref.v_ref, ...), custom_call_target="tpu_custom_call", output_to_operand_aliasing={{0}: (4, {}), {1}: (5, {})} | custom-call | flops 536870912 | bytes 1843200 | tf_op jit(solution)/shard_map/pallas_call | solution.py:74
  72.5 5.6 %shard_map.59 = (f32[1024,1]{1,0:T(8,128)}, f32[1024,128]{1,0:T(8,128)}) custom-call(s32[3]{0:T(128)} %pad_add_fusion.11.sc_ref, bf16[1024,128]{1,0:T(8,128)(2,1)} %bitcast.111, bf16[2,1024,128]{2,1,0:T(8,128)(2,1)} %collective-permute-done.1.k_ref.v_ref, ...), custom_call_target="tpu_custom_call", output_to_operand_aliasing={{0}: (4, {}), {1}: (5, {})} | custom-call | flops 536870912 | bytes 1843200 | tf_op jit(solution)/shard_map/pallas_call | solution.py:74
  80.1 5.6 %shard_map.60 = (f32[1024,1]{1,0:T(8,128)}, f32[1024,128]{1,0:T(8,128)}) custom-call(s32[3]{0:T(128)} %pad_add_fusion.13.sc_ref, bf16[1024,128]{1,0:T(8,128)(2,1)} %bitcast.112, bf16[2,1024,128]{2,1,0:T(8,128)(2,1)} %collective-permute-done.k_ref.v_ref, ...), custom_call_target="tpu_custom_call", output_to_operand_aliasing={{0}: (4, {}), {1}: (5, {})} | custom-call | flops 536870912 | bytes 1843200 | tf_op jit(solution)/shard_map/pallas_call | solution.py:74
  89.5 5.6 %shard_map.61 = (f32[1024,1]{1,0:T(8,128)}, f32[1024,128]{1,0:T(8,128)}) custom-call(s32[3]{0:T(128)} %pad_add_fusion.4.sc_ref, bf16[1024,128]{1,0:T(8,128)(2,1)} %bitcast.113, bf16[2,1024,128]{2,1,0:T(8,128)(2,1)} %collective-permute-done.9.k_ref.v_ref, ...), custom_call_target="tpu_custom_call", output_to_operand_aliasing={{0}: (4, {}), {1}: (5, {})} | custom-call | flops 536870912 | bytes 1843200 | tf_op jit(solution)/shard_map/pallas_call | solution.py:74
  95.1 3.2 %collective-permute-start.14 = (bf16[2,1024,128]{2,1,0:T(8,128)(2,1)}, bf16[2,1024,128]{2,1,0:T(8,128)(2,1)}, u32[]{:S(2)}, u32[]{:S(2)}) collective-permute-start(bf16[2,1024,128]{2,1,0:T(8,128)(2,1)} %pad_maximum_fusion.15), channel_id=1, source_target_pairs={{0,11},{1,10},{2,9},{3,8},{4,15},{5,14},{6,13},{7,12},{8,3},{9,2},... | collective-permute-start | bytes 1572872 | tf_op jit(solution)/shard_map/ppermute | solution.py:124
  98.3 5.6 %shard_map.62 = (f32[1024,1]{1,0:T(8,128)}, f32[1024,128]{1,0:T(8,128)}) custom-call(s32[3]{0:T(128)} %pad_add_fusion.5.sc_ref, bf16[1024,128]{1,0:T(8,128)(2,1)} %bitcast.114, bf16[2,1024,128]{2,1,0:T(8,128)(2,1)} %collective-permute-done.8.k_ref.v_ref, ...), custom_call_target="tpu_custom_call", output_to_operand_aliasing={{0}: (4, {}), {1}: (5, {})} | custom-call | flops 536870912 | bytes 1843200 | tf_op jit(solution)/shard_map/pallas_call | solution.py:74
  105.8 4.4 %shard_map.63 = (f32[1024,1]{1,0:T(8,128)}, f32[1024,128]{1,0:T(8,128)}) custom-call(s32[3]{0:T(128)} %pad_add_fusion.6.sc_ref, bf16[1024,128]{1,0:T(8,128)(2,1)} %bitcast.115, bf16[2,1024,128]{2,1,0:T(8,128)(2,1)} %collective-permute-done.7.k_ref.v_ref, ...), custom_call_target="tpu_custom_call", output_to_operand_aliasing={{0}: (4, {}), {1}: (5, {})} | custom-call | flops 536870912 | bytes 1843200 | tf_op jit(solution)/shard_map/pallas_call | solution.py:74
  110.2 2.2 collective-permute-start.12
  112.4 4.4 %shard_map.64 = (f32[1024,1]{1,0:T(8,128)}, f32[1024,128]{1,0:T(8,128)}) custom-call(s32[3]{0:T(128)} %pad_add_fusion.7.sc_ref, bf16[1024,128]{1,0:T(8,128)(2,1)} %bitcast.116, bf16[2,1024,128]{2,1,0:T(8,128)(2,1)} %collective-permute-done.6.k_ref.v_ref, ...), custom_call_target="tpu_custom_call", output_to_operand_aliasing={{0}: (4, {}), {1}: (5, {})} | custom-call | flops 536870912 | bytes 1843200 | tf_op jit(solution)/shard_map/pallas_call | solution.py:74
  116.9 4.2 %collective-permute-start.11 = (bf16[2,1024,128]{2,1,0:T(8,128)(2,1)S(1)}, bf16[2,1024,128]{2,1,0:T(8,128)(2,1)}, u32[]{:S(2)}, u32[]{:S(2)}) collective-permute-start(bf16[2,1024,128]{2,1,0:T(8,128)(2,1)S(1)} %copy-done.6), channel_id=1, source_target_pairs={{0,14},{1,15},{2,12},{3,13},{4,10},{5,11},{6,8},{7,9},{8,6},{9,7},... | collective-permute-start | bytes 1572872 | tf_op jit(solution)/shard_map/ppermute | solution.py:124
  121.1 5.6 %shard_map.65 = (f32[1024,1]{1,0:T(8,128)}, f32[1024,128]{1,0:T(8,128)}) custom-call(s32[3]{0:T(128)} %pad_add_fusion.14.sc_ref, bf16[1024,128]{1,0:T(8,128)(2,1)} %bitcast.117, bf16[2,1024,128]{2,1,0:T(8,128)(2,1)} %collective-permute-done.5.k_ref.v_ref, ...), custom_call_target="tpu_custom_call", output_to_operand_aliasing={{0}: (4, {}), {1}: (5, {})} | custom-call | flops 536870912 | bytes 1843200 | tf_op jit(solution)/shard_map/pallas_call | solution.py:74
  130.0 5.7 %shard_map.66 = (f32[1024,1]{1,0:T(8,128)}, f32[1024,128]{1,0:T(8,128)}) custom-call(s32[3]{0:T(128)} %pad_add_fusion.sc_ref, bf16[1024,128]{1,0:T(8,128)(2,1)} %bitcast.118, bf16[2,1024,128]{2,1,0:T(8,128)(2,1)} %collective-permute-done.14.k_ref.v_ref, ...), custom_call_target="tpu_custom_call", output_to_operand_aliasing={{0}: (4, {}), {1}: (5, {})} | custom-call | flops 536870912 | bytes 1843200 | tf_op jit(solution)/shard_map/pallas_call | solution.py:74
  135.6 4.4 %collective-permute-done.13.k_ref.v_ref = bf16[2,1024,128]{2,1,0:T(8,128)(2,1)} collective-permute-done((bf16[2,1024,128]{2,1,0:T(8,128)(2,1)}, bf16[2,1024,128]{2,1,0:T(8,128)(2,1)}, u32[]{:S(2)}, u32[]{:S(2)}) %collective-permute-start.13) | collective-permute-done | bytes 524320 | tf_op jit(solution)/shard_map/ppermute | solution.py:124
  140.0 4.4 %shard_map.67 = (f32[1024,1]{1,0:T(8,128)}, f32[1024,128]{1,0:T(8,128)}) custom-call(s32[3]{0:T(128)} %pad_add_fusion.1.sc_ref, bf16[1024,128]{1,0:T(8,128)(2,1)} %bitcast.119, bf16[2,1024,128]{2,1,0:T(8,128)(2,1)} %collective-permute-done.13.k_ref.v_ref, ...), custom_call_target="tpu_custom_call", output_to_operand_aliasing={{0}: (4, {}), {1}: (5, {})} | custom-call | flops 536870912 | bytes 1843200 | tf_op jit(solution)/shard_map/pallas_call | solution.py:74
  144.4 6.7 %collective-permute-done.12.k_ref.v_ref = bf16[2,1024,128]{2,1,0:T(8,128)(2,1)} collective-permute-done((bf16[2,1024,128]{2,1,0:T(8,128)(2,1)S(1)}, bf16[2,1024,128]{2,1,0:T(8,128)(2,1)}, u32[]{:S(2)}, u32[]{:S(2)}) %collective-permute-start.12) | collective-permute-done | bytes 524320 | tf_op jit(solution)/shard_map/ppermute | solution.py:124
  151.1 4.4 %shard_map.68 = (f32[1024,1]{1,0:T(8,128)}, f32[1024,128]{1,0:T(8,128)}) custom-call(s32[3]{0:T(128)} %pad_add_fusion.2.sc_ref, bf16[1024,128]{1,0:T(8,128)(2,1)} %bitcast.120, bf16[2,1024,128]{2,1,0:T(8,128)(2,1)} %collective-permute-done.12.k_ref.v_ref, ...), custom_call_target="tpu_custom_call", output_to_operand_aliasing={{0}: (4, {}), {1}: (5, {})} | custom-call | flops 536870912 | bytes 1843200 | tf_op jit(solution)/shard_map/pallas_call | solution.py:74
  155.5 8.4 %collective-permute-done.11.k_ref.v_ref = bf16[2,1024,128]{2,1,0:T(8,128)(2,1)} collective-permute-done((bf16[2,1024,128]{2,1,0:T(8,128)(2,1)S(1)}, bf16[2,1024,128]{2,1,0:T(8,128)(2,1)}, u32[]{:S(2)}, u32[]{:S(2)}) %collective-permute-start.11) | collective-permute-done | bytes 524320 | tf_op jit(solution)/shard_map/ppermute | solution.py:124
  163.9 4.4 %shard_map.69 = (f32[1024,1]{1,0:T(8,128)}, f32[1024,128]{1,0:T(8,128)}) custom-call(s32[3]{0:T(128)} %pad_add_fusion.3.sc_ref, bf16[1024,128]{1,0:T(8,128)(2,1)} %bitcast.121, bf16[2,1024,128]{2,1,0:T(8,128)(2,1)} %collective-permute-done.11.k_ref.v_ref, ...), custom_call_target="tpu_custom_call", output_to_operand_aliasing={{0}: (4, {}), {1}: (5, {})} | custom-call | flops 536870912 | bytes 1843200 | tf_op jit(solution)/shard_map/pallas_call | solution.py:74
  168.3 6.7 %collective-permute-done.10.k_ref.v_ref = bf16[2,1024,128]{2,1,0:T(8,128)(2,1)} collective-permute-done((bf16[2,1024,128]{2,1,0:T(8,128)(2,1)}, bf16[2,1024,128]{2,1,0:T(8,128)(2,1)}, u32[]{:S(2)}, u32[]{:S(2)}) %collective-permute-start.10) | collective-permute-done | bytes 524320 | tf_op jit(solution)/shard_map/ppermute | solution.py:124
  175.0 4.4 %shard_map.70 = (f32[1024,1]{1,0:T(8,128)}, f32[1024,128]{1,0:T(8,128)}) custom-call(s32[3]{0:T(128)} %pad_add_fusion.15.sc_ref, bf16[1024,128]{1,0:T(8,128)(2,1)} %bitcast.122, bf16[2,1024,128]{2,1,0:T(8,128)(2,1)} %collective-permute-done.10.k_ref.v_ref, ...), custom_call_target="tpu_custom_call", output_to_operand_aliasing={{0}: (4, {}), {1}: (5, {})} | custom-call | flops 536870912 | bytes 1843200 | tf_op jit(solution)/shard_map/pallas_call | solution.py:74
  183.8 2.8 %dynamic-slice_bitcast_fusion = f32[8,32,4608]{2,1,0:T(8,128)} fusion(f32[8,2,32,4608]{3,2,1,0:T(8,128)S(1)} %fusion.1, s32[]{:T(128)S(6)} %select_n.88), kind=kLoop, calls=%fused_computation.3 | loop fusion | bytes 9437188 | tf_op jit(solution)/shard_map/jit(dynamic_index_in_dim)/squeeze | solution.py:139
  186.7 2.2 copy-done.1
  189.0 8.1 %collective-permute-done.15 = f32[8,32,4608]{2,1,0:T(8,128)} collective-permute-done((f32[8,32,4608]{2,1,0:T(8,128)}, f32[8,32,4608]{2,1,0:T(8,128)}, u32[]{:S(2)}, u32[]{:S(2)}) %collective-permute-start.15) | collective-permute-done | bytes 4718624 | tf_op jit(solution)/shard_map/ppermute | solution.py:140
  197.1 4.3 %fusion = bf16[8,32,4608]{2,1,0:T(8,128)(2,1)S(1)} fusion(f32[8,32,4608]{2,1,0:T(8,128)} %collective-permute-done.15, f32[8,2,32,4608]{3,2,1,0:T(8,128)} %copy-done.1, s32[]{:T(128)S(6)} %select_n.87), kind=kLoop, calls=%fused_computation.1 | loop fusion | flops 2359296 | bytes 11796484 | tf_op jit(solution)/shard_map/convert_element_type | solution.py:142
  201.4 37.2 %all_to_all.5 = bf16[8,32,4608]{2,1,0:T(8,128)(2,1)S(1)} all-to-all(bf16[8,32,4608]{2,1,0:T(8,128)(2,1)S(1)} %fusion), channel_id=1, replica_groups=mesh['pb'=8,'kx'=8,'kc'=2] {'kx'}, dimensions={0} | all-to-all | bytes 4718592 | tf_op jit(solution)/shard_map/all_to_all | solution.py:141
  (77 shorter events, 52.4 us)
Async XLA Ops:
  0.0 182.4 %copy-start = (bf16[256,4608]{1,0:T(8,128)(2,1)S(1)}, bf16[256,4608]{1,0:T(8,128)(2,1)}, u32[]{:S(2)}) copy-start(bf16[256,4608]{1,0:T(8,128)(2,1)} %param.9) | copy-start | bytes 7077892
  18.9 61.2 %collective-permute-start = (bf16[2,1024,128]{2,1,0:T(8,128)(2,1)}, bf16[2,1024,128]{2,1,0:T(8,128)(2,1)}, u32[]{:S(2)}, u32[]{:S(2)}) collective-permute-start(bf16[2,1024,128]{2,1,0:T(8,128)(2,1)} %pad_maximum_fusion.2), channel_id=1, source_target_pairs={{0,5},{1,4},{2,7},{3,6},{4,1},{5,0},{6,3},{7,2},{8,13},{9,12},{10,... | collective-permute-start | bytes 1572872 | tf_op jit(solution)/shard_map/ppermute | solution.py:124
  21.7 50.8 %collective-permute-start.1 = (bf16[2,1024,128]{2,1,0:T(8,128)(2,1)}, bf16[2,1024,128]{2,1,0:T(8,128)(2,1)}, u32[]{:S(2)}, u32[]{:S(2)}) collective-permute-start(bf16[2,1024,128]{2,1,0:T(8,128)(2,1)} %pad_maximum_fusion.5), channel_id=1, source_target_pairs={{0,4},{1,5},{2,6},{3,7},{4,0},{5,1},{6,2},{7,3},{8,12},{9,13},{10,... | collective-permute-start | bytes 1572872 | tf_op jit(solution)/shard_map/ppermute | solution.py:116
  24.2 42.8 %collective-permute-start.2 = (bf16[2,1024,128]{2,1,0:T(8,128)(2,1)}, bf16[2,1024,128]{2,1,0:T(8,128)(2,1)}, u32[]{:S(2)}, u32[]{:S(2)}) collective-permute-start(bf16[2,1024,128]{2,1,0:T(8,128)(2,1)} %pad_maximum_fusion.7), channel_id=1, source_target_pairs={{0,3},{1,2},{2,1},{3,0},{4,7},{5,6},{6,5},{7,4},{8,11},{9,10},{10,... | collective-permute-start | bytes 1572872 | tf_op jit(solution)/shard_map/ppermute | solution.py:116
  27.2 32.0 %collective-permute-start.3 = (bf16[2,1024,128]{2,1,0:T(8,128)(2,1)}, bf16[2,1024,128]{2,1,0:T(8,128)(2,1)}, u32[]{:S(2)}, u32[]{:S(2)}) collective-permute-start(bf16[2,1024,128]{2,1,0:T(8,128)(2,1)} %pad_maximum_fusion.9), channel_id=1, source_target_pairs={{0,2},{1,3},{2,0},{3,1},{4,6},{5,7},{6,4},{7,5},{8,10},{9,11},{10,... | collective-permute-start | bytes 1572872 | tf_op jit(solution)/shard_map/ppermute | solution.py:116
  31.4 20.0 %collective-permute-start.4 = (bf16[2,1024,128]{2,1,0:T(8,128)(2,1)}, bf16[2,1024,128]{2,1,0:T(8,128)(2,1)}, u32[]{:S(2)}, u32[]{:S(2)}) collective-permute-start(bf16[2,1024,128]{2,1,0:T(8,128)(2,1)} %pad_maximum_fusion.11), channel_id=1, source_target_pairs={{0,1},{1,0},{2,3},{3,2},{4,5},{5,4},{6,7},{7,6},{8,9},{9,8},{10,11... | collective-permute-start | bytes 1572872 | tf_op jit(solution)/shard_map/ppermute | solution.py:116
  31.5 12.7 %copy-start.4 = (bf16[1,1024,128]{2,1,0:T(8,128)(2,1)S(1)}, bf16[1,1024,128]{2,1,0:T(8,128)(2,1)}, u32[]{:S(2)}) copy-start(bf16[1,1024,128]{2,1,0:T(8,128)(2,1)} %get-tuple-element.135) | copy-start | bytes 786436
  31.5 12.7 %copy-start.5 = (bf16[1,1024,128]{2,1,0:T(8,128)(2,1)S(1)}, bf16[1,1024,128]{2,1,0:T(8,128)(2,1)}, u32[]{:S(2)}) copy-start(bf16[1,1024,128]{2,1,0:T(8,128)(2,1)} %get-tuple-element.154) | copy-start | bytes 786436
  31.5 13.5 %copy-start.2 = (bf16[1,1024,128]{2,1,0:T(8,128)(2,1)S(1)}, bf16[1,1024,128]{2,1,0:T(8,128)(2,1)}, u32[]{:S(2)}) copy-start(bf16[1,1024,128]{2,1,0:T(8,128)(2,1)} %get-tuple-element.137) | copy-start | bytes 786436
  31.5 13.5 %copy-start.3 = (bf16[1,1024,128]{2,1,0:T(8,128)(2,1)S(1)}, bf16[1,1024,128]{2,1,0:T(8,128)(2,1)}, u32[]{:S(2)}) copy-start(bf16[1,1024,128]{2,1,0:T(8,128)(2,1)} %get-tuple-element.152) | copy-start | bytes 786436
  57.1 32.4 %collective-permute-start.9 = (bf16[2,1024,128]{2,1,0:T(8,128)(2,1)}, bf16[2,1024,128]{2,1,0:T(8,128)(2,1)}, u32[]{:S(2)}, u32[]{:S(2)}) collective-permute-start(bf16[2,1024,128]{2,1,0:T(8,128)(2,1)} %pad_maximum_fusion.10), channel_id=1, source_target_pairs={{0,6},{1,7},{2,4},{3,5},{4,2},{5,3},{6,0},{7,1},{8,14},{9,15},{10,... | collective-permute-start | bytes 1572872 | tf_op jit(solution)/shard_map/ppermute | solution.py:124
  64.8 33.4 %collective-permute-start.8 = (bf16[2,1024,128]{2,1,0:T(8,128)(2,1)}, bf16[2,1024,128]{2,1,0:T(8,128)(2,1)}, u32[]{:S(2)}, u32[]{:S(2)}) collective-permute-start(bf16[2,1024,128]{2,1,0:T(8,128)(2,1)} %pad_maximum_fusion.8), channel_id=1, source_target_pairs={{0,7},{1,6},{2,5},{3,4},{4,3},{5,2},{6,1},{7,0},{8,15},{9,14},{10,... | collective-permute-start | bytes 1572872 | tf_op jit(solution)/shard_map/ppermute | solution.py:124
  72.5 33.3 %collective-permute-start.7 = (bf16[2,1024,128]{2,1,0:T(8,128)(2,1)}, bf16[2,1024,128]{2,1,0:T(8,128)(2,1)}, u32[]{:S(2)}, u32[]{:S(2)}) collective-permute-start(bf16[2,1024,128]{2,1,0:T(8,128)(2,1)} %pad_maximum_fusion.6), channel_id=1, source_target_pairs={{0,8},{1,9},{2,10},{3,11},{4,12},{5,13},{6,14},{7,15},{8,0},{9,1},... | collective-permute-start | bytes 1572872 | tf_op jit(solution)/shard_map/ppermute | solution.py:124
  78.1 34.3 %collective-permute-start.6 = (bf16[2,1024,128]{2,1,0:T(8,128)(2,1)}, bf16[2,1024,128]{2,1,0:T(8,128)(2,1)}, u32[]{:S(2)}, u32[]{:S(2)}) collective-permute-start(bf16[2,1024,128]{2,1,0:T(8,128)(2,1)} %pad_maximum_fusion.4), channel_id=1, source_target_pairs={{0,9},{1,8},{2,11},{3,10},{4,13},{5,12},{6,15},{7,14},{8,1},{9,0},... | collective-permute-start | bytes 1572872 | tf_op jit(solution)/shard_map/ppermute | solution.py:124
  85.7 35.4 %collective-permute-start.5 = (bf16[2,1024,128]{2,1,0:T(8,128)(2,1)}, bf16[2,1024,128]{2,1,0:T(8,128)(2,1)}, u32[]{:S(2)}, u32[]{:S(2)}) collective-permute-start(bf16[2,1024,128]{2,1,0:T(8,128)(2,1)} %pad_maximum_fusion.1), channel_id=1, source_target_pairs={{0,10},{1,11},{2,8},{3,9},{4,14},{5,15},{6,12},{7,13},{8,2},{9,3},... | collective-permute-start | bytes 1572872 | tf_op jit(solution)/shard_map/ppermute | solution.py:124
  95.1 15.1 %copy-start.7 = (bf16[2,1024,128]{2,1,0:T(8,128)(2,1)S(1)}, bf16[2,1024,128]{2,1,0:T(8,128)(2,1)}, u32[]{:S(2)}) copy-start(bf16[2,1024,128]{2,1,0:T(8,128)(2,1)} %pad_maximum_fusion.13) | copy-start | bytes 1572868
  95.1 34.9 %collective-permute-start.14 = (bf16[2,1024,128]{2,1,0:T(8,128)(2,1)}, bf16[2,1024,128]{2,1,0:T(8,128)(2,1)}, u32[]{:S(2)}, u32[]{:S(2)}) collective-permute-start(bf16[2,1024,128]{2,1,0:T(8,128)(2,1)} %pad_maximum_fusion.15), channel_id=1, source_target_pairs={{0,11},{1,10},{2,9},{3,8},{4,15},{5,14},{6,13},{7,12},{8,3},{9,2},... | collective-permute-start | bytes 1572872 | tf_op jit(solution)/shard_map/ppermute | solution.py:124
  103.9 13.0 %copy-start.6 = (bf16[2,1024,128]{2,1,0:T(8,128)(2,1)S(1)}, bf16[2,1024,128]{2,1,0:T(8,128)(2,1)}, u32[]{:S(2)}) copy-start(bf16[2,1024,128]{2,1,0:T(8,128)(2,1)} %pad_maximum_fusion.12) | copy-start | bytes 1572868
  103.9 36.1 %collective-permute-start.13 = (bf16[2,1024,128]{2,1,0:T(8,128)(2,1)}, bf16[2,1024,128]{2,1,0:T(8,128)(2,1)}, u32[]{:S(2)}, u32[]{:S(2)}) collective-permute-start(bf16[2,1024,128]{2,1,0:T(8,128)(2,1)} %pad_maximum_fusion.14), channel_id=1, source_target_pairs={{0,12},{1,13},{2,14},{3,15},{4,8},{5,9},{6,10},{7,11},{8,4},{9,5},... | collective-permute-start | bytes 1572872 | tf_op jit(solution)/shard_map/ppermute | solution.py:124
  110.2 40.9 %collective-permute-start.12 = (bf16[2,1024,128]{2,1,0:T(8,128)(2,1)S(1)}, bf16[2,1024,128]{2,1,0:T(8,128)(2,1)}, u32[]{:S(2)}, u32[]{:S(2)}) collective-permute-start(bf16[2,1024,128]{2,1,0:T(8,128)(2,1)S(1)} %copy-done.7), channel_id=1, source_target_pairs={{0,13},{1,12},{2,15},{3,14},{4,9},{5,8},{6,11},{7,10},{8,5},{9,4},... | collective-permute-start | bytes 1572872 | tf_op jit(solution)/shard_map/ppermute | solution.py:124
  116.9 47.0 %collective-permute-start.11 = (bf16[2,1024,128]{2,1,0:T(8,128)(2,1)S(1)}, bf16[2,1024,128]{2,1,0:T(8,128)(2,1)}, u32[]{:S(2)}, u32[]{:S(2)}) collective-permute-start(bf16[2,1024,128]{2,1,0:T(8,128)(2,1)S(1)} %copy-done.6), channel_id=1, source_target_pairs={{0,14},{1,15},{2,12},{3,13},{4,10},{5,11},{6,8},{7,9},{8,6},{9,7},... | collective-permute-start | bytes 1572872 | tf_op jit(solution)/shard_map/ppermute | solution.py:124
  126.7 48.3 %collective-permute-start.10 = (bf16[2,1024,128]{2,1,0:T(8,128)(2,1)}, bf16[2,1024,128]{2,1,0:T(8,128)(2,1)}, u32[]{:S(2)}, u32[]{:S(2)}) collective-permute-start(bf16[2,1024,128]{2,1,0:T(8,128)(2,1)} %pad_maximum_fusion), channel_id=1, source_target_pairs={{0,15},{1,14},{2,13},{3,12},{4,11},{5,10},{6,9},{7,8},{8,7},{9,6},... | collective-permute-start | bytes 1572872 | tf_op jit(solution)/shard_map/ppermute | solution.py:124
  183.8 5.1 %copy-start.1 = (f32[8,2,32,4608]{3,2,1,0:T(8,128)}, f32[8,2,32,4608]{3,2,1,0:T(8,128)S(1)}, u32[]{:S(2)}) copy-start(f32[8,2,32,4608]{3,2,1,0:T(8,128)S(1)} %fusion.1) | copy-start | bytes 28311556
  188.9 8.3 %collective-permute-start.15 = (f32[8,32,4608]{2,1,0:T(8,128)}, f32[8,32,4608]{2,1,0:T(8,128)}, u32[]{:S(2)}, u32[]{:S(2)}) collective-permute-start(f32[8,32,4608]{2,1,0:T(8,128)} %dynamic-slice_bitcast_fusion), channel_id=1, source_target_pairs={{0,1},{1,0},{2,3},{3,2},{4,5},{5,4},{6,7},{7,6},{8,9},{9,8},{10,11... | collective-permute-start | bytes 14155784 | tf_op jit(solution)/shard_map/ppermute | solution.py:140

commit v13 on v4

--- a/solution.py
+++ b/solution.py
@@ -108,7 +108,13 @@
             ),
             axis=0,
         )
-        if shift:
+        if shift & 2:
+            n_pb = lax.axis_size("pb")
+            pairs = [
+                (p * n_kv + j, (p ^ 1) * n_kv + (j ^ shift)) for p in range(n_pb) for j in range(n_kv)
+            ]
+            block = lax.ppermute(block, ("pb",) + KV, pairs)
+        elif shift:
             block = lax.ppermute(block, KV, [(j, j ^ shift) for j in range(n_kv)])
         scalars = jnp.stack([row_first, src * key_dev, jnp.int32(rows_dev)]).astype(jnp.int32)
         total, summed = attend_kernel(scalars, q_block, block, total, summed)

time: 236 us -> 234 us (level); the launches traced: 236 us -> 231 us
  Pallas kernels: 85 us -> 81.6 us
    ppermute x15 -> x7, waiting for transfers between devices: 25.7 us -> 0.85 us  [by_heads(): block = lax.ppermute(block, KV, [(j, j ^ shift) for j in range(n_kv)])]
    ppermute x0 -> x8, waiting for transfers between devices: none -> 24 us  [by_heads(): block = lax.ppermute(block, ('pb',) + KV, pairs)]
    ppermute x15 -> x7, starting transfers between devices: 24.4 us -> 6.89 us  [by_heads(): block = lax.ppermute(block, KV, [(j, j ^ shift) for j in range(n_kv)])]
    ppermute x0 -> x8, starting transfers between devices: none -> 17.1 us  [by_heads(): block = lax.ppermute(block, ('pb',) + KV, pairs)]
    pallas_call x16, Pallas kernels: 85 us -> 81.6 us  [attend_kernel(): pl.pallas_call(block_kernel, grid_spec=grid_spec, out_shape=(jax.ShapeDty...]
  transfers between devices with their start and end apart: 16 -> 16, of which waited for: 5 -> 5; matrix products, arithmetic and copies ran while one was open for 12% -> 13% of each run, Pallas kernels for 34% -> 33%
where the time goes in v13:
time: 234 us; the launch traced here: 231 us
  Pallas kernels  81.6 us (35%)
  blocking collectives  39.6 us (17%)
  other arithmetic  34.8 us (15%)
  waiting for transfers between devices  32.9 us (14%)
  starting transfers between devices  24.1 us (10%)
  local copies, waits for them, and re-layouts  15.8 us (7%)
    pallas_call x16, Pallas kernels, attend_kernel(): pl.pallas_call(block_kernel, grid_spec=grid_spec, out_shape=(jax.ShapeDty...  81.6 us
    all_to_all x1, blocking collectives, per_device(): lax.all_to_all(on_chip.astype(jnp.bfloat16), 'kx', split_axis=0, concat_a...  39.6 us
    ppermute x8, waiting for transfers between devices, by_heads(): block = lax.ppermute(block, ('pb',) + KV, pairs)  24 us
    ppermute x8, starting transfers between devices, by_heads(): block = lax.ppermute(block, ('pb',) + KV, pairs)  17.1 us
    another operation x16, other arithmetic, by_heads(): jnp.stack((lax.dynamic_slice_in_dim(keys, dest * kv_feat, kv_feat, 1), la...  17 us
    another operation x16, other arithmetic, by_heads(): jnp.stack([row_first, src * key_dev, jnp.int32(rows_dev)]).astype(jnp.int32)  9.82 us
    ppermute x1, waiting for transfers between devices, per_device(): on_chip = mine + lax.ppermute(theirs, 'kc', [(0, 1), (1, 0)])  8.11 us
    ppermute x7, starting transfers between devices, by_heads(): block = lax.ppermute(block, KV, [(j, j ^ shift) for j in range(n_kv)])  6.89 us
  transfers between devices with their start and end apart: 16, of which 5 were waited for; matrix products, arithmetic and copies ran while one was open for 13% of the time, Pallas kernels for 33%

profile of v13, /device:TPU:120, one launch (start us, length us, event | category | flops | bytes accessed | tf_op | source)
XLA Modules:
  0.0 231.1 jit_solution(7647416673828619352)
XLA Ops:
  0.0 6.7 %dynamic-slice_bitcast_fusion.1 = (bf16[1,1024,128]{2,1,0:T(8,128)(2,1)}, bf16[1,1024,128]{2,1,0:T(8,128)(2,1)}, bf16[1,1024,128]{2,1,0:T(8,128)(2,1)}, bf16[1,1...) fusion(bf16[1024,2048]{1,0:T(8,128)(2,1)} %param.8, ...), kind=kLoop, calls=%fused_computation.24 | loop fusion | bytes 16777280 | tf_op jit(solution)/shard_map/stack | solution.py:104
  8.4 2.7 %collective-permute-start.5 = (bf16[2,1024,128]{2,1,0:T(8,128)(2,1)}, bf16[2,1024,128]{2,1,0:T(8,128)(2,1)}, u32[]{:S(2)}, u32[]{:S(2)}) collective-permute-start(bf16[2,1024,128]{2,1,0:T(8,128)(2,1)} %pad_maximum_fusion.5), channel_id=1, source_target_pairs={{0,26},{1,27},{2,24},{3,25},{4,30},{5,31},{6,28},{7,29},{8,18},{9,... | collective-permute-start | bytes 1572872 | tf_op jit(solution)/shard_map/ppermute | solution.py:116
  13.2 2.9 %collective-permute-start.7 = (bf16[2,1024,128]{2,1,0:T(8,128)(2,1)}, bf16[2,1024,128]{2,1,0:T(8,128)(2,1)}, u32[]{:S(2)}, u32[]{:S(2)}) collective-permute-start(bf16[2,1024,128]{2,1,0:T(8,128)(2,1)} %pad_maximum_fusion.7), channel_id=1, source_target_pairs={{0,8},{1,9},{2,10},{3,11},{4,12},{5,13},{6,14},{7,15},{8,0},{9,1},... | collective-permute-start | bytes 1572872 | tf_op jit(solution)/shard_map/ppermute | solution.py:118
  16.9 2.7 %collective-permute-start.8 = (bf16[2,1024,128]{2,1,0:T(8,128)(2,1)}, bf16[2,1024,128]{2,1,0:T(8,128)(2,1)}, u32[]{:S(2)}, u32[]{:S(2)}) collective-permute-start(bf16[2,1024,128]{2,1,0:T(8,128)(2,1)} %pad_maximum_fusion.8), channel_id=1, source_target_pairs={{0,23},{1,22},{2,21},{3,20},{4,19},{5,18},{6,17},{7,16},{8,31},{9,... | collective-permute-start | bytes 1572872 | tf_op jit(solution)/shard_map/ppermute | solution.py:116
  43.5 2.8 %collective-permute-start.12 = (bf16[2,1024,128]{2,1,0:T(8,128)(2,1)}, bf16[2,1024,128]{2,1,0:T(8,128)(2,1)}, u32[]{:S(2)}, u32[]{:S(2)}) collective-permute-start(bf16[2,1024,128]{2,1,0:T(8,128)(2,1)} %pad_maximum_fusion.12), channel_id=1, source_target_pairs={{0,19},{1,18},{2,17},{3,16},{4,23},{5,22},{6,21},{7,20},{8,27},{9,... | collective-permute-start | bytes 1572872 | tf_op jit(solution)/shard_map/ppermute | solution.py:116
  47.1 3.0 %collective-permute-start.13 = (bf16[2,1024,128]{2,1,0:T(8,128)(2,1)}, bf16[2,1024,128]{2,1,0:T(8,128)(2,1)}, u32[]{:S(2)}, u32[]{:S(2)}) collective-permute-start(bf16[2,1024,128]{2,1,0:T(8,128)(2,1)} %pad_maximum_fusion.13), channel_id=1, source_target_pairs={{0,18},{1,19},{2,16},{3,17},{4,22},{5,23},{6,20},{7,21},{8,26},{9,... | collective-permute-start | bytes 1572872 | tf_op jit(solution)/shard_map/ppermute | solution.py:116
  50.7 9.4 %collective-permute-done.8.k_ref.v_ref = bf16[2,1024,128]{2,1,0:T(8,128)(2,1)} collective-permute-done((bf16[2,1024,128]{2,1,0:T(8,128)(2,1)}, bf16[2,1024,128]{2,1,0:T(8,128)(2,1)}, u32[]{:S(2)}, u32[]{:S(2)}) %collective-permute-start.8) | collective-permute-done | bytes 524320 | tf_op jit(solution)/shard_map/ppermute | solution.py:116
  63.8 8.2 %collective-permute-done.9.k_ref.v_ref = bf16[2,1024,128]{2,1,0:T(8,128)(2,1)S(1)} collective-permute-done((bf16[2,1024,128]{2,1,0:T(8,128)(2,1)}, bf16[2,1024,128]{2,1,0:T(8,128)(2,1)S(1)}, u32[]{:S(2)}, u32[]{:S(2)}) %collective-permute-start.9) | collective-permute-done | bytes 524320 | tf_op jit(solution)/shard_map/ppermute | solution.py:116
  74.5 5.6 %shard_map.55 = (f32[1024,1]{1,0:T(8,128)}, f32[1024,128]{1,0:T(8,128)}) custom-call(s32[3]{0:T(128)} %pad_add_fusion.sc_ref, bf16[1024,128]{1,0:T(8,128)(2,1)} %bitcast.107, bf16[2,1024,128]{2,1,0:T(8,128)(2,1)} %pad_maximum_fusion.15.k_ref.v_ref, ...), custom_call_target="tpu_custom_call", output_to_operand_aliasing={{0}: (4, {}), {1}: (5, {})} | custom-call | flops 536870912 | bytes 1843200 | tf_op jit(solution)/shard_map/pallas_call | solution.py:73
  81.1 5.6 %shard_map.56 = (f32[1024,1]{1,0:T(8,128)}, f32[1024,128]{1,0:T(8,128)}) custom-call(s32[3]{0:T(128)} %pad_add_fusion.1.sc_ref, bf16[1024,128]{1,0:T(8,128)(2,1)} %bitcast.108, bf16[2,1024,128]{2,1,0:T(8,128)(2,1)} %collective-permute-done.14.k_ref.v_ref, ...), custom_call_target="tpu_custom_call", output_to_operand_aliasing={{0}: (4, {}), {1}: (5, {})} | custom-call | flops 536870912 | bytes 1843200 | tf_op jit(solution)/shard_map/pallas_call | solution.py:73
  86.6 6.3 %collective-permute-done.13.k_ref.v_ref = bf16[2,1024,128]{2,1,0:T(8,128)(2,1)} collective-permute-done((bf16[2,1024,128]{2,1,0:T(8,128)(2,1)}, bf16[2,1024,128]{2,1,0:T(8,128)(2,1)}, u32[]{:S(2)}, u32[]{:S(2)}) %collective-permute-start.13) | collective-permute-done | bytes 524320 | tf_op jit(solution)/shard_map/ppermute | solution.py:116
  93.6 5.6 %shard_map.57 = (f32[1024,1]{1,0:T(8,128)}, f32[1024,128]{1,0:T(8,128)}) custom-call(s32[3]{0:T(128)} %pad_add_fusion.2.sc_ref, bf16[1024,128]{1,0:T(8,128)(2,1)} %bitcast.109, bf16[2,1024,128]{2,1,0:T(8,128)(2,1)} %collective-permute-done.13.k_ref.v_ref, ...), custom_call_target="tpu_custom_call", output_to_operand_aliasing={{0}: (4, {}), {1}: (5, {})} | custom-call | flops 536870912 | bytes 1843200 | tf_op jit(solution)/shard_map/pallas_call | solution.py:73
  99.2 2.3 collective-permute-start.1
  101.4 5.6 %shard_map.58 = (f32[1024,1]{1,0:T(8,128)}, f32[1024,128]{1,0:T(8,128)}) custom-call(s32[3]{0:T(128)} %pad_add_fusion.3.sc_ref, bf16[1024,128]{1,0:T(8,128)(2,1)} %bitcast.110, bf16[2,1024,128]{2,1,0:T(8,128)(2,1)} %collective-permute-done.12.k_ref.v_ref, ...), custom_call_target="tpu_custom_call", output_to_operand_aliasing={{0}: (4, {}), {1}: (5, {})} | custom-call | flops 536870912 | bytes 1843200 | tf_op jit(solution)/shard_map/pallas_call | solution.py:73
  107.0 2.0 collective-permute-start
  109.1 5.8 %shard_map.59 = (f32[1024,1]{1,0:T(8,128)}, f32[1024,128]{1,0:T(8,128)}) custom-call(s32[3]{0:T(128)} %pad_add_fusion.4.sc_ref, bf16[1024,128]{1,0:T(8,128)(2,1)} %bitcast.111, bf16[2,1024,128]{2,1,0:T(8,128)(2,1)} %collective-permute-done.11.k_ref.v_ref, ...), custom_call_target="tpu_custom_call", output_to_operand_aliasing={{0}: (4, {}), {1}: (5, {})} | custom-call | flops 536870912 | bytes 1843200 | tf_op jit(solution)/shard_map/pallas_call | solution.py:73
  114.8 5.6 %shard_map.60 = (f32[1024,1]{1,0:T(8,128)}, f32[1024,128]{1,0:T(8,128)}) custom-call(s32[3]{0:T(128)} %pad_add_fusion.5.sc_ref, bf16[1024,128]{1,0:T(8,128)(2,1)} %bitcast.112, bf16[2,1024,128]{2,1,0:T(8,128)(2,1)} %collective-permute-done.10.k_ref.v_ref, ...), custom_call_target="tpu_custom_call", output_to_operand_aliasing={{0}: (4, {}), {1}: (5, {})} | custom-call | flops 536870912 | bytes 1843200 | tf_op jit(solution)/shard_map/pallas_call | solution.py:73
  120.4 5.6 %shard_map.61 = (f32[1024,1]{1,0:T(8,128)}, f32[1024,128]{1,0:T(8,128)}) custom-call(s32[3]{0:T(128)} %pad_add_fusion.6.sc_ref, bf16[1024,128]{1,0:T(8,128)(2,1)} %bitcast.113, bf16[2,1024,128]{2,1,0:T(8,128)(2,1)} %copy-done.13, bf16[2,1024,128]{2,1,0:T(8,128)(2,1)} %copy-done.13, ...), custom_call_target="tpu_custom_call", output_to_operand_aliasing={{0}: (4, {}), {1}: (5, {})} | custom-call | flops 536870912 | bytes 1843200 | tf_op jit(solution)/shard_map/pallas_call | solution.py:73
  126.0 5.6 %shard_map.62 = (f32[1024,1]{1,0:T(8,128)}, f32[1024,128]{1,0:T(8,128)}) custom-call(s32[3]{0:T(128)} %pad_add_fusion.7.sc_ref, bf16[1024,128]{1,0:T(8,128)(2,1)} %bitcast.114, bf16[2,1024,128]{2,1,0:T(8,128)(2,1)} %collective-permute-done.8.k_ref.v_ref, ...), custom_call_target="tpu_custom_call", output_to_operand_aliasing={{0}: (4, {}), {1}: (5, {})} | custom-call | flops 536870912 | bytes 1843200 | tf_op jit(solution)/shard_map/pallas_call | solution.py:73
  131.6 4.4 %shard_map.63 = (f32[1024,1]{1,0:T(8,128)}, f32[1024,128]{1,0:T(8,128)}) custom-call(s32[3]{0:T(128)} %pad_add_fusion.8.sc_ref, bf16[1024,128]{1,0:T(8,128)(2,1)} %bitcast.115, bf16[2,1024,128]{2,1,0:T(8,128)(2,1)} %collective-permute-done.7.k_ref.v_ref, ...), custom_call_target="tpu_custom_call", output_to_operand_aliasing={{0}: (4, {}), {1}: (5, {})} | custom-call | flops 536870912 | bytes 1843200 | tf_op jit(solution)/shard_map/pallas_call | solution.py:73
  136.0 4.4 %shard_map.64 = (f32[1024,1]{1,0:T(8,128)}, f32[1024,128]{1,0:T(8,128)}) custom-call(s32[3]{0:T(128)} %pad_add_fusion.9.sc_ref, bf16[1024,128]{1,0:T(8,128)(2,1)} %bitcast.116, bf16[2,1024,128]{2,1,0:T(8,128)(2,1)} %collective-permute-done.6.k_ref.v_ref, ...), custom_call_target="tpu_custom_call", output_to_operand_aliasing={{0}: (4, {}), {1}: (5, {})} | custom-call | flops 536870912 | bytes 1843200 | tf_op jit(solution)/shard_map/pallas_call | solution.py:73
  140.5 5.6 %shard_map.65 = (f32[1024,1]{1,0:T(8,128)}, f32[1024,128]{1,0:T(8,128)}) custom-call(s32[3]{0:T(128)} %pad_add_fusion.10.sc_ref, bf16[1024,128]{1,0:T(8,128)(2,1)} %bitcast.117, bf16[2,1024,128]{2,1,0:T(8,128)(2,1)} %collective-permute-done.5.k_ref.v_ref, ...), custom_call_target="tpu_custom_call", output_to_operand_aliasing={{0}: (4, {}), {1}: (5, {})} | custom-call | flops 536870912 | bytes 1843200 | tf_op jit(solution)/shard_map/pallas_call | solution.py:73
  146.1 4.4 %shard_map.66 = (f32[1024,1]{1,0:T(8,128)}, f32[1024,128]{1,0:T(8,128)}) custom-call(s32[3]{0:T(128)} %pad_add_fusion.11.sc_ref, bf16[1024,128]{1,0:T(8,128)(2,1)} %bitcast.118, bf16[2,1024,128]{2,1,0:T(8,128)(2,1)} %collective-permute-done.4.k_ref.v_ref, ...), custom_call_target="tpu_custom_call", output_to_operand_aliasing={{0}: (4, {}), {1}: (5, {})} | custom-call | flops 536870912 | bytes 1843200 | tf_op jit(solution)/shard_map/pallas_call | solution.py:73
  150.6 4.4 %shard_map.67 = (f32[1024,1]{1,0:T(8,128)}, f32[1024,128]{1,0:T(8,128)}) custom-call(s32[3]{0:T(128)} %pad_add_fusion.12.sc_ref, bf16[1024,128]{1,0:T(8,128)(2,1)} %bitcast.119, bf16[2,1024,128]{2,1,0:T(8,128)(2,1)} %collective-permute-done.3.k_ref.v_ref, ...), custom_call_target="tpu_custom_call", output_to_operand_aliasing={{0}: (4, {}), {1}: (5, {})} | custom-call | flops 536870912 | bytes 1843200 | tf_op jit(solution)/shard_map/pallas_call | solution.py:73
  155.0 4.4 %shard_map.68 = (f32[1024,1]{1,0:T(8,128)}, f32[1024,128]{1,0:T(8,128)}) custom-call(s32[3]{0:T(128)} %pad_add_fusion.13.sc_ref, bf16[1024,128]{1,0:T(8,128)(2,1)} %bitcast.120, bf16[2,1024,128]{2,1,0:T(8,128)(2,1)} %collective-permute-done.2.k_ref.v_ref, ...), custom_call_target="tpu_custom_call", output_to_operand_aliasing={{0}: (4, {}), {1}: (5, {})} | custom-call | flops 536870912 | bytes 1843200 | tf_op jit(solution)/shard_map/pallas_call | solution.py:73
  159.4 4.4 %shard_map.69 = (f32[1024,1]{1,0:T(8,128)}, f32[1024,128]{1,0:T(8,128)}) custom-call(s32[3]{0:T(128)} %pad_add_fusion.14.sc_ref, bf16[1024,128]{1,0:T(8,128)(2,1)} %bitcast.121, bf16[2,1024,128]{2,1,0:T(8,128)(2,1)} %collective-permute-done.1.k_ref.v_ref, ...), custom_call_target="tpu_custom_call", output_to_operand_aliasing={{0}: (4, {}), {1}: (5, {})} | custom-call | flops 536870912 | bytes 1843200 | tf_op jit(solution)/shard_map/pallas_call | solution.py:73
  163.9 4.4 %shard_map.70 = (f32[1024,1]{1,0:T(8,128)}, f32[1024,128]{1,0:T(8,128)}) custom-call(s32[3]{0:T(128)} %pad_add_fusion.15.sc_ref, bf16[1024,128]{1,0:T(8,128)(2,1)} %bitcast.122, bf16[2,1024,128]{2,1,0:T(8,128)(2,1)} %collective-permute-done.k_ref.v_ref, ...), custom_call_target="tpu_custom_call", output_to_operand_aliasing={{0}: (4, {}), {1}: (5, {})} | custom-call | flops 536870912 | bytes 1843200 | tf_op jit(solution)/shard_map/pallas_call | solution.py:73
  172.7 2.9 %dynamic-slice_bitcast_fusion = f32[8,32,4608]{2,1,0:T(8,128)} fusion(f32[8,2,32,4608]{3,2,1,0:T(8,128)S(1)} %fusion.1, s32[]{:T(128)S(6)} %select_n.88), kind=kLoop, calls=%fused_computation.3 | loop fusion | bytes 9437188 | tf_op jit(solution)/shard_map/jit(dynamic_index_in_dim)/squeeze | solution.py:135
  175.5 2.2 copy-done.1
  177.9 8.1 %collective-permute-done.15 = f32[8,32,4608]{2,1,0:T(8,128)} collective-permute-done((f32[8,32,4608]{2,1,0:T(8,128)}, f32[8,32,4608]{2,1,0:T(8,128)}, u32[]{:S(2)}, u32[]{:S(2)}) %collective-permute-start.15) | collective-permute-done | bytes 4718624 | tf_op jit(solution)/shard_map/ppermute | solution.py:136
  186.0 4.3 %fusion = bf16[8,32,4608]{2,1,0:T(8,128)(2,1)S(1)} fusion(f32[8,32,4608]{2,1,0:T(8,128)} %collective-permute-done.15, f32[8,2,32,4608]{3,2,1,0:T(8,128)} %copy-done.1, s32[]{:T(128)S(6)} %select_n.87), kind=kLoop, calls=%fused_computation.1 | loop fusion | flops 2359296 | bytes 11796484 | tf_op jit(solution)/shard_map/convert_element_type | solution.py:138
  190.3 39.6 %all_to_all.5 = bf16[8,32,4608]{2,1,0:T(8,128)(2,1)S(1)} all-to-all(bf16[8,32,4608]{2,1,0:T(8,128)(2,1)S(1)} %fusion), channel_id=1, replica_groups=mesh['pb'=8,'kx'=8,'kc'=2] {'kx'}, dimensions={0} | all-to-all | bytes 4718592 | tf_op jit(solution)/shard_map/all_to_all | solution.py:137
  (89 shorter events, 42.6 us)
Async XLA Ops:
  0.0 171.3 %copy-start = (bf16[256,4608]{1,0:T(8,128)(2,1)S(1)}, bf16[256,4608]{1,0:T(8,128)(2,1)}, u32[]{:S(2)}) copy-start(bf16[256,4608]{1,0:T(8,128)(2,1)} %param.9) | copy-start | bytes 7077892
  7.5 33.6 %collective-permute-start.14 = (bf16[2,1024,128]{2,1,0:T(8,128)(2,1)}, bf16[2,1024,128]{2,1,0:T(8,128)(2,1)}, u32[]{:S(2)}, u32[]{:S(2)}) collective-permute-start(bf16[2,1024,128]{2,1,0:T(8,128)(2,1)} %pad_maximum_fusion.14), channel_id=1, source_target_pairs={{0,1},{1,0},{2,3},{3,2},{4,5},{5,4},{6,7},{7,6},{8,9},{9,8},{10,11... | collective-permute-start | bytes 1572872 | tf_op jit(solution)/shard_map/ppermute | solution.py:118
  8.4 34.0 %collective-permute-start.5 = (bf16[2,1024,128]{2,1,0:T(8,128)(2,1)}, bf16[2,1024,128]{2,1,0:T(8,128)(2,1)}, u32[]{:S(2)}, u32[]{:S(2)}) collective-permute-start(bf16[2,1024,128]{2,1,0:T(8,128)(2,1)} %pad_maximum_fusion.5), channel_id=1, source_target_pairs={{0,26},{1,27},{2,24},{3,25},{4,30},{5,31},{6,28},{7,29},{8,18},{9,... | collective-permute-start | bytes 1572872 | tf_op jit(solution)/shard_map/ppermute | solution.py:116
  11.9 31.6 %collective-permute-start.6 = (bf16[2,1024,128]{2,1,0:T(8,128)(2,1)}, bf16[2,1024,128]{2,1,0:T(8,128)(2,1)}, u32[]{:S(2)}, u32[]{:S(2)}) collective-permute-start(bf16[2,1024,128]{2,1,0:T(8,128)(2,1)} %pad_maximum_fusion.6), channel_id=1, source_target_pairs={{0,9},{1,8},{2,11},{3,10},{4,13},{5,12},{6,15},{7,14},{8,1},{9,0},... | collective-permute-start | bytes 1572872 | tf_op jit(solution)/shard_map/ppermute | solution.py:118
  13.2 33.9 %collective-permute-start.7 = (bf16[2,1024,128]{2,1,0:T(8,128)(2,1)}, bf16[2,1024,128]{2,1,0:T(8,128)(2,1)}, u32[]{:S(2)}, u32[]{:S(2)}) collective-permute-start(bf16[2,1024,128]{2,1,0:T(8,128)(2,1)} %pad_maximum_fusion.7), channel_id=1, source_target_pairs={{0,8},{1,9},{2,10},{3,11},{4,12},{5,13},{6,14},{7,15},{8,0},{9,1},... | collective-permute-start | bytes 1572872 | tf_op jit(solution)/shard_map/ppermute | solution.py:118
  16.9 43.1 %collective-permute-start.8 = (bf16[2,1024,128]{2,1,0:T(8,128)(2,1)}, bf16[2,1024,128]{2,1,0:T(8,128)(2,1)}, u32[]{:S(2)}, u32[]{:S(2)}) collective-permute-start(bf16[2,1024,128]{2,1,0:T(8,128)(2,1)} %pad_maximum_fusion.8), channel_id=1, source_target_pairs={{0,23},{1,22},{2,21},{3,20},{4,19},{5,18},{6,17},{7,16},{8,31},{9,... | collective-permute-start | bytes 1572872 | tf_op jit(solution)/shard_map/ppermute | solution.py:116
  20.3 13.9 %copy-start.10 = (bf16[1,1024,128]{2,1,0:T(8,128)(2,1)S(1)}, bf16[1,1024,128]{2,1,0:T(8,128)(2,1)}, u32[]{:S(2)}) copy-start(bf16[1,1024,128]{2,1,0:T(8,128)(2,1)} %get-tuple-element.89) | copy-start | bytes 786436
  20.3 13.9 %copy-start.11 = (bf16[1,1024,128]{2,1,0:T(8,128)(2,1)S(1)}, bf16[1,1024,128]{2,1,0:T(8,128)(2,1)}, u32[]{:S(2)}) copy-start(bf16[1,1024,128]{2,1,0:T(8,128)(2,1)} %get-tuple-element.112) | copy-start | bytes 786436
  20.3 14.8 %copy-start.8 = (bf16[1,1024,128]{2,1,0:T(8,128)(2,1)S(1)}, bf16[1,1024,128]{2,1,0:T(8,128)(2,1)}, u32[]{:S(2)}) copy-start(bf16[1,1024,128]{2,1,0:T(8,128)(2,1)} %get-tuple-element.90) | copy-start | bytes 786436
  20.3 14.8 %copy-start.9 = (bf16[1,1024,128]{2,1,0:T(8,128)(2,1)S(1)}, bf16[1,1024,128]{2,1,0:T(8,128)(2,1)}, u32[]{:S(2)}) copy-start(bf16[1,1024,128]{2,1,0:T(8,128)(2,1)} %get-tuple-element.111) | copy-start | bytes 786436
  20.3 15.6 %copy-start.6 = (bf16[1,1024,128]{2,1,0:T(8,128)(2,1)S(1)}, bf16[1,1024,128]{2,1,0:T(8,128)(2,1)}, u32[]{:S(2)}) copy-start(bf16[1,1024,128]{2,1,0:T(8,128)(2,1)} %get-tuple-element.95) | copy-start | bytes 786436
  20.3 15.6 %copy-start.7 = (bf16[1,1024,128]{2,1,0:T(8,128)(2,1)S(1)}, bf16[1,1024,128]{2,1,0:T(8,128)(2,1)}, u32[]{:S(2)}) copy-start(bf16[1,1024,128]{2,1,0:T(8,128)(2,1)} %get-tuple-element.106) | copy-start | bytes 786436
  20.3 16.4 %copy-start.4 = (bf16[1,1024,128]{2,1,0:T(8,128)(2,1)S(1)}, bf16[1,1024,128]{2,1,0:T(8,128)(2,1)}, u32[]{:S(2)}) copy-start(bf16[1,1024,128]{2,1,0:T(8,128)(2,1)} %get-tuple-element.96) | copy-start | bytes 786436
  20.3 16.4 %copy-start.5 = (bf16[1,1024,128]{2,1,0:T(8,128)(2,1)S(1)}, bf16[1,1024,128]{2,1,0:T(8,128)(2,1)}, u32[]{:S(2)}) copy-start(bf16[1,1024,128]{2,1,0:T(8,128)(2,1)} %get-tuple-element.105) | copy-start | bytes 786436
  26.5 11.1 %copy-start.2 = (bf16[1,1024,128]{2,1,0:T(8,128)(2,1)S(1)}, bf16[1,1024,128]{2,1,0:T(8,128)(2,1)}, u32[]{:S(2)}) copy-start(bf16[1,1024,128]{2,1,0:T(8,128)(2,1)} %get-tuple-element.97) | copy-start | bytes 786436
  26.5 11.1 %copy-start.3 = (bf16[1,1024,128]{2,1,0:T(8,128)(2,1)S(1)}, bf16[1,1024,128]{2,1,0:T(8,128)(2,1)}, u32[]{:S(2)}) copy-start(bf16[1,1024,128]{2,1,0:T(8,128)(2,1)} %get-tuple-element.104) | copy-start | bytes 786436
  41.2 30.9 %collective-permute-start.9 = (bf16[2,1024,128]{2,1,0:T(8,128)(2,1)}, bf16[2,1024,128]{2,1,0:T(8,128)(2,1)S(1)}, u32[]{:S(2)}, u32[]{:S(2)}) collective-permute-start(bf16[2,1024,128]{2,1,0:T(8,128)(2,1)} %pad_maximum_fusion.9), channel_id=1, source_target_pairs={{0,22},{1,23},{2,20},{3,21},{4,18},{5,19},{6,16},{7,17},{8,30},{9,... | collective-permute-start | bytes 1572872 | tf_op jit(solution)/shard_map/ppermute | solution.py:116
  42.3 37.8 %collective-permute-start.10 = (bf16[2,1024,128]{2,1,0:T(8,128)(2,1)}, bf16[2,1024,128]{2,1,0:T(8,128)(2,1)}, u32[]{:S(2)}, u32[]{:S(2)}) collective-permute-start(bf16[2,1024,128]{2,1,0:T(8,128)(2,1)} %pad_maximum_fusion.10), channel_id=1, source_target_pairs={{0,5},{1,4},{2,7},{3,6},{4,1},{5,0},{6,3},{7,2},{8,13},{9,12},{10,... | collective-permute-start | bytes 1572872 | tf_op jit(solution)/shard_map/ppermute | solution.py:118
  43.5 55.7 %collective-permute-start.12 = (bf16[2,1024,128]{2,1,0:T(8,128)(2,1)}, bf16[2,1024,128]{2,1,0:T(8,128)(2,1)}, u32[]{:S(2)}, u32[]{:S(2)}) collective-permute-start(bf16[2,1024,128]{2,1,0:T(8,128)(2,1)} %pad_maximum_fusion.12), channel_id=1, source_target_pairs={{0,19},{1,18},{2,17},{3,16},{4,23},{5,22},{6,21},{7,20},{8,27},{9,... | collective-permute-start | bytes 1572872 | tf_op jit(solution)/shard_map/ppermute | solution.py:116
  47.1 45.8 %collective-permute-start.13 = (bf16[2,1024,128]{2,1,0:T(8,128)(2,1)}, bf16[2,1024,128]{2,1,0:T(8,128)(2,1)}, u32[]{:S(2)}, u32[]{:S(2)}) collective-permute-start(bf16[2,1024,128]{2,1,0:T(8,128)(2,1)} %pad_maximum_fusion.13), channel_id=1, source_target_pairs={{0,18},{1,19},{2,16},{3,17},{4,22},{5,23},{6,20},{7,21},{8,26},{9,... | collective-permute-start | bytes 1572872 | tf_op jit(solution)/shard_map/ppermute | solution.py:116
  60.1 47.0 %collective-permute-start.11 = (bf16[2,1024,128]{2,1,0:T(8,128)(2,1)}, bf16[2,1024,128]{2,1,0:T(8,128)(2,1)}, u32[]{:S(2)}, u32[]{:S(2)}) collective-permute-start(bf16[2,1024,128]{2,1,0:T(8,128)(2,1)} %pad_maximum_fusion.11), channel_id=1, source_target_pairs={{0,4},{1,5},{2,6},{3,7},{4,0},{5,1},{6,2},{7,3},{8,12},{9,13},{10,... | collective-permute-start | bytes 1572872 | tf_op jit(solution)/shard_map/ppermute | solution.py:118
  72.1 0.8 copy-start.13
  72.1 74.0 %collective-permute-start.4 = (bf16[2,1024,128]{2,1,0:T(8,128)(2,1)}, bf16[2,1024,128]{2,1,0:T(8,128)(2,1)}, u32[]{:S(2)}, u32[]{:S(2)}) collective-permute-start(bf16[2,1024,128]{2,1,0:T(8,128)(2,1)} %pad_maximum_fusion.4), channel_id=1, source_target_pairs={{0,27},{1,26},{2,25},{3,24},{4,31},{5,30},{6,29},{7,28},{8,19},{9,... | collective-permute-start | bytes 1572872 | tf_op jit(solution)/shard_map/ppermute | solution.py:116
  73.7 19.3 %copy-start.12 = (bf16[2,1024,128]{2,1,0:T(8,128)(2,1)S(1)}, bf16[2,1024,128]{2,1,0:T(8,128)(2,1)}, u32[]{:S(2)}) copy-start(bf16[2,1024,128]{2,1,0:T(8,128)(2,1)} %pad_maximum_fusion.2) | copy-start | bytes 1572868
  80.1 70.5 %collective-permute-start.3 = (bf16[2,1024,128]{2,1,0:T(8,128)(2,1)}, bf16[2,1024,128]{2,1,0:T(8,128)(2,1)}, u32[]{:S(2)}, u32[]{:S(2)}) collective-permute-start(bf16[2,1024,128]{2,1,0:T(8,128)(2,1)} %pad_maximum_fusion.3), channel_id=1, source_target_pairs={{0,12},{1,13},{2,14},{3,15},{4,8},{5,9},{6,10},{7,11},{8,4},{9,5},... | collective-permute-start | bytes 1572872 | tf_op jit(solution)/shard_map/ppermute | solution.py:118
  93.0 62.0 %collective-permute-start.2 = (bf16[2,1024,128]{2,1,0:T(8,128)(2,1)S(1)}, bf16[2,1024,128]{2,1,0:T(8,128)(2,1)}, u32[]{:S(2)}, u32[]{:S(2)}) collective-permute-start(bf16[2,1024,128]{2,1,0:T(8,128)(2,1)S(1)} %copy-done.12), channel_id=1, source_target_pairs={{0,13},{1,12},{2,15},{3,14},{4,9},{5,8},{6,11},{7,10},{8,5},{9,4},... | collective-permute-start | bytes 1572872 | tf_op jit(solution)/shard_map/ppermute | solution.py:118
  99.2 60.3 %collective-permute-start.1 = (bf16[2,1024,128]{2,1,0:T(8,128)(2,1)}, bf16[2,1024,128]{2,1,0:T(8,128)(2,1)}, u32[]{:S(2)}, u32[]{:S(2)}) collective-permute-start(bf16[2,1024,128]{2,1,0:T(8,128)(2,1)} %pad_maximum_fusion.1), channel_id=1, source_target_pairs={{0,30},{1,31},{2,28},{3,29},{4,26},{5,27},{6,24},{7,25},{8,22},{9,... | collective-permute-start | bytes 1572872 | tf_op jit(solution)/shard_map/ppermute | solution.py:116
  107.0 56.8 %collective-permute-start = (bf16[2,1024,128]{2,1,0:T(8,128)(2,1)S(1)}, bf16[2,1024,128]{2,1,0:T(8,128)(2,1)}, u32[]{:S(2)}, u32[]{:S(2)}) collective-permute-start(bf16[2,1024,128]{2,1,0:T(8,128)(2,1)S(1)} %pad_maximum_fusion), channel_id=1, source_target_pairs={{0,31},{1,30},{2,29},{3,28},{4,27},{5,26},{6,25},{7,24},{8,23},{9,... | collective-permute-start | bytes 1572872 | tf_op jit(solution)/shard_map/ppermute | solution.py:116
  172.7 5.0 %copy-start.1 = (f32[8,2,32,4608]{3,2,1,0:T(8,128)}, f32[8,2,32,4608]{3,2,1,0:T(8,128)S(1)}, u32[]{:S(2)}) copy-start(f32[8,2,32,4608]{3,2,1,0:T(8,128)S(1)} %fusion.1) | copy-start | bytes 28311556
  177.7 8.3 %collective-permute-start.15 = (f32[8,32,4608]{2,1,0:T(8,128)}, f32[8,32,4608]{2,1,0:T(8,128)}, u32[]{:S(2)}, u32[]{:S(2)}) collective-permute-start(f32[8,32,4608]{2,1,0:T(8,128)} %dynamic-slice_bitcast_fusion), channel_id=1, source_target_pairs={{0,1},{1,0},{2,3},{3,2},{4,5},{5,4},{6,7},{7,6},{8,9},{9,8},{10,11... | collective-permute-start | bytes 14155784 | tf_op jit(solution)/shard_map/ppermute | solution.py:136

commit v14 on v4

--- a/solution.py
+++ b/solution.py
@@ -10,7 +10,8 @@
 HD = 128
 CAP = 50
 SCALAR = 144
-KV = ("kx", "kc")
+CHIP = ("kxx", "kxy")
+KV = CHIP + ("kc",)
 TQ = 256
 
 
@@ -121,22 +122,28 @@
     row_first = slab_start[0] + lax.axis_index("pb") * rows_dev
     attended = by_heads(queries, keys, values, row_first)
     partial = jnp.dot(attended, out_weight, preferred_element_type=jnp.float32)
-    n_chip = lax.axis_size("kx")
+    n_chip = lax.axis_size(CHIP)
     n_core = lax.axis_size("kc")
     partial = partial.reshape(n_chip, n_core, rows_dev // (n_chip * n_core), partial.shape[1])
     core = lax.axis_index("kc")
     mine = lax.dynamic_index_in_dim(partial, core, 1, keepdims=False)
     theirs = lax.dynamic_index_in_dim(partial, 1 - core, 1, keepdims=False)
     on_chip = mine + lax.ppermute(theirs, "kc", [(0, 1), (1, 0)])
+    n_y = lax.axis_size("kxy")
+    on_chip = on_chip.reshape(n_chip // n_y, n_y, *on_chip.shape[1:])
+    y = lax.axis_index("kxy")
+    near = lax.dynamic_index_in_dim(on_chip, y, 1, keepdims=False)
+    far = lax.dynamic_index_in_dim(on_chip, 1 - y, 1, keepdims=False).astype(jnp.bfloat16)
+    on_row = near + lax.ppermute(far, "kxy", [(0, 1), (1, 0)]).astype(jnp.float32)
     parts = lax.all_to_all(
-        on_chip.astype(jnp.bfloat16), "kx", split_axis=0, concat_axis=0, tiled=True
+        on_row.astype(jnp.bfloat16), "kxx", split_axis=0, concat_axis=0, tiled=True
     )
     return jnp.sum(parts.astype(jnp.float32), axis=0)
 
 
 def solution(mesh):
     n_pb, n_kv = mesh.devices.shape
-    split = Mesh(mesh.devices.reshape(n_pb, n_kv // 2, 2), ("pb", "kx", "kc"))
+    split = Mesh(mesh.devices.reshape(n_pb, n_kv // 4, 2, 2), ("pb",) + KV)
     in_specs = (P(), P("pb", KV), P(KV, None), P(KV, None), P(KV, None))
     out_specs = P(("pb",) + KV, None)
     return jax.shard_map(

time: 236 us -> 252 us (1.068); the launches traced: 236 us -> 249 us
  blocking collectives: 40.4 us -> 19.9 us
  waiting for transfers between devices: 33.6 us -> 54.1 us
  Pallas kernels: 85 us -> 89.8 us
  local copies, waits for them, and re-layouts: 15.5 us -> 18.9 us
    ppermute x0 -> x1, waiting for transfers between devices: none -> 27.7 us  [per_device(): lax.ppermute(far, 'kxy', [(0, 1), (1, 0)]).astype(jnp.float32)]
    all_to_all x1, blocking collectives: 40.4 us -> 19.9 us  [per_device(): lax.all_to_all(on_row.astype(jnp.bfloat16), 'kxx', split_axis=0, concat_a...]
    ppermute x15, waiting for transfers between devices: 25.7 us -> 18.6 us  [by_heads(): block = lax.ppermute(block, KV, [(j, j ^ shift) for j in range(n_kv)])]
    pallas_call x16, Pallas kernels: 85 us -> 89.8 us  [attend_kernel(): pl.pallas_call(block_kernel, grid_spec=grid_spec, out_shape=(jax.ShapeDty...]
    add x0 -> x1, other arithmetic: none -> 4.37 us  [per_device(): on_chip = mine + lax.ppermute(theirs, 'kc', [(0, 1), (1, 0)])]
  transfers between devices with their start and end apart: 16 -> 17, of which waited for: 5 -> 7; matrix products, arithmetic and copies ran while one was open for 12% -> 12% of each run, Pallas kernels for 34% -> 34%
where the time goes in v14:
time: 252 us; the launch traced here: 249 us
  Pallas kernels  89.8 us (36%)
  waiting for transfers between devices  54.1 us (21%)
  other arithmetic  36.6 us (15%)
  starting transfers between devices  27.2 us (11%)
  blocking collectives  19.9 us (8%)
  local copies, waits for them, and re-layouts  18.9 us (7%)
    pallas_call x16, Pallas kernels, attend_kernel(): pl.pallas_call(block_kernel, grid_spec=grid_spec, out_shape=(jax.ShapeDty...  89.8 us
    ppermute x1, waiting for transfers between devices, per_device(): lax.ppermute(far, 'kxy', [(0, 1), (1, 0)]).astype(jnp.float32)  27.7 us
    ppermute x15, starting transfers between devices, by_heads(): block = lax.ppermute(block, KV, [(j, j ^ shift) for j in range(n_kv)])  23.6 us
    all_to_all x1, blocking collectives, per_device(): lax.all_to_all(on_row.astype(jnp.bfloat16), 'kxx', split_axis=0, concat_a...  19.9 us
    ppermute x15, waiting for transfers between devices, by_heads(): block = lax.ppermute(block, KV, [(j, j ^ shift) for j in range(n_kv)])  18.6 us
    another operation x16, other arithmetic, by_heads(): jnp.stack((lax.dynamic_slice_in_dim(keys, dest * kv_feat, kv_feat, 1), la...  17.1 us
    another operation x16, other arithmetic, by_heads(): jnp.stack([row_first, src * key_dev, jnp.int32(rows_dev)]).astype(jnp.int32)  9.83 us
    ppermute x1, waiting for transfers between devices, per_device(): on_chip = mine + lax.ppermute(theirs, 'kc', [(0, 1), (1, 0)])  7.88 us
  transfers between devices with their start and end apart: 17, of which 7 were waited for; matrix products, arithmetic and copies ran while one was open for 12% of the time, Pallas kernels for 34%

profile of v14, /device:TPU:120, one launch (start us, length us, event | category | flops | bytes accessed | tf_op | source)
XLA Modules:
  0.0 248.8 jit_solution(16999892016646205500)
XLA Ops:
  0.0 6.8 %dynamic-slice_bitcast_fusion.1 = (bf16[1,1024,128]{2,1,0:T(8,128)(2,1)}, bf16[1,1024,128]{2,1,0:T(8,128)(2,1)S(1)}, bf16[1,1024,128]{2,1,0:T(8,128)(2,1)S(1)}, ...) fusion(bf16[1024,2048]{1,0:T(8,128)(2,1)} %param.8, ...), kind=kLoop, calls=%fused_computation.27 | loop fusion | bytes 16777280 | tf_op jit(solution)/shard_map/stack | solution.py:105
  37.5 2.2 collective-permute-start.9
  42.5 3.0 %collective-permute-start.7 = (bf16[2,1024,128]{2,1,0:T(8,128)(2,1)}, bf16[2,1024,128]{2,1,0:T(8,128)(2,1)}, u32[]{:S(2)}, u32[]{:S(2)}) collective-permute-start(bf16[2,1024,128]{2,1,0:T(8,128)(2,1)} %pad_maximum_fusion.7), channel_id=1, source_target_pairs={{0,8},{1,9},{2,10},{3,11},{4,12},{5,13},{6,14},{7,15},{8,0},{9,1},... | collective-permute-start | bytes 1572872 | tf_op jit(solution)/shard_map/ppermute | solution.py:113
  46.3 3.7 %collective-permute-start.5 = (bf16[2,1024,128]{2,1,0:T(8,128)(2,1)}, bf16[2,1024,128]{2,1,0:T(8,128)(2,1)}, u32[]{:S(2)}, u32[]{:S(2)}) collective-permute-start(bf16[2,1024,128]{2,1,0:T(8,128)(2,1)} %pad_maximum_fusion.5), channel_id=1, source_target_pairs={{0,10},{1,11},{2,8},{3,9},{4,14},{5,15},{6,12},{7,13},{8,2},{9,3},... | collective-permute-start | bytes 1572872 | tf_op jit(solution)/shard_map/ppermute | solution.py:113
  52.3 2.7 %collective-permute-done.9.k_ref.v_ref = bf16[2,1024,128]{2,1,0:T(8,128)(2,1)S(1)} collective-permute-done((bf16[2,1024,128]{2,1,0:T(8,128)(2,1)}, bf16[2,1024,128]{2,1,0:T(8,128)(2,1)S(1)}, u32[]{:S(2)}, u32[]{:S(2)}) %collective-permute-start.9) | collective-permute-done | bytes 524320 | tf_op jit(solution)/shard_map/ppermute | solution.py:113
  55.0 2.5 collective-permute-start.4
  59.2 5.6 %shard_map.55 = (f32[1024,1]{1,0:T(8,128)}, f32[1024,128]{1,0:T(8,128)}) custom-call(s32[3]{0:T(128)} %pad_add_fusion.sc_ref, bf16[1024,128]{1,0:T(8,128)(2,1)} %bitcast.114, bf16[2,1024,128]{2,1,0:T(8,128)(2,1)} %pad_maximum_fusion.15.k_ref.v_ref, ...), custom_call_target="tpu_custom_call", output_to_operand_aliasing={{0}: (4, {}), {1}: (5, {})} | custom-call | flops 536870912 | bytes 1843200 | tf_op jit(solution)/shard_map/pallas_call | solution.py:74
  65.5 2.8 %collective-permute-start.3 = (bf16[2,1024,128]{2,1,0:T(8,128)(2,1)}, bf16[2,1024,128]{2,1,0:T(8,128)(2,1)}, u32[]{:S(2)}, u32[]{:S(2)}) collective-permute-start(bf16[2,1024,128]{2,1,0:T(8,128)(2,1)} %pad_maximum_fusion.3), channel_id=1, source_target_pairs={{0,12},{1,13},{2,14},{3,15},{4,8},{5,9},{6,10},{7,11},{8,4},{9,5},... | collective-permute-start | bytes 1572872 | tf_op jit(solution)/shard_map/ppermute | solution.py:113
  68.2 5.6 %shard_map.56 = (f32[1024,1]{1,0:T(8,128)}, f32[1024,128]{1,0:T(8,128)}) custom-call(s32[3]{0:T(128)} %pad_add_fusion.1.sc_ref, bf16[1024,128]{1,0:T(8,128)(2,1)} %bitcast.115, bf16[2,1024,128]{2,1,0:T(8,128)(2,1)} %collective-permute-done.14.k_ref.v_ref, ...), custom_call_target="tpu_custom_call", output_to_operand_aliasing={{0}: (4, {}), {1}: (5, {})} | custom-call | flops 536870912 | bytes 1843200 | tf_op jit(solution)/shard_map/pallas_call | solution.py:74
  73.8 4.4 %collective-permute-done.7.k_ref.v_ref = bf16[2,1024,128]{2,1,0:T(8,128)(2,1)} collective-permute-done((bf16[2,1024,128]{2,1,0:T(8,128)(2,1)}, bf16[2,1024,128]{2,1,0:T(8,128)(2,1)}, u32[]{:S(2)}, u32[]{:S(2)}) %collective-permute-start.7) | collective-permute-done | bytes 524320 | tf_op jit(solution)/shard_map/ppermute | solution.py:113
  78.2 5.6 %shard_map.57 = (f32[1024,1]{1,0:T(8,128)}, f32[1024,128]{1,0:T(8,128)}) custom-call(s32[3]{0:T(128)} %pad_add_fusion.2.sc_ref, bf16[1024,128]{1,0:T(8,128)(2,1)} %bitcast.116, bf16[2,1024,128]{2,1,0:T(8,128)(2,1)} %collective-permute-done.13.k_ref.v_ref, ...), custom_call_target="tpu_custom_call", output_to_operand_aliasing={{0}: (4, {}), {1}: (5, {})} | custom-call | flops 536870912 | bytes 1843200 | tf_op jit(solution)/shard_map/pallas_call | solution.py:74
  83.8 4.7 %collective-permute-done.6.k_ref.v_ref = bf16[2,1024,128]{2,1,0:T(8,128)(2,1)} collective-permute-done((bf16[2,1024,128]{2,1,0:T(8,128)(2,1)}, bf16[2,1024,128]{2,1,0:T(8,128)(2,1)}, u32[]{:S(2)}, u32[]{:S(2)}) %collective-permute-start.6) | collective-permute-done | bytes 524320 | tf_op jit(solution)/shard_map/ppermute | solution.py:113
  90.7 5.6 %shard_map.58 = (f32[1024,1]{1,0:T(8,128)}, f32[1024,128]{1,0:T(8,128)}) custom-call(s32[3]{0:T(128)} %pad_add_fusion.3.sc_ref, bf16[1024,128]{1,0:T(8,128)(2,1)} %bitcast.117, bf16[2,1024,128]{2,1,0:T(8,128)(2,1)} %collective-permute-done.12.k_ref.v_ref, ...), custom_call_target="tpu_custom_call", output_to_operand_aliasing={{0}: (4, {}), {1}: (5, {})} | custom-call | flops 536870912 | bytes 1843200 | tf_op jit(solution)/shard_map/pallas_call | solution.py:74
  96.3 6.1 %collective-permute-done.5.k_ref.v_ref = bf16[2,1024,128]{2,1,0:T(8,128)(2,1)} collective-permute-done((bf16[2,1024,128]{2,1,0:T(8,128)(2,1)}, bf16[2,1024,128]{2,1,0:T(8,128)(2,1)}, u32[]{:S(2)}, u32[]{:S(2)}) %collective-permute-start.5) | collective-permute-done | bytes 524320 | tf_op jit(solution)/shard_map/ppermute | solution.py:113
  102.4 5.8 %shard_map.59 = (f32[1024,1]{1,0:T(8,128)}, f32[1024,128]{1,0:T(8,128)}) custom-call(s32[3]{0:T(128)} %pad_add_fusion.4.sc_ref, bf16[1024,128]{1,0:T(8,128)(2,1)} %bitcast.118, bf16[2,1024,128]{2,1,0:T(8,128)(2,1)} %collective-permute-done.11.k_ref.v_ref, ...), custom_call_target="tpu_custom_call", output_to_operand_aliasing={{0}: (4, {}), {1}: (5, {})} | custom-call | flops 536870912 | bytes 1843200 | tf_op jit(solution)/shard_map/pallas_call | solution.py:74
  108.2 5.6 %shard_map.60 = (f32[1024,1]{1,0:T(8,128)}, f32[1024,128]{1,0:T(8,128)}) custom-call(s32[3]{0:T(128)} %pad_add_fusion.5.sc_ref, bf16[1024,128]{1,0:T(8,128)(2,1)} %bitcast.119, bf16[2,1024,128]{2,1,0:T(8,128)(2,1)} %collective-permute-done.10.k_ref.v_ref, ...), custom_call_target="tpu_custom_call", output_to_operand_aliasing={{0}: (4, {}), {1}: (5, {})} | custom-call | flops 536870912 | bytes 1843200 | tf_op jit(solution)/shard_map/pallas_call | solution.py:74
  113.8 5.6 %shard_map.61 = (f32[1024,1]{1,0:T(8,128)}, f32[1024,128]{1,0:T(8,128)}) custom-call(s32[3]{0:T(128)} %pad_add_fusion.6.sc_ref, bf16[1024,128]{1,0:T(8,128)(2,1)} %bitcast.120, bf16[2,1024,128]{2,1,0:T(8,128)(2,1)} %copy-done.14, bf16[2,1024,128]{2,1,0:T(8,128)(2,1)} %copy-done.14, ...), custom_call_target="tpu_custom_call", output_to_operand_aliasing={{0}: (4, {}), {1}: (5, {})} | custom-call | flops 536870912 | bytes 1843200 | tf_op jit(solution)/shard_map/pallas_call | solution.py:74
  119.3 5.6 %shard_map.62 = (f32[1024,1]{1,0:T(8,128)}, f32[1024,128]{1,0:T(8,128)}) custom-call(s32[3]{0:T(128)} %pad_add_fusion.7.sc_ref, bf16[1024,128]{1,0:T(8,128)(2,1)} %bitcast.121, bf16[2,1024,128]{2,1,0:T(8,128)(2,1)} %collective-permute-done.8.k_ref.v_ref, ...), custom_call_target="tpu_custom_call", output_to_operand_aliasing={{0}: (4, {}), {1}: (5, {})} | custom-call | flops 536870912 | bytes 1843200 | tf_op jit(solution)/shard_map/pallas_call | solution.py:74
  124.9 5.6 %shard_map.63 = (f32[1024,1]{1,0:T(8,128)}, f32[1024,128]{1,0:T(8,128)}) custom-call(s32[3]{0:T(128)} %pad_add_fusion.8.sc_ref, bf16[1024,128]{1,0:T(8,128)(2,1)} %bitcast.122, bf16[2,1024,128]{2,1,0:T(8,128)(2,1)} %collective-permute-done.7.k_ref.v_ref, ...), custom_call_target="tpu_custom_call", output_to_operand_aliasing={{0}: (4, {}), {1}: (5, {})} | custom-call | flops 536870912 | bytes 1843200 | tf_op jit(solution)/shard_map/pallas_call | solution.py:74
  130.5 5.6 %shard_map.64 = (f32[1024,1]{1,0:T(8,128)}, f32[1024,128]{1,0:T(8,128)}) custom-call(s32[3]{0:T(128)} %pad_add_fusion.9.sc_ref, bf16[1024,128]{1,0:T(8,128)(2,1)} %bitcast.123, bf16[2,1024,128]{2,1,0:T(8,128)(2,1)} %collective-permute-done.6.k_ref.v_ref, ...), custom_call_target="tpu_custom_call", output_to_operand_aliasing={{0}: (4, {}), {1}: (5, {})} | custom-call | flops 536870912 | bytes 1843200 | tf_op jit(solution)/shard_map/pallas_call | solution.py:74
  136.1 5.6 %shard_map.65 = (f32[1024,1]{1,0:T(8,128)}, f32[1024,128]{1,0:T(8,128)}) custom-call(s32[3]{0:T(128)} %pad_add_fusion.10.sc_ref, bf16[1024,128]{1,0:T(8,128)(2,1)} %bitcast.124, bf16[2,1024,128]{2,1,0:T(8,128)(2,1)} %collective-permute-done.5.k_ref.v_ref, ...), custom_call_target="tpu_custom_call", output_to_operand_aliasing={{0}: (4, {}), {1}: (5, {})} | custom-call | flops 536870912 | bytes 1843200 | tf_op jit(solution)/shard_map/pallas_call | solution.py:74
  141.7 5.6 %shard_map.66 = (f32[1024,1]{1,0:T(8,128)}, f32[1024,128]{1,0:T(8,128)}) custom-call(s32[3]{0:T(128)} %pad_add_fusion.11.sc_ref, bf16[1024,128]{1,0:T(8,128)(2,1)} %bitcast.125, bf16[2,1024,128]{2,1,0:T(8,128)(2,1)} %collective-permute-done.4.k_ref.v_ref, ...), custom_call_target="tpu_custom_call", output_to_operand_aliasing={{0}: (4, {}), {1}: (5, {})} | custom-call | flops 536870912 | bytes 1843200 | tf_op jit(solution)/shard_map/pallas_call | solution.py:74
  147.3 5.6 %shard_map.67 = (f32[1024,1]{1,0:T(8,128)}, f32[1024,128]{1,0:T(8,128)}) custom-call(s32[3]{0:T(128)} %pad_add_fusion.12.sc_ref, bf16[1024,128]{1,0:T(8,128)(2,1)} %bitcast.126, bf16[2,1024,128]{2,1,0:T(8,128)(2,1)} %collective-permute-done.3.k_ref.v_ref, ...), custom_call_target="tpu_custom_call", output_to_operand_aliasing={{0}: (4, {}), {1}: (5, {})} | custom-call | flops 536870912 | bytes 1843200 | tf_op jit(solution)/shard_map/pallas_call | solution.py:74
  152.9 5.7 %shard_map.68 = (f32[1024,1]{1,0:T(8,128)}, f32[1024,128]{1,0:T(8,128)}) custom-call(s32[3]{0:T(128)} %pad_add_fusion.13.sc_ref, bf16[1024,128]{1,0:T(8,128)(2,1)} %bitcast.127, bf16[2,1024,128]{2,1,0:T(8,128)(2,1)} %collective-permute-done.2.k_ref.v_ref, ...), custom_call_target="tpu_custom_call", output_to_operand_aliasing={{0}: (4, {}), {1}: (5, {})} | custom-call | flops 536870912 | bytes 1843200 | tf_op jit(solution)/shard_map/pallas_call | solution.py:74
  158.6 5.6 %shard_map.69 = (f32[1024,1]{1,0:T(8,128)}, f32[1024,128]{1,0:T(8,128)}) custom-call(s32[3]{0:T(128)} %pad_add_fusion.14.sc_ref, bf16[1024,128]{1,0:T(8,128)(2,1)} %bitcast.128, bf16[2,1024,128]{2,1,0:T(8,128)(2,1)} %collective-permute-done.1.k_ref.v_ref, ...), custom_call_target="tpu_custom_call", output_to_operand_aliasing={{0}: (4, {}), {1}: (5, {})} | custom-call | flops 536870912 | bytes 1843200 | tf_op jit(solution)/shard_map/pallas_call | solution.py:74
  164.2 5.6 %shard_map.70 = (f32[1024,1]{1,0:T(8,128)}, f32[1024,128]{1,0:T(8,128)}) custom-call(s32[3]{0:T(128)} %pad_add_fusion.15.sc_ref, bf16[1024,128]{1,0:T(8,128)(2,1)} %bitcast.129, bf16[2,1024,128]{2,1,0:T(8,128)(2,1)} %collective-permute-done.k_ref.v_ref, ...), custom_call_target="tpu_custom_call", output_to_operand_aliasing={{0}: (4, {}), {1}: (5, {})} | custom-call | flops 536870912 | bytes 1843200 | tf_op jit(solution)/shard_map/pallas_call | solution.py:74
  174.2 2.9 %dynamic-slice_bitcast_fusion = f32[8,32,4608]{2,1,0:T(8,128)} fusion(f32[8,2,32,4608]{3,2,1,0:T(8,128)S(1)} %fusion, s32[]{:T(128)S(6)} %select_n.95), kind=kLoop, calls=%fused_computation.1 | loop fusion | bytes 9437188 | tf_op jit(solution)/shard_map/jit(dynamic_index_in_dim)/squeeze | solution.py:130
  180.5 7.9 %collective-permute-done.15 = f32[8,32,4608]{2,1,0:T(8,128)} collective-permute-done((f32[8,32,4608]{2,1,0:T(8,128)}, f32[8,32,4608]{2,1,0:T(8,128)}, u32[]{:S(2)}, u32[]{:S(2)}) %collective-permute-start.15) | collective-permute-done | bytes 4718624 | tf_op jit(solution)/shard_map/ppermute | solution.py:131
  188.4 4.4 %bitcast_add_fusion = f32[8,32,4608]{2,1,0:T(8,128)S(1)} fusion(f32[8,32,4608]{2,1,0:T(8,128)} %collective-permute-done.15, f32[8,2,32,4608]{3,2,1,0:T(8,128)} %copy-done.1, s32[]{:T(128)S(6)} %select_n.94), kind=kLoop, calls=%fused_computation | loop fusion | flops 1179648 | bytes 14155780 | tf_op jit(solution)/shard_map/add | solution.py:131
  196.1 2.3 collective-permute-start.16
  198.4 27.7 %collective-permute-done.16 = bf16[4,32,4608]{2,1,0:T(8,128)(2,1)S(1)} collective-permute-done((bf16[4,32,4608]{2,1,0:T(8,128)(2,1)}, bf16[4,32,4608]{2,1,0:T(8,128)(2,1)S(1)}, u32[]{:S(2)}, u32[]{:S(2)}) %collective-permute-start.16) | collective-permute-done | bytes 1179680 | tf_op jit(solution)/shard_map/ppermute | solution.py:137
  227.9 19.9 %all_to_all.5 = bf16[4,32,4608]{2,1,0:T(8,128)(2,1)S(1)} all-to-all(bf16[4,32,4608]{2,1,0:T(8,128)(2,1)S(1)} %fusion.2), channel_id=1, replica_groups=mesh['pb'=8,'kxx'=4,'kxy'=2,'kc'=2] {'kxx'}, dimensions={0} | all-to-all | bytes 2359296 | tf_op jit(solution)/shard_map/all_to_all | solution.py:138
  (95 shorter events, 54.3 us)
Async XLA Ops:
  0.0 172.8 %copy-start = (bf16[256,4608]{1,0:T(8,128)(2,1)S(1)}, bf16[256,4608]{1,0:T(8,128)(2,1)}, u32[]{:S(2)}) copy-start(bf16[256,4608]{1,0:T(8,128)(2,1)} %param.9) | copy-start | bytes 7077892
  7.6 29.9 %collective-permute-start.14 = (bf16[2,1024,128]{2,1,0:T(8,128)(2,1)}, bf16[2,1024,128]{2,1,0:T(8,128)(2,1)}, u32[]{:S(2)}, u32[]{:S(2)}) collective-permute-start(bf16[2,1024,128]{2,1,0:T(8,128)(2,1)} %pad_maximum_fusion.14), channel_id=1, source_target_pairs={{0,1},{1,0},{2,3},{3,2},{4,5},{5,4},{6,7},{7,6},{8,9},{9,8},{10,11... | collective-permute-start | bytes 1572872 | tf_op jit(solution)/shard_map/ppermute | solution.py:113
  8.5 31.3 %collective-permute-start.13 = (bf16[2,1024,128]{2,1,0:T(8,128)(2,1)}, bf16[2,1024,128]{2,1,0:T(8,128)(2,1)}, u32[]{:S(2)}, u32[]{:S(2)}) collective-permute-start(bf16[2,1024,128]{2,1,0:T(8,128)(2,1)} %pad_maximum_fusion.13), channel_id=1, source_target_pairs={{0,2},{1,3},{2,0},{3,1},{4,6},{5,7},{6,4},{7,5},{8,10},{9,11},{10,... | collective-permute-start | bytes 1572872 | tf_op jit(solution)/shard_map/ppermute | solution.py:113
  10.6 31.9 %collective-permute-start.12 = (bf16[2,1024,128]{2,1,0:T(8,128)(2,1)}, bf16[2,1024,128]{2,1,0:T(8,128)(2,1)}, u32[]{:S(2)}, u32[]{:S(2)}) collective-permute-start(bf16[2,1024,128]{2,1,0:T(8,128)(2,1)} %pad_maximum_fusion.12), channel_id=1, source_target_pairs={{0,3},{1,2},{2,1},{3,0},{4,7},{5,6},{6,5},{7,4},{8,11},{9,10},{10,... | collective-permute-start | bytes 1572872 | tf_op jit(solution)/shard_map/ppermute | solution.py:113
  13.6 32.0 %collective-permute-start.11 = (bf16[2,1024,128]{2,1,0:T(8,128)(2,1)}, bf16[2,1024,128]{2,1,0:T(8,128)(2,1)}, u32[]{:S(2)}, u32[]{:S(2)}) collective-permute-start(bf16[2,1024,128]{2,1,0:T(8,128)(2,1)} %pad_maximum_fusion.11), channel_id=1, source_target_pairs={{0,4},{1,5},{2,6},{3,7},{4,0},{5,1},{6,2},{7,3},{8,12},{9,13},{10,... | collective-permute-start | bytes 1572872 | tf_op jit(solution)/shard_map/ppermute | solution.py:113
  15.9 30.4 %collective-permute-start.10 = (bf16[2,1024,128]{2,1,0:T(8,128)(2,1)}, bf16[2,1024,128]{2,1,0:T(8,128)(2,1)}, u32[]{:S(2)}, u32[]{:S(2)}) collective-permute-start(bf16[2,1024,128]{2,1,0:T(8,128)(2,1)} %pad_maximum_fusion.10), channel_id=1, source_target_pairs={{0,5},{1,4},{2,7},{3,6},{4,1},{5,0},{6,3},{7,2},{8,13},{9,12},{10,... | collective-permute-start | bytes 1572872 | tf_op jit(solution)/shard_map/ppermute | solution.py:113
  16.7 13.7 %copy-start.11 = (bf16[1,1024,128]{2,1,0:T(8,128)(2,1)S(1)}, bf16[1,1024,128]{2,1,0:T(8,128)(2,1)}, u32[]{:S(2)}) copy-start(bf16[1,1024,128]{2,1,0:T(8,128)(2,1)} %get-tuple-element.93) | copy-start | bytes 786436
  16.7 13.7 %copy-start.12 = (bf16[1,1024,128]{2,1,0:T(8,128)(2,1)S(1)}, bf16[1,1024,128]{2,1,0:T(8,128)(2,1)}, u32[]{:S(2)}) copy-start(bf16[1,1024,128]{2,1,0:T(8,128)(2,1)} %get-tuple-element.108) | copy-start | bytes 786436
  16.7 14.6 %copy-start.9 = (bf16[1,1024,128]{2,1,0:T(8,128)(2,1)S(1)}, bf16[1,1024,128]{2,1,0:T(8,128)(2,1)}, u32[]{:S(2)}) copy-start(bf16[1,1024,128]{2,1,0:T(8,128)(2,1)} %get-tuple-element.94) | copy-start | bytes 786436
  16.7 14.6 %copy-start.10 = (bf16[1,1024,128]{2,1,0:T(8,128)(2,1)S(1)}, bf16[1,1024,128]{2,1,0:T(8,128)(2,1)}, u32[]{:S(2)}) copy-start(bf16[1,1024,128]{2,1,0:T(8,128)(2,1)} %get-tuple-element.107) | copy-start | bytes 786436
  16.7 15.4 %copy-start.7 = (bf16[1,1024,128]{2,1,0:T(8,128)(2,1)S(1)}, bf16[1,1024,128]{2,1,0:T(8,128)(2,1)}, u32[]{:S(2)}) copy-start(bf16[1,1024,128]{2,1,0:T(8,128)(2,1)} %get-tuple-element.95) | copy-start | bytes 786436
  16.7 15.4 %copy-start.8 = (bf16[1,1024,128]{2,1,0:T(8,128)(2,1)S(1)}, bf16[1,1024,128]{2,1,0:T(8,128)(2,1)}, u32[]{:S(2)}) copy-start(bf16[1,1024,128]{2,1,0:T(8,128)(2,1)} %get-tuple-element.106) | copy-start | bytes 786436
  16.7 16.3 %copy-start.5 = (bf16[1,1024,128]{2,1,0:T(8,128)(2,1)S(1)}, bf16[1,1024,128]{2,1,0:T(8,128)(2,1)}, u32[]{:S(2)}) copy-start(bf16[1,1024,128]{2,1,0:T(8,128)(2,1)} %get-tuple-element.96) | copy-start | bytes 786436
  16.8 16.3 %copy-start.6 = (bf16[1,1024,128]{2,1,0:T(8,128)(2,1)S(1)}, bf16[1,1024,128]{2,1,0:T(8,128)(2,1)}, u32[]{:S(2)}) copy-start(bf16[1,1024,128]{2,1,0:T(8,128)(2,1)} %get-tuple-element.105) | copy-start | bytes 786436
  22.8 11.1 %copy-start.3 = (bf16[1,1024,128]{2,1,0:T(8,128)(2,1)S(1)}, bf16[1,1024,128]{2,1,0:T(8,128)(2,1)}, u32[]{:S(2)}) copy-start(bf16[1,1024,128]{2,1,0:T(8,128)(2,1)} %get-tuple-element.97) | copy-start | bytes 786436
  22.8 11.1 %copy-start.4 = (bf16[1,1024,128]{2,1,0:T(8,128)(2,1)S(1)}, bf16[1,1024,128]{2,1,0:T(8,128)(2,1)}, u32[]{:S(2)}) copy-start(bf16[1,1024,128]{2,1,0:T(8,128)(2,1)} %get-tuple-element.104) | copy-start | bytes 786436
  37.5 17.5 %collective-permute-start.9 = (bf16[2,1024,128]{2,1,0:T(8,128)(2,1)}, bf16[2,1024,128]{2,1,0:T(8,128)(2,1)S(1)}, u32[]{:S(2)}, u32[]{:S(2)}) collective-permute-start(bf16[2,1024,128]{2,1,0:T(8,128)(2,1)} %pad_maximum_fusion.9), channel_id=1, source_target_pairs={{0,6},{1,7},{2,4},{3,5},{4,2},{5,3},{6,0},{7,1},{8,14},{9,15},{10,... | collective-permute-start | bytes 1572872 | tf_op jit(solution)/shard_map/ppermute | solution.py:113
  39.8 25.7 %collective-permute-start.8 = (bf16[2,1024,128]{2,1,0:T(8,128)(2,1)}, bf16[2,1024,128]{2,1,0:T(8,128)(2,1)}, u32[]{:S(2)}, u32[]{:S(2)}) collective-permute-start(bf16[2,1024,128]{2,1,0:T(8,128)(2,1)} %pad_maximum_fusion.8), channel_id=1, source_target_pairs={{0,7},{1,6},{2,5},{3,4},{4,3},{5,2},{6,1},{7,0},{8,15},{9,14},{10,... | collective-permute-start | bytes 1572872 | tf_op jit(solution)/shard_map/ppermute | solution.py:113
  42.5 35.7 %collective-permute-start.7 = (bf16[2,1024,128]{2,1,0:T(8,128)(2,1)}, bf16[2,1024,128]{2,1,0:T(8,128)(2,1)}, u32[]{:S(2)}, u32[]{:S(2)}) collective-permute-start(bf16[2,1024,128]{2,1,0:T(8,128)(2,1)} %pad_maximum_fusion.7), channel_id=1, source_target_pairs={{0,8},{1,9},{2,10},{3,11},{4,12},{5,13},{6,14},{7,15},{8,0},{9,1},... | collective-permute-start | bytes 1572872 | tf_op jit(solution)/shard_map/ppermute | solution.py:113
  45.5 42.9 %collective-permute-start.6 = (bf16[2,1024,128]{2,1,0:T(8,128)(2,1)}, bf16[2,1024,128]{2,1,0:T(8,128)(2,1)}, u32[]{:S(2)}, u32[]{:S(2)}) collective-permute-start(bf16[2,1024,128]{2,1,0:T(8,128)(2,1)} %pad_maximum_fusion.6), channel_id=1, source_target_pairs={{0,9},{1,8},{2,11},{3,10},{4,13},{5,12},{6,15},{7,14},{8,1},{9,0},... | collective-permute-start | bytes 1572872 | tf_op jit(solution)/shard_map/ppermute | solution.py:113
  46.3 56.1 %collective-permute-start.5 = (bf16[2,1024,128]{2,1,0:T(8,128)(2,1)}, bf16[2,1024,128]{2,1,0:T(8,128)(2,1)}, u32[]{:S(2)}, u32[]{:S(2)}) collective-permute-start(bf16[2,1024,128]{2,1,0:T(8,128)(2,1)} %pad_maximum_fusion.5), channel_id=1, source_target_pairs={{0,10},{1,11},{2,8},{3,9},{4,14},{5,15},{6,12},{7,13},{8,2},{9,3},... | collective-permute-start | bytes 1572872 | tf_op jit(solution)/shard_map/ppermute | solution.py:113
  55.0 2.5 %copy-start.14 = (bf16[2,1024,128]{2,1,0:T(8,128)(2,1)}, bf16[2,1024,128]{2,1,0:T(8,128)(2,1)S(1)}, u32[]{:S(2)}) copy-start(bf16[2,1024,128]{2,1,0:T(8,128)(2,1)S(1)} %collective-permute-done.9.k_ref.v_ref) | copy-start | bytes 1572868
  55.0 86.7 %collective-permute-start.4 = (bf16[2,1024,128]{2,1,0:T(8,128)(2,1)}, bf16[2,1024,128]{2,1,0:T(8,128)(2,1)}, u32[]{:S(2)}, u32[]{:S(2)}) collective-permute-start(bf16[2,1024,128]{2,1,0:T(8,128)(2,1)} %pad_maximum_fusion.4), channel_id=1, source_target_pairs={{0,11},{1,10},{2,9},{3,8},{4,15},{5,14},{6,13},{7,12},{8,3},{9,2},... | collective-permute-start | bytes 1572872 | tf_op jit(solution)/shard_map/ppermute | solution.py:113
  58.3 19.8 %copy-start.13 = (bf16[2,1024,128]{2,1,0:T(8,128)(2,1)S(1)}, bf16[2,1024,128]{2,1,0:T(8,128)(2,1)}, u32[]{:S(2)}) copy-start(bf16[2,1024,128]{2,1,0:T(8,128)(2,1)} %pad_maximum_fusion.2) | copy-start | bytes 1572868
  65.5 81.9 %collective-permute-start.3 = (bf16[2,1024,128]{2,1,0:T(8,128)(2,1)}, bf16[2,1024,128]{2,1,0:T(8,128)(2,1)}, u32[]{:S(2)}, u32[]{:S(2)}) collective-permute-start(bf16[2,1024,128]{2,1,0:T(8,128)(2,1)} %pad_maximum_fusion.3), channel_id=1, source_target_pairs={{0,12},{1,13},{2,14},{3,15},{4,8},{5,9},{6,10},{7,11},{8,4},{9,5},... | collective-permute-start | bytes 1572872 | tf_op jit(solution)/shard_map/ppermute | solution.py:113
  78.2 74.8 %collective-permute-start.2 = (bf16[2,1024,128]{2,1,0:T(8,128)(2,1)S(1)}, bf16[2,1024,128]{2,1,0:T(8,128)(2,1)}, u32[]{:S(2)}, u32[]{:S(2)}) collective-permute-start(bf16[2,1024,128]{2,1,0:T(8,128)(2,1)S(1)} %copy-done.13), channel_id=1, source_target_pairs={{0,13},{1,12},{2,15},{3,14},{4,9},{5,8},{6,11},{7,10},{8,5},{9,4},... | collective-permute-start | bytes 1572872 | tf_op jit(solution)/shard_map/ppermute | solution.py:113
  88.5 70.1 %collective-permute-start.1 = (bf16[2,1024,128]{2,1,0:T(8,128)(2,1)}, bf16[2,1024,128]{2,1,0:T(8,128)(2,1)}, u32[]{:S(2)}, u32[]{:S(2)}) collective-permute-start(bf16[2,1024,128]{2,1,0:T(8,128)(2,1)} %pad_maximum_fusion.1), channel_id=1, source_target_pairs={{0,14},{1,15},{2,12},{3,13},{4,10},{5,11},{6,8},{7,9},{8,6},{9,7},... | collective-permute-start | bytes 1572872 | tf_op jit(solution)/shard_map/ppermute | solution.py:113
  102.4 61.8 %collective-permute-start = (bf16[2,1024,128]{2,1,0:T(8,128)(2,1)S(1)}, bf16[2,1024,128]{2,1,0:T(8,128)(2,1)}, u32[]{:S(2)}, u32[]{:S(2)}) collective-permute-start(bf16[2,1024,128]{2,1,0:T(8,128)(2,1)S(1)} %pad_maximum_fusion), channel_id=1, source_target_pairs={{0,15},{1,14},{2,13},{3,12},{4,11},{5,10},{6,9},{7,8},{8,7},{9,6},... | collective-permute-start | bytes 1572872 | tf_op jit(solution)/shard_map/ppermute | solution.py:113
  174.2 5.0 %copy-start.1 = (f32[8,2,32,4608]{3,2,1,0:T(8,128)}, f32[8,2,32,4608]{3,2,1,0:T(8,128)S(1)}, u32[]{:S(2)}) copy-start(f32[8,2,32,4608]{3,2,1,0:T(8,128)S(1)} %fusion) | copy-start | bytes 28311556
  179.2 9.1 %collective-permute-start.15 = (f32[8,32,4608]{2,1,0:T(8,128)}, f32[8,32,4608]{2,1,0:T(8,128)}, u32[]{:S(2)}, u32[]{:S(2)}) collective-permute-start(f32[8,32,4608]{2,1,0:T(8,128)} %dynamic-slice_bitcast_fusion), channel_id=1, source_target_pairs={{0,1},{1,0},{2,3},{3,2},{4,5},{5,4},{6,7},{7,6},{8,9},{9,8},{10,11... | collective-permute-start | bytes 14155784 | tf_op jit(solution)/shard_map/ppermute | solution.py:131
  192.7 2.1 copy-start.2
  196.1 30.0 %collective-permute-start.16 = (bf16[4,32,4608]{2,1,0:T(8,128)(2,1)}, bf16[4,32,4608]{2,1,0:T(8,128)(2,1)S(1)}, u32[]{:S(2)}, u32[]{:S(2)}) collective-permute-start(bf16[4,32,4608]{2,1,0:T(8,128)(2,1)} %fusion.3), channel_id=1, source_target_pairs={{0,2},{2,0},{1,3},{3,1},{4,6},{6,4},{5,7},{7,5},{8,10},{10,8},{9,1... | collective-permute-start | bytes 3538952 | tf_op jit(solution)/shard_map/ppermute | solution.py:137

commit v15 on v6

--- a/solution.py
+++ b/solution.py
@@ -100,16 +100,20 @@
     q_block = queries.reshape(rows_dev, kv_local * group, HD).transpose(1, 0, 2).reshape(n_q, HD)
     total = jnp.zeros((n_q, 1), jnp.float32)
     summed = jnp.zeros((n_q, HD), jnp.float32)
-    table = jnp.stack(
-        (keys.reshape(key_dev, n_kv, kv_feat), values.reshape(key_dev, n_kv, kv_feat)), axis=0
-    ).transpose(2, 0, 1, 3)
     sources = me ^ jnp.arange(n_kv, dtype=jnp.int32)
     scalars = jnp.concatenate([row_first[None], sources * key_dev]).astype(jnp.int32)
     for shift in range(n_kv):
-        block = lax.dynamic_index_in_dim(table, me ^ shift, 0, keepdims=False)
+        dest = me ^ shift
+        src = dest
+        block = jnp.stack(
+            (
+                lax.dynamic_slice_in_dim(keys, dest * kv_feat, kv_feat, 1),
+                lax.dynamic_slice_in_dim(values, dest * kv_feat, kv_feat, 1),
+            ),
+            axis=0,
+        )
         if shift:
             block = lax.ppermute(block, KV, [(j, j ^ shift) for j in range(n_kv)])
-        block = block.reshape(2, key_dev, kv_feat)
         total, summed = attend_kernel(scalars, shift, rows_dev, q_block, block, total, summed)
     mixed = (summed / total).astype(jnp.bfloat16)
     return mixed.reshape(kv_local * group, rows_dev, HD).transpose(1, 0, 2).reshape(rows_dev, n_q // rows_dev * HD)

time: 239 us -> 229 us (0.958); the launches traced: 239 us -> 226 us
  local copies, waits for them, and re-layouts: 31.7 us -> 14.3 us
  other arithmetic: 8.51 us -> 17.3 us
  waiting for transfers between devices: 46.9 us -> 41.9 us
  Pallas kernels: 86.6 us -> 82.9 us
  starting transfers between devices: 24.1 us -> 27.6 us
    unnamed x17 -> x12, local copies, waits for them, and re-layouts: 13.3 us -> 2.26 us
    another operation x0 -> x16, other arithmetic: none -> 8.79 us  [by_heads(): jnp.stack((lax.dynamic_slice_in_dim(keys, dest * kv_feat, kv_feat, 1), la...]
    squeeze x1 -> x0, local copies, waits for them, and re-layouts: 6.51 us -> none  [by_heads(): block = lax.dynamic_index_in_dim(table, me ^ shift, 0, keepdims=False)]
    ppermute x15, waiting for transfers between devices: 39.1 us -> 34 us  [by_heads(): block = lax.ppermute(block, KV, [(j, j ^ shift) for j in range(n_kv)])]
    ppermute x15, starting transfers between devices: 22.4 us -> 26.2 us  [by_heads(): block = lax.ppermute(block, KV, [(j, j ^ shift) for j in range(n_kv)])]
    pallas_call x16, Pallas kernels: 86.6 us -> 82.9 us  [attend_kernel(): pl.pallas_call(functools.partial(block_kernel, slot=slot, rows=rows), gri...]
  transfers between devices with their start and end apart: 16 -> 16, of which waited for: 7 -> 5; matrix products, arithmetic and copies ran while one was open for 2% -> 6% of each run, Pallas kernels for 34% -> 35%
where the time goes in v15:
time: 229 us; the launch traced here: 226 us
  Pallas kernels  82.9 us (36%)
  waiting for transfers between devices  41.9 us (18%)
  blocking collectives  39.9 us (17%)
  starting transfers between devices  27.6 us (12%)
  other arithmetic  17.3 us (8%)
  local copies, waits for them, and re-layouts  14.3 us (6%)
    pallas_call x16, Pallas kernels, attend_kernel(): pl.pallas_call(functools.partial(block_kernel, slot=slot, rows=rows), gri...  82.9 us
    all_to_all x1, blocking collectives, per_device(): lax.all_to_all(on_chip.astype(jnp.bfloat16), 'kx', split_axis=0, concat_a...  39.9 us
    ppermute x15, waiting for transfers between devices, by_heads(): block = lax.ppermute(block, KV, [(j, j ^ shift) for j in range(n_kv)])  34 us
    ppermute x15, starting transfers between devices, by_heads(): block = lax.ppermute(block, KV, [(j, j ^ shift) for j in range(n_kv)])  26.2 us
    another operation x16, other arithmetic, by_heads(): jnp.stack((lax.dynamic_slice_in_dim(keys, dest * kv_feat, kv_feat, 1), la...  8.79 us
    ppermute x1, waiting for transfers between devices, per_device(): on_chip = mine + lax.ppermute(theirs, 'kc', [(0, 1), (1, 0)])  7.88 us
    another operation x1, local copies, waits for them, and re-layouts, by_heads(): jnp.stack((lax.dynamic_slice_in_dim(keys, dest * kv_feat, kv_feat, 1), la...  5.44 us
  transfers between devices with their start and end apart: 16, of which 5 were waited for; matrix products, arithmetic and copies ran while one was open for 6% of the time, Pallas kernels for 35%

profile of v15, /device:TPU:120, one launch (start us, length us, event | category | flops | bytes accessed | tf_op | source)
XLA Modules:
  0.0 226.1 jit_solution(182431654889986744)
XLA Ops:
  0.0 5.4 %dynamic-slice_bitcast_fusion.1 = (bf16[1,1024,128]{2,1,0:T(8,128)(2,1)S(1)}, bf16[1,1024,128]{2,1,0:T(8,128)(2,1)S(1)}, bf16[1,1024,128]{2,1,0:T(8,128)(2,1)S(1...) fusion(bf16[1024,2048]{1,0:T(8,128)(2,1)} %param.8, ...), kind=kLoop, calls=%fused_computation.24 | loop fusion | bytes 16777280 | tf_op jit(solution)/shard_map/stack | solution.py:108
  5.7 3.8 %collective-permute-start.5 = (bf16[2,1024,128]{2,1,0:T(8,128)(2,1)S(1)}, bf16[2,1024,128]{2,1,0:T(8,128)(2,1)S(1)}, u32[]{:S(2)}, u32[]{:S(2)}) collective-permute-start(bf16[2,1024,128]{2,1,0:T(8,128)(2,1)S(1)} %pad_maximum_fusion.5), channel_id=1, source_target_pairs={{0,10},{1,11},{2,8},{3,9},{4,14},{5,15},{6,12},{7,13},{8,2},{9,3},... | collective-permute-start | bytes 1572872 | tf_op jit(solution)/shard_map/ppermute | solution.py:116
  9.9 3.1 %collective-permute-start.7 = (bf16[2,1024,128]{2,1,0:T(8,128)(2,1)S(1)}, bf16[2,1024,128]{2,1,0:T(8,128)(2,1)S(1)}, u32[]{:S(2)}, u32[]{:S(2)}) collective-permute-start(bf16[2,1024,128]{2,1,0:T(8,128)(2,1)S(1)} %pad_maximum_fusion.7), channel_id=1, source_target_pairs={{0,8},{1,9},{2,10},{3,11},{4,12},{5,13},{6,14},{7,15},{8,0},{9,1},... | collective-permute-start | bytes 1572872 | tf_op jit(solution)/shard_map/ppermute | solution.py:116
  22.8 2.2 collective-permute-start.9
  26.2 6.8 %collective-permute-done.6.k_ref.v_ref = bf16[2,1024,128]{2,1,0:T(8,128)(2,1)S(1)} collective-permute-done((bf16[2,1024,128]{2,1,0:T(8,128)(2,1)S(1)}, bf16[2,1024,128]{2,1,0:T(8,128)(2,1)S(1)}, u32[]{:S(2)}, u32[]{:S(2)}) %collective-permute-start.6) | collective-permute-done | bytes 524320 | tf_op jit(solution)/shard_map/ppermute | solution.py:116
  33.0 2.7 %collective-permute-start.12 = (bf16[2,1024,128]{2,1,0:T(8,128)(2,1)}, bf16[2,1024,128]{2,1,0:T(8,128)(2,1)}, u32[]{:S(2)}, u32[]{:S(2)}) collective-permute-start(bf16[2,1024,128]{2,1,0:T(8,128)(2,1)} %pad_maximum_fusion.12), channel_id=1, source_target_pairs={{0,3},{1,2},{2,1},{3,0},{4,7},{5,6},{6,5},{7,4},{8,11},{9,10},{10,... | collective-permute-start | bytes 1572872 | tf_op jit(solution)/shard_map/ppermute | solution.py:116
  35.7 9.5 %collective-permute-done.7.k_ref.v_ref = bf16[2,1024,128]{2,1,0:T(8,128)(2,1)S(1)} collective-permute-done((bf16[2,1024,128]{2,1,0:T(8,128)(2,1)S(1)}, bf16[2,1024,128]{2,1,0:T(8,128)(2,1)S(1)}, u32[]{:S(2)}, u32[]{:S(2)}) %collective-permute-start.7) | collective-permute-done | bytes 524320 | tf_op jit(solution)/shard_map/ppermute | solution.py:116
  45.2 2.3 %collective-permute-start.13 = (bf16[2,1024,128]{2,1,0:T(8,128)(2,1)}, bf16[2,1024,128]{2,1,0:T(8,128)(2,1)}, u32[]{:S(2)}, u32[]{:S(2)}) collective-permute-start(bf16[2,1024,128]{2,1,0:T(8,128)(2,1)} %pad_maximum_fusion.13), channel_id=1, source_target_pairs={{0,2},{1,3},{2,0},{3,1},{4,6},{5,7},{6,4},{7,5},{8,10},{9,11},{10,... | collective-permute-start | bytes 1572872 | tf_op jit(solution)/shard_map/ppermute | solution.py:116
  48.2 9.3 %collective-permute-done.8.k_ref.v_ref = bf16[2,1024,128]{2,1,0:T(8,128)(2,1)} collective-permute-done((bf16[2,1024,128]{2,1,0:T(8,128)(2,1)}, bf16[2,1024,128]{2,1,0:T(8,128)(2,1)}, u32[]{:S(2)}, u32[]{:S(2)}) %collective-permute-start.8) | collective-permute-done | bytes 524320 | tf_op jit(solution)/shard_map/ppermute | solution.py:116
  61.2 8.4 %collective-permute-done.9.k_ref.v_ref = bf16[2,1024,128]{2,1,0:T(8,128)(2,1)} collective-permute-done((bf16[2,1024,128]{2,1,0:T(8,128)(2,1)}, bf16[2,1024,128]{2,1,0:T(8,128)(2,1)}, u32[]{:S(2)}, u32[]{:S(2)}) %collective-permute-start.9) | collective-permute-done | bytes 524320 | tf_op jit(solution)/shard_map/ppermute | solution.py:116
  72.7 5.6 %shard_map.55 = (f32[1024,1]{1,0:T(8,128)}, f32[1024,128]{1,0:T(8,128)}) custom-call(s32[17]{0:T(128)} %pad_add_fusion.sc_ref, bf16[1024,128]{1,0:T(8,128)(2,1)} %bitcast.91, bf16[2,1024,128]{2,1,0:T(8,128)(2,1)} %pad_maximum_fusion.15.k_ref.v_ref, ...), custom_call_target="tpu_custom_call", output_to_operand_aliasing={{0}: (4, {}), {1}: (5, {})} | custom-call | flops 536870912 | bytes 1843200 | tf_op jit(solution)/shard_map/pallas_call | solution.py:75
  79.3 5.6 %shard_map.56 = (f32[1024,1]{1,0:T(8,128)}, f32[1024,128]{1,0:T(8,128)}) custom-call(s32[17]{0:T(128)} %pad_add_fusion.sc_ref, bf16[1024,128]{1,0:T(8,128)(2,1)} %bitcast.92, bf16[2,1024,128]{2,1,0:T(8,128)(2,1)} %copy-done.5, bf16[2,1024,128]{2,1,0:T(8,128)(2,1)} %copy-done.5, ...), custom_call_target="tpu_custom_call", output_to_operand_aliasing={{0}: (4, {}), {1}: (5, {})} | custom-call | flops 536870912 | bytes 1843200 | tf_op jit(solution)/shard_map/pallas_call | solution.py:75
  86.8 5.6 %shard_map.57 = (f32[1024,1]{1,0:T(8,128)}, f32[1024,128]{1,0:T(8,128)}) custom-call(s32[17]{0:T(128)} %pad_add_fusion.sc_ref, bf16[1024,128]{1,0:T(8,128)(2,1)} %bitcast.93, bf16[2,1024,128]{2,1,0:T(8,128)(2,1)} %collective-permute-done.13.k_ref.v_ref, ...), custom_call_target="tpu_custom_call", output_to_operand_aliasing={{0}: (4, {}), {1}: (5, {})} | custom-call | flops 536870912 | bytes 1843200 | tf_op jit(solution)/shard_map/pallas_call | solution.py:75
  92.4 2.7 %collective-permute-start.1 = (bf16[2,1024,128]{2,1,0:T(8,128)(2,1)S(1)}, bf16[2,1024,128]{2,1,0:T(8,128)(2,1)}, u32[]{:S(2)}, u32[]{:S(2)}) collective-permute-start(bf16[2,1024,128]{2,1,0:T(8,128)(2,1)S(1)} %pad_maximum_fusion.1), channel_id=1, source_target_pairs={{0,14},{1,15},{2,12},{3,13},{4,10},{5,11},{6,8},{7,9},{8,6},{9,7},... | collective-permute-start | bytes 1572872 | tf_op jit(solution)/shard_map/ppermute | solution.py:116
  95.2 5.6 %shard_map.58 = (f32[1024,1]{1,0:T(8,128)}, f32[1024,128]{1,0:T(8,128)}) custom-call(s32[17]{0:T(128)} %pad_add_fusion.sc_ref, bf16[1024,128]{1,0:T(8,128)(2,1)} %bitcast.94, bf16[2,1024,128]{2,1,0:T(8,128)(2,1)} %collective-permute-done.12.k_ref.v_ref, ...), custom_call_target="tpu_custom_call", output_to_operand_aliasing={{0}: (4, {}), {1}: (5, {})} | custom-call | flops 536870912 | bytes 1843200 | tf_op jit(solution)/shard_map/pallas_call | solution.py:75
  101.6 5.6 %shard_map.59 = (f32[1024,1]{1,0:T(8,128)}, f32[1024,128]{1,0:T(8,128)}) custom-call(s32[17]{0:T(128)} %pad_add_fusion.sc_ref, bf16[1024,128]{1,0:T(8,128)(2,1)} %bitcast.95, bf16[2,1024,128]{2,1,0:T(8,128)(2,1)} %collective-permute-done.11.k_ref.v_ref, ...), custom_call_target="tpu_custom_call", output_to_operand_aliasing={{0}: (4, {}), {1}: (5, {})} | custom-call | flops 536870912 | bytes 1843200 | tf_op jit(solution)/shard_map/pallas_call | solution.py:75
  107.2 5.6 %shard_map.60 = (f32[1024,1]{1,0:T(8,128)}, f32[1024,128]{1,0:T(8,128)}) custom-call(s32[17]{0:T(128)} %pad_add_fusion.sc_ref, bf16[1024,128]{1,0:T(8,128)(2,1)} %bitcast.96, bf16[2,1024,128]{2,1,0:T(8,128)(2,1)} %collective-permute-done.10.k_ref.v_ref, ...), custom_call_target="tpu_custom_call", output_to_operand_aliasing={{0}: (4, {}), {1}: (5, {})} | custom-call | flops 536870912 | bytes 1843200 | tf_op jit(solution)/shard_map/pallas_call | solution.py:75
  112.8 5.6 %shard_map.61 = (f32[1024,1]{1,0:T(8,128)}, f32[1024,128]{1,0:T(8,128)}) custom-call(s32[17]{0:T(128)} %pad_add_fusion.sc_ref, bf16[1024,128]{1,0:T(8,128)(2,1)} %bitcast.97, bf16[2,1024,128]{2,1,0:T(8,128)(2,1)} %collective-permute-done.9.k_ref.v_ref, ...), custom_call_target="tpu_custom_call", output_to_operand_aliasing={{0}: (4, {}), {1}: (5, {})} | custom-call | flops 536870912 | bytes 1843200 | tf_op jit(solution)/shard_map/pallas_call | solution.py:75
  118.4 5.6 %shard_map.62 = (f32[1024,1]{1,0:T(8,128)}, f32[1024,128]{1,0:T(8,128)}) custom-call(s32[17]{0:T(128)} %pad_add_fusion.sc_ref, bf16[1024,128]{1,0:T(8,128)(2,1)} %bitcast.98, bf16[2,1024,128]{2,1,0:T(8,128)(2,1)} %collective-permute-done.8.k_ref.v_ref, ...), custom_call_target="tpu_custom_call", output_to_operand_aliasing={{0}: (4, {}), {1}: (5, {})} | custom-call | flops 536870912 | bytes 1843200 | tf_op jit(solution)/shard_map/pallas_call | solution.py:75
  124.0 4.4 %shard_map.63 = (f32[1024,1]{1,0:T(8,128)}, f32[1024,128]{1,0:T(8,128)}) custom-call(s32[17]{0:T(128)} %pad_add_fusion.sc_ref, bf16[1024,128]{1,0:T(8,128)(2,1)} %bitcast.99, bf16[2,1024,128]{2,1,0:T(8,128)(2,1)} %copy-done.4, bf16[2,1024,128]{2,1,0:T(8,128)(2,1)} %copy-done.4, ...), custom_call_target="tpu_custom_call", output_to_operand_aliasing={{0}: (4, {}), {1}: (5, {})} | custom-call | flops 536870912 | bytes 1843200 | tf_op jit(solution)/shard_map/pallas_call | solution.py:75
  128.4 4.4 %shard_map.64 = (f32[1024,1]{1,0:T(8,128)}, f32[1024,128]{1,0:T(8,128)}) custom-call(s32[17]{0:T(128)} %pad_add_fusion.sc_ref, bf16[1024,128]{1,0:T(8,128)(2,1)} %bitcast.100, bf16[2,1024,128]{2,1,0:T(8,128)(2,1)} %copy-done.3, bf16[2,1024,128]{2,1,0:T(8,128)(2,1)} %copy-done.3, ...), custom_call_target="tpu_custom_call", output_to_operand_aliasing={{0}: (4, {}), {1}: (5, {})} | custom-call | flops 536870912 | bytes 1843200 | tf_op jit(solution)/shard_map/pallas_call | solution.py:75
  132.9 5.6 %shard_map.65 = (f32[1024,1]{1,0:T(8,128)}, f32[1024,128]{1,0:T(8,128)}) custom-call(s32[17]{0:T(128)} %pad_add_fusion.sc_ref, bf16[1024,128]{1,0:T(8,128)(2,1)} %bitcast.101, bf16[2,1024,128]{2,1,0:T(8,128)(2,1)} %copy-done.2, bf16[2,1024,128]{2,1,0:T(8,128)(2,1)} %copy-done.2, ...), custom_call_target="tpu_custom_call", output_to_operand_aliasing={{0}: (4, {}), {1}: (5, {})} | custom-call | flops 536870912 | bytes 1843200 | tf_op jit(solution)/shard_map/pallas_call | solution.py:75
  138.5 5.7 %shard_map.66 = (f32[1024,1]{1,0:T(8,128)}, f32[1024,128]{1,0:T(8,128)}) custom-call(s32[17]{0:T(128)} %pad_add_fusion.sc_ref, bf16[1024,128]{1,0:T(8,128)(2,1)} %bitcast.102, bf16[2,1024,128]{2,1,0:T(8,128)(2,1)} %collective-permute-done.4.k_ref.v_ref, ...), custom_call_target="tpu_custom_call", output_to_operand_aliasing={{0}: (4, {}), {1}: (5, {})} | custom-call | flops 536870912 | bytes 1843200 | tf_op jit(solution)/shard_map/pallas_call | solution.py:75
  144.2 4.4 %shard_map.67 = (f32[1024,1]{1,0:T(8,128)}, f32[1024,128]{1,0:T(8,128)}) custom-call(s32[17]{0:T(128)} %pad_add_fusion.sc_ref, bf16[1024,128]{1,0:T(8,128)(2,1)} %bitcast.103, bf16[2,1024,128]{2,1,0:T(8,128)(2,1)} %collective-permute-done.3.k_ref.v_ref, ...), custom_call_target="tpu_custom_call", output_to_operand_aliasing={{0}: (4, {}), {1}: (5, {})} | custom-call | flops 536870912 | bytes 1843200 | tf_op jit(solution)/shard_map/pallas_call | solution.py:75
  148.6 4.4 %shard_map.68 = (f32[1024,1]{1,0:T(8,128)}, f32[1024,128]{1,0:T(8,128)}) custom-call(s32[17]{0:T(128)} %pad_add_fusion.sc_ref, bf16[1024,128]{1,0:T(8,128)(2,1)} %bitcast.104, bf16[2,1024,128]{2,1,0:T(8,128)(2,1)} %collective-permute-done.2.k_ref.v_ref, ...), custom_call_target="tpu_custom_call", output_to_operand_aliasing={{0}: (4, {}), {1}: (5, {})} | custom-call | flops 536870912 | bytes 1843200 | tf_op jit(solution)/shard_map/pallas_call | solution.py:75
  153.0 4.4 %shard_map.69 = (f32[1024,1]{1,0:T(8,128)}, f32[1024,128]{1,0:T(8,128)}) custom-call(s32[17]{0:T(128)} %pad_add_fusion.sc_ref, bf16[1024,128]{1,0:T(8,128)(2,1)} %bitcast.105, bf16[2,1024,128]{2,1,0:T(8,128)(2,1)} %collective-permute-done.1.k_ref.v_ref, ...), custom_call_target="tpu_custom_call", output_to_operand_aliasing={{0}: (4, {}), {1}: (5, {})} | custom-call | flops 536870912 | bytes 1843200 | tf_op jit(solution)/shard_map/pallas_call | solution.py:75
  157.5 4.7 %shard_map.70 = (f32[1024,1]{1,0:T(8,128)}, f32[1024,128]{1,0:T(8,128)}) custom-call(s32[17]{0:T(128)} %pad_add_fusion.sc_ref, bf16[1024,128]{1,0:T(8,128)(2,1)} %bitcast.106, bf16[2,1024,128]{2,1,0:T(8,128)(2,1)} %collective-permute-done.k_ref.v_ref, ...), custom_call_target="tpu_custom_call", output_to_operand_aliasing={{0}: (4, {}), {1}: (5, {})} | custom-call | flops 536870912 | bytes 1843200 | tf_op jit(solution)/shard_map/pallas_call | solution.py:75
  166.5 2.8 %dynamic-slice_bitcast_fusion = f32[8,32,4608]{2,1,0:T(8,128)} fusion(f32[8,2,32,4608]{3,2,1,0:T(8,128)S(1)} %fusion.1, s32[]{:T(128)S(6)} %select_n.88), kind=kLoop, calls=%fused_computation.3 | loop fusion | bytes 9437188 | tf_op jit(solution)/shard_map/jit(dynamic_index_in_dim)/squeeze | solution.py:132
  169.3 2.2 copy-done.1
  172.9 7.9 %collective-permute-done.15 = f32[8,32,4608]{2,1,0:T(8,128)} collective-permute-done((f32[8,32,4608]{2,1,0:T(8,128)}, f32[8,32,4608]{2,1,0:T(8,128)}, u32[]{:S(2)}, u32[]{:S(2)}) %collective-permute-start.15) | collective-permute-done | bytes 4718624 | tf_op jit(solution)/shard_map/ppermute | solution.py:133
  180.8 4.3 %fusion = bf16[8,32,4608]{2,1,0:T(8,128)(2,1)S(1)} fusion(f32[8,32,4608]{2,1,0:T(8,128)} %collective-permute-done.15, f32[8,2,32,4608]{3,2,1,0:T(8,128)} %copy-done.1, s32[]{:T(128)S(6)} %select_n.87), kind=kLoop, calls=%fused_computation.1 | loop fusion | flops 2359296 | bytes 11796484 | tf_op jit(solution)/shard_map/convert_element_type | solution.py:135
  185.1 39.9 %all_to_all.5 = bf16[8,32,4608]{2,1,0:T(8,128)(2,1)S(1)} all-to-all(bf16[8,32,4608]{2,1,0:T(8,128)(2,1)S(1)} %fusion), channel_id=1, replica_groups=mesh['pb'=8,'kx'=8,'kc'=2] {'kx'}, dimensions={0} | all-to-all | bytes 4718592 | tf_op jit(solution)/shard_map/all_to_all | solution.py:134
  (59 shorter events, 29.1 us)
Async XLA Ops:
  0.0 165.1 %copy-start = (bf16[256,4608]{1,0:T(8,128)(2,1)S(1)}, bf16[256,4608]{1,0:T(8,128)(2,1)}, u32[]{:S(2)}) copy-start(bf16[256,4608]{1,0:T(8,128)(2,1)} %param.9) | copy-start | bytes 7077892
  5.5 17.2 %collective-permute-start.14 = (bf16[2,1024,128]{2,1,0:T(8,128)(2,1)S(1)}, bf16[2,1024,128]{2,1,0:T(8,128)(2,1)S(1)}, u32[]{:S(2)}, u32[]{:S(2)}) collective-permute-start(bf16[2,1024,128]{2,1,0:T(8,128)(2,1)S(1)} %pad_maximum_fusion.14), channel_id=1, source_target_pairs={{0,1},{1,0},{2,3},{3,2},{4,5},{5,4},{6,7},{7,6},{8,9},{9,8},{10,11... | collective-permute-start | bytes 1572872 | tf_op jit(solution)/shard_map/ppermute | solution.py:116
  5.7 19.3 %collective-permute-start.5 = (bf16[2,1024,128]{2,1,0:T(8,128)(2,1)S(1)}, bf16[2,1024,128]{2,1,0:T(8,128)(2,1)S(1)}, u32[]{:S(2)}, u32[]{:S(2)}) collective-permute-start(bf16[2,1024,128]{2,1,0:T(8,128)(2,1)S(1)} %pad_maximum_fusion.5), channel_id=1, source_target_pairs={{0,10},{1,11},{2,8},{3,9},{4,14},{5,15},{6,12},{7,13},{8,2},{9,3},... | collective-permute-start | bytes 1572872 | tf_op jit(solution)/shard_map/ppermute | solution.py:116
  9.5 23.5 %collective-permute-start.6 = (bf16[2,1024,128]{2,1,0:T(8,128)(2,1)S(1)}, bf16[2,1024,128]{2,1,0:T(8,128)(2,1)S(1)}, u32[]{:S(2)}, u32[]{:S(2)}) collective-permute-start(bf16[2,1024,128]{2,1,0:T(8,128)(2,1)S(1)} %pad_maximum_fusion.6), channel_id=1, source_target_pairs={{0,9},{1,8},{2,11},{3,10},{4,13},{5,12},{6,15},{7,14},{8,1},{9,0},... | collective-permute-start | bytes 1572872 | tf_op jit(solution)/shard_map/ppermute | solution.py:116
  9.9 35.2 %collective-permute-start.7 = (bf16[2,1024,128]{2,1,0:T(8,128)(2,1)S(1)}, bf16[2,1024,128]{2,1,0:T(8,128)(2,1)S(1)}, u32[]{:S(2)}, u32[]{:S(2)}) collective-permute-start(bf16[2,1024,128]{2,1,0:T(8,128)(2,1)S(1)} %pad_maximum_fusion.7), channel_id=1, source_target_pairs={{0,8},{1,9},{2,10},{3,11},{4,12},{5,13},{6,14},{7,15},{8,0},{9,1},... | collective-permute-start | bytes 1572872 | tf_op jit(solution)/shard_map/ppermute | solution.py:116
  13.9 43.6 %collective-permute-start.8 = (bf16[2,1024,128]{2,1,0:T(8,128)(2,1)}, bf16[2,1024,128]{2,1,0:T(8,128)(2,1)}, u32[]{:S(2)}, u32[]{:S(2)}) collective-permute-start(bf16[2,1024,128]{2,1,0:T(8,128)(2,1)} %pad_maximum_fusion.8), channel_id=1, source_target_pairs={{0,7},{1,6},{2,5},{3,4},{4,3},{5,2},{6,1},{7,0},{8,15},{9,14},{10,... | collective-permute-start | bytes 1572872 | tf_op jit(solution)/shard_map/ppermute | solution.py:116
  22.8 24.7 %copy-start.5 = (bf16[2,1024,128]{2,1,0:T(8,128)(2,1)}, bf16[2,1024,128]{2,1,0:T(8,128)(2,1)S(1)}, u32[]{:S(2)}) copy-start(bf16[2,1024,128]{2,1,0:T(8,128)(2,1)S(1)} %collective-permute-done.14.k_ref.v_ref) | copy-start | bytes 1572868
  22.8 46.9 %collective-permute-start.9 = (bf16[2,1024,128]{2,1,0:T(8,128)(2,1)}, bf16[2,1024,128]{2,1,0:T(8,128)(2,1)}, u32[]{:S(2)}, u32[]{:S(2)}) collective-permute-start(bf16[2,1024,128]{2,1,0:T(8,128)(2,1)} %pad_maximum_fusion.9), channel_id=1, source_target_pairs={{0,6},{1,7},{2,4},{3,5},{4,2},{5,3},{6,0},{7,1},{8,14},{9,15},{10,... | collective-permute-start | bytes 1572872 | tf_op jit(solution)/shard_map/ppermute | solution.py:116
  25.0 20.2 %copy-start.2 = (bf16[2,1024,128]{2,1,0:T(8,128)(2,1)}, bf16[2,1024,128]{2,1,0:T(8,128)(2,1)S(1)}, u32[]{:S(2)}) copy-start(bf16[2,1024,128]{2,1,0:T(8,128)(2,1)S(1)} %collective-permute-done.5.k_ref.v_ref) | copy-start | bytes 1572868
  25.0 53.4 %collective-permute-start.10 = (bf16[2,1024,128]{2,1,0:T(8,128)(2,1)}, bf16[2,1024,128]{2,1,0:T(8,128)(2,1)}, u32[]{:S(2)}, u32[]{:S(2)}) collective-permute-start(bf16[2,1024,128]{2,1,0:T(8,128)(2,1)} %pad_maximum_fusion.10), channel_id=1, source_target_pairs={{0,5},{1,4},{2,7},{3,6},{4,1},{5,0},{6,3},{7,2},{8,13},{9,12},{10,... | collective-permute-start | bytes 1572872 | tf_op jit(solution)/shard_map/ppermute | solution.py:116
  33.0 14.5 %copy-start.3 = (bf16[2,1024,128]{2,1,0:T(8,128)(2,1)}, bf16[2,1024,128]{2,1,0:T(8,128)(2,1)S(1)}, u32[]{:S(2)}) copy-start(bf16[2,1024,128]{2,1,0:T(8,128)(2,1)S(1)} %collective-permute-done.6.k_ref.v_ref) | copy-start | bytes 1572868
  33.0 59.4 %collective-permute-start.12 = (bf16[2,1024,128]{2,1,0:T(8,128)(2,1)}, bf16[2,1024,128]{2,1,0:T(8,128)(2,1)}, u32[]{:S(2)}, u32[]{:S(2)}) collective-permute-start(bf16[2,1024,128]{2,1,0:T(8,128)(2,1)} %pad_maximum_fusion.12), channel_id=1, source_target_pairs={{0,3},{1,2},{2,1},{3,0},{4,7},{5,6},{6,5},{7,4},{8,11},{9,10},{10,... | collective-permute-start | bytes 1572872 | tf_op jit(solution)/shard_map/ppermute | solution.py:116
  45.2 2.3 %copy-start.4 = (bf16[2,1024,128]{2,1,0:T(8,128)(2,1)}, bf16[2,1024,128]{2,1,0:T(8,128)(2,1)S(1)}, u32[]{:S(2)}) copy-start(bf16[2,1024,128]{2,1,0:T(8,128)(2,1)S(1)} %collective-permute-done.7.k_ref.v_ref) | copy-start | bytes 1572868
  45.2 39.8 %collective-permute-start.13 = (bf16[2,1024,128]{2,1,0:T(8,128)(2,1)}, bf16[2,1024,128]{2,1,0:T(8,128)(2,1)}, u32[]{:S(2)}, u32[]{:S(2)}) collective-permute-start(bf16[2,1024,128]{2,1,0:T(8,128)(2,1)} %pad_maximum_fusion.13), channel_id=1, source_target_pairs={{0,2},{1,3},{2,0},{3,1},{4,6},{5,7},{6,4},{7,5},{8,10},{9,11},{10,... | collective-permute-start | bytes 1572872 | tf_op jit(solution)/shard_map/ppermute | solution.py:116
  57.5 43.3 %collective-permute-start.11 = (bf16[2,1024,128]{2,1,0:T(8,128)(2,1)}, bf16[2,1024,128]{2,1,0:T(8,128)(2,1)}, u32[]{:S(2)}, u32[]{:S(2)}) collective-permute-start(bf16[2,1024,128]{2,1,0:T(8,128)(2,1)} %pad_maximum_fusion.11), channel_id=1, source_target_pairs={{0,4},{1,5},{2,6},{3,7},{4,0},{5,1},{6,2},{7,3},{8,12},{9,13},{10,... | collective-permute-start | bytes 1572872 | tf_op jit(solution)/shard_map/ppermute | solution.py:116
  69.6 68.9 %collective-permute-start.4 = (bf16[2,1024,128]{2,1,0:T(8,128)(2,1)}, bf16[2,1024,128]{2,1,0:T(8,128)(2,1)}, u32[]{:S(2)}, u32[]{:S(2)}) collective-permute-start(bf16[2,1024,128]{2,1,0:T(8,128)(2,1)} %pad_maximum_fusion.4), channel_id=1, source_target_pairs={{0,11},{1,10},{2,9},{3,8},{4,15},{5,14},{6,13},{7,12},{8,3},{9,2},... | collective-permute-start | bytes 1572872 | tf_op jit(solution)/shard_map/ppermute | solution.py:116
  78.3 65.8 %collective-permute-start.3 = (bf16[2,1024,128]{2,1,0:T(8,128)(2,1)}, bf16[2,1024,128]{2,1,0:T(8,128)(2,1)}, u32[]{:S(2)}, u32[]{:S(2)}) collective-permute-start(bf16[2,1024,128]{2,1,0:T(8,128)(2,1)} %pad_maximum_fusion.3), channel_id=1, source_target_pairs={{0,12},{1,13},{2,14},{3,15},{4,8},{5,9},{6,10},{7,11},{8,4},{9,5},... | collective-permute-start | bytes 1572872 | tf_op jit(solution)/shard_map/ppermute | solution.py:116
  84.9 63.6 %collective-permute-start.2 = (bf16[2,1024,128]{2,1,0:T(8,128)(2,1)S(1)}, bf16[2,1024,128]{2,1,0:T(8,128)(2,1)}, u32[]{:S(2)}, u32[]{:S(2)}) collective-permute-start(bf16[2,1024,128]{2,1,0:T(8,128)(2,1)S(1)} %pad_maximum_fusion.2), channel_id=1, source_target_pairs={{0,13},{1,12},{2,15},{3,14},{4,9},{5,8},{6,11},{7,10},{8,5},{9,4},... | collective-permute-start | bytes 1572872 | tf_op jit(solution)/shard_map/ppermute | solution.py:116
  92.4 60.6 %collective-permute-start.1 = (bf16[2,1024,128]{2,1,0:T(8,128)(2,1)S(1)}, bf16[2,1024,128]{2,1,0:T(8,128)(2,1)}, u32[]{:S(2)}, u32[]{:S(2)}) collective-permute-start(bf16[2,1024,128]{2,1,0:T(8,128)(2,1)S(1)} %pad_maximum_fusion.1), channel_id=1, source_target_pairs={{0,14},{1,15},{2,12},{3,13},{4,10},{5,11},{6,8},{7,9},{8,6},{9,7},... | collective-permute-start | bytes 1572872 | tf_op jit(solution)/shard_map/ppermute | solution.py:116
  100.8 56.7 %collective-permute-start = (bf16[2,1024,128]{2,1,0:T(8,128)(2,1)}, bf16[2,1024,128]{2,1,0:T(8,128)(2,1)}, u32[]{:S(2)}, u32[]{:S(2)}) collective-permute-start(bf16[2,1024,128]{2,1,0:T(8,128)(2,1)} %pad_maximum_fusion), channel_id=1, source_target_pairs={{0,15},{1,14},{2,13},{3,12},{4,11},{5,10},{6,9},{7,8},{8,7},{9,6},... | collective-permute-start | bytes 1572872 | tf_op jit(solution)/shard_map/ppermute | solution.py:116
  166.5 5.1 %copy-start.1 = (f32[8,2,32,4608]{3,2,1,0:T(8,128)}, f32[8,2,32,4608]{3,2,1,0:T(8,128)S(1)}, u32[]{:S(2)}) copy-start(f32[8,2,32,4608]{3,2,1,0:T(8,128)S(1)} %fusion.1) | copy-start | bytes 28311556
  171.6 9.2 %collective-permute-start.15 = (f32[8,32,4608]{2,1,0:T(8,128)}, f32[8,32,4608]{2,1,0:T(8,128)}, u32[]{:S(2)}, u32[]{:S(2)}) collective-permute-start(f32[8,32,4608]{2,1,0:T(8,128)} %dynamic-slice_bitcast_fusion), channel_id=1, source_target_pairs={{0,1},{1,0},{2,3},{3,2},{4,5},{5,4},{6,7},{7,6},{8,9},{9,8},{10,11... | collective-permute-start | bytes 14155784 | tf_op jit(solution)/shard_map/ppermute | solution.py:133
